TPU v7x, 32 devices: a whole 2x2x4 slice. The times are simulated.
32 devices in a mesh: dp: 8 (over z, x), head: 4 (over y, core).
Axes of the slice: x: 2, y: 2, z: 4, core: 2. Of those that a mesh axis runs over, the one named last changes fastest.
Arguments:
- tokens: bfloat16 [8192, 1024], P(('dp', 'head'))
- doc_ids: int32 [8, 1024], P('dp'), may hold values from 0 to 7, never falling along the last dimension, each value on 1 to 512 neighbouring positions
- gain_attn: float32 [1024], replicated, may hold values from 0.1 to 1.9
- a_weight: bfloat16 [1024, 160], P(None, 'head'), may hold values from -0.4375 to 0.4375
- b_weight: bfloat16 [1024, 640], replicated, may hold values from -0.1875 to 0.1875
- out_weight: bfloat16 [1024, 1024], P('head'), may hold values from -0.5 to 0.5
- gain_ffn: float32 [1024], replicated, may hold values from 0.1 to 1.9
- gate_weight: bfloat16 [1024, 2816], P(None, 'head'), may hold values from -0.1875 to 0.1875
- up_weight: bfloat16 [1024, 2816], P(None, 'head'), may hold values from -0.1875 to 0.1875
- down_weight: bfloat16 [2816, 1024], P('head'), may hold values from -0.109375 to 0.109375
- cotangent: bfloat16 [8192, 1024], P(('dp', 'head'))
Outputs:
- output: bfloat16 [8192, 1024], P(('dp', 'head'))
- input_grad: float32 [8192, 1024], P(('dp', 'head'))
- grad_gain_attn: float32 [1024], replicated
- grad_a: float32 [1024, 160], P(None, 'head')
- grad_b: float32 [1024, 640], replicated
- grad_out: float32 [1024, 1024], P('head')
- grad_gain_ffn: float32 [1024], replicated
- grad_gate: float32 [1024, 2816], P(None, 'head')
- grad_up: float32 [1024, 2816], P(None, 'head')
- grad_down: float32 [2816, 1024], P('head')
Inputs may be any that keep to these rules, and one draw needn't show every extreme that they name: `doc_ids`: within a row the document number never falls; a document holds 1 to 512 positions.
All inputs are finite; a program needn't handle non-finite values.
Results may differ from a plain program's by a relative error of at most 0.019.
The roundings to bfloat16 on the way count: a program that leaves them out, or rounds other values in their place, can miss the bound.
Values may be sent and summed in bfloat16 or wider, within the bound.
No kernel may reach another device: no remote copies, remote signals or barrier semaphores. Data moves between devices by JAX's collectives and lax.ppermute only.
A program may use at most 192 MiB of HBM per device.

v0:
```python
import math

import jax
import jax.numpy as jnp
from jax import lax
from jax.sharding import PartitionSpec as P

DH = 64
RQ = 6
RK = 2


EPSILON = 1e-06
MASKED = -1e30
PRECISE = lax.Precision.HIGHEST


def rope_tables(total_rows, length):
    half_depth = DH // 2
    position = (jnp.arange(total_rows, dtype=jnp.int32) % length).astype(jnp.float32)
    frequency = jnp.exp(jnp.arange(half_depth, dtype=jnp.float32) * (-2.0 * math.log(10000.0) / DH))
    angle = position[:, None] * frequency[None, :]
    return (jnp.cos(angle), jnp.sin(angle))


def rotate(basis, cosine, sine):
    half_depth = basis.shape[-1] // 2
    first_half = basis[..., :half_depth]
    second_half = basis[..., half_depth:]
    cosine_row = cosine[:, None, :]
    sine_row = sine[:, None, :]
    return jnp.concatenate(
        [
            first_half * cosine_row - second_half * sine_row,
            second_half * cosine_row + first_half * sine_row,
        ],
        axis=-1,
    )


def unrotate(grad_basis, cosine, sine):
    half_depth = grad_basis.shape[-1] // 2
    first_half = grad_basis[..., :half_depth]
    second_half = grad_basis[..., half_depth:]
    cosine_row = cosine[:, None, :]
    sine_row = sine[:, None, :]
    return jnp.concatenate(
        [
            first_half * cosine_row + second_half * sine_row,
            second_half * cosine_row - first_half * sine_row,
        ],
        axis=-1,
    )


def dot_last(left, right):
    return lax.dot_general(
        left, right, (((1,), (1,)), ((), ())), preferred_element_type=jnp.float32
    )


def dot_first(left, right):
    return lax.dot_general(
        left, right, (((0,), (0,)), ((), ())), preferred_element_type=jnp.float32
    )


def norm_backward(inputs, inverse, gain, grad_normed):
    scaled = gain * grad_normed
    inner = jnp.mean(scaled * inputs, axis=-1, keepdims=True)
    grad_inputs = inverse * scaled - inputs * (inverse * inverse * inverse) * inner
    grad_gain = jnp.sum(grad_normed * inputs * inverse, axis=0)
    return (grad_inputs, grad_gain)


def block_scores(queries, key_rows, doc_row, first_row, last_row):
    position = jnp.arange(last_row, dtype=jnp.int32)
    allowed = (doc_row[first_row:last_row, None] == doc_row[None, :last_row]) & (
        position[None, :] <= position[first_row:last_row, None]
    )
    score_scale = 1.0 / math.sqrt(queries.shape[2])
    scores = (
        jnp.einsum(
            "qhd,khd->hqk",
            queries[first_row:last_row],
            key_rows[:last_row],
            preferred_element_type=jnp.float32,
        )
        * score_scale
    )
    return jnp.where(allowed[None], scores, MASKED)


def attend_row(row_item):
    queries, key_rows, value_rows, doc_row = row_item
    length = queries.shape[0]
    block_rows = min(512, length)
    mixed_parts = []
    total_parts = []
    for first_row in range(0, length, block_rows):
        last_row = first_row + block_rows
        scores = block_scores(queries, key_rows, doc_row, first_row, last_row)
        row_peak = jnp.max(scores, axis=-1, keepdims=True)
        exponent = jnp.exp(scores - row_peak)
        row_total = jnp.sum(exponent, axis=-1, keepdims=True)
        weights = (exponent / row_total).astype(jnp.bfloat16)
        mixed_parts.append(
            jnp.einsum(
                "hqk,khd->qhd", weights, value_rows[:last_row], preferred_element_type=jnp.float32
            ).astype(jnp.bfloat16)
        )
        total_parts.append(row_peak[..., 0] + jnp.log(row_total[..., 0]))
    return (jnp.concatenate(mixed_parts, axis=0), jnp.concatenate(total_parts, axis=1))


def attend_back(row_item):
    queries, key_rows, value_rows, doc_row, log_total, grad_mixed = row_item
    length = queries.shape[0]
    block_rows = min(512, length)
    score_scale = 1.0 / math.sqrt(queries.shape[2])
    grad_query_parts = []
    grad_keys = jnp.zeros(key_rows.shape, jnp.float32)
    grad_values = jnp.zeros(value_rows.shape, jnp.float32)
    for first_row in range(0, length, block_rows):
        last_row = first_row + block_rows
        scores = block_scores(queries, key_rows, doc_row, first_row, last_row)
        weights = jnp.exp(scores - log_total[:, first_row:last_row, None])
        grad_weights = jnp.einsum(
            "qhd,khd->hqk",
            grad_mixed[first_row:last_row],
            value_rows[:last_row],
            preferred_element_type=jnp.float32,
        )
        inner = jnp.sum(weights * grad_weights, axis=-1, keepdims=True)
        grad_scores = (weights * (grad_weights - inner)).astype(jnp.bfloat16)
        grad_query_parts.append(
            jnp.einsum(
                "hqk,khd->qhd", grad_scores, key_rows[:last_row], preferred_element_type=jnp.float32
            )
            * score_scale
        )
        padding = ((0, length - last_row), (0, 0), (0, 0))
        key_part = (
            jnp.einsum(
                "hqk,qhd->khd",
                grad_scores,
                queries[first_row:last_row],
                preferred_element_type=jnp.float32,
            )
            * score_scale
        )
        value_part = jnp.einsum(
            "hqk,qhd->khd",
            weights.astype(jnp.bfloat16),
            grad_mixed[first_row:last_row],
            preferred_element_type=jnp.float32,
        )
        grad_keys = grad_keys + jnp.pad(key_part, padding)
        grad_values = grad_values + jnp.pad(value_part, padding)
    return (jnp.concatenate(grad_query_parts, axis=0), grad_keys, grad_values)


def rounded(values_in):
    return lax.optimization_barrier(values_in.astype(jnp.bfloat16)).astype(jnp.float32)


def local(
    tokens,
    doc_ids,
    gain_attn,
    a_weight,
    b_weight,
    out_weight,
    gain_ffn,
    gate_weight,
    up_weight,
    down_weight,
    cotangent,
):
    rows_dev, length = doc_ids.shape
    total_rows = rows_dev * length
    own_rows = tokens.shape[0]
    local_heads = out_weight.shape[0] // DH
    rank_all = RQ + 2 * RK
    x_own = tokens.astype(jnp.float32)
    inv_one = lax.rsqrt(jnp.mean(x_own * x_own, axis=-1, keepdims=True) + EPSILON)
    normed_one = (x_own * inv_one * gain_attn).astype(jnp.bfloat16)
    normed_all, grad_out_all = (
        lax.all_gather(normed_one, "head", axis=0, tiled=True),
        lax.all_gather(cotangent, "head", axis=0, tiled=True),
    )
    factor_a = jnp.dot(normed_all, a_weight, preferred_element_type=jnp.float32).reshape(
        total_rows, local_heads, rank_all
    )
    factor_b = jnp.dot(normed_all, b_weight, preferred_element_type=jnp.float32)
    cosine, sine = rope_tables(total_rows, length)
    basis_query = rotate(factor_b[:, : RQ * DH].reshape(total_rows, RQ, DH), cosine, sine)
    basis_key = rotate(
        factor_b[:, RQ * DH : (RQ + RK) * DH].reshape(total_rows, RK, DH), cosine, sine
    )
    basis_value = factor_b[:, (RQ + RK) * DH :].reshape(total_rows, RK, DH)
    coef_query = factor_a[:, :, :RQ]
    coef_key = factor_a[:, :, RQ : RQ + RK]
    coef_value = factor_a[:, :, RQ + RK :]
    queries = (jnp.einsum("thr,trd->thd", coef_query, basis_query, precision=PRECISE) / RQ).astype(
        jnp.bfloat16
    )
    key_rows = (jnp.einsum("thr,trd->thd", coef_key, basis_key, precision=PRECISE) / RK).astype(
        jnp.bfloat16
    )
    value_rows = (
        jnp.einsum("thr,trd->thd", coef_value, basis_value, precision=PRECISE) / RK
    ).astype(jnp.bfloat16)
    row_shape = (rows_dev, length, local_heads, DH)
    query_rows = queries.reshape(row_shape)
    keys_rows = key_rows.reshape(row_shape)
    values_rows = value_rows.reshape(row_shape)
    mixed_rows, log_total = lax.map(attend_row, (query_rows, keys_rows, values_rows, doc_ids))
    mixed = mixed_rows.reshape(total_rows, local_heads * DH)
    piece = lax.slice_in_dim(mixed, 0, lax.axis_size("head") * own_rows, axis=0)
    resid_own = x_own + lax.psum_scatter(
        jnp.dot(piece, out_weight, preferred_element_type=jnp.float32),
        "head",
        scatter_dimension=0,
        tiled=True,
    )
    inv_two = lax.rsqrt(jnp.mean(resid_own * resid_own, axis=-1, keepdims=True) + EPSILON)
    normed_two = (resid_own * inv_two * gain_ffn).astype(jnp.bfloat16)
    normed_two_all = lax.all_gather(normed_two, "head", axis=0, tiled=True)
    gate_act = jnp.dot(normed_two_all, gate_weight, preferred_element_type=jnp.float32)
    up_act = jnp.dot(normed_two_all, up_weight, preferred_element_type=jnp.float32)
    sigmoid_gate = jax.nn.sigmoid(gate_act)
    silu_gate = sigmoid_gate * gate_act
    hidden = (silu_gate * up_act).astype(jnp.bfloat16)
    piece = lax.slice_in_dim(hidden, 0, lax.axis_size("head") * own_rows, axis=0)
    output = (
        resid_own
        + lax.psum_scatter(
            jnp.dot(piece, down_weight, preferred_element_type=jnp.float32).astype(jnp.bfloat16),
            "head",
            scatter_dimension=0,
            tiled=True,
        ).astype(jnp.float32)
    ).astype(jnp.bfloat16)
    grad_down = dot_first(hidden, grad_out_all)
    grad_hidden = dot_last(grad_out_all, down_weight)
    grad_gate_act = (
        grad_hidden * up_act * (sigmoid_gate * (1.0 + gate_act * (1.0 - sigmoid_gate)))
    ).astype(jnp.bfloat16)
    grad_up_act = (grad_hidden * silu_gate).astype(jnp.bfloat16)
    grad_gate = dot_first(normed_two_all, grad_gate_act)
    grad_up = dot_first(normed_two_all, grad_up_act)
    gate_piece = lax.slice_in_dim(grad_gate_act, 0, lax.axis_size("head") * own_rows, axis=0)
    up_piece = lax.slice_in_dim(grad_up_act, 0, lax.axis_size("head") * own_rows, axis=0)
    grad_normed_two = lax.psum_scatter(
        dot_last(gate_piece, gate_weight) + dot_last(up_piece, up_weight),
        "head",
        scatter_dimension=0,
        tiled=True,
    )
    resid_part, grad_gain_ffn_own = norm_backward(resid_own, inv_two, gain_ffn, grad_normed_two)
    grad_resid = cotangent.astype(jnp.float32) + resid_part
    grad_branch = lax.all_gather(grad_resid.astype(jnp.bfloat16), "head", axis=0, tiled=True)
    grad_mixed = dot_last(grad_branch, out_weight).astype(jnp.bfloat16)
    grad_out = dot_first(mixed, grad_branch)
    grad_query_rows, grad_key_rows, grad_value_rows = lax.map(
        attend_back,
        (query_rows, keys_rows, values_rows, doc_ids, log_total, grad_mixed.reshape(row_shape)),
    )
    head_shape = (total_rows, local_heads, DH)
    grad_query = rounded(grad_query_rows.reshape(head_shape))
    grad_key = rounded(grad_key_rows.reshape(head_shape))
    grad_value = rounded(grad_value_rows.reshape(head_shape))
    grad_coef_query = jnp.einsum("thd,trd->thr", grad_query, basis_query, precision=PRECISE) / RQ
    grad_coef_key = jnp.einsum("thd,trd->thr", grad_key, basis_key, precision=PRECISE) / RK
    grad_coef_value = jnp.einsum("thd,trd->thr", grad_value, basis_value, precision=PRECISE) / RK
    grad_basis_query = unrotate(
        jnp.einsum("thr,thd->trd", coef_query, grad_query, precision=PRECISE) / RQ, cosine, sine
    )
    grad_basis_key = unrotate(
        jnp.einsum("thr,thd->trd", coef_key, grad_key, precision=PRECISE) / RK, cosine, sine
    )
    grad_basis_value = jnp.einsum("thr,thd->trd", coef_value, grad_value, precision=PRECISE) / RK
    grad_factor_a = (
        jnp.concatenate([grad_coef_query, grad_coef_key, grad_coef_value], axis=-1)
        .reshape(total_rows, local_heads * rank_all)
        .astype(jnp.bfloat16)
    )
    grad_factor_b = jnp.concatenate(
        [
            grad_basis_query.reshape(total_rows, RQ * DH),
            grad_basis_key.reshape(total_rows, RK * DH),
            grad_basis_value.reshape(total_rows, RK * DH),
        ],
        axis=-1,
    )
    factor_own = lax.psum_scatter(
        grad_factor_b.astype(jnp.bfloat16), "head", scatter_dimension=0, tiled=True
    )
    piece = grad_factor_a
    grad_normed_one = lax.psum_scatter(
        dot_last(piece, a_weight).astype(jnp.bfloat16), "head", scatter_dimension=0, tiled=True
    ).astype(jnp.float32) + dot_last(factor_own, b_weight)
    input_part, grad_gain_attn_own = norm_backward(x_own, inv_one, gain_attn, grad_normed_one)
    input_grad = grad_resid + input_part
    grad_a = dot_first(normed_all, grad_factor_a)
    grad_b = dot_first(normed_one, factor_own)
    grad_a, grad_out, grad_gate, grad_up, grad_down = (
        lax.psum(grad_a.astype(jnp.bfloat16), "dp").astype(jnp.float32),
        lax.psum(grad_out.astype(jnp.bfloat16), "dp").astype(jnp.float32),
        lax.psum(grad_gate.astype(jnp.bfloat16), "dp").astype(jnp.float32),
        lax.psum(grad_up.astype(jnp.bfloat16), "dp").astype(jnp.float32),
        lax.psum(grad_down.astype(jnp.bfloat16), "dp").astype(jnp.float32),
    )
    grad_b, grad_gain_attn, grad_gain_ffn = lax.psum(
        (grad_b, grad_gain_attn_own, grad_gain_ffn_own), ("dp", "head")
    )
    return (
        output,
        input_grad,
        grad_gain_attn,
        grad_a,
        grad_b,
        grad_out,
        grad_gain_ffn,
        grad_gate,
        grad_up,
        grad_down,
    )


def solution(mesh):
    return jax.shard_map(
        local,
        mesh=mesh,
        in_specs=(
            P(("dp", "head"), None),
            P("dp", None),
            P(),
            P(None, "head"),
            P(),
            P("head", None),
            P(),
            P(None, "head"),
            P(None, "head"),
            P("head", None),
            P(("dp", "head"), None),
        ),
        out_specs=(
            P(("dp", "head"), None),
            P(("dp", "head"), None),
            P(),
            P(None, "head"),
            P(),
            P("head", None),
            P(),
            P(None, "head"),
            P(None, "head"),
            P("head", None),
        ),
        check_vma=False,
    )
```

profile of v0, /device:TPU:0, one launch (start us, length us, event | category | flops | bytes accessed | tf_op | source)
XLA Modules:
  0.0 814.9 jit_solution(9056532252986092779)
XLA Ops:
  9.7 2.0 fusion.41
  13.5 2.1 fusion.12
  15.6 3.1 multiply_cosine_fusion
  18.7 18.6 %all-gather.5.cloned.1.call-done = bf16[1024,1024]{1,0:T(8,128)(2,1)} async-done(((bf16[256,1024]{1,0:T(8,128)(2,1)}), bf16[1024,1024]{1,0:T(8,128)(2,1)}) %all-gather.5.cloned.1.call-update) | async-done | bytes 2097168 | tf_op jit(solution)/shard_map/all_gather | solution.py:189
  37.2 3.1 fusion.71
  45.2 2.9 fusion.72
  56.5 2.7 fusion.63
  59.2 2.2 copy.174
  61.4 2.1 copy.216
  63.5 2.1 copy.215
  65.6 2.6 multiply_subtract_fusion.1
  69.5 10.4 %fusion.60 = f32[1024,4,64]{2,1,0:T(4,128)} fusion(f32[1024,4,2]{1,2,0:T(2,128)S(1)} %copy-done.22, f32[1024,2,32]{2,1,0:T(2,128)S(1)} %get-tuple-element.84, f32[1024,2,32]{2,1,0:T(2,128)S(1)} %get-tuple-element.83), kind=kOutput, calls=%fused_computation.132 | convolution fusion | flops 6422528 | bytes 1605632 | tf_op jit(solution)/shard_map/thr,trd->thd/dot_general | solution.py:208
  79.9 2.7 copy.182
  82.6 2.1 multiply_convert_fusion.7
  84.7 11.1 %fusion.73 = f32[1024,4,64]{2,1,0:T(4,128)} fusion(f32[1024,4,2]{1,2,0:T(2,128)} %copy.210, f32[1024,2,64]{2,1,0:T(2,128)} %copy.174), kind=kOutput, calls=%fused_computation.145 | convolution fusion | flops 6291456 | bytes 1605632 | tf_op jit(solution)/shard_map/thr,trd->thd/dot_general | solution.py:212
  95.9 2.7 copy.175
  98.5 2.1 multiply_convert_fusion.8
  100.7 3.6 copy.213
  104.3 3.6 copy.212
  107.9 4.1 multiply_subtract_fusion
  112.0 8.1 multiply_convert_fusion.5
  135.4 2.1 fusion.37
  138.5 2.7 fusion.74
  141.2 44.7 %reduce-scatter.6.cloned.1.call-done = f32[256,1024]{1,0:T(8,128)} async-done(((f32[1024,1024]{1,0:T(8,128)}), f32[256,1024]{1,0:T(8,128)}) %reduce-scatter.6.cloned.1.call-update) | async-done | bytes 1048592 | tf_op jit(solution)/shard_map/reduce_scatter | solution.py:221
  190.9 22.1 %all-gather.7.cloned.1.call-done = bf16[1024,1024]{1,0:T(8,128)(2,1)} async-done(((bf16[256,1024]{1,0:T(8,128)(2,1)}), bf16[1024,1024]{1,0:T(8,128)(2,1)}) %all-gather.7.cloned.1.call-update) | async-done | bytes 2097168 | tf_op jit(solution)/shard_map/all_gather | solution.py:229
  213.0 5.4 fusion.76
  218.4 3.3 fusion.75
  221.7 15.3 %all-gather.9.cloned.1.call-done = bf16[1024,1024]{1,0:T(8,128)(2,1)} async-done(((bf16[256,1024]{1,0:T(8,128)(2,1)}), bf16[1024,1024]{1,0:T(8,128)(2,1)}) %all-gather.9.cloned.1.call-update) | async-done | bytes 2097168 | tf_op jit(solution)/shard_map/all_gather | solution.py:190
  237.0 6.5 multiply_convert_fusion.2
  245.9 3.9 convolution_add_fusion
  249.9 4.5 convolution_convert_fusion.1
  254.5 40.1 %reduce-scatter.10.cloned.1.call-done = f32[256,1024]{1,0:T(8,128)} async-done(((f32[1024,1024]{1,0:T(8,128)}), f32[256,1024]{1,0:T(8,128)}) %reduce-scatter.10.cloned.1.call-update) | async-done | bytes 1048592 | tf_op jit(solution)/shard_map/reduce_scatter | solution.py:255
  294.6 2.4 multiply_reduce_fusion.2
  297.0 31.8 %reduce-scatter.8.cloned.1.call-done = bf16[256,1024]{1,0:T(8,128)(2,1)} async-done(((bf16[1024,1024]{1,0:T(8,128)(2,1)}), bf16[256,1024]{1,0:T(8,128)(2,1)}) %reduce-scatter.8.cloned.1.call-update) | async-done | bytes 524304 | tf_op jit(solution)/shard_map/reduce_scatter | solution.py:238
  328.8 3.2 fusion.61
  332.2 22.6 %all-gather.11.cloned.1.call-done = bf16[1024,1024]{1,0:T(8,128)(2,1)} async-done(((bf16[256,1024]{1,0:T(8,128)(2,1)}), bf16[1024,1024]{1,0:T(8,128)(2,1)}) %all-gather.11.cloned.1.call-update) | async-done | bytes 2097168 | tf_op jit(solution)/shard_map/all_gather | solution.py:263
  354.8 2.6 convolution_convert_fusion.6
  363.5 4.8 multiply_reduce_fusion
  371.5 5.1 fusion.26
  377.6 6.7 multiply_convert_fusion
  388.3 2.5 copy.192
  390.9 5.1 convolution_multiply_fusion.3
  397.6 2.2 pad_maximum_fusion.8
  401.7 2.3 copy.187
  404.0 5.5 convolution_multiply_fusion
  409.5 2.7 add_convert_fusion
  412.2 2.5 copy.200
  417.7 2.2 pad_maximum_fusion.3
  420.0 5.7 convolution_multiply_fusion.4
  427.1 6.5 convolution_multiply_fusion.5
  434.9 8.0 convolution_multiply_fusion.1
  443.8 2.1 convolution_convert_fusion
  446.2 5.0 convolution_convert_fusion.4
  451.2 2.8 convolution_convert_fusion.2
  454.0 2.8 convolution_convert_fusion.3
  461.3 3.2 fusion.78
  464.5 16.3 %reduce-scatter.12.cloned.1.call-done = bf16[256,1024]{1,0:T(8,128)(2,1)} async-done(((bf16[1024,1024]{1,0:T(8,128)(2,1)}), bf16[256,1024]{1,0:T(8,128)(2,1)}) %reduce-scatter.12.cloned.1.call-update) | async-done | bytes 524304 | tf_op jit(solution)/shard_map/reduce_scatter | solution.py:301
  480.8 2.3 fusion.47
  483.1 44.8 %all-reduce.2 = (f32[1024]{0:T(1024)}, f32[1024]{0:T(1024)}) all-reduce(f32[1024]{0:T(1024)S(1)} %get-tuple-element.53, f32[1024]{0:T(1024)S(1)} %copy-done.50), channel_id=1, replica_groups=mesh['dp'=8,'head'=4] {'dp','head'}, use_global_device_ids=true, to_apply=%region_16.17 | all-reduce | flops 2048 | bytes 16384 | tf_op jit(solution)/shard_map/psum | solution.py:315
  529.2 134.1 %all-reduce.9.cloned.1.call-done = (bf16[1024,40]{0,1:T(8,128)(2,1)}, bf16[256,1024]{1,0:T(8,128)(2,1)}, bf16[1024,704]{0,1:T(8,128)(2,1)}, bf16[1024,704]{0,1:T(8,128)(2,1)}, bf16[704,1024]{1,0:T(8,128)(2,1)}) async-done(((bf16[1024,40]{0,1:T(8,128)(2,1)}, bf16[256,1024]{1,0:T(8,128)(2,1)}, bf16[1024,704]{0,1:T(8,128)(2,1)}, bf16[1024,704]{0,1:T(8,128)(2,1)}, bf16[704,1024]{1,0:T(8,128)(2,1)}), ...) | async-done | bytes 4931600 | tf_op jit(solution)/shard_map/psum | solution.py:309
  664.8 2.2 convert_element_type.209
  667.1 3.3 convert_element_type.211
  674.3 130.3 %all-reduce.7.cloned.1.call-done = f32[1024,640]{1,0:T(8,128)} async-done(((f32[1024,640]{1,0:T(8,128)}), f32[1024,640]{1,0:T(8,128)}) %all-reduce.7.cloned.1.call-update) | async-done | bytes 2621456 | tf_op jit(solution)/shard_map/psum | solution.py:315
  804.6 3.4 copy.223
  (220 shorter events, 78.6 us)
Async XLA Ops:
  7.2 229.9 %copy-start = (bf16[704,1024]{1,0:T(8,128)(2,1)S(1)}, bf16[704,1024]{1,0:T(8,128)(2,1)}, u32[]{:S(2)}) copy-start(bf16[704,1024]{1,0:T(8,128)(2,1)} %param.20) | copy-start | bytes 4325380
  7.2 30.0 %all-gather.5.cloned.1.call-start = ((), (), s32[]{:S(2)}) async-start(), calls=%async_computation.5 | async-start | bytes 2621440 | tf_op jit(solution)/shard_map/all_gather | solution.py:189
  11.8 174.1 %reduce-scatter.6.cloned.1.call-start = ((), (), s32[]{:S(2)}) async-start(), calls=%async_computation.6 | async-start | bytes 5242880 | tf_op jit(solution)/shard_map/reduce_scatter | solution.py:221
  37.2 8.0 copy-start.9
  48.1 2.3 copy-start.41
  48.1 3.6 copy-start.40
  65.6 3.9 copy-start.22
  112.0 8.1 copy-start.5
  112.0 8.1 copy-start.6
  127.5 2.3 copy-start.3
  127.5 1.4 copy-start.27
  128.9 1.4 copy-start.32
  132.2 3.3 copy-start.2
  135.4 2.1 copy-start.45
  135.4 3.0 copy-start.37
  141.2 71.8 %all-gather.7.cloned.1.call-start = ((), (), s32[]{:S(2)}) async-start(), calls=%async_computation.7 | async-start | bytes 2621440 | tf_op jit(solution)/shard_map/all_gather | solution.py:229
  190.3 46.7 %all-gather.9.cloned.1.call-start = ((), (), s32[]{:S(2)}) async-start(), calls=%async_computation.9 | async-start | bytes 2621440 | tf_op jit(solution)/shard_map/all_gather | solution.py:190
  190.9 103.7 %reduce-scatter.10.cloned.1.call-start = ((), (), s32[]{:S(2)}) async-start(), calls=%async_computation.10 | async-start | bytes 5242880 | tf_op jit(solution)/shard_map/reduce_scatter | solution.py:255
  213.0 5.4 copy-start.55
  213.0 5.4 copy-start.58
  237.0 6.5 copy-start.59
  243.5 1.9 copy-start.63
  243.5 1.9 copy-start.61
  243.5 2.4 copy-start.60
  249.9 78.9 %reduce-scatter.8.cloned.1.call-start = ((), (), s32[]{:S(2)}) async-start(), calls=%async_computation.8 | async-start | bytes 2621440 | tf_op jit(solution)/shard_map/reduce_scatter | solution.py:238
  254.5 74.3 %copy-start.8 = (f32[256,1024]{1,0:T(8,128)S(1)}, f32[256,1024]{1,0:T(8,128)}, u32[]{:S(2)}) copy-start(f32[256,1024]{1,0:T(8,128)} %copy-done.7) | copy-start | bytes 3145732
  254.5 74.3 %copy-start.42 = (f32[1024]{0:T(1024)S(1)}, f32[1024]{0:T(1024)}, u32[]{:S(2)}) copy-start(f32[1024]{0:T(1024)} %param.17) | copy-start | bytes 12292
  254.5 74.3 %copy-start.48 = (f32[256]{0:T(256)S(1)}, f32[256]{0:T(256)}, u32[]{:S(2)}) copy-start(f32[256]{0:T(256)} %copy-done.47) | copy-start | bytes 3076
  254.5 74.3 %copy-start.54 = (f32[256]{0:T(256)S(1)}, f32[256]{0:T(256)}, u32[]{:S(2)}) copy-start(f32[256]{0:T(256)} %get-tuple-element.106) | copy-start | bytes 3076
  254.5 100.3 %all-gather.11.cloned.1.call-start = ((), (), s32[]{:S(2)}) async-start(), calls=%async_computation.11 | async-start | bytes 2621440 | tf_op jit(solution)/shard_map/all_gather | solution.py:263
  328.8 3.3 copy-start.44
  328.8 3.3 copy-start.46
  332.1 128.4 %reduce-scatter.14.cloned.1.call-start = ((), (), s32[]{:S(2)}) async-start(), calls=%async_computation.13 | async-start | bytes 1638400 | tf_op jit(solution)/shard_map/reduce_scatter | solution.py:297
  354.8 3.0 copy-start.4
  359.5 4.1 slice-start
  359.5 4.0 slice-start.1
  360.7 1.6 copy-start.15
  384.3 1.4 copy-start.30
  385.7 1.7 copy-start.36
  388.3 7.6 copy-start.11
  388.3 7.6 copy-start.12
  416.6 3.4 copy-start.24
  419.9 7.2 copy-start.19
  419.9 7.2 copy-start.21
  419.9 60.9 %reduce-scatter.12.cloned.1.call-start = ((), (), s32[]{:S(2)}) async-start(), calls=%async_computation.12 | async-start | bytes 2621440 | tf_op jit(solution)/shard_map/reduce_scatter | solution.py:301
  427.1 7.8 copy-start.13
  434.9 8.9 %copy-start.38 = (bf16[1024,40]{0,1:T(8,128)(2,1)S(1)}, bf16[1024,40]{0,1:T(8,128)(2,1)}, u32[]{:S(2)}) copy-start(bf16[1024,40]{0,1:T(8,128)(2,1)} %param.14) | copy-start | bytes 245764
  445.9 5.3 copy-start.56
  445.9 217.4 %all-reduce.9.cloned.1.call-start = ((), (), s32[]{:S(2)}) async-start(), calls=%async_computation.15 | async-start | bytes 9863168 | tf_op jit(solution)/shard_map/psum | solution.py:309
  446.2 5.0 copy-start.62
  451.2 2.8 copy-start.64
  454.0 2.8 copy-start.10
  456.8 2.0 copy-start.57
  460.3 20.5 %copy-start.16 = (bf16[256,1024]{1,0:T(8,128)(2,1)S(1)}, bf16[256,1024]{1,0:T(8,128)(2,1)}, u32[]{:S(2)}) copy-start(bf16[256,1024]{1,0:T(8,128)(2,1)} %param.11) | copy-start | bytes 1572868
  460.3 20.5 %copy-start.49 = (f32[1024]{0:T(1024)S(1)}, f32[1024]{0:T(1024)}, u32[]{:S(2)}) copy-start(f32[1024]{0:T(1024)} %param.13) | copy-start | bytes 12292
  460.3 20.5 %copy-start.52 = (f32[256]{0:T(256)S(1)}, f32[256]{0:T(256)}, u32[]{:S(2)}) copy-start(f32[256]{0:T(256)} %copy-done.51) | copy-start | bytes 3076
  460.3 344.2 %all-reduce.7.cloned.1.call-start = ((), (), s32[]{:S(2)}) async-start(), calls=%async_computation.14 | async-start | bytes 5242880 | tf_op jit(solution)/shard_map/psum | solution.py:315
  461.3 19.5 %copy-start.39 = (bf16[256,640]{0,1:T(8,128)(2,1)S(1)}, bf16[256,640]{0,1:T(8,128)(2,1)}, u32[]{:S(2)}) copy-start(bf16[256,640]{0,1:T(8,128)(2,1)} %reduce-scatter.14.cloned.1.call-done) | copy-start | bytes 983044
  464.5 18.6 %copy-start.50 = (f32[1024]{0:T(1024)S(1)}, f32[1024]{0:T(1024)}, u32[]{:S(2)}) copy-start(f32[1024]{0:T(1024)} %get-tuple-element.51) | copy-start | bytes 12292
  464.5 63.4 %copy-start.23 = (f32[256,1024]{1,0:T(8,128)S(1)}, f32[256,1024]{1,0:T(8,128)}, u32[]{:S(2)}) copy-start(f32[256,1024]{1,0:T(8,128)} %get-tuple-element.73) | copy-start | bytes 3145732
  464.5 63.4 %copy-start.53 = (f32[256]{0:T(256)S(1)}, f32[256]{0:T(256)}, u32[]{:S(2)}) copy-start(f32[256]{0:T(256)} %get-tuple-element.104) | copy-start | bytes 3076
  664.8 5.5 copy-start.35
  670.4 1.9 copy-start.34
  672.3 135.6 %copy-start.1 = (bf16[704,1024]{1,0:T(8,128)(2,1)S(1)}, bf16[704,1024]{1,0:T(8,128)(2,1)}, u32[]{:S(2)}) copy-start(bf16[704,1024]{1,0:T(8,128)(2,1)} %param.20) | copy-start | bytes 4325380
  (14 other events, 14.6 us)
Sparse Core Ops, SparseCore 0:
  11.9 25.2 all-gather.4
  141.3 44.5 reduce-scatter.5
  190.4 22.5 all-gather.6
  214.4 22.5 all-gather.8
  250.0 44.5 reduce-scatter.9
  297.6 31.1 reduce-scatter.7
  332.2 22.5 all-gather.10
  420.1 26.3 reduce-scatter.13
  449.6 31.1 reduce-scatter.11
  486.1 177.1 all-reduce.8
  669.3 135.2 all-reduce.6
where the time goes:
time: 824 us; the launch traced here: 815 us
  waiting for transfers between devices  476 us (58%)
  matrix products  144 us (17%)
  local copies, waits for them, and re-layouts  70.4 us (9%)
  other arithmetic  64 us (8%)
  blocking collectives  44.8 us (5%)
  between operations  15.1 us (2%)
    psum x1, waiting for transfers between devices, local(): lax.psum(grad_a.astype(jnp.bfloat16), 'dp').astype(jnp.float32)  134 us
    psum x1, waiting for transfers between devices, local(): lax.psum((grad_b, grad_gain_attn_own, grad_gain_ffn_own), ('dp', 'head'))  130 us
    psum x1, blocking collectives, local(): lax.psum((grad_b, grad_gain_attn_own, grad_gain_ffn_own), ('dp', 'head'))  44.8 us
    reduce_scatter x1, waiting for transfers between devices, local(): lax.psum_scatter(jnp.dot(piece, out_weight, preferred_element_type=jnp.fl...  44.7 us
    reduce_scatter x1, waiting for transfers between devices, local(): lax.psum_scatter(dot_last(gate_piece, gate_weight) + dot_last(up_piece, u...  40.1 us
    reduce_scatter x1, waiting for transfers between devices, local(): lax.psum_scatter(jnp.dot(piece, down_weight, preferred_element_type=jnp.f...  31.8 us
    unnamed x142, local copies, waits for them, and re-layouts  28.1 us
    all_gather x1, waiting for transfers between devices, local(): lax.all_gather(grad_resid.astype(jnp.bfloat16), 'head', axis=0, tiled=True)  22.6 us
  transfers between devices with their start and end apart: 11, of which 10 were waited for; matrix products, arithmetic and copies ran while one was open for 10% of the time, Pallas kernels for 0%

commit v1 on v0

--- a/solution.py
+++ b/solution.py
@@ -294,27 +294,52 @@
         ],
         axis=-1,
     )
-    factor_own = lax.psum_scatter(
-        grad_factor_b.astype(jnp.bfloat16), "head", scatter_dimension=0, tiled=True
+    head_count = lax.axis_size("head")
+    basis_cols = grad_factor_b.shape[1] // head_count
+    factor_cols = lax.psum_scatter(
+        grad_factor_b.astype(jnp.bfloat16), "head", scatter_dimension=1, tiled=True
+    )
+    weight_cols = lax.dynamic_slice_in_dim(
+        b_weight, lax.axis_index("head") * basis_cols, basis_cols, axis=1
     )
     piece = grad_factor_a
     grad_normed_one = lax.psum_scatter(
-        dot_last(piece, a_weight).astype(jnp.bfloat16), "head", scatter_dimension=0, tiled=True
-    ).astype(jnp.float32) + dot_last(factor_own, b_weight)
+        (dot_last(piece, a_weight) + dot_last(factor_cols, weight_cols)).astype(jnp.bfloat16),
+        "head",
+        scatter_dimension=0,
+        tiled=True,
+    ).astype(jnp.float32)
     input_part, grad_gain_attn_own = norm_backward(x_own, inv_one, gain_attn, grad_normed_one)
     input_grad = grad_resid + input_part
     grad_a = dot_first(normed_all, grad_factor_a)
-    grad_b = dot_first(normed_one, factor_own)
-    grad_a, grad_out, grad_gate, grad_up, grad_down = (
-        lax.psum(grad_a.astype(jnp.bfloat16), "dp").astype(jnp.float32),
-        lax.psum(grad_out.astype(jnp.bfloat16), "dp").astype(jnp.float32),
-        lax.psum(grad_gate.astype(jnp.bfloat16), "dp").astype(jnp.float32),
-        lax.psum(grad_up.astype(jnp.bfloat16), "dp").astype(jnp.float32),
-        lax.psum(grad_down.astype(jnp.bfloat16), "dp").astype(jnp.float32),
-    )
-    grad_b, grad_gain_attn, grad_gain_ffn = lax.psum(
-        (grad_b, grad_gain_attn_own, grad_gain_ffn_own), ("dp", "head")
-    )
+    grad_b_cols = dot_first(normed_all, factor_cols)
+
+    def dp_sum(values):
+        return lax.all_gather(
+            lax.psum_scatter(values.astype(jnp.bfloat16), "dp", scatter_dimension=1, tiled=True),
+            "dp",
+            axis=1,
+            tiled=True,
+        ).astype(jnp.float32)
+
+    grad_gate, grad_up, grad_down = dp_sum(grad_gate), dp_sum(grad_up), dp_sum(grad_down)
+    grad_out = lax.psum(grad_out.astype(jnp.bfloat16), "dp").astype(jnp.float32)
+    features = grad_gain_attn_own.shape[0]
+    gain_rows = -(-2 * features // basis_cols)
+    gains = jnp.pad(
+        jnp.concatenate([grad_gain_attn_own, grad_gain_ffn_own]),
+        (0, gain_rows * basis_cols - 2 * features),
+    ).reshape(gain_rows, basis_cols)
+    grad_a, packed = lax.psum(
+        (grad_a.astype(jnp.bfloat16), jnp.concatenate([grad_b_cols, gains], axis=0)), "dp"
+    )
+    grad_a = grad_a.astype(jnp.float32)
+    packed = lax.all_gather(packed, "head", axis=1, tiled=True)
+    grad_b = packed[: grad_b_cols.shape[0]]
+    gains = jnp.sum(
+        packed[grad_b_cols.shape[0] :].reshape(gain_rows, head_count, basis_cols), axis=1
+    ).reshape(-1)
+    grad_gain_attn, grad_gain_ffn = gains[:features], gains[features : 2 * features]
     return (
         output,
         input_grad,

time: 824 us -> 1030 us (1.25)
  waiting for transfers between devices: 476 us -> 707 us
  blocking collectives: 44.8 us -> 0 us
  local copies, waits for them, and re-layouts: 70.4 us -> 81.7 us
    all_gather x0 -> x4, waiting for transfers between devices: none -> 147 us  [the longest x3 124 us: dp_sum(): lax.all_gather(lax.psum_scatter(values.astype(jnp.bfloat16), 'dp', scatte...]
    reduce_scatter x1 -> x3, waiting for transfers between devices: 16.3 us -> 150 us  [the longest x2 135 us: dp_sum(): lax.psum_scatter(values.astype(jnp.bfloat16), 'dp', scatter_dimension=1,...]
    psum x2, waiting for transfers between devices: 264 us -> 147 us  [local(): lax.psum((grad_a.astype(jnp.bfloat16), jnp.concatenate([grad_b_cols, gain...]
    unnamed x11 -> x19, waiting for transfers between devices: 0.69 us -> 67.7 us
    psum x1 -> x0, blocking collectives: 44.8 us -> none  [local(): lax.psum((grad_b, grad_gain_attn_own, grad_gain_ffn_own), ('dp', 'head'))]
    unnamed x142 -> x130, local copies, waits for them, and re-layouts: 28.1 us -> 32.4 us
  transfers between devices with their start and end apart: 11 -> 18, of which waited for: 10 -> 18; matrix products, arithmetic and copies ran while one was open for 10% -> 8% of each run, Pallas kernels for 0% -> 0%
where the time goes in v1:
time: 1030 us; the launch traced here: 1020 us
  waiting for transfers between devices  707 us (69%)
  matrix products  146 us (14%)
  local copies, waits for them, and re-layouts  81.7 us (8%)
  other arithmetic  69.3 us (7%)
  between operations  15.3 us (1%)
    psum x2, waiting for transfers between devices, local(): lax.psum((grad_a.astype(jnp.bfloat16), jnp.concatenate([grad_b_cols, gain...  147 us
    reduce_scatter x2, waiting for transfers between devices, dp_sum(): lax.psum_scatter(values.astype(jnp.bfloat16), 'dp', scatter_dimension=1,...  135 us
    all_gather x3, waiting for transfers between devices, dp_sum(): lax.all_gather(lax.psum_scatter(values.astype(jnp.bfloat16), 'dp', scatte...  124 us
    unnamed x19, waiting for transfers between devices  67.7 us
    reduce_scatter x1, waiting for transfers between devices, local(): lax.psum_scatter(jnp.dot(piece, out_weight, preferred_element_type=jnp.fl...  44.7 us
    reduce_scatter x1, waiting for transfers between devices, local(): lax.psum_scatter(dot_last(gate_piece, gate_weight) + dot_last(up_piece, u...  40.1 us
    unnamed x130, local copies, waits for them, and re-layouts  32.4 us
    reduce_scatter x1, waiting for transfers between devices, local(): lax.psum_scatter(jnp.dot(piece, down_weight, preferred_element_type=jnp.f...  31.8 us
  transfers between devices with their start and end apart: 18, of which 18 were waited for; matrix products, arithmetic and copies ran while one was open for 8% of the time, Pallas kernels for 0%

profile of v1, /device:TPU:0, one launch (start us, length us, event | category | flops | bytes accessed | tf_op | source)
XLA Modules:
  0.0 1020.7 jit_solution(12582645795029141843)
XLA Ops:
  15.5 3.0 multiply_cosine_fusion
  18.5 18.7 %all-gather.9.cloned.1.call-done = bf16[1024,1024]{1,0:T(8,128)(2,1)} async-done(((bf16[256,1024]{1,0:T(8,128)(2,1)}), bf16[1024,1024]{1,0:T(8,128)(2,1)}) %all-gather.9.cloned.1.call-update) | async-done | bytes 2097168 | tf_op jit(solution)/shard_map/all_gather | solution.py:189
  37.2 3.1 fusion.76
  45.2 2.9 fusion.77
  54.3 2.6 copy.270
  58.7 2.7 fusion.67
  61.4 2.2 copy.228
  67.8 2.6 multiply_subtract_fusion.1
  71.7 10.4 %fusion.64 = f32[1024,4,64]{2,1,0:T(4,128)} fusion(f32[1024,4,2]{1,2,0:T(2,128)S(1)} %copy-done.19, f32[1024,2,32]{2,1,0:T(2,128)S(1)} %get-tuple-element.139, f32[1024,2,32]{2,1,0:T(2,128)S(1)} %get-tuple-element.138), kind=kOutput, calls=%fused_computation.139 | convolution fusion | flops 6422528 | bytes 1605632 | tf_op jit(solution)/shard_map/thr,trd->thd/dot_general | solution.py:208
  82.1 2.7 copy.236
  86.9 10.8 %fusion.78 = f32[1024,4,64]{2,1,0:T(4,128)} fusion(f32[1024,4,2]{1,2,0:T(2,128)} %copy.269, f32[1024,2,64]{2,1,0:T(2,128)} %copy.228), kind=kOutput, calls=%fused_computation.153 | convolution fusion | flops 6291456 | bytes 1605632 | tf_op jit(solution)/shard_map/thr,trd->thd/dot_general | solution.py:212
  97.8 2.7 copy.229
  102.5 3.6 copy.272
  106.2 3.7 copy.271
  109.8 4.3 multiply_subtract_fusion
  114.2 8.1 multiply_convert_fusion.5
  140.7 2.7 fusion.79
  143.4 44.7 %reduce-scatter.11.cloned.1.call-done = f32[256,1024]{1,0:T(8,128)} async-done(((f32[1024,1024]{1,0:T(8,128)}), f32[256,1024]{1,0:T(8,128)}) %reduce-scatter.11.cloned.1.call-update) | async-done | bytes 1048592 | tf_op jit(solution)/shard_map/reduce_scatter | solution.py:221
  193.2 22.1 %all-gather.11.cloned.1.call-done = bf16[1024,1024]{1,0:T(8,128)(2,1)} async-done(((bf16[256,1024]{1,0:T(8,128)(2,1)}), bf16[1024,1024]{1,0:T(8,128)(2,1)}) %all-gather.11.cloned.1.call-update) | async-done | bytes 2097168 | tf_op jit(solution)/shard_map/all_gather | solution.py:229
  215.3 5.4 fusion.81
  220.7 3.3 fusion.80
  224.0 15.3 %all-gather.13.cloned.1.call-done = bf16[1024,1024]{1,0:T(8,128)(2,1)} async-done(((bf16[256,1024]{1,0:T(8,128)(2,1)}), bf16[1024,1024]{1,0:T(8,128)(2,1)}) %all-gather.13.cloned.1.call-update) | async-done | bytes 2097168 | tf_op jit(solution)/shard_map/all_gather | solution.py:190
  239.3 6.7 multiply_convert_fusion.2
  248.4 3.9 convolution_add_fusion
  252.3 4.5 convolution_convert_fusion
  256.9 40.1 %reduce-scatter.15.cloned.1.call-done = f32[256,1024]{1,0:T(8,128)} async-done(((f32[1024,1024]{1,0:T(8,128)}), f32[256,1024]{1,0:T(8,128)}) %reduce-scatter.15.cloned.1.call-update) | async-done | bytes 1048592 | tf_op jit(solution)/shard_map/reduce_scatter | solution.py:255
  297.0 2.4 multiply_reduce_fusion.2
  299.4 31.8 %reduce-scatter.13.cloned.1.call-done = bf16[256,1024]{1,0:T(8,128)(2,1)} async-done(((bf16[1024,1024]{1,0:T(8,128)(2,1)}), bf16[256,1024]{1,0:T(8,128)(2,1)}) %reduce-scatter.13.cloned.1.call-update) | async-done | bytes 524304 | tf_op jit(solution)/shard_map/reduce_scatter | solution.py:238
  331.2 3.2 fusion.65
  334.5 22.6 %all-gather.15.cloned.1.call-done = bf16[1024,1024]{1,0:T(8,128)(2,1)} async-done(((bf16[256,1024]{1,0:T(8,128)(2,1)}), bf16[1024,1024]{1,0:T(8,128)(2,1)}) %all-gather.15.cloned.1.call-update) | async-done | bytes 2097168 | tf_op jit(solution)/shard_map/all_gather | solution.py:263
  357.1 2.6 convolution_convert_fusion.5
  365.9 4.5 multiply_reduce_fusion
  373.5 5.1 fusion.26
  379.6 6.7 multiply_convert_fusion
  390.4 2.8 copy.246
  393.2 5.1 convolution_multiply_fusion.3
  399.9 2.2 pad_maximum_fusion.9
  404.0 2.3 copy.241
  406.3 6.1 convolution_multiply_fusion
  412.4 3.1 add_convert_fusion.1
  415.5 2.4 copy.254
  417.9 3.0 copy.255
  422.0 2.2 pad_maximum_fusion.3
  424.3 5.6 convolution_multiply_fusion.4
  431.2 7.2 convolution_multiply_fusion.5
  439.7 8.9 convolution_multiply_fusion.1
  455.3 3.7 convolution_convert_fusion.3
  460.6 5.1 convolution_convert_fusion.1
  465.9 4.3 convolution_convert_fusion.2
  471.8 14.6 %reduce-scatter.19.cloned.1.call-done = bf16[256,1024]{1,0:T(8,128)(2,1)} async-done(((bf16[1024,1024]{1,0:T(8,128)(2,1)}), bf16[256,1024]{1,0:T(8,128)(2,1)}) %reduce-scatter.19.cloned.1.call-update) | async-done | bytes 524304 | tf_op jit(solution)/shard_map/reduce_scatter | solution.py:306
  489.0 66.9 %reduce-scatter.25.cloned.1.call-done = bf16[128,704]{1,0:T(8,128)(2,1)} async-done(((bf16[1024,704]{1,0:T(8,128)(2,1)}), bf16[128,704]{1,0:T(8,128)(2,1)}) %reduce-scatter.25.cloned.1.call-update) | async-done | bytes 180240
  557.7 66.7 %reduce-scatter.23.cloned.1.call-done = bf16[1024,88]{0,1:T(8,128)(2,1)} async-done(((bf16[1024,704]{0,1:T(8,128)(2,1)}), bf16[1024,88]{0,1:T(8,128)(2,1)}) %reduce-scatter.23.cloned.1.call-update) | async-done | bytes 180240 | tf_op jit(solution)/shard_map/reduce_scatter | solution.py:319
  624.4 68.3 %reduce-scatter.21.cloned.1.call-done = bf16[1024,88]{0,1:T(8,128)(2,1)} async-done(((bf16[1024,704]{0,1:T(8,128)(2,1)}), bf16[1024,88]{0,1:T(8,128)(2,1)}) %reduce-scatter.21.cloned.1.call-update) | async-done | bytes 180240 | tf_op jit(solution)/shard_map/reduce_scatter | solution.py:319
  696.0 74.5 %all-reduce.7.cloned.1.call-done = f32[1037,160]{0,1:T(8,128)} async-done(((f32[1037,160]{0,1:T(8,128)}), f32[1037,160]{0,1:T(8,128)}) %all-reduce.7.cloned.1.call-update) | async-done | bytes 663696 | tf_op jit(solution)/shard_map/psum | solution.py:333
  770.6 44.4 %all-gather.23.cloned.1.call-done = bf16[704,1024]{1,0:T(8,128)(2,1)} async-done(((bf16[704,128]{1,0:T(8,128)(2,1)}), bf16[704,1024]{1,0:T(8,128)(2,1)}) %all-gather.23.cloned.1.call-update) | async-done | bytes 1441808 | tf_op jit(solution)/shard_map/all_gather | solution.py:318
  815.0 3.3 convert_element_type.217
  818.3 39.7 %all-gather.21.cloned.1.call-done = bf16[1024,704]{0,1:T(8,128)(2,1)} async-done(((bf16[1024,88]{0,1:T(8,128)(2,1)}), bf16[1024,704]{0,1:T(8,128)(2,1)}) %all-gather.21.cloned.1.call-update) | async-done | bytes 1441808 | tf_op jit(solution)/shard_map/all_gather | solution.py:318
  858.0 3.3 convert_element_type.215
  861.3 40.1 %all-gather.19.cloned.1.call-done = bf16[1024,704]{0,1:T(8,128)(2,1)} async-done(((bf16[1024,88]{0,1:T(8,128)(2,1)}), bf16[1024,704]{0,1:T(8,128)(2,1)}) %all-gather.19.cloned.1.call-update) | async-done | bytes 1441808 | tf_op jit(solution)/shard_map/all_gather | solution.py:318
  901.4 3.3 convert_element_type.213
  904.8 72.9 %all-reduce.9.cloned.1.call-done = (bf16[1024,40]{0,1:T(8,128)(2,1)}, bf16[256,1024]{1,0:T(8,128)(2,1)}) async-done(((bf16[1024,40]{0,1:T(8,128)(2,1)}, bf16[256,1024]{1,0:T(8,128)(2,1)}), (bf16[1024,40]{0,1:T(8,128)(2,1)}, bf16[256,1024]{1,0:T(8,128)(2,1)})) %all-reduce.9.cloned.1.call-update) | async-done | bytes 606224 | tf_op jit(solution)/shard_map/psum | solution.py:333
  982.7 23.2 %all-gather.17.cloned.1.call-done = f32[1037,640]{0,1:T(8,128)} async-done(((f32[1037,160]{0,1:T(8,128)}), f32[1037,640]{0,1:T(8,128)}) %all-gather.17.cloned.1.call-update) | async-done | bytes 2654736 | tf_op jit(solution)/shard_map/all_gather | solution.py:337
  1005.9 3.7 slice.177
  1009.6 3.3 copy.262
  (240 shorter events, 102.0 us)
Async XLA Ops:
  7.2 232.1 %copy-start = (bf16[704,1024]{1,0:T(8,128)(2,1)S(1)}, bf16[704,1024]{1,0:T(8,128)(2,1)}, u32[]{:S(2)}) copy-start(bf16[704,1024]{1,0:T(8,128)(2,1)} %param.20) | copy-start | bytes 4325380
  7.2 30.0 %all-gather.9.cloned.1.call-start = ((), (), s32[]{:S(2)}) async-start(), calls=%async_computation.8 | async-start | bytes 2621440 | tf_op jit(solution)/shard_map/all_gather | solution.py:189
  11.7 176.4 %reduce-scatter.11.cloned.1.call-start = ((), (), s32[]{:S(2)}) async-start(), calls=%async_computation.9 | async-start | bytes 5242880 | tf_op jit(solution)/shard_map/reduce_scatter | solution.py:221
  37.2 8.0 copy-start.7
  67.8 3.9 copy-start.19
  109.8 4.3 copy-start.8
  114.1 8.1 copy-start.5
  114.1 8.1 copy-start.6
  129.6 2.3 copy-start.3
  134.3 3.3 copy-start.2
  137.7 2.1 copy-start.41
  137.7 3.0 copy-start.35
  143.4 71.9 %all-gather.11.cloned.1.call-start = ((), (), s32[]{:S(2)}) async-start(), calls=%async_computation.10 | async-start | bytes 2621440 | tf_op jit(solution)/shard_map/all_gather | solution.py:229
  192.6 46.7 %all-gather.13.cloned.1.call-start = ((), (), s32[]{:S(2)}) async-start(), calls=%async_computation.12 | async-start | bytes 2621440 | tf_op jit(solution)/shard_map/all_gather | solution.py:190
  193.1 103.8 %reduce-scatter.15.cloned.1.call-start = ((), (), s32[]{:S(2)}) async-start(), calls=%async_computation.13 | async-start | bytes 5242880 | tf_op jit(solution)/shard_map/reduce_scatter | solution.py:255
  215.3 5.4 copy-start.51
  215.3 5.4 copy-start.52
  239.3 6.7 copy-start.53
  245.9 1.9 copy-start.56
  245.9 1.9 copy-start.55
  245.9 2.4 copy-start.54
  252.2 78.9 %reduce-scatter.13.cloned.1.call-start = ((), (), s32[]{:S(2)}) async-start(), calls=%async_computation.11 | async-start | bytes 2621440 | tf_op jit(solution)/shard_map/reduce_scatter | solution.py:238
  256.8 74.3 %copy-start.10 = (f32[256,1024]{1,0:T(8,128)S(1)}, f32[256,1024]{1,0:T(8,128)}, u32[]{:S(2)}) copy-start(f32[256,1024]{1,0:T(8,128)} %copy-done.9) | copy-start | bytes 3145732
  256.8 74.3 %copy-start.37 = (f32[1024]{0:T(1024)S(1)}, f32[1024]{0:T(1024)}, u32[]{:S(2)}) copy-start(f32[1024]{0:T(1024)} %param.17) | copy-start | bytes 12292
  256.8 74.3 %copy-start.46 = (f32[256]{0:T(256)S(1)}, f32[256]{0:T(256)}, u32[]{:S(2)}) copy-start(f32[256]{0:T(256)} %copy-done.45) | copy-start | bytes 3076
  256.8 74.3 %copy-start.49 = (f32[256]{0:T(256)S(1)}, f32[256]{0:T(256)}, u32[]{:S(2)}) copy-start(f32[256]{0:T(256)} %get-tuple-element.163) | copy-start | bytes 3076
  256.8 100.3 %all-gather.15.cloned.1.call-start = ((), (), s32[]{:S(2)}) async-start(), calls=%async_computation.14 | async-start | bytes 2621440 | tf_op jit(solution)/shard_map/all_gather | solution.py:263
  331.1 3.3 copy-start.40
  331.2 3.3 copy-start.42
  334.4 116.4 %reduce-scatter.17.cloned.1.call-start = ((), (), s32[]{:S(2)}) async-start(), calls=%async_computation.15 | async-start | bytes 1638400 | tf_op jit(solution)/shard_map/reduce_scatter | solution.py:299
  357.1 3.0 copy-start.4
  361.8 4.1 slice-start
  361.8 4.0 slice-start.1
  363.1 1.6 copy-start.16
  387.8 1.7 copy-start.32
  390.4 7.9 copy-start.12
  390.4 7.9 copy-start.13
  420.8 3.4 copy-start.21
  424.2 62.2 %reduce-scatter.19.cloned.1.call-start = ((), (), s32[]{:S(2)}) async-start(), calls=%async_computation.16 | async-start | bytes 2621440 | tf_op jit(solution)/shard_map/reduce_scatter | solution.py:306
  431.2 8.6 copy-start.14
  450.5 2.5 copy-start.36
  450.7 4.4 copy-start.33
  455.0 100.9 %reduce-scatter.25.cloned.1.call-start = ((), (), s32[]{:S(2)}) async-start(), calls=%async_computation.24 | async-start | bytes 1769472
  460.6 5.3 copy-start.57
  460.6 163.8 %reduce-scatter.23.cloned.1.call-start = ((), (), s32[]{:S(2)}) async-start(), calls=%async_computation.21 | async-start | bytes 1622016 | tf_op jit(solution)/shard_map/reduce_scatter | solution.py:319
  465.8 226.9 %reduce-scatter.21.cloned.1.call-start = ((), (), s32[]{:S(2)}) async-start(), calls=%async_computation.19 | async-start | bytes 1622016 | tf_op jit(solution)/shard_map/reduce_scatter | solution.py:319
  470.2 16.2 %copy-start.11 = (bf16[256,1024]{1,0:T(8,128)(2,1)S(1)}, bf16[256,1024]{1,0:T(8,128)(2,1)}, u32[]{:S(2)}) copy-start(bf16[256,1024]{1,0:T(8,128)(2,1)} %param.11) | copy-start | bytes 1572868
  470.2 16.2 %copy-start.38 = (f32[1024]{0:T(1024)S(1)}, f32[1024]{0:T(1024)}, u32[]{:S(2)}) copy-start(f32[1024]{0:T(1024)} %param.13) | copy-start | bytes 12292
  470.2 16.2 %copy-start.44 = (f32[256]{0:T(256)S(1)}, f32[256]{0:T(256)}, u32[]{:S(2)}) copy-start(f32[256]{0:T(256)} %copy-done.43) | copy-start | bytes 3076
  470.2 17.6 %copy-start.47 = (f32[1024]{0:T(1024)S(1)}, f32[1024]{0:T(1024)}, u32[]{:S(2)}) copy-start(f32[1024]{0:T(1024)} %get-tuple-element.121) | copy-start | bytes 12292
  470.2 300.3 %all-reduce.7.cloned.1.call-start = ((), (), s32[]{:S(2)}) async-start(), calls=%async_computation.17 | async-start | bytes 1474560 | tf_op jit(solution)/shard_map/psum | solution.py:333
  471.8 221.0 %copy-start.34 = (bf16[1024,40]{0,1:T(8,128)(2,1)S(1)}, bf16[1024,40]{0,1:T(8,128)(2,1)}, u32[]{:S(2)}) copy-start(bf16[1024,40]{0,1:T(8,128)(2,1)} %copy-done.33) | copy-start | bytes 245764
  488.9 205.0 %copy-start.23 = (bf16[1024,4,64]{0,2,1:T(8,128)(2,1)S(1)}, bf16[1024,4,64]{0,2,1:T(8,128)(2,1)}, u32[]{:S(2)}) copy-start(bf16[1024,4,64]{0,2,1:T(8,128)(2,1)} %copy-done.22) | copy-start | bytes 1572868
  488.9 326.1 %all-gather.23.cloned.1.call-start = ((), (), s32[]{:S(2)}) async-start(), calls=%async_computation.23 | async-start | bytes 1622016 | tf_op jit(solution)/shard_map/all_gather | solution.py:318
  557.7 300.3 %all-gather.21.cloned.1.call-start = ((), (), s32[]{:S(2)}) async-start(), calls=%async_computation.22 | async-start | bytes 1622016 | tf_op jit(solution)/shard_map/all_gather | solution.py:318
  624.4 277.0 %all-gather.19.cloned.1.call-start = ((), (), s32[]{:S(2)}) async-start(), calls=%async_computation.20 | async-start | bytes 1622016 | tf_op jit(solution)/shard_map/all_gather | solution.py:318
  692.8 284.9 %all-reduce.9.cloned.1.call-start = ((), (), s32[]{:S(2)}) async-start(), calls=%async_computation.25 | async-start | bytes 1212416 | tf_op jit(solution)/shard_map/psum | solution.py:333
  692.8 1.6 copy-start.50
  696.0 309.9 %all-gather.17.cloned.1.call-start = ((), (), s32[]{:S(2)}) async-start(), calls=%async_computation.18 | async-start | bytes 3686400 | tf_op jit(solution)/shard_map/all_gather | solution.py:337
  861.3 120.1 %copy-start.20 = (f32[256,1024]{1,0:T(8,128)S(1)}, f32[256,1024]{1,0:T(8,128)}, u32[]{:S(2)}) copy-start(f32[256,1024]{1,0:T(8,128)} %get-tuple-element.128) | copy-start | bytes 3145732
  861.3 120.1 %copy-start.29 = (bf16[256,1024]{1,0:T(8,128)(2,1)S(1)}, bf16[256,1024]{1,0:T(8,128)(2,1)}, u32[]{:S(2)}) copy-start(bf16[256,1024]{1,0:T(8,128)(2,1)} %reduce-scatter.19.cloned.1.call-done) | copy-start | bytes 1572868
  861.3 120.1 %copy-start.48 = (f32[256]{0:T(256)S(1)}, f32[256]{0:T(256)}, u32[]{:S(2)}) copy-start(f32[256]{0:T(256)} %get-tuple-element.161) | copy-start | bytes 3076
  1005.9 7.8 copy-start.1
  1009.6 3.3 slice-start.2
  (15 other events, 16.7 us)
Sparse Core Ops, SparseCore 0:
  11.8 25.2 all-gather.8
  143.5 44.5 reduce-scatter.10
  192.7 22.5 all-gather.10
  216.7 22.5 all-gather.12
  252.4 44.5 reduce-scatter.14
  299.9 31.1 reduce-scatter.12
  334.5 22.5 all-gather.14
  424.3 26.4 reduce-scatter.16
  455.2 31.1 reduce-scatter.18
  490.2 65.6 reduce-scatter.24
  559.9 64.4 reduce-scatter.22
  628.2 64.4 reduce-scatter.20
  696.8 73.7 all-reduce.6
  773.0 41.9 all-gather.22
  817.1 40.9 all-gather.20
  860.1 41.3 all-gather.18
  905.4 72.2 all-reduce.8
  979.1 26.7 all-gather.16

commit v2 on v1

--- a/solution.py
+++ b/solution.py
@@ -314,27 +314,31 @@
     grad_a = dot_first(normed_all, grad_factor_a)
     grad_b_cols = dot_first(normed_all, factor_cols)
 
-    def dp_sum(values):
-        return lax.all_gather(
-            lax.psum_scatter(values.astype(jnp.bfloat16), "dp", scatter_dimension=1, tiled=True),
-            "dp",
-            axis=1,
-            tiled=True,
-        ).astype(jnp.float32)
-
-    grad_gate, grad_up, grad_down = dp_sum(grad_gate), dp_sum(grad_up), dp_sum(grad_down)
-    grad_out = lax.psum(grad_out.astype(jnp.bfloat16), "dp").astype(jnp.float32)
     features = grad_gain_attn_own.shape[0]
     gain_rows = -(-2 * features // basis_cols)
     gains = jnp.pad(
         jnp.concatenate([grad_gain_attn_own, grad_gain_ffn_own]),
         (0, gain_rows * basis_cols - 2 * features),
     ).reshape(gain_rows, basis_cols)
-    grad_a, packed = lax.psum(
-        (grad_a.astype(jnp.bfloat16), jnp.concatenate([grad_b_cols, gains], axis=0)), "dp"
+    grad_a, grad_out, grad_gate, grad_up, grad_down, packed = lax.psum(
+        (
+            grad_a.astype(jnp.bfloat16),
+            grad_out.astype(jnp.bfloat16),
+            grad_gate.astype(jnp.bfloat16),
+            grad_up.astype(jnp.bfloat16),
+            grad_down.astype(jnp.bfloat16),
+            jnp.concatenate([grad_b_cols, gains], axis=0).astype(jnp.bfloat16),
+        ),
+        "dp",
+    )
+    grad_out, grad_gate, grad_up, grad_down = (
+        grad_out.astype(jnp.float32),
+        grad_gate.astype(jnp.float32),
+        grad_up.astype(jnp.float32),
+        grad_down.astype(jnp.float32),
     )
     grad_a = grad_a.astype(jnp.float32)
-    packed = lax.all_gather(packed, "head", axis=1, tiled=True)
+    packed = lax.all_gather(packed, "head", axis=1, tiled=True).astype(jnp.float32)
     grad_b = packed[: grad_b_cols.shape[0]]
     gains = jnp.sum(
         packed[grad_b_cols.shape[0] :].reshape(gain_rows, head_count, basis_cols), axis=1

time: 1030 us -> 721 us (0.70)
  waiting for transfers between devices: 707 us -> 412 us
    all_gather x4 -> x1, waiting for transfers between devices: 147 us -> 10.6 us  [local(): lax.all_gather(packed, 'head', axis=1, tiled=True).astype(jnp.float32)]
    reduce_scatter x2 -> x0, waiting for transfers between devices: 135 us -> none  [dp_sum(): lax.psum_scatter(values.astype(jnp.bfloat16), 'dp', scatter_dimension=1,...]
    unnamed x19 -> x11, waiting for transfers between devices: 67.7 us -> 0.69 us
    psum x2 -> x1, waiting for transfers between devices: 147 us -> 188 us  [local(): lax.psum((grad_a.astype(jnp.bfloat16), grad_out.astype(jnp.bfloat16), gra...]
    unnamed x130 -> x140, local copies, waits for them, and re-layouts: 32.4 us -> 29.2 us
  transfers between devices with their start and end apart: 18 -> 11, of which waited for: 18 -> 11; matrix products, arithmetic and copies ran while one was open for 8% -> 10% of each run, Pallas kernels for 0% -> 0%
where the time goes in v2:
time: 721 us; the launch traced here: 712 us
  waiting for transfers between devices  412 us (57%)
  matrix products  142 us (20%)
  local copies, waits for them, and re-layouts  79.1 us (11%)
  other arithmetic  63.2 us (9%)
  between operations  14.8 us (2%)
    psum x1, waiting for transfers between devices, local(): lax.psum((grad_a.astype(jnp.bfloat16), grad_out.astype(jnp.bfloat16), gra...  188 us
    reduce_scatter x1, waiting for transfers between devices, local(): lax.psum_scatter(jnp.dot(piece, out_weight, preferred_element_type=jnp.fl...  44.7 us
    reduce_scatter x1, waiting for transfers between devices, local(): lax.psum_scatter(dot_last(gate_piece, gate_weight) + dot_last(up_piece, u...  40.1 us
    reduce_scatter x1, waiting for transfers between devices, local(): lax.psum_scatter(jnp.dot(piece, down_weight, preferred_element_type=jnp.f...  31.8 us
    unnamed x140, local copies, waits for them, and re-layouts  29.2 us
    all_gather x1, waiting for transfers between devices, local(): lax.all_gather(grad_resid.astype(jnp.bfloat16), 'head', axis=0, tiled=True)  22.6 us
    all_gather x1, waiting for transfers between devices, local(): normed_two_all = lax.all_gather(normed_two, 'head', axis=0, tiled=True)  22.1 us
    dot_general x6, matrix products, dot_last(): lax.dot_general(left, right, (((1,), (1,)), ((), ())), preferred_element_...  19.1 us
  transfers between devices with their start and end apart: 11, of which 11 were waited for; matrix products, arithmetic and copies ran while one was open for 10% of the time, Pallas kernels for 0%

profile of v2, /device:TPU:0, one launch (start us, length us, event | category | flops | bytes accessed | tf_op | source)
XLA Modules:
  0.0 711.8 jit_solution(14160441183032752317)
XLA Ops:
  9.7 2.0 fusion.44
  13.5 2.1 fusion.12
  15.6 3.0 multiply_cosine_fusion
  18.6 18.6 %all-gather.6.cloned.1.call-done = bf16[1024,1024]{1,0:T(8,128)(2,1)} async-done(((bf16[256,1024]{1,0:T(8,128)(2,1)}), bf16[1024,1024]{1,0:T(8,128)(2,1)}) %all-gather.6.cloned.1.call-update) | async-done | bytes 2097168 | tf_op jit(solution)/shard_map/all_gather | solution.py:189
  37.2 3.1 fusion.79
  45.2 2.9 fusion.80
  54.3 2.6 copy.268
  58.7 2.7 fusion.70
  61.4 2.2 copy.228
  63.6 2.1 copy.273
  65.7 2.1 copy.272
  67.8 2.6 multiply_subtract_fusion.1
  71.8 10.4 %fusion.67 = f32[1024,4,64]{2,1,0:T(4,128)} fusion(f32[1024,4,2]{1,2,0:T(2,128)S(1)} %copy-done.19, f32[1024,2,32]{2,1,0:T(2,128)S(1)} %get-tuple-element.143, f32[1024,2,32]{2,1,0:T(2,128)S(1)} %get-tuple-element.142), kind=kOutput, calls=%fused_computation.142 | convolution fusion | flops 6422528 | bytes 1605632 | tf_op jit(solution)/shard_map/thr,trd->thd/dot_general | solution.py:208
  82.2 2.7 copy.236
  84.8 2.1 multiply_convert_fusion.7
  86.9 10.8 %fusion.81 = f32[1024,4,64]{2,1,0:T(4,128)} fusion(f32[1024,4,2]{1,2,0:T(2,128)} %copy.267, f32[1024,2,64]{2,1,0:T(2,128)} %copy.228), kind=kOutput, calls=%fused_computation.156 | convolution fusion | flops 6291456 | bytes 1605632 | tf_op jit(solution)/shard_map/thr,trd->thd/dot_general | solution.py:212
  97.8 2.7 copy.229
  100.5 2.1 multiply_convert_fusion.8
  102.6 3.6 copy.270
  106.2 3.6 copy.269
  109.9 4.3 multiply_subtract_fusion
  114.2 8.1 %multiply_convert_fusion.5 = bf16[1024,4,64]{2,1,0:T(4,128)(2,1)S(1)} fusion(f32[1024,4,6]{2,1,0:T(4,128)S(1)} %copy-done.8, f32[1024,6,32]{2,1,0:T(8,128)S(1)} %get-tuple-element.136, f32[1024,6,32]{2,1,0:T(8,128)S(1)} %get-tuple-element.135), kind=kOutput, calls=%fused_computation.40 | convolution fusion | flops 19791872 | bytes 2195456 | tf_op jit(solution)/shard_map/thr,trd->thd/dot_general | solution.py:205
  127.6 2.0 fusion.78
  137.7 2.1 fusion.38
  140.7 2.7 fusion.82
  143.5 44.7 %reduce-scatter.6.cloned.1.call-done = f32[256,1024]{1,0:T(8,128)} async-done(((f32[1024,1024]{1,0:T(8,128)}), f32[256,1024]{1,0:T(8,128)}) %reduce-scatter.6.cloned.1.call-update) | async-done | bytes 1048592 | tf_op jit(solution)/shard_map/reduce_scatter | solution.py:221
  193.2 22.1 %all-gather.8.cloned.1.call-done = bf16[1024,1024]{1,0:T(8,128)(2,1)} async-done(((bf16[256,1024]{1,0:T(8,128)(2,1)}), bf16[1024,1024]{1,0:T(8,128)(2,1)}) %all-gather.8.cloned.1.call-update) | async-done | bytes 2097168 | tf_op jit(solution)/shard_map/all_gather | solution.py:229
  215.3 5.4 fusion.84
  220.7 3.3 fusion.83
  224.0 15.3 %all-gather.10.cloned.1.call-done = bf16[1024,1024]{1,0:T(8,128)(2,1)} async-done(((bf16[256,1024]{1,0:T(8,128)(2,1)}), bf16[1024,1024]{1,0:T(8,128)(2,1)}) %all-gather.10.cloned.1.call-update) | async-done | bytes 2097168 | tf_op jit(solution)/shard_map/all_gather | solution.py:190
  239.3 6.6 multiply_convert_fusion.2
  248.4 3.9 convolution_add_fusion
  252.3 4.5 convolution_convert_fusion
  256.9 40.1 %reduce-scatter.10.cloned.1.call-done = f32[256,1024]{1,0:T(8,128)} async-done(((f32[1024,1024]{1,0:T(8,128)}), f32[256,1024]{1,0:T(8,128)}) %reduce-scatter.10.cloned.1.call-update) | async-done | bytes 1048592 | tf_op jit(solution)/shard_map/reduce_scatter | solution.py:255
  297.0 2.4 multiply_reduce_fusion.2
  299.4 31.8 %reduce-scatter.8.cloned.1.call-done = bf16[256,1024]{1,0:T(8,128)(2,1)} async-done(((bf16[1024,1024]{1,0:T(8,128)(2,1)}), bf16[256,1024]{1,0:T(8,128)(2,1)}) %reduce-scatter.8.cloned.1.call-update) | async-done | bytes 524304 | tf_op jit(solution)/shard_map/reduce_scatter | solution.py:238
  331.2 3.2 fusion.68
  334.5 22.6 %all-gather.12.cloned.1.call-done = bf16[1024,1024]{1,0:T(8,128)(2,1)} async-done(((bf16[256,1024]{1,0:T(8,128)(2,1)}), bf16[1024,1024]{1,0:T(8,128)(2,1)}) %all-gather.12.cloned.1.call-update) | async-done | bytes 2097168 | tf_op jit(solution)/shard_map/all_gather | solution.py:263
  357.1 2.6 convolution_convert_fusion.5
  365.9 4.5 multiply_reduce_fusion
  373.6 5.1 fusion.26
  379.7 6.7 multiply_convert_fusion
  390.4 2.8 copy.246
  393.2 5.1 convolution_multiply_fusion.3
  399.9 2.2 pad_maximum_fusion.8
  404.1 2.3 copy.241
  406.4 6.1 convolution_multiply_fusion
  412.5 3.1 add_convert_fusion.1
  415.6 2.4 copy.254
  418.0 3.0 copy.255
  422.1 2.2 pad_maximum_fusion.3
  424.4 5.6 convolution_multiply_fusion.4
  431.3 7.2 %convolution_multiply_fusion.5 = bf16[1024,4,2]{1,2,0:T(2,128)(2,1)} fusion(bf16[1024,4,64]{2,1,0:T(4,128)(2,1)} %copy.246, f32[1024,2,32]{2,1,0:T(2,128)} %copy-done.18, f32[1024,2,32]{2,1,0:T(2,128)} %copy-done.17), kind=kOutput, calls=%fused_computation.53 | convolution fusion | flops 6438912 | bytes 1064960 | tf_op jit(solution)/shard_map/thd,trd->thr/dot_general | solution.py:275
  439.8 8.9 %convolution_multiply_fusion.1 = bf16[1024,4,6]{2,1,0:T(4,128)(2,1)} fusion(bf16[1024,4,64]{2,1,0:T(4,128)(2,1)S(1)} %copy-done.14, f32[1024,6,32]{2,1,0:T(8,128)} %copy-done.6, f32[1024,6,32]{2,1,0:T(8,128)} %copy-done.5), kind=kOutput, calls=%fused_computation.48 | convolution fusion | flops 19316736 | bytes 2146304 | tf_op jit(solution)/shard_map/thd,trd->thr/dot_general | solution.py:274
  450.8 2.2 fusion.50
  453.0 2.1 add_convert_fusion
  455.3 5.0 convolution_convert_fusion.3
  460.3 2.8 convolution_convert_fusion.1
  463.1 2.8 convolution_convert_fusion.2
  469.7 16.8 %reduce-scatter.14.cloned.1.call-done = bf16[256,1024]{1,0:T(8,128)(2,1)} async-done(((bf16[1024,1024]{1,0:T(8,128)(2,1)}), bf16[256,1024]{1,0:T(8,128)(2,1)}) %reduce-scatter.14.cloned.1.call-update) | async-done | bytes 524304 | tf_op jit(solution)/shard_map/reduce_scatter | solution.py:306
  489.0 188.3 %all-reduce.6.cloned.1.call-done = (bf16[1037,160]{0,1:T(8,128)(2,1)}, bf16[1024,40]{0,1:T(8,128)(2,1)}, bf16[256,1024]{1,0:T(8,128)(2,1)}, bf16[1024,704]{0,1:T...) async-done(((bf16[1037,160]{0,1:T(8,128)(2,1)}, bf16[1024,40]{0,1:T(8,128)(2,1)}, bf16[256,1024]{1,0:T(8,128)(2,1)}, bf16[1024,704]{0,1:T(8,128)(2,1)}, ...) | async-done | bytes 5263440 | tf_op jit(solution)/shard_map/psum | solution.py:323
  686.2 10.6 %all-gather.14.cloned.1.call-done = bf16[1037,640]{0,1:T(8,128)(2,1)} async-done(((bf16[1037,160]{0,1:T(8,128)(2,1)}), bf16[1037,640]{0,1:T(8,128)(2,1)}) %all-gather.14.cloned.1.call-update) | async-done | bytes 1327376 | tf_op jit(solution)/shard_map/all_gather | solution.py:341
  698.6 3.2 slice.177
  701.8 3.2 copy.262
  (228 shorter events, 81.4 us)
Async XLA Ops:
  7.2 232.1 %copy-start = (bf16[704,1024]{1,0:T(8,128)(2,1)S(1)}, bf16[704,1024]{1,0:T(8,128)(2,1)}, u32[]{:S(2)}) copy-start(bf16[704,1024]{1,0:T(8,128)(2,1)} %param.20) | copy-start | bytes 4325380
  7.2 30.0 %all-gather.6.cloned.1.call-start = ((), (), s32[]{:S(2)}) async-start(), calls=%async_computation.5 | async-start | bytes 2621440 | tf_op jit(solution)/shard_map/all_gather | solution.py:189
  11.8 176.4 %reduce-scatter.6.cloned.1.call-start = ((), (), s32[]{:S(2)}) async-start(), calls=%async_computation.6 | async-start | bytes 5242880 | tf_op jit(solution)/shard_map/reduce_scatter | solution.py:221
  37.2 8.0 %copy-start.7 = (bf16[1024,1024]{1,0:T(8,128)(2,1)S(1)}, bf16[1024,1024]{1,0:T(8,128)(2,1)}, u32[]{:S(2)}) copy-start(bf16[1024,1024]{1,0:T(8,128)(2,1)} %all-gather.6.cloned.1.call-done) | copy-start | bytes 6291460
  67.8 3.9 copy-start.19
  109.9 4.3 copy-start.8
  114.1 8.1 %copy-start.5 = (f32[1024,6,32]{2,1,0:T(8,128)}, f32[1024,6,32]{2,1,0:T(8,128)S(1)}, u32[]{:S(2)}) copy-start(f32[1024,6,32]{2,1,0:T(8,128)S(1)} %get-tuple-element.135) | copy-start | bytes 2359300
  114.1 8.1 %copy-start.6 = (f32[1024,6,32]{2,1,0:T(8,128)}, f32[1024,6,32]{2,1,0:T(8,128)S(1)}, u32[]{:S(2)}) copy-start(f32[1024,6,32]{2,1,0:T(8,128)S(1)} %get-tuple-element.136) | copy-start | bytes 2359300
  129.7 2.3 copy-start.3
  129.7 1.4 copy-start.24
  131.1 1.4 copy-start.29
  134.4 3.3 copy-start.2
  137.7 2.1 copy-start.45
  137.7 3.0 copy-start.37
  143.5 71.8 %all-gather.8.cloned.1.call-start = ((), (), s32[]{:S(2)}) async-start(), calls=%async_computation.7 | async-start | bytes 2621440 | tf_op jit(solution)/shard_map/all_gather | solution.py:229
  192.6 46.7 %all-gather.10.cloned.1.call-start = ((), (), s32[]{:S(2)}) async-start(), calls=%async_computation.9 | async-start | bytes 2621440 | tf_op jit(solution)/shard_map/all_gather | solution.py:190
  193.2 103.8 %reduce-scatter.10.cloned.1.call-start = ((), (), s32[]{:S(2)}) async-start(), calls=%async_computation.10 | async-start | bytes 5242880 | tf_op jit(solution)/shard_map/reduce_scatter | solution.py:255
  215.3 5.4 copy-start.54
  215.3 5.4 copy-start.57
  239.3 6.6 copy-start.58
  245.9 1.9 copy-start.62
  246.0 1.9 copy-start.60
  246.0 2.4 copy-start.59
  252.3 78.9 %reduce-scatter.8.cloned.1.call-start = ((), (), s32[]{:S(2)}) async-start(), calls=%async_computation.8 | async-start | bytes 2621440 | tf_op jit(solution)/shard_map/reduce_scatter | solution.py:238
  256.8 74.3 %copy-start.10 = (f32[256,1024]{1,0:T(8,128)S(1)}, f32[256,1024]{1,0:T(8,128)}, u32[]{:S(2)}) copy-start(f32[256,1024]{1,0:T(8,128)} %copy-done.9) | copy-start | bytes 3145732
  256.8 74.3 %copy-start.41 = (f32[1024]{0:T(1024)S(1)}, f32[1024]{0:T(1024)}, u32[]{:S(2)}) copy-start(f32[1024]{0:T(1024)} %param.17) | copy-start | bytes 12292
  256.8 74.3 %copy-start.50 = (f32[256]{0:T(256)S(1)}, f32[256]{0:T(256)}, u32[]{:S(2)}) copy-start(f32[256]{0:T(256)} %copy-done.49) | copy-start | bytes 3076
  256.8 74.3 %copy-start.53 = (f32[256]{0:T(256)S(1)}, f32[256]{0:T(256)}, u32[]{:S(2)}) copy-start(f32[256]{0:T(256)} %get-tuple-element.167) | copy-start | bytes 3076
  256.9 100.3 %all-gather.12.cloned.1.call-start = ((), (), s32[]{:S(2)}) async-start(), calls=%async_computation.11 | async-start | bytes 2621440 | tf_op jit(solution)/shard_map/all_gather | solution.py:263
  331.2 3.3 copy-start.44
  331.2 3.3 copy-start.46
  334.4 116.4 %reduce-scatter.12.cloned.1.call-start = ((), (), s32[]{:S(2)}) async-start(), calls=%async_computation.12 | async-start | bytes 1638400 | tf_op jit(solution)/shard_map/reduce_scatter | solution.py:299
  357.1 3.0 copy-start.4
  361.8 4.1 slice-start
  361.9 4.0 slice-start.1
  363.1 1.6 copy-start.16
  386.4 1.4 copy-start.27
  386.4 1.4 copy-start.31
  387.8 1.7 copy-start.36
  390.4 7.9 %copy-start.12 = (f32[1024,32]{1,0:T(8,128)S(1)}, f32[1024,32]{1,0:T(8,128)}, u32[]{:S(2)}) copy-start(f32[1024,32]{1,0:T(8,128)} %get-tuple-element.161) | copy-start | bytes 393220
  390.4 7.9 %copy-start.13 = (f32[1024,32]{1,0:T(8,128)S(1)}, f32[1024,32]{1,0:T(8,128)}, u32[]{:S(2)}) copy-start(f32[1024,32]{1,0:T(8,128)} %get-tuple-element.162) | copy-start | bytes 393220
  420.9 3.4 copy-start.20
  424.3 62.2 %reduce-scatter.14.cloned.1.call-start = ((), (), s32[]{:S(2)}) async-start(), calls=%async_computation.13 | async-start | bytes 2621440 | tf_op jit(solution)/shard_map/reduce_scatter | solution.py:306
  431.3 8.6 %copy-start.14 = (bf16[1024,4,64]{2,1,0:T(4,128)(2,1)S(1)}, bf16[1024,4,64]{2,1,0:T(4,128)(2,1)}, u32[]{:S(2)}) copy-start(bf16[1024,4,64]{2,1,0:T(4,128)(2,1)} %copy.241) | copy-start | bytes 1572868
  450.6 2.4 copy-start.39
  455.1 222.2 %all-reduce.6.cloned.1.call-start = ((), (), s32[]{:S(2)}) async-start(), calls=%async_computation.15 | async-start | bytes 10600448 | tf_op jit(solution)/shard_map/psum | solution.py:323
  455.3 5.0 copy-start.55
  455.3 5.0 copy-start.61
  460.3 2.8 copy-start.63
  465.9 1.8 copy-start.56
  465.9 3.3 copy-start.35
  467.7 18.8 %copy-start.11 = (bf16[256,1024]{1,0:T(8,128)(2,1)S(1)}, bf16[256,1024]{1,0:T(8,128)(2,1)}, u32[]{:S(2)}) copy-start(bf16[256,1024]{1,0:T(8,128)(2,1)} %param.11) | copy-start | bytes 1572868
  467.7 18.8 %copy-start.42 = (f32[1024]{0:T(1024)S(1)}, f32[1024]{0:T(1024)}, u32[]{:S(2)}) copy-start(f32[1024]{0:T(1024)} %param.13) | copy-start | bytes 12292
  467.7 18.8 %copy-start.48 = (f32[256]{0:T(256)S(1)}, f32[256]{0:T(256)}, u32[]{:S(2)}) copy-start(f32[256]{0:T(256)} %copy-done.47) | copy-start | bytes 3076
  467.7 20.2 %copy-start.51 = (bf16[1024]{0:T(1024)(128)(2,1)S(1)}, bf16[1024]{0:T(1024)(128)(2,1)}, u32[]{:S(2)}) copy-start(bf16[1024]{0:T(1024)(128)(2,1)} %get-tuple-element.121) | copy-start | bytes 6148
  488.9 188.4 %copy-start.21 = (f32[256,1024]{1,0:T(8,128)S(1)}, f32[256,1024]{1,0:T(8,128)}, u32[]{:S(2)}) copy-start(f32[256,1024]{1,0:T(8,128)} %get-tuple-element.132) | copy-start | bytes 3145732
  488.9 188.4 %copy-start.30 = (bf16[256,1024]{1,0:T(8,128)(2,1)S(1)}, bf16[256,1024]{1,0:T(8,128)(2,1)}, u32[]{:S(2)}) copy-start(bf16[256,1024]{1,0:T(8,128)(2,1)} %reduce-scatter.14.cloned.1.call-done) | copy-start | bytes 1572868
  488.9 188.4 %copy-start.52 = (f32[256]{0:T(256)S(1)}, f32[256]{0:T(256)}, u32[]{:S(2)}) copy-start(f32[256]{0:T(256)} %get-tuple-element.165) | copy-start | bytes 3076
  488.9 208.0 %all-gather.14.cloned.1.call-start = ((), (), s32[]{:S(2)}) async-start(), calls=%async_computation.14 | async-start | bytes 1843200 | tf_op jit(solution)/shard_map/all_gather | solution.py:341
  677.3 2.0 copy-start.38
  677.3 3.1 copy-start.34
  679.3 3.0 copy-start.33
  682.3 1.9 copy-start.32
  698.6 6.4 copy-start.1
  (13 other events, 13.5 us)
Sparse Core Ops, SparseCore 0:
  11.9 25.2 all-gather.5
  143.6 44.5 reduce-scatter.5
  192.7 22.5 all-gather.7
  216.7 22.5 all-gather.9
  252.4 44.5 reduce-scatter.9
  299.9 31.1 reduce-scatter.7
  334.5 22.5 all-gather.11
  424.4 26.3 reduce-scatter.11
  455.2 31.2 reduce-scatter.13
  492.0 185.2 all-reduce.5
  678.8 18.0 all-gather.13

commit v3 on v2

--- a/solution.py
+++ b/solution.py
@@ -219,11 +219,11 @@
     mixed = mixed_rows.reshape(total_rows, local_heads * DH)
     piece = lax.slice_in_dim(mixed, 0, lax.axis_size("head") * own_rows, axis=0)
     resid_own = x_own + lax.psum_scatter(
-        jnp.dot(piece, out_weight, preferred_element_type=jnp.float32),
+        jnp.dot(piece, out_weight, preferred_element_type=jnp.float32).astype(jnp.bfloat16),
         "head",
         scatter_dimension=0,
         tiled=True,
-    )
+    ).astype(jnp.float32)
     inv_two = lax.rsqrt(jnp.mean(resid_own * resid_own, axis=-1, keepdims=True) + EPSILON)
     normed_two = (resid_own * inv_two * gain_ffn).astype(jnp.bfloat16)
     normed_two_all = lax.all_gather(normed_two, "head", axis=0, tiled=True)
@@ -253,11 +253,11 @@
     gate_piece = lax.slice_in_dim(grad_gate_act, 0, lax.axis_size("head") * own_rows, axis=0)
     up_piece = lax.slice_in_dim(grad_up_act, 0, lax.axis_size("head") * own_rows, axis=0)
     grad_normed_two = lax.psum_scatter(
-        dot_last(gate_piece, gate_weight) + dot_last(up_piece, up_weight),
+        (dot_last(gate_piece, gate_weight) + dot_last(up_piece, up_weight)).astype(jnp.bfloat16),
         "head",
         scatter_dimension=0,
         tiled=True,
-    )
+    ).astype(jnp.float32)
     resid_part, grad_gain_ffn_own = norm_backward(resid_own, inv_two, gain_ffn, grad_normed_two)
     grad_resid = cotangent.astype(jnp.float32) + resid_part
     grad_branch = lax.all_gather(grad_resid.astype(jnp.bfloat16), "head", axis=0, tiled=True)

time: 721 us -> 689 us (0.956)
  waiting for transfers between devices: 412 us -> 382 us
    reduce_scatter x1, waiting for transfers between devices: 44.7 us -> 31.3 us  [local(): lax.psum_scatter(jnp.dot(piece, out_weight, preferred_element_type=jnp.fl...]
    reduce_scatter x1, waiting for transfers between devices: 40.1 us -> 31.3 us  [local(): lax.psum_scatter((dot_last(gate_piece, gate_weight) + dot_last(up_piece,...]
    unnamed x140 -> x142, local copies, waits for them, and re-layouts: 29.2 us -> 25.9 us
  transfers between devices with their start and end apart: 11 -> 11, of which waited for: 11 -> 10; matrix products, arithmetic and copies ran while one was open for 10% -> 11% of each run, Pallas kernels for 0% -> 0%
where the time goes in v3:
time: 689 us; the launch traced here: 680 us
  waiting for transfers between devices  382 us (55%)
  matrix products  141 us (20%)
  local copies, waits for them, and re-layouts  73 us (11%)
  other arithmetic  67.7 us (10%)
  between operations  15.1 us (2%)
    psum x1, waiting for transfers between devices, local(): lax.psum((grad_a.astype(jnp.bfloat16), grad_out.astype(jnp.bfloat16), gra...  183 us
    reduce_scatter x1, waiting for transfers between devices, local(): lax.psum_scatter(jnp.dot(piece, down_weight, preferred_element_type=jnp.f...  31.8 us
    reduce_scatter x1, waiting for transfers between devices, local(): lax.psum_scatter((dot_last(gate_piece, gate_weight) + dot_last(up_piece,...  31.3 us
    reduce_scatter x1, waiting for transfers between devices, local(): lax.psum_scatter(jnp.dot(piece, out_weight, preferred_element_type=jnp.fl...  31.3 us
    unnamed x142, local copies, waits for them, and re-layouts  25.9 us
    all_gather x1, waiting for transfers between devices, local(): normed_two_all = lax.all_gather(normed_two, 'head', axis=0, tiled=True)  22.1 us
    all_gather x1, waiting for transfers between devices, local(): lax.all_gather(grad_resid.astype(jnp.bfloat16), 'head', axis=0, tiled=True)  21.3 us
    all_gather x1, waiting for transfers between devices, local(): lax.all_gather(normed_one, 'head', axis=0, tiled=True)  18.6 us
  transfers between devices with their start and end apart: 11, of which 10 were waited for; matrix products, arithmetic and copies ran while one was open for 11% of the time, Pallas kernels for 0%

profile of v3, /device:TPU:0, one launch (start us, length us, event | category | flops | bytes accessed | tf_op | source)
XLA Modules:
  0.0 679.7 jit_solution(2196270893880328581)
XLA Ops:
  9.7 2.0 fusion.51
  13.5 2.1 fusion.12
  15.5 3.0 multiply_cosine_fusion
  18.6 18.6 %all-gather.6.cloned.1.call-done = bf16[1024,1024]{1,0:T(8,128)(2,1)} async-done(((bf16[256,1024]{1,0:T(8,128)(2,1)}), bf16[1024,1024]{1,0:T(8,128)(2,1)}) %all-gather.6.cloned.1.call-update) | async-done | bytes 2097168 | tf_op jit(solution)/shard_map/all_gather | solution.py:189
  37.2 3.1 fusion.86
  45.2 2.9 fusion.87
  54.7 2.3 fusion.80
  56.9 2.7 fusion.77
  59.6 2.2 copy.228
  61.8 2.1 copy.273
  63.9 2.1 copy.272
  66.0 2.6 multiply_subtract_fusion.1
  69.9 10.4 %fusion.74 = f32[1024,4,64]{2,1,0:T(4,128)} fusion(f32[1024,4,2]{1,2,0:T(2,128)S(1)} %copy-done.20, f32[1024,2,32]{2,1,0:T(2,128)S(1)} %get-tuple-element.139, f32[1024,2,32]{2,1,0:T(2,128)S(1)} %get-tuple-element.138), kind=kOutput, calls=%fused_computation.149 | convolution fusion | flops 6422528 | bytes 1605632 | tf_op jit(solution)/shard_map/thr,trd->thd/dot_general | solution.py:208
  80.3 2.7 copy.236
  83.0 2.1 multiply_convert_fusion.7
  85.1 10.9 %fusion.88 = f32[1024,4,64]{2,1,0:T(4,128)} fusion(f32[1024,4,2]{1,2,0:T(2,128)} %copy.267, f32[1024,2,64]{2,1,0:T(2,128)} %copy.228), kind=kOutput, calls=%fused_computation.163 | convolution fusion | flops 6291456 | bytes 1605632 | tf_op jit(solution)/shard_map/thr,trd->thd/dot_general | solution.py:212
  96.0 2.7 copy.229
  98.7 2.1 multiply_convert_fusion.8
  100.8 3.6 copy.270
  104.4 3.6 copy.269
  108.0 4.1 multiply_subtract_fusion
  112.2 8.3 %multiply_convert_fusion.5 = bf16[1024,4,64]{2,1,0:T(4,128)(2,1)S(1)} fusion(f32[1024,4,6]{2,1,0:T(4,128)S(1)} %copy.268, f32[1024,6,32]{2,1,0:T(8,128)S(1)} %get-tuple-element.132, f32[1024,6,32]{2,1,0:T(8,128)S(1)} %get-tuple-element.131), kind=kOutput, calls=%fused_computation.41 | convolution fusion | flops 19791872 | bytes 2195456 | tf_op jit(solution)/shard_map/thr,trd->thd/dot_general | solution.py:205
  131.3 2.1 fusion.40
  133.5 2.1 convolution_convert_fusion
  135.7 31.3 %reduce-scatter.6.cloned.1.call-done = bf16[256,1024]{1,0:T(8,128)(2,1)} async-done(((bf16[1024,1024]{1,0:T(8,128)(2,1)}), bf16[256,1024]{1,0:T(8,128)(2,1)}) %reduce-scatter.6.cloned.1.call-update) | async-done | bytes 524304 | tf_op jit(solution)/shard_map/reduce_scatter | solution.py:221
  168.8 2.0 multiply_convert_fusion.6
  171.5 22.1 %all-gather.8.cloned.1.call-done = bf16[1024,1024]{1,0:T(8,128)(2,1)} async-done(((bf16[256,1024]{1,0:T(8,128)(2,1)}), bf16[1024,1024]{1,0:T(8,128)(2,1)}) %all-gather.8.cloned.1.call-update) | async-done | bytes 2097168 | tf_op jit(solution)/shard_map/all_gather | solution.py:229
  193.6 5.4 fusion.90
  199.0 3.3 fusion.89
  202.3 15.3 %all-gather.10.cloned.1.call-done = bf16[1024,1024]{1,0:T(8,128)(2,1)} async-done(((bf16[256,1024]{1,0:T(8,128)(2,1)}), bf16[1024,1024]{1,0:T(8,128)(2,1)}) %all-gather.10.cloned.1.call-update) | async-done | bytes 2097168 | tf_op jit(solution)/shard_map/all_gather | solution.py:190
  217.6 6.5 multiply_convert_fusion.2
  226.5 3.2 add_convert_fusion.2
  229.8 31.3 %reduce-scatter.10.cloned.1.call-done = bf16[256,1024]{1,0:T(8,128)(2,1)} async-done(((bf16[1024,1024]{1,0:T(8,128)(2,1)}), bf16[256,1024]{1,0:T(8,128)(2,1)}) %reduce-scatter.10.cloned.1.call-update) | async-done | bytes 524304 | tf_op jit(solution)/shard_map/reduce_scatter | solution.py:255
  263.6 2.3 fusion.75
  267.4 21.3 %all-gather.12.cloned.1.call-done = bf16[1024,1024]{1,0:T(8,128)(2,1)} async-done(((bf16[256,1024]{1,0:T(8,128)(2,1)}), bf16[1024,1024]{1,0:T(8,128)(2,1)}) %all-gather.12.cloned.1.call-update) | async-done | bytes 2097168 | tf_op jit(solution)/shard_map/all_gather | solution.py:263
  288.6 2.6 convolution_convert_fusion.6
  297.3 4.6 multiply_reduce_fusion
  305.0 5.1 fusion.26
  311.1 6.7 multiply_convert_fusion
  321.8 2.8 copy.246
  324.6 5.1 convolution_multiply_fusion.3
  331.3 2.2 pad_maximum_fusion.8
  335.5 2.3 copy.241
  337.8 6.1 convolution_multiply_fusion
  343.9 3.1 add_convert_fusion.1
  347.0 3.1 copy.254
  350.1 3.0 copy.255
  354.3 2.2 pad_maximum_fusion.3
  356.6 5.6 convolution_multiply_fusion.4
  363.5 7.2 %convolution_multiply_fusion.5 = bf16[1024,4,2]{1,2,0:T(2,128)(2,1)} fusion(bf16[1024,4,64]{2,1,0:T(4,128)(2,1)} %copy.246, f32[1024,2,32]{2,1,0:T(2,128)} %copy-done.19, f32[1024,2,32]{2,1,0:T(2,128)} %copy-done.18), kind=kOutput, calls=%fused_computation.54 | convolution fusion | flops 6438912 | bytes 1064960 | tf_op jit(solution)/shard_map/thd,trd->thr/dot_general | solution.py:275
  372.7 8.8 %convolution_multiply_fusion.1 = bf16[1024,4,6]{2,1,0:T(4,128)(2,1)} fusion(bf16[1024,4,64]{2,1,0:T(4,128)(2,1)S(1)} %copy-done.13, f32[1024,6,32]{2,1,0:T(8,128)} %copy-done.5, f32[1024,6,32]{2,1,0:T(8,128)} %copy-done.4), kind=kOutput, calls=%fused_computation.49 | convolution fusion | flops 19316736 | bytes 2146304 | tf_op jit(solution)/shard_map/thd,trd->thr/dot_general | solution.py:274
  384.2 2.2 fusion.57
  386.4 2.1 add_convert_fusion
  388.7 4.9 convolution_convert_fusion.2
  393.7 2.8 convolution_convert_fusion.3
  396.5 2.8 convolution_convert_fusion.4
  403.1 16.9 %reduce-scatter.14.cloned.1.call-done = bf16[256,1024]{1,0:T(8,128)(2,1)} async-done(((bf16[1024,1024]{1,0:T(8,128)(2,1)}), bf16[256,1024]{1,0:T(8,128)(2,1)}) %reduce-scatter.14.cloned.1.call-update) | async-done | bytes 524304 | tf_op jit(solution)/shard_map/reduce_scatter | solution.py:306
  423.1 4.6 convolution_convert_fusion.1
  427.8 183.2 %all-reduce.6.cloned.1.call-done = (bf16[1037,160]{0,1:T(8,128)(2,1)}, bf16[1024,40]{0,1:T(8,128)(2,1)}, bf16[256,1024]{1,0:T(8,128)(2,1)}, bf16[1024,704]{0,1:T...) async-done(((bf16[1037,160]{0,1:T(8,128)(2,1)}, bf16[1024,40]{0,1:T(8,128)(2,1)}, bf16[256,1024]{1,0:T(8,128)(2,1)}, bf16[1024,704]{0,1:T(8,128)(2,1)}, ...) | async-done | bytes 5263440 | tf_op jit(solution)/shard_map/psum | solution.py:323
  612.2 31.8 %reduce-scatter.8.cloned.1.call-done = bf16[256,1024]{1,0:T(8,128)(2,1)} async-done(((bf16[1024,1024]{1,0:T(8,128)(2,1)}), bf16[256,1024]{1,0:T(8,128)(2,1)}) %reduce-scatter.8.cloned.1.call-update) | async-done | bytes 524304 | tf_op jit(solution)/shard_map/reduce_scatter | solution.py:238
  644.1 3.2 fusion.43
  654.9 9.9 %all-gather.14.cloned.1.call-done = bf16[1037,640]{0,1:T(8,128)(2,1)} async-done(((bf16[1037,160]{0,1:T(8,128)(2,1)}), bf16[1037,640]{0,1:T(8,128)(2,1)}) %all-gather.14.cloned.1.call-update) | async-done | bytes 1327376 | tf_op jit(solution)/shard_map/all_gather | solution.py:341
  666.5 3.1 slice.177
  669.6 3.2 copy.262
  (230 shorter events, 79.5 us)
Async XLA Ops:
  7.2 210.5 %copy-start = (bf16[704,1024]{1,0:T(8,128)(2,1)S(1)}, bf16[704,1024]{1,0:T(8,128)(2,1)}, u32[]{:S(2)}) copy-start(bf16[704,1024]{1,0:T(8,128)(2,1)} %param.20) | copy-start | bytes 4325380
  7.2 30.0 %all-gather.6.cloned.1.call-start = ((), (), s32[]{:S(2)}) async-start(), calls=%async_computation.5 | async-start | bytes 2621440 | tf_op jit(solution)/shard_map/all_gather | solution.py:189
  11.8 155.2 %reduce-scatter.6.cloned.1.call-start = ((), (), s32[]{:S(2)}) async-start(), calls=%async_computation.6 | async-start | bytes 2621440 | tf_op jit(solution)/shard_map/reduce_scatter | solution.py:221
  37.2 8.0 %copy-start.7 = (bf16[1024,1024]{1,0:T(8,128)(2,1)S(1)}, bf16[1024,1024]{1,0:T(8,128)(2,1)}, u32[]{:S(2)}) copy-start(bf16[1024,1024]{1,0:T(8,128)(2,1)} %all-gather.6.cloned.1.call-done) | copy-start | bytes 6291460
  48.1 2.3 copy-start.41
  48.1 3.6 copy-start.40
  54.6 57.5 %copy-start.9 = (f32[1024,4,6]{2,1,0:T(4,128)}, f32[1024,4,6]{2,1,0:T(4,128)S(1)}, u32[]{:S(2)}) copy-start(f32[1024,4,6]{2,1,0:T(4,128)S(1)} %copy.268) | copy-start | bytes 294916
  66.0 3.9 copy-start.20
  112.2 8.3 %copy-start.4 = (f32[1024,6,32]{2,1,0:T(8,128)}, f32[1024,6,32]{2,1,0:T(8,128)S(1)}, u32[]{:S(2)}) copy-start(f32[1024,6,32]{2,1,0:T(8,128)S(1)} %get-tuple-element.131) | copy-start | bytes 2359300
  112.2 8.3 %copy-start.5 = (f32[1024,6,32]{2,1,0:T(8,128)}, f32[1024,6,32]{2,1,0:T(8,128)S(1)}, u32[]{:S(2)}) copy-start(f32[1024,6,32]{2,1,0:T(8,128)S(1)} %get-tuple-element.132) | copy-start | bytes 2359300
  121.2 2.3 copy-start.26
  121.6 4.2 copy-start.24
  123.5 2.3 copy-start.2
  128.0 3.3 copy-start.1
  131.3 2.1 copy-start.47
  131.3 2.2 copy-start.38
  133.5 34.8 %copy-start.29 = (bf16[1024,4,64]{0,2,1:T(8,128)(2,1)}, bf16[1024,4,64]{0,2,1:T(8,128)(2,1)S(1)}, u32[]{:S(2)}) copy-start(bf16[1024,4,64]{0,2,1:T(8,128)(2,1)S(1)} %pad_maximum_fusion.6) | copy-start | bytes 1572868
  133.5 33.5 %copy-start.6 = (bf16[256,1024]{1,0:T(8,128)(2,1)S(1)}, bf16[256,1024]{1,0:T(8,128)(2,1)}, u32[]{:S(2)}) copy-start(bf16[256,1024]{1,0:T(8,128)(2,1)} %param.11) | copy-start | bytes 1572868
  133.5 35.3 %copy-start.43 = (f32[1024]{0:T(1024)S(1)}, f32[1024]{0:T(1024)}, u32[]{:S(2)}) copy-start(f32[1024]{0:T(1024)} %param.17) | copy-start | bytes 12292
  135.7 58.0 %all-gather.8.cloned.1.call-start = ((), (), s32[]{:S(2)}) async-start(), calls=%async_computation.7 | async-start | bytes 2621440 | tf_op jit(solution)/shard_map/all_gather | solution.py:229
  168.8 30.2 %copy-start.48 = (f32[256]{0:T(256)}, f32[256]{0:T(256)S(1)}, u32[]{:S(2)}) copy-start(f32[256]{0:T(256)S(1)} %get-tuple-element.165) | copy-start | bytes 3076
  170.9 46.7 %all-gather.10.cloned.1.call-start = ((), (), s32[]{:S(2)}) async-start(), calls=%async_computation.9 | async-start | bytes 2621440 | tf_op jit(solution)/shard_map/all_gather | solution.py:190
  171.5 89.6 %reduce-scatter.10.cloned.1.call-start = ((), (), s32[]{:S(2)}) async-start(), calls=%async_computation.10 | async-start | bytes 2621440 | tf_op jit(solution)/shard_map/reduce_scatter | solution.py:255
  193.6 5.4 copy-start.54
  193.6 5.4 copy-start.58
  217.6 6.5 copy-start.59
  224.1 1.9 copy-start.61
  224.1 1.9 copy-start.63
  224.1 2.4 copy-start.60
  226.5 34.5 %copy-start.10 = (bf16[256,1024]{1,0:T(8,128)(2,1)S(1)}, bf16[256,1024]{1,0:T(8,128)(2,1)}, u32[]{:S(2)}) copy-start(bf16[256,1024]{1,0:T(8,128)(2,1)} %reduce-scatter.6.cloned.1.call-done) | copy-start | bytes 1572868
  229.7 34.0 %copy-start.16 = (bf16[256,1024]{1,0:T(8,128)(2,1)S(1)}, bf16[256,1024]{1,0:T(8,128)(2,1)}, u32[]{:S(2)}) copy-start(bf16[256,1024]{1,0:T(8,128)(2,1)} %param.21) | copy-start | bytes 1572868
  229.7 58.9 %all-gather.12.cloned.1.call-start = ((), (), s32[]{:S(2)}) async-start(), calls=%async_computation.11 | async-start | bytes 2621440 | tf_op jit(solution)/shard_map/all_gather | solution.py:263
  265.9 118.2 %reduce-scatter.12.cloned.1.call-start = ((), (), s32[]{:S(2)}) async-start(), calls=%async_computation.12 | async-start | bytes 1638400 | tf_op jit(solution)/shard_map/reduce_scatter | solution.py:299
  288.6 3.0 copy-start.3
  293.3 4.0 slice-start
  293.4 4.0 slice-start.1
  321.8 7.9 %copy-start.11 = (f32[1024,32]{1,0:T(8,128)S(1)}, f32[1024,32]{1,0:T(8,128)}, u32[]{:S(2)}) copy-start(f32[1024,32]{1,0:T(8,128)} %get-tuple-element.158) | copy-start | bytes 393220
  321.8 7.9 %copy-start.12 = (f32[1024,32]{1,0:T(8,128)S(1)}, f32[1024,32]{1,0:T(8,128)}, u32[]{:S(2)}) copy-start(f32[1024,32]{1,0:T(8,128)} %get-tuple-element.159) | copy-start | bytes 393220
  353.0 3.5 copy-start.21
  356.5 63.5 %reduce-scatter.14.cloned.1.call-start = ((), (), s32[]{:S(2)}) async-start(), calls=%async_computation.13 | async-start | bytes 2621440 | tf_op jit(solution)/shard_map/reduce_scatter | solution.py:306
  363.5 9.2 %copy-start.13 = (bf16[1024,4,64]{2,1,0:T(4,128)(2,1)S(1)}, bf16[1024,4,64]{2,1,0:T(4,128)(2,1)}, u32[]{:S(2)}) copy-start(bf16[1024,4,64]{2,1,0:T(4,128)(2,1)} %copy.241) | copy-start | bytes 1572868
  383.2 3.1 copy-start.39
  388.4 222.5 %all-reduce.6.cloned.1.call-start = ((), (), s32[]{:S(2)}) async-start(), calls=%async_computation.15 | async-start | bytes 10600448 | tf_op jit(solution)/shard_map/psum | solution.py:323
  388.7 5.0 copy-start.55
  388.7 5.0 copy-start.62
  393.7 2.8 copy-start.56
  393.7 2.8 copy-start.64
  396.4 2.8 copy-start.8
  399.2 1.8 copy-start.57
  399.2 3.3 copy-start.35
  401.0 19.0 %copy-start.45 = (f32[1024]{0:T(1024)S(1)}, f32[1024]{0:T(1024)}, u32[]{:S(2)}) copy-start(f32[1024]{0:T(1024)} %param.13) | copy-start | bytes 12292
  401.0 19.0 %copy-start.51 = (f32[256]{0:T(256)S(1)}, f32[256]{0:T(256)}, u32[]{:S(2)}) copy-start(f32[256]{0:T(256)} %copy-done.50) | copy-start | bytes 3076
  401.0 21.0 %copy-start.53 = (bf16[1024]{0:T(1024)(128)(2,1)S(1)}, bf16[1024]{0:T(1024)(128)(2,1)}, u32[]{:S(2)}) copy-start(bf16[1024]{0:T(1024)(128)(2,1)} %get-tuple-element.121) | copy-start | bytes 6148
  423.0 221.0 %copy-start.15 = (bf16[256,1024]{1,0:T(8,128)(2,1)S(1)}, bf16[256,1024]{1,0:T(8,128)(2,1)}, u32[]{:S(2)}) copy-start(bf16[256,1024]{1,0:T(8,128)(2,1)} %reduce-scatter.10.cloned.1.call-done) | copy-start | bytes 1572868
  423.0 221.0 %copy-start.17 = (bf16[256,1024]{1,0:T(8,128)(2,1)S(1)}, bf16[256,1024]{1,0:T(8,128)(2,1)}, u32[]{:S(2)}) copy-start(bf16[256,1024]{1,0:T(8,128)(2,1)} %param.21) | copy-start | bytes 1572868
  423.0 221.0 %copy-start.44 = (f32[1024]{0:T(1024)S(1)}, f32[1024]{0:T(1024)}, u32[]{:S(2)}) copy-start(f32[1024]{0:T(1024)} %param.17) | copy-start | bytes 12292
  423.0 221.0 %copy-start.49 = (f32[256]{0:T(256)S(1)}, f32[256]{0:T(256)}, u32[]{:S(2)}) copy-start(f32[256]{0:T(256)} %copy-done.48) | copy-start | bytes 3076
  423.1 221.0 %reduce-scatter.8.cloned.1.call-start = ((), (), s32[]{:S(2)}) async-start(), calls=%async_computation.8 | async-start | bytes 2621440 | tf_op jit(solution)/shard_map/reduce_scatter | solution.py:238
  427.7 237.0 %all-gather.14.cloned.1.call-start = ((), (), s32[]{:S(2)}) async-start(), calls=%async_computation.14 | async-start | bytes 1843200 | tf_op jit(solution)/shard_map/all_gather | solution.py:341
  644.0 3.2 copy-start.42
  644.0 3.9 copy-start.37
  644.1 5.0 copy-start.34
  648.0 3.0 copy-start.33
  651.0 1.9 copy-start.32
  (14 other events, 16.0 us)
Sparse Core Ops, SparseCore 0:
  11.9 25.2 all-gather.5
  135.8 31.1 reduce-scatter.5
  171.0 22.5 all-gather.7
  195.0 22.5 all-gather.9
  229.8 31.1 reduce-scatter.9
  266.0 22.5 all-gather.11
  356.6 26.4 reduce-scatter.11
  388.6 31.4 reduce-scatter.13
  425.6 185.2 all-reduce.5
  613.9 30.0 reduce-scatter.7
  645.6 19.0 all-gather.13

commit v4 on v3

--- a/solution.py
+++ b/solution.py
@@ -162,6 +162,19 @@
 
 def rounded(values_in):
     return lax.optimization_barrier(values_in.astype(jnp.bfloat16)).astype(jnp.float32)
+
+
+def head_reduce_scatter(values, axis):
+    count = lax.axis_size("head")
+    own = lax.axis_index("head")
+    width = values.shape[axis] // count
+    total = lax.dynamic_slice_in_dim(values, own * width, width, axis=axis).astype(jnp.float32)
+    for shift in range(1, count):
+        sent = lax.dynamic_slice_in_dim(values, ((own + shift) % count) * width, width, axis=axis)
+        total = total + lax.ppermute(
+            sent, "head", [(device, (device + shift) % count) for device in range(count)]
+        ).astype(jnp.float32)
+    return total
 
 
 def local(
@@ -260,6 +273,7 @@
     ).astype(jnp.float32)
     resid_part, grad_gain_ffn_own = norm_backward(resid_own, inv_two, gain_ffn, grad_normed_two)
     grad_resid = cotangent.astype(jnp.float32) + resid_part
+    output, grad_resid = lax.optimization_barrier((output, grad_resid))
     grad_branch = lax.all_gather(grad_resid.astype(jnp.bfloat16), "head", axis=0, tiled=True)
     grad_mixed = dot_last(grad_branch, out_weight).astype(jnp.bfloat16)
     grad_out = dot_first(mixed, grad_branch)
@@ -296,19 +310,14 @@
     )
     head_count = lax.axis_size("head")
     basis_cols = grad_factor_b.shape[1] // head_count
-    factor_cols = lax.psum_scatter(
-        grad_factor_b.astype(jnp.bfloat16), "head", scatter_dimension=1, tiled=True
-    )
+    factor_cols = head_reduce_scatter(grad_factor_b.astype(jnp.bfloat16), 1).astype(jnp.bfloat16)
     weight_cols = lax.dynamic_slice_in_dim(
         b_weight, lax.axis_index("head") * basis_cols, basis_cols, axis=1
     )
     piece = grad_factor_a
-    grad_normed_one = lax.psum_scatter(
-        (dot_last(piece, a_weight) + dot_last(factor_cols, weight_cols)).astype(jnp.bfloat16),
-        "head",
-        scatter_dimension=0,
-        tiled=True,
-    ).astype(jnp.float32)
+    grad_normed_one = head_reduce_scatter(
+        (dot_last(piece, a_weight) + dot_last(factor_cols, weight_cols)).astype(jnp.bfloat16), 0
+    )
     input_part, grad_gain_attn_own = norm_backward(x_own, inv_one, gain_attn, grad_normed_one)
     input_grad = grad_resid + input_part
     grad_a = dot_first(normed_all, grad_factor_a)
@@ -320,17 +329,20 @@
         jnp.concatenate([grad_gain_attn_own, grad_gain_ffn_own]),
         (0, gain_rows * basis_cols - 2 * features),
     ).reshape(gain_rows, basis_cols)
-    grad_a, grad_out, grad_gate, grad_up, grad_down, packed = lax.psum(
+    grad_out, grad_gate, grad_up, grad_down = lax.psum(
         (
-            grad_a.astype(jnp.bfloat16),
             grad_out.astype(jnp.bfloat16),
             grad_gate.astype(jnp.bfloat16),
             grad_up.astype(jnp.bfloat16),
             grad_down.astype(jnp.bfloat16),
-            jnp.concatenate([grad_b_cols, gains], axis=0).astype(jnp.bfloat16),
         ),
         "dp",
     )
+    tail = (grad_a.astype(jnp.bfloat16), jnp.concatenate([grad_b_cols, gains], axis=0).astype(jnp.bfloat16))
+    tail, (grad_out, grad_gate, grad_up, grad_down) = lax.optimization_barrier(
+        (tail, (grad_out, grad_gate, grad_up, grad_down))
+    )
+    grad_a, packed = lax.psum(tail, "dp")
     grad_out, grad_gate, grad_up, grad_down = (
         grad_out.astype(jnp.float32),
         grad_gate.astype(jnp.float32),

time: 689 us -> 674 us (0.978)
  waiting for transfers between devices: 382 us -> 371 us
  other arithmetic: 67.7 us -> 58.9 us
    ppermute x0 -> x6, waiting for transfers between devices: none -> 36 us  [head_reduce_scatter(): lax.ppermute(sent, 'head', [(device, (device + shift) % count) for device...]
    psum x1 -> x2, waiting for transfers between devices: 183 us -> 164 us  [the longest x1 89.1 us: local(): lax.psum((grad_out.astype(jnp.bfloat16), grad_gate.astype(jnp.bfloat16),...]
    reduce_scatter x2 -> x0, waiting for transfers between devices: 17 us -> none  [the longest x1 16.9 us: local(): lax.psum_scatter((dot_last(piece, a_weight) + dot_last(factor_cols, weigh...]
    all_gather x1, waiting for transfers between devices: 21.3 us -> 12 us  [local(): lax.all_gather(grad_resid.astype(jnp.bfloat16), 'head', axis=0, tiled=True)]
    unnamed x142 -> x154, local copies, waits for them, and re-layouts: 25.9 us -> 24.8 us
  transfers between devices with their start and end apart: 11 -> 16, of which waited for: 10 -> 16; matrix products, arithmetic and copies ran while one was open for 11% -> 13% of each run, Pallas kernels for 0% -> 0%
where the time goes in v4:
time: 674 us; the launch traced here: 664 us
  waiting for transfers between devices  371 us (55%)
  matrix products  145 us (22%)
  local copies, waits for them, and re-layouts  69.3 us (10%)
  other arithmetic  58.9 us (9%)
  between operations  15.6 us (2%)
    psum x1, waiting for transfers between devices, local(): lax.psum((grad_out.astype(jnp.bfloat16), grad_gate.astype(jnp.bfloat16),...  89.1 us
    psum x1, waiting for transfers between devices, local(): grad_a, packed = lax.psum(tail, 'dp')  75.3 us
    ppermute x6, waiting for transfers between devices, head_reduce_scatter(): lax.ppermute(sent, 'head', [(device, (device + shift) % count) for device...  36 us
    reduce_scatter x1, waiting for transfers between devices, local(): lax.psum_scatter(jnp.dot(piece, down_weight, preferred_element_type=jnp.f...  32.7 us
    reduce_scatter x1, waiting for transfers between devices, local(): lax.psum_scatter(jnp.dot(piece, out_weight, preferred_element_type=jnp.fl...  31.2 us
    reduce_scatter x1, waiting for transfers between devices, local(): lax.psum_scatter((dot_last(gate_piece, gate_weight) + dot_last(up_piece,...  26.6 us
    unnamed x154, local copies, waits for them, and re-layouts  24.8 us
    all_gather x1, waiting for transfers between devices, local(): normed_two_all = lax.all_gather(normed_two, 'head', axis=0, tiled=True)  22.1 us
  transfers between devices with their start and end apart: 16, of which 16 were waited for; matrix products, arithmetic and copies ran while one was open for 13% of the time, Pallas kernels for 0%

profile of v4, /device:TPU:0, one launch (start us, length us, event | category | flops | bytes accessed | tf_op | source)
XLA Modules:
  0.0 664.1 jit_solution(16538023197283299411)
XLA Ops:
  13.5 2.1 fusion.12
  15.6 3.1 multiply_cosine_fusion
  18.6 18.6 %all-gather.6.cloned.1.call-done = bf16[1024,1024]{1,0:T(8,128)(2,1)} async-done(((bf16[256,1024]{1,0:T(8,128)(2,1)}), bf16[1024,1024]{1,0:T(8,128)(2,1)}) %all-gather.6.cloned.1.call-update) | async-done | bytes 2097168 | tf_op jit(solution)/shard_map/all_gather | solution.py:202
  37.2 3.1 fusion.83
  45.2 2.9 fusion.84
  54.7 2.3 fusion.77
  56.9 2.7 fusion.74
  59.7 2.2 copy.228
  61.8 2.1 copy.273
  63.9 2.1 copy.272
  66.1 2.6 multiply_subtract_fusion.1
  70.0 10.4 %fusion.72 = f32[1024,4,64]{2,1,0:T(4,128)} fusion(f32[1024,4,2]{1,2,0:T(2,128)S(1)} %copy-done.20, f32[1024,2,32]{2,1,0:T(2,128)S(1)} %get-tuple-element.156, f32[1024,2,32]{2,1,0:T(2,128)S(1)} %get-tuple-element.155), kind=kOutput, calls=%fused_computation.154 | convolution fusion | flops 6422528 | bytes 1605632 | tf_op jit(solution)/shard_map/thr,trd->thd/dot_general | solution.py:221
  80.4 2.7 copy.236
  83.1 2.1 multiply_convert_fusion.7
  85.2 10.9 %fusion.85 = f32[1024,4,64]{2,1,0:T(4,128)} fusion(f32[1024,4,2]{1,2,0:T(2,128)} %copy.267, f32[1024,2,64]{2,1,0:T(2,128)} %copy.228), kind=kOutput, calls=%fused_computation.167 | convolution fusion | flops 6291456 | bytes 1605632 | tf_op jit(solution)/shard_map/thr,trd->thd/dot_general | solution.py:225
  96.1 2.7 copy.229
  98.7 2.1 multiply_convert_fusion.8
  100.8 3.6 copy.270
  104.5 3.7 copy.269
  108.1 4.2 multiply_subtract_fusion
  112.3 8.3 %multiply_convert_fusion.5 = bf16[1024,4,64]{2,1,0:T(4,128)(2,1)S(1)} fusion(f32[1024,4,6]{2,1,0:T(4,128)S(1)} %copy.268, f32[1024,6,32]{2,1,0:T(8,128)S(1)} %get-tuple-element.149, f32[1024,6,32]{2,1,0:T(8,128)S(1)} %get-tuple-element.148), kind=kOutput, calls=%fused_computation.41 | convolution fusion | flops 19791872 | bytes 2195456 | tf_op jit(solution)/shard_map/thr,trd->thd/dot_general | solution.py:218
  131.5 2.1 fusion.39
  133.7 2.1 convolution_convert_fusion
  135.9 31.2 %reduce-scatter.4.cloned.1.call-done = bf16[256,1024]{1,0:T(8,128)(2,1)} async-done(((bf16[1024,1024]{1,0:T(8,128)(2,1)}), bf16[256,1024]{1,0:T(8,128)(2,1)}) %reduce-scatter.4.cloned.1.call-update) | async-done | bytes 524304 | tf_op jit(solution)/shard_map/reduce_scatter | solution.py:234
  171.7 22.1 %all-gather.8.cloned.1.call-done = bf16[1024,1024]{1,0:T(8,128)(2,1)} async-done(((bf16[256,1024]{1,0:T(8,128)(2,1)}), bf16[1024,1024]{1,0:T(8,128)(2,1)}) %all-gather.8.cloned.1.call-update) | async-done | bytes 2097168 | tf_op jit(solution)/shard_map/all_gather | solution.py:242
  193.8 5.4 fusion.87
  199.2 3.3 fusion.86
  202.5 15.3 %all-gather.10.cloned.1.call-done = bf16[1024,1024]{1,0:T(8,128)(2,1)} async-done(((bf16[256,1024]{1,0:T(8,128)(2,1)}), bf16[1024,1024]{1,0:T(8,128)(2,1)}) %all-gather.10.cloned.1.call-update) | async-done | bytes 2097168 | tf_op jit(solution)/shard_map/all_gather | solution.py:203
  217.8 6.5 multiply_convert_fusion.2
  226.7 3.2 add_convert_fusion.2
  229.9 4.6 convolution_convert_fusion.1
  234.6 26.6 %reduce-scatter.8.cloned.1.call-done = bf16[256,1024]{1,0:T(8,128)(2,1)} async-done(((bf16[1024,1024]{1,0:T(8,128)(2,1)}), bf16[256,1024]{1,0:T(8,128)(2,1)}) %reduce-scatter.8.cloned.1.call-update) | async-done | bytes 524304 | tf_op jit(solution)/shard_map/reduce_scatter | solution.py:268
  262.6 32.7 %reduce-scatter.6.cloned.1.call-done = bf16[256,1024]{1,0:T(8,128)(2,1)} async-done(((bf16[1024,1024]{1,0:T(8,128)(2,1)}), bf16[256,1024]{1,0:T(8,128)(2,1)}) %reduce-scatter.6.cloned.1.call-update) | async-done | bytes 524304 | tf_op jit(solution)/shard_map/reduce_scatter | solution.py:251
  295.4 2.5 fusion.42
  298.9 4.9 convolution_convert_fusion.4
  303.9 2.8 convolution_convert_fusion.2
  306.7 2.8 convolution_convert_fusion.3
  309.4 12.0 %all-gather.12.cloned.1.call-done = bf16[1024,1024]{1,0:T(8,128)(2,1)} async-done(((bf16[256,1024]{1,0:T(8,128)(2,1)}), bf16[1024,1024]{1,0:T(8,128)(2,1)}) %all-gather.12.cloned.1.call-update) | async-done | bytes 2097168 | tf_op jit(solution)/shard_map/all_gather | solution.py:277
  321.5 2.5 convolution_convert_fusion.6
  325.1 5.7 fusion.22
  330.8 2.7 copy.249
  333.5 5.7 fusion.26
  339.2 5.9 convolution_multiply_fusion.4
  350.1 4.4 multiply_reduce_fusion
  356.9 6.9 %multiply_convert_fusion = bf16[4,512,1024]{2,1,0:T(8,128)(2,1)S(1)} fusion(f32[4,512,1024]{2,1,0:T(8,128)} %get-tuple-element.194, f32[4,512,1024]{2,1,0:T(8,128)} %copy-done.2, f32[4,512]{1,0:T(4,128)S(1)} %get-tuple-element.193, f32[4,512]{1,0:T(4,128)S(1)} %log_add_fusion), kind=kLoop, calls=%fused_computation | loop fusion | flops 8388608 | bytes 20987904 | tf_op jit(solution)/shard_map/while/body/eval_jaxpr/convert_element_type | solution.py:135
  368.4 6.6 %convolution_multiply_fusion.5 = bf16[1024,4,2]{1,2,0:T(2,128)(2,1)} fusion(bf16[1024,4,64]{2,1,0:T(4,128)(2,1)} %copy.246, f32[1024,2,32]{2,1,0:T(2,128)} %copy-done.19, f32[1024,2,32]{2,1,0:T(2,128)S(1)} %copy-done.18), kind=kOutput, calls=%fused_computation.54 | convolution fusion | flops 6438912 | bytes 1064960 | tf_op jit(solution)/shard_map/thd,trd->thr/dot_general | solution.py:289
  376.5 3.1 convolution_convert_fusion.5
  379.7 5.1 convolution_multiply_fusion.3
  386.7 2.2 pad_maximum_fusion.8
  392.2 9.1 %convolution_multiply_fusion.1 = bf16[1024,4,6]{2,1,0:T(4,128)(2,1)} fusion(bf16[1024,4,64]{2,1,0:T(4,128)(2,1)} %copy.241, f32[1024,6,32]{2,1,0:T(8,128)} %copy-done.7, f32[1024,6,32]{2,1,0:T(8,128)} %copy-done.6), kind=kOutput, calls=%fused_computation.49 | convolution fusion | flops 19316736 | bytes 2146304 | tf_op jit(solution)/shard_map/thd,trd->thr/dot_general | solution.py:288
  403.5 6.1 convolution_multiply_fusion
  409.6 3.1 add_convert_fusion.1
  412.7 2.3 copy.254
  415.0 2.3 copy.255
  420.5 6.6 collective-permute-done
  427.5 7.2 %collective-permute-done.1 = bf16[1024,160]{0,1:T(8,128)(2,1)S(1)} collective-permute-done((bf16[1024,160]{0,1:T(8,128)(2,1)S(1)}, bf16[1024,160]{0,1:T(8,128)(2,1)S(1)}, u32[]{:S(2)}, u32[]{:S(2)}) %collective-permute-start.1) | collective-permute-done | bytes 327712 | tf_op jit(solution)/shard_map/ppermute | solution.py:174
  435.0 2.1 add_convert_fusion
  441.0 9.9 %collective-permute-done.3 = bf16[256,1024]{1,0:T(8,128)(2,1)S(1)} collective-permute-done((bf16[256,1024]{1,0:T(8,128)(2,1)S(1)}, bf16[256,1024]{1,0:T(8,128)(2,1)S(1)}, u32[]{:S(2)}, u32[]{:S(2)}) %collective-permute-start.3) | collective-permute-done | bytes 524320 | tf_op jit(solution)/shard_map/ppermute | solution.py:174
  451.4 11.4 %collective-permute-done.4 = bf16[256,1024]{1,0:T(8,128)(2,1)S(1)} collective-permute-done((bf16[256,1024]{1,0:T(8,128)(2,1)S(1)}, bf16[256,1024]{1,0:T(8,128)(2,1)S(1)}, u32[]{:S(2)}, u32[]{:S(2)}) %collective-permute-start.4) | collective-permute-done | bytes 524320 | tf_op jit(solution)/shard_map/ppermute | solution.py:174
  464.3 89.1 %all-reduce.10.cloned.1.call-done = (bf16[256,1024]{1,0:T(8,128)(2,1)}, bf16[1024,704]{0,1:T(8,128)(2,1)}, bf16[1024,704]{0,1:T(8,128)(2,1)}, bf16[704,1024]{1,0:T(8,128)(2,1)}) async-done(((bf16[256,1024]{1,0:T(8,128)(2,1)}, bf16[1024,704]{0,1:T(8,128)(2,1)}, bf16[1024,704]{0,1:T(8,128)(2,1)}, bf16[704,1024]{1,0:T(8,128)(2,1)}), (bf16[256,1024]{1,0:T(8,128)(2,1)}, bf16[1024,704]{0,1:T(8,128)(2,1)}, ...) | async-done | bytes 4849680 | tf_op jit(solution)/shard_map/psum | solution.py:332
  553.5 75.3 %all-reduce.8.cloned.1.call-done = (bf16[1037,160]{0,1:T(8,128)(2,1)}, bf16[1024,40]{0,1:T(8,128)(2,1)}) async-done(((bf16[1037,160]{0,1:T(8,128)(2,1)}, bf16[1024,40]{0,1:T(8,128)(2,1)}), (bf16[1037,160]{0,1:T(8,128)(2,1)}, bf16[1024,40]{0,1:T(8,128)(2,1)})) %all-reduce.8.cloned.1.call-update) | async-done | bytes 413776 | tf_op jit(solution)/shard_map/psum | solution.py:345
  637.7 11.0 %all-gather.14.cloned.1.call-done = bf16[1037,640]{0,1:T(8,128)(2,1)} async-done(((bf16[1037,160]{0,1:T(8,128)(2,1)}), bf16[1037,640]{0,1:T(8,128)(2,1)}) %all-gather.14.cloned.1.call-update) | async-done | bytes 1327376 | tf_op jit(solution)/shard_map/all_gather | solution.py:353
  650.4 3.2 slice.177
  653.7 3.2 copy.262
  (255 shorter events, 81.4 us)
Async XLA Ops:
  7.2 210.6 %copy-start = (bf16[704,1024]{1,0:T(8,128)(2,1)S(1)}, bf16[704,1024]{1,0:T(8,128)(2,1)}, u32[]{:S(2)}) copy-start(bf16[704,1024]{1,0:T(8,128)(2,1)} %param.20) | copy-start | bytes 4325380
  7.2 30.0 %all-gather.6.cloned.1.call-start = ((), (), s32[]{:S(2)}) async-start(), calls=%async_computation.3 | async-start | bytes 2621440 | tf_op jit(solution)/shard_map/all_gather | solution.py:202
  11.8 155.3 %reduce-scatter.4.cloned.1.call-start = ((), (), s32[]{:S(2)}) async-start(), calls=%async_computation.4 | async-start | bytes 2621440 | tf_op jit(solution)/shard_map/reduce_scatter | solution.py:234
  37.2 8.0 %copy-start.9 = (bf16[1024,1024]{1,0:T(8,128)(2,1)S(1)}, bf16[1024,1024]{1,0:T(8,128)(2,1)}, u32[]{:S(2)}) copy-start(bf16[1024,1024]{1,0:T(8,128)(2,1)} %all-gather.6.cloned.1.call-done) | copy-start | bytes 6291460
  49.1 2.5 copy-start.47
  54.7 57.7 %copy-start.11 = (f32[1024,4,6]{2,1,0:T(4,128)}, f32[1024,4,6]{2,1,0:T(4,128)S(1)}, u32[]{:S(2)}) copy-start(f32[1024,4,6]{2,1,0:T(4,128)S(1)} %copy.268) | copy-start | bytes 294916
  66.1 3.9 copy-start.20
  112.3 8.3 %copy-start.6 = (f32[1024,6,32]{2,1,0:T(8,128)}, f32[1024,6,32]{2,1,0:T(8,128)S(1)}, u32[]{:S(2)}) copy-start(f32[1024,6,32]{2,1,0:T(8,128)S(1)} %get-tuple-element.148) | copy-start | bytes 2359300
  112.3 8.3 %copy-start.7 = (f32[1024,6,32]{2,1,0:T(8,128)}, f32[1024,6,32]{2,1,0:T(8,128)S(1)}, u32[]{:S(2)}) copy-start(f32[1024,6,32]{2,1,0:T(8,128)S(1)} %get-tuple-element.149) | copy-start | bytes 2359300
  121.7 4.2 copy-start.24
  128.1 3.4 copy-start.2
  133.7 33.4 %copy-start.8 = (bf16[256,1024]{1,0:T(8,128)(2,1)S(1)}, bf16[256,1024]{1,0:T(8,128)(2,1)}, u32[]{:S(2)}) copy-start(bf16[256,1024]{1,0:T(8,128)(2,1)} %param.11) | copy-start | bytes 1572868
  135.8 33.2 %copy-start.50 = (f32[1024]{0:T(1024)S(1)}, f32[1024]{0:T(1024)}, u32[]{:S(2)}) copy-start(f32[1024]{0:T(1024)} %param.17) | copy-start | bytes 12292
  135.8 57.9 %all-gather.8.cloned.1.call-start = ((), (), s32[]{:S(2)}) async-start(), calls=%async_computation.5 | async-start | bytes 2621440 | tf_op jit(solution)/shard_map/all_gather | solution.py:242
  169.0 92.2 %copy-start.57 = (f32[256]{0:T(256)}, f32[256]{0:T(256)S(1)}, u32[]{:S(2)}) copy-start(f32[256]{0:T(256)S(1)} %get-tuple-element.188) | copy-start | bytes 3076
  171.1 46.7 %all-gather.10.cloned.1.call-start = ((), (), s32[]{:S(2)}) async-start(), calls=%async_computation.7 | async-start | bytes 2621440 | tf_op jit(solution)/shard_map/all_gather | solution.py:203
  171.6 89.6 %reduce-scatter.8.cloned.1.call-start = ((), (), s32[]{:S(2)}) async-start(), calls=%async_computation.8 | async-start | bytes 2621440 | tf_op jit(solution)/shard_map/reduce_scatter | solution.py:268
  193.8 5.4 copy-start.62
  193.8 5.4 copy-start.64
  217.8 6.5 copy-start.65
  224.2 2.4 copy-start.66
  229.9 65.5 %reduce-scatter.6.cloned.1.call-start = ((), (), s32[]{:S(2)}) async-start(), calls=%async_computation.6 | async-start | bytes 2621440 | tf_op jit(solution)/shard_map/reduce_scatter | solution.py:251
  229.9 31.3 %copy-start.15 = (bf16[256,1024]{1,0:T(8,128)(2,1)S(1)}, bf16[256,1024]{1,0:T(8,128)(2,1)}, u32[]{:S(2)}) copy-start(bf16[256,1024]{1,0:T(8,128)(2,1)} %reduce-scatter.4.cloned.1.call-done) | copy-start | bytes 1572868
  234.5 60.9 %copy-start.16 = (bf16[256,1024]{1,0:T(8,128)(2,1)S(1)}, bf16[256,1024]{1,0:T(8,128)(2,1)}, u32[]{:S(2)}) copy-start(bf16[256,1024]{1,0:T(8,128)(2,1)} %reduce-scatter.4.cloned.1.call-done) | copy-start | bytes 1572868
  234.5 60.9 %copy-start.30 = (bf16[256,1024]{1,0:T(8,128)(2,1)S(1)}, bf16[256,1024]{1,0:T(8,128)(2,1)}, u32[]{:S(2)}) copy-start(bf16[256,1024]{1,0:T(8,128)(2,1)} %param.21) | copy-start | bytes 1572868
  234.5 60.9 %copy-start.51 = (f32[1024]{0:T(1024)S(1)}, f32[1024]{0:T(1024)}, u32[]{:S(2)}) copy-start(f32[1024]{0:T(1024)} %param.17) | copy-start | bytes 12292
  234.5 60.9 %copy-start.61 = (f32[256]{0:T(256)S(1)}, f32[256]{0:T(256)}, u32[]{:S(2)}) copy-start(f32[256]{0:T(256)} %get-tuple-element.187) | copy-start | bytes 3076
  234.5 86.9 %all-gather.12.cloned.1.call-start = ((), (), s32[]{:S(2)}) async-start(), calls=%async_computation.9 | async-start | bytes 2621440 | tf_op jit(solution)/shard_map/all_gather | solution.py:277
  295.4 3.5 copy-start.54
  295.4 3.5 copy-start.56
  298.8 254.6 %all-reduce.10.cloned.1.call-start = ((), (), s32[]{:S(2)}) async-start(), calls=%async_computation.12 | async-start | bytes 9699328 | tf_op jit(solution)/shard_map/psum | solution.py:332
  298.9 4.9 copy-start.63
  298.9 4.9 copy-start.70
  303.9 2.8 copy-start.68
  306.7 14.8 %copy-start.45 = (bf16[256,1024]{1,0:T(8,128)(2,1)S(1)}, bf16[256,1024]{1,0:T(8,128)(2,1)}, u32[]{:S(2)}) copy-start(bf16[256,1024]{1,0:T(8,128)(2,1)} %param.16) | copy-start | bytes 1572868
  321.5 2.8 copy-start.4
  325.1 8.4 %copy-start.21 = (f32[1024,4,2]{1,2,0:T(2,128)S(1)}, f32[1024,4,2]{1,2,0:T(2,128)}, u32[]{:S(2)}) copy-start(f32[1024,4,2]{1,2,0:T(2,128)} %copy.267) | copy-start | bytes 98308
  333.5 11.6 %copy-start.5 = (f32[4,512,512]{1,2,0:T(8,128)S(1)}, f32[4,512,512]{1,2,0:T(8,128)}, u32[]{:S(2)}) copy-start(f32[4,512,512]{1,2,0:T(8,128)} %copy-done.3) | copy-start | bytes 12582916
  339.2 5.9 copy-start.23
  339.2 5.9 copy-start.27
  346.1 4.0 slice-start
  346.1 4.0 slice-start.1
  350.1 5.8 copy-start.43
  365.2 3.2 copy-start.18
  368.4 8.0 %copy-start.34 = (bf16[1024,4,64]{0,2,1:T(8,128)(2,1)S(1)}, bf16[1024,4,64]{0,2,1:T(8,128)(2,1)}, u32[]{:S(2)}) copy-start(bf16[1024,4,64]{0,2,1:T(8,128)(2,1)} %copy-done.33) | copy-start | bytes 1572868
  379.6 5.2 copy-start.12
  379.6 5.2 copy-start.13
  379.6 249.1 %all-reduce.8.cloned.1.call-start = ((), (), s32[]{:S(2)}) async-start(), calls=%async_computation.11 | async-start | bytes 901120 | tf_op jit(solution)/shard_map/psum | solution.py:345
  384.9 6.0 copy-start.32
  415.0 2.4 copy-start.39
  415.0 2.4 copy-start.40
  417.6 9.4 %collective-permute-start = (bf16[1024,160]{0,1:T(8,128)(2,1)S(1)}, bf16[1024,160]{0,1:T(8,128)(2,1)S(1)}, u32[]{:S(2)}, u32[]{:S(2)}) collective-permute-start(bf16[1024,160]{0,1:T(8,128)(2,1)S(1)} %get-tuple-element.166), channel_id=1, source_target_pairs={{0,1},{1,2},{2,3},{3,0},{4,5},{5,6},{6,7},{7,4},{8,9},{9,10},{10,1... | collective-permute-start | bytes 983048 | tf_op jit(solution)/shard_map/ppermute | solution.py:174
  417.9 9.6 %collective-permute-start.2 = (bf16[1024,160]{0,1:T(8,128)(2,1)S(1)}, bf16[1024,160]{0,1:T(8,128)(2,1)S(1)}, u32[]{:S(2)}, u32[]{:S(2)}) collective-permute-start(bf16[1024,160]{0,1:T(8,128)(2,1)S(1)} %get-tuple-element.167), channel_id=1, source_target_pairs={{0,3},{1,0},{2,1},{3,2},{4,7},{5,4},{6,5},{7,6},{8,11},{9,8},{10,9... | collective-permute-start | bytes 983048 | tf_op jit(solution)/shard_map/ppermute | solution.py:174
  419.4 15.3 %collective-permute-start.1 = (bf16[1024,160]{0,1:T(8,128)(2,1)S(1)}, bf16[1024,160]{0,1:T(8,128)(2,1)S(1)}, u32[]{:S(2)}, u32[]{:S(2)}) collective-permute-start(bf16[1024,160]{0,1:T(8,128)(2,1)S(1)} %get-tuple-element.168), channel_id=1, source_target_pairs={{0,2},{1,3},{2,0},{3,1},{4,6},{5,7},{6,4},{7,5},{8,10},{9,11},{10,... | collective-permute-start | bytes 983048 | tf_op jit(solution)/shard_map/ppermute | solution.py:174
  437.2 13.7 %collective-permute-start.3 = (bf16[256,1024]{1,0:T(8,128)(2,1)S(1)}, bf16[256,1024]{1,0:T(8,128)(2,1)S(1)}, u32[]{:S(2)}, u32[]{:S(2)}) collective-permute-start(bf16[256,1024]{1,0:T(8,128)(2,1)S(1)} %get-tuple-element.159), channel_id=1, source_target_pairs={{0,1},{1,2},{2,3},{3,0},{4,5},{5,6},{6,7},{7,4},{8,9},{9,10},{10,1... | collective-permute-start | bytes 1572872 | tf_op jit(solution)/shard_map/ppermute | solution.py:174
  437.3 14.0 %collective-permute-start.5 = (bf16[256,1024]{1,0:T(8,128)(2,1)S(1)}, bf16[256,1024]{1,0:T(8,128)(2,1)S(1)}, u32[]{:S(2)}, u32[]{:S(2)}) collective-permute-start(bf16[256,1024]{1,0:T(8,128)(2,1)S(1)} %get-tuple-element.160), channel_id=1, source_target_pairs={{0,3},{1,0},{2,1},{3,2},{4,7},{5,4},{6,5},{7,6},{8,11},{9,8},{10,9... | collective-permute-start | bytes 1572872 | tf_op jit(solution)/shard_map/ppermute | solution.py:174
  439.0 23.7 %copy-start.52 = (f32[1024]{0:T(1024)S(1)}, f32[1024]{0:T(1024)}, u32[]{:S(2)}) copy-start(f32[1024]{0:T(1024)} %param.13) | copy-start | bytes 12292
  439.1 23.7 %copy-start.59 = (f32[256]{0:T(256)S(1)}, f32[256]{0:T(256)}, u32[]{:S(2)}) copy-start(f32[256]{0:T(256)} %copy-done.58) | copy-start | bytes 3076
  439.1 23.7 %collective-permute-start.4 = (bf16[256,1024]{1,0:T(8,128)(2,1)S(1)}, bf16[256,1024]{1,0:T(8,128)(2,1)S(1)}, u32[]{:S(2)}, u32[]{:S(2)}) collective-permute-start(bf16[256,1024]{1,0:T(8,128)(2,1)S(1)} %get-tuple-element.161), channel_id=1, source_target_pairs={{0,2},{1,3},{2,0},{3,1},{4,6},{5,7},{6,4},{7,5},{8,10},{9,11},{10,... | collective-permute-start | bytes 1572872 | tf_op jit(solution)/shard_map/ppermute | solution.py:174
  441.0 187.8 %copy-start.60 = (f32[256]{0:T(256)S(1)}, f32[256]{0:T(256)}, u32[]{:S(2)}) copy-start(f32[256]{0:T(256)} %get-tuple-element.185) | copy-start | bytes 3076
  553.4 76.7 %copy-start.42 = (bf16[256,1024]{1,0:T(8,128)(2,1)S(1)}, bf16[256,1024]{1,0:T(8,128)(2,1)}, u32[]{:S(2)}) copy-start(bf16[256,1024]{1,0:T(8,128)(2,1)} %get-tuple-element.73) | copy-start | bytes 1572868
  553.4 95.3 %all-gather.14.cloned.1.call-start = ((), (), s32[]{:S(2)}) async-start(), calls=%async_computation.10 | async-start | bytes 1843200 | tf_op jit(solution)/shard_map/all_gather | solution.py:353
  630.1 3.0 copy-start.37
  650.4 6.4 copy-start.1
  (25 other events, 41.5 us)
Sparse Core Ops, SparseCore 0:
  11.9 25.2 all-gather.5
  135.9 31.1 reduce-scatter.3
  171.2 22.5 all-gather.7
  195.2 22.5 all-gather.9
  230.0 31.1 reduce-scatter.7
  264.1 31.1 reduce-scatter.5
  298.9 22.5 all-gather.11
  379.7 173.6 all-reduce.9
  557.4 71.2 all-reduce.7
  630.2 18.4 all-gather.13

commit v5 on v4

--- a/solution.py
+++ b/solution.py
@@ -175,6 +175,25 @@
             sent, "head", [(device, (device + shift) % count) for device in range(count)]
         ).astype(jnp.float32)
     return total
+
+
+def head_all_gather(values, axis):
+    count = lax.axis_size("head")
+    own = lax.axis_index("head")
+    width = values.shape[axis]
+    shape = list(values.shape)
+    shape[axis] = width * count
+    gathered = lax.dynamic_update_slice_in_dim(
+        jnp.zeros(shape, values.dtype), values, own * width, axis=axis
+    )
+    for shift in range(1, count):
+        arrived = lax.ppermute(
+            values, "head", [(device, (device + shift) % count) for device in range(count)]
+        )
+        gathered = lax.dynamic_update_slice_in_dim(
+            gathered, arrived, ((own - shift) % count) * width, axis=axis
+        )
+    return gathered
 
 
 def local(
@@ -248,12 +267,9 @@
     piece = lax.slice_in_dim(hidden, 0, lax.axis_size("head") * own_rows, axis=0)
     output = (
         resid_own
-        + lax.psum_scatter(
-            jnp.dot(piece, down_weight, preferred_element_type=jnp.float32).astype(jnp.bfloat16),
-            "head",
-            scatter_dimension=0,
-            tiled=True,
-        ).astype(jnp.float32)
+        + head_reduce_scatter(
+            jnp.dot(piece, down_weight, preferred_element_type=jnp.float32).astype(jnp.bfloat16), 0
+        )
     ).astype(jnp.bfloat16)
     grad_down = dot_first(hidden, grad_out_all)
     grad_hidden = dot_last(grad_out_all, down_weight)
@@ -271,10 +287,13 @@
         scatter_dimension=0,
         tiled=True,
     ).astype(jnp.float32)
+    ffn_grads = (grad_gate.astype(jnp.bfloat16), grad_up.astype(jnp.bfloat16), grad_down.astype(jnp.bfloat16))
+    ffn_grads, grad_normed_two = lax.optimization_barrier((ffn_grads, grad_normed_two))
+    grad_gate, grad_up, grad_down = lax.psum(ffn_grads, "dp")
     resid_part, grad_gain_ffn_own = norm_backward(resid_own, inv_two, gain_ffn, grad_normed_two)
     grad_resid = cotangent.astype(jnp.float32) + resid_part
     output, grad_resid = lax.optimization_barrier((output, grad_resid))
-    grad_branch = lax.all_gather(grad_resid.astype(jnp.bfloat16), "head", axis=0, tiled=True)
+    grad_branch = head_all_gather(grad_resid.astype(jnp.bfloat16), 0)
     grad_mixed = dot_last(grad_branch, out_weight).astype(jnp.bfloat16)
     grad_out = dot_first(mixed, grad_branch)
     grad_query_rows, grad_key_rows, grad_value_rows = lax.map(
@@ -329,20 +348,15 @@
         jnp.concatenate([grad_gain_attn_own, grad_gain_ffn_own]),
         (0, gain_rows * basis_cols - 2 * features),
     ).reshape(gain_rows, basis_cols)
-    grad_out, grad_gate, grad_up, grad_down = lax.psum(
-        (
-            grad_out.astype(jnp.bfloat16),
-            grad_gate.astype(jnp.bfloat16),
-            grad_up.astype(jnp.bfloat16),
-            grad_down.astype(jnp.bfloat16),
-        ),
-        "dp",
-    )
-    tail = (grad_a.astype(jnp.bfloat16), jnp.concatenate([grad_b_cols, gains], axis=0).astype(jnp.bfloat16))
-    tail, (grad_out, grad_gate, grad_up, grad_down) = lax.optimization_barrier(
-        (tail, (grad_out, grad_gate, grad_up, grad_down))
-    )
-    grad_a, packed = lax.psum(tail, "dp")
+    tail = (
+        grad_a.astype(jnp.bfloat16),
+        grad_out.astype(jnp.bfloat16),
+        jnp.concatenate([grad_b_cols, gains], axis=0).astype(jnp.bfloat16),
+    )
+    tail, (grad_gate, grad_up, grad_down) = lax.optimization_barrier(
+        (tail, (grad_gate, grad_up, grad_down))
+    )
+    grad_a, grad_out, packed = lax.psum(tail, "dp")
     grad_out, grad_gate, grad_up, grad_down = (
         grad_out.astype(jnp.float32),
         grad_gate.astype(jnp.float32),

time: 674 us -> 570 us (0.85)
  waiting for transfers between devices: 371 us -> 261 us
  starting transfers between devices: 4.64 us -> 14.3 us
  local copies, waits for them, and re-layouts: 69.3 us -> 77.1 us
  matrix products: 145 us -> 138 us
    psum x2, waiting for transfers between devices: 164 us -> 88.3 us  [the longest x1 80.3 us: local(): grad_a, grad_out, packed = lax.psum(tail, 'dp')]
    reduce_scatter x1 -> x0, waiting for transfers between devices: 32.7 us -> none  [local(): lax.psum_scatter(jnp.dot(piece, down_weight, preferred_element_type=jnp.f...]
    ppermute x0 -> x3, waiting for transfers between devices: none -> 18.2 us  [head_all_gather(): lax.ppermute(values, 'head', [(device, (device + shift) % count) for devi...]
    all_gather x1 -> x0, waiting for transfers between devices: 12 us -> none  [local(): lax.all_gather(grad_resid.astype(jnp.bfloat16), 'head', axis=0, tiled=True)]
    ppermute x6 -> x9, starting transfers between devices: 4.23 us -> 12 us  [head_reduce_scatter(): lax.ppermute(sent, 'head', [(device, (device + shift) % count) for device...]
    ppermute x6 -> x9, waiting for transfers between devices: 36 us -> 28.7 us  [head_reduce_scatter(): lax.ppermute(sent, 'head', [(device, (device + shift) % count) for device...]
    unnamed x154 -> x172, local copies, waits for them, and re-layouts: 24.8 us -> 26.9 us
  transfers between devices with their start and end apart: 16 -> 20, of which waited for: 16 -> 16; matrix products, arithmetic and copies ran while one was open for 13% -> 24% of each run, Pallas kernels for 0% -> 0%
where the time goes in v5:
time: 570 us; the launch traced here: 560 us
  waiting for transfers between devices  261 us (46%)
  matrix products  138 us (24%)
  local copies, waits for them, and re-layouts  77.1 us (14%)
  other arithmetic  53.7 us (9%)
  between operations  15.7 us (3%)
  starting transfers between devices  14.3 us (3%)
    psum x1, waiting for transfers between devices, local(): grad_a, grad_out, packed = lax.psum(tail, 'dp')  80.3 us
    reduce_scatter x1, waiting for transfers between devices, local(): lax.psum_scatter(jnp.dot(piece, out_weight, preferred_element_type=jnp.fl...  31.3 us
    ppermute x9, waiting for transfers between devices, head_reduce_scatter(): lax.ppermute(sent, 'head', [(device, (device + shift) % count) for device...  28.7 us
    reduce_scatter x1, waiting for transfers between devices, local(): lax.psum_scatter((dot_last(gate_piece, gate_weight) + dot_last(up_piece,...  27.2 us
    unnamed x172, local copies, waits for them, and re-layouts  26.9 us
    all_gather x1, waiting for transfers between devices, local(): normed_two_all = lax.all_gather(normed_two, 'head', axis=0, tiled=True)  22.1 us
    all_gather x1, waiting for transfers between devices, local(): lax.all_gather(normed_one, 'head', axis=0, tiled=True)  18.6 us
    ppermute x3, waiting for transfers between devices, head_all_gather(): lax.ppermute(values, 'head', [(device, (device + shift) % count) for devi...  18.2 us
  transfers between devices with their start and end apart: 20, of which 16 were waited for; matrix products, arithmetic and copies ran while one was open for 24% of the time, Pallas kernels for 0%

profile of v5, /device:TPU:0, one launch (start us, length us, event | category | flops | bytes accessed | tf_op | source)
XLA Modules:
  0.0 560.1 jit_solution(13606160335779538417)
XLA Ops:
  15.5 3.1 multiply_cosine_fusion
  18.6 18.6 %all-gather.5.cloned.1.call-done = bf16[1024,1024]{1,0:T(8,128)(2,1)} async-done(((bf16[256,1024]{1,0:T(8,128)(2,1)}), bf16[1024,1024]{1,0:T(8,128)(2,1)}) %all-gather.5.cloned.1.call-update) | async-done | bytes 2097168 | tf_op jit(solution)/shard_map/all_gather | solution.py:221
  37.2 3.1 fusion.76
  45.2 2.9 fusion.77
  54.6 2.3 fusion.70
  56.9 2.8 fusion.67
  59.7 2.2 copy.228
  61.8 2.1 copy.273
  64.0 2.1 copy.272
  66.1 2.6 multiply_subtract_fusion.1
  69.9 10.4 %fusion.65 = f32[1024,4,64]{2,1,0:T(4,128)} fusion(f32[1024,4,2]{1,2,0:T(2,128)S(1)} %copy-done.22, f32[1024,2,32]{2,1,0:T(2,128)S(1)} %get-tuple-element.166, f32[1024,2,32]{2,1,0:T(2,128)S(1)} %get-tuple-element.165), kind=kOutput, calls=%fused_computation.155 | convolution fusion | flops 6422528 | bytes 1605632 | tf_op jit(solution)/shard_map/thr,trd->thd/dot_general | solution.py:240
  80.3 2.7 copy.236
  83.0 2.1 multiply_convert_fusion.7
  85.1 10.9 %fusion.78 = f32[1024,4,64]{2,1,0:T(4,128)} fusion(f32[1024,4,2]{1,2,0:T(2,128)} %copy.267, f32[1024,2,64]{2,1,0:T(2,128)} %copy.228), kind=kOutput, calls=%fused_computation.168 | convolution fusion | flops 6291456 | bytes 1605632 | tf_op jit(solution)/shard_map/thr,trd->thd/dot_general | solution.py:244
  96.0 2.7 copy.229
  98.7 2.1 multiply_convert_fusion.8
  100.8 3.6 copy.270
  104.4 3.7 copy.269
  108.1 4.2 multiply_subtract_fusion
  112.3 8.3 %multiply_convert_fusion.5 = bf16[1024,4,64]{2,1,0:T(4,128)(2,1)S(1)} fusion(f32[1024,4,6]{2,1,0:T(4,128)S(1)} %copy.268, f32[1024,6,32]{2,1,0:T(8,128)S(1)} %get-tuple-element.159, f32[1024,6,32]{2,1,0:T(8,128)S(1)} %get-tuple-element.158), kind=kOutput, calls=%fused_computation.41 | convolution fusion | flops 19791872 | bytes 2195456 | tf_op jit(solution)/shard_map/thr,trd->thd/dot_general | solution.py:237
  131.5 2.1 fusion.37
  134.5 2.1 convolution_convert_fusion
  136.6 31.3 %reduce-scatter.3.cloned.1.call-done = bf16[256,1024]{1,0:T(8,128)(2,1)} async-done(((bf16[1024,1024]{1,0:T(8,128)(2,1)}), bf16[256,1024]{1,0:T(8,128)(2,1)}) %reduce-scatter.3.cloned.1.call-update) | async-done | bytes 524304 | tf_op jit(solution)/shard_map/reduce_scatter | solution.py:253
  172.4 22.1 %all-gather.7.cloned.1.call-done = bf16[1024,1024]{1,0:T(8,128)(2,1)} async-done(((bf16[256,1024]{1,0:T(8,128)(2,1)}), bf16[1024,1024]{1,0:T(8,128)(2,1)}) %all-gather.7.cloned.1.call-update) | async-done | bytes 2097168 | tf_op jit(solution)/shard_map/all_gather | solution.py:261
  194.5 5.4 fusion.80
  200.0 3.3 fusion.79
  203.2 15.3 %all-gather.9.cloned.1.call-done = bf16[1024,1024]{1,0:T(8,128)(2,1)} async-done(((bf16[256,1024]{1,0:T(8,128)(2,1)}), bf16[1024,1024]{1,0:T(8,128)(2,1)}) %all-gather.9.cloned.1.call-update) | async-done | bytes 2097168 | tf_op jit(solution)/shard_map/all_gather | solution.py:222
  218.6 6.5 %multiply_convert_fusion.2 = (bf16[1024,704]{0,1:T(8,128)(2,1)S(1)}, bf16[1024,704]{0,1:T(8,128)(2,1)S(1)}, bf16[1024,704]{0,1:T(8,128)(2,1)}) fusion(f32[1024,704]{0,1:T(8,128)} %fusion.79, f32[1024,704]{0,1:T(8,128)} %fusion.80, bf16[1024,1024]{1,0:T(8,128)(2,1)} %all-gather.9.cloned.1.call-done, bf16[704,1024]{1,0:T(8,128)(2,1)S(1)} %copy-done), kind=kOutput, calls=%fused_computation.26 | convolution fusion | flops 1487208448 | bytes 13631488 | tf_op jit(solution)/shard_map/dot_general | solution.py:57
  227.5 3.2 add_convert_fusion.2
  230.8 3.3 convolution_convert_fusion.1
  237.4 2.8 convolution_convert_fusion.4
  240.2 2.8 convolution_convert_fusion.2
  243.0 2.9 convolution_convert_fusion.3
  245.8 27.2 %reduce-scatter.5.cloned.1.call-done = bf16[256,1024]{1,0:T(8,128)(2,1)} async-done(((bf16[1024,1024]{1,0:T(8,128)(2,1)}), bf16[256,1024]{1,0:T(8,128)(2,1)}) %reduce-scatter.5.cloned.1.call-update) | async-done | bytes 524304 | tf_op jit(solution)/shard_map/reduce_scatter | solution.py:284
  275.6 3.0 subtract_add_fusion
  283.4 11.6 %collective-permute-done.3 = bf16[256,1024]{1,0:T(8,128)(2,1)S(1)} collective-permute-done((bf16[256,1024]{1,0:T(8,128)(2,1)S(1)}, bf16[256,1024]{1,0:T(8,128)(2,1)S(1)}, u32[]{:S(2)}, u32[]{:S(2)}) %collective-permute-start.3) | collective-permute-done | bytes 524320 | tf_op jit(solution)/shard_map/ppermute | solution.py:190
  298.5 5.8 %collective-permute-done.5 = bf16[256,1024]{1,0:T(8,128)(2,1)} collective-permute-done((bf16[256,1024]{1,0:T(8,128)(2,1)S(1)}, bf16[256,1024]{1,0:T(8,128)(2,1)}, u32[]{:S(2)}, u32[]{:S(2)}) %collective-permute-start.5) | collective-permute-done | bytes 524320 | tf_op jit(solution)/shard_map/ppermute | solution.py:190
  306.2 2.5 convolution_convert_fusion.6
  309.8 5.8 %fusion.22 = bf16[1024,4,64]{0,2,1:T(8,128)(2,1)} fusion(bf16[512,4,64]{0,2,1:T(8,128)(2,1)S(1)} %bitcast.111, f32[4,512,1024]{2,1,0:T(8,128)} %copy-done.2, f32[4,512]{1,0:T(4,128)S(1)} %log_add_fusion, f32[512,4,64]{0,2,1:T(8,128)S(1)} %fusion.27), kind=kOutput, calls=%fused_computation.60 | convolution fusion | flops 273154048 | bytes 9707520 | tf_op jit(solution)/shard_map/while/body/eval_jaxpr/hqk,qhd->khd/dot_general | solution.py:152
  315.7 2.4 copy.249
  318.0 5.7 %fusion.26 = bf16[1024,2,64]{2,1,0:T(2,128)(2,1)} fusion(f32[1024,4,2]{1,2,0:T(2,128)S(1)} %copy-done.24, bf16[1024,4,64]{2,1,0:T(4,128)(2,1)} %copy.249), kind=kOutput, calls=%fused_computation.62 | convolution fusion | flops 6553600 | bytes 819200 | tf_op jit(solution)/shard_map/thr,thd->trd/dot_general | solution.py:316
  323.7 5.6 %convolution_multiply_fusion.4 = bf16[1024,4,2]{1,2,0:T(2,128)(2,1)} fusion(bf16[1024,4,64]{2,1,0:T(4,128)(2,1)} %copy.249, f32[1024,2,64]{2,1,0:T(2,128)S(1)} %copy-done.25), kind=kOutput, calls=%fused_computation.53 | convolution fusion | flops 6307840 | bytes 1064960 | tf_op jit(solution)/shard_map/thd,trd->thr/dot_general | solution.py:309
  333.9 2.6 multiply_reduce_fusion
  338.4 2.1 fusion.35
  342.9 6.4 %convolution_multiply_fusion.5 = bf16[1024,4,2]{1,2,0:T(2,128)(2,1)} fusion(bf16[1024,4,64]{2,1,0:T(4,128)(2,1)} %copy.246, f32[1024,2,32]{2,1,0:T(2,128)S(1)} %copy-done.21, f32[1024,2,32]{2,1,0:T(2,128)S(1)} %copy-done.19), kind=kOutput, calls=%fused_computation.54 | convolution fusion | flops 6438912 | bytes 1064960 | tf_op jit(solution)/shard_map/thd,trd->thr/dot_general | solution.py:308
  349.3 3.7 convolution_multiply_fusion.3
  362.9 8.8 %convolution_multiply_fusion.1 = bf16[1024,4,6]{2,1,0:T(4,128)(2,1)} fusion(bf16[1024,4,64]{2,1,0:T(4,128)(2,1)S(1)} %copy.241, f32[1024,6,32]{2,1,0:T(8,128)} %copy-done.7, f32[1024,6,32]{2,1,0:T(8,128)} %copy-done.6), kind=kOutput, calls=%fused_computation.49 | convolution fusion | flops 19316736 | bytes 2146304 | tf_op jit(solution)/shard_map/thd,trd->thr/dot_general | solution.py:307
  373.6 5.8 %convolution_multiply_fusion = f32[1024,6,64]{2,1,0:T(8,128)S(1)} fusion(f32[1024,4,6]{2,1,0:T(4,128)} %copy-done.11, bf16[1024,4,64]{2,1,0:T(4,128)(2,1)S(1)} %copy.241), kind=kOutput, calls=%fused_computation.37 | convolution fusion | flops 19267584 | bytes 2195456 | tf_op jit(solution)/shard_map/thr,thd->trd/dot_general | solution.py:311
  379.5 3.1 add_convert_fusion.1
  382.6 2.3 copy.254
  384.9 2.3 copy.255
  387.5 4.1 collective-permute-start.6
  393.5 3.4 convolution_convert_fusion.5
  397.7 2.2 collective-permute-done.8
  399.9 6.5 %collective-permute-done.7 = bf16[1024,160]{0,1:T(8,128)(2,1)S(1)} collective-permute-done((bf16[1024,160]{0,1:T(8,128)(2,1)S(1)}, bf16[1024,160]{0,1:T(8,128)(2,1)S(1)}, u32[]{:S(2)}, u32[]{:S(2)}) %collective-permute-start.7) | collective-permute-done | bytes 327712 | tf_op jit(solution)/shard_map/ppermute | solution.py:174
  406.7 2.1 add_convert_fusion
  414.5 6.4 %collective-permute-done.9 = bf16[256,1024]{1,0:T(8,128)(2,1)S(1)} collective-permute-done((bf16[256,1024]{1,0:T(8,128)(2,1)S(1)}, bf16[256,1024]{1,0:T(8,128)(2,1)S(1)}, u32[]{:S(2)}, u32[]{:S(2)}) %collective-permute-start.9) | collective-permute-done | bytes 524320 | tf_op jit(solution)/shard_map/ppermute | solution.py:174
  420.9 2.2 collective-permute-done.11
  423.1 11.4 %collective-permute-done.10 = bf16[256,1024]{1,0:T(8,128)(2,1)S(1)} collective-permute-done((bf16[256,1024]{1,0:T(8,128)(2,1)S(1)}, bf16[256,1024]{1,0:T(8,128)(2,1)S(1)}, u32[]{:S(2)}, u32[]{:S(2)}) %collective-permute-start.10) | collective-permute-done | bytes 524320 | tf_op jit(solution)/shard_map/ppermute | solution.py:174
  436.1 8.0 %all-reduce.10.cloned.1.call-done = (bf16[1024,704]{0,1:T(8,128)(2,1)}, bf16[1024,704]{0,1:T(8,128)(2,1)}, bf16[704,1024]{1,0:T(8,128)(2,1)}) async-done(((bf16[1024,704]{0,1:T(8,128)(2,1)}, bf16[1024,704]{0,1:T(8,128)(2,1)}, bf16[704,1024]{1,0:T(8,128)(2,1)}), (bf16[1024,704]{0,1:T(8,128)(2,1)}, bf16[1024,704]{0,1:T(8,128)(2,1)}, bf16[704,1024]{1,0:T(8,128)(2,1)})) %all-reduce.10.cloned.1.call-update) | async-done | bytes 4325392 | tf_op jit(solution)/shard_map/psum | solution.py:292
  444.1 80.3 %all-reduce.8.cloned.1.call-done = (bf16[1037,160]{0,1:T(8,128)(2,1)}, bf16[1024,40]{0,1:T(8,128)(2,1)}, bf16[256,1024]{1,0:T(8,128)(2,1)}) async-done(((bf16[1037,160]{0,1:T(8,128)(2,1)}, bf16[1024,40]{0,1:T(8,128)(2,1)}, bf16[256,1024]{1,0:T(8,128)(2,1)}), (bf16[1037,160]{0,1:T(8,128)(2,1)}, bf16[1024,40]{0,1:T(8,128)(2,1)}, bf16[256,1024]{1,0:T(8,128)(2,1)})) %all-reduce.8.cloned.1.call-update) | async-done | bytes 938064 | tf_op jit(solution)/shard_map/psum | solution.py:359
  533.6 11.0 %all-gather.11.cloned.1.call-done = bf16[1037,640]{0,1:T(8,128)(2,1)} async-done(((bf16[1037,160]{0,1:T(8,128)(2,1)}), bf16[1037,640]{0,1:T(8,128)(2,1)}) %all-gather.11.cloned.1.call-update) | async-done | bytes 1327376 | tf_op jit(solution)/shard_map/all_gather | solution.py:367
  546.4 3.2 slice.177
  549.6 3.2 copy.262
  (285 shorter events, 98.2 us)
Async XLA Ops:
  7.2 211.4 %copy-start = (bf16[704,1024]{1,0:T(8,128)(2,1)S(1)}, bf16[704,1024]{1,0:T(8,128)(2,1)}, u32[]{:S(2)}) copy-start(bf16[704,1024]{1,0:T(8,128)(2,1)} %param.20) | copy-start | bytes 4325380
  7.2 30.0 %all-gather.5.cloned.1.call-start = ((), (), s32[]{:S(2)}) async-start(), calls=%async_computation.2 | async-start | bytes 2621440 | tf_op jit(solution)/shard_map/all_gather | solution.py:221
  11.7 156.2 %reduce-scatter.3.cloned.1.call-start = ((), (), s32[]{:S(2)}) async-start(), calls=%async_computation.3 | async-start | bytes 2621440 | tf_op jit(solution)/shard_map/reduce_scatter | solution.py:253
  37.2 8.0 %copy-start.9 = (bf16[1024,1024]{1,0:T(8,128)(2,1)S(1)}, bf16[1024,1024]{1,0:T(8,128)(2,1)}, u32[]{:S(2)}) copy-start(bf16[1024,1024]{1,0:T(8,128)(2,1)} %all-gather.5.cloned.1.call-done) | copy-start | bytes 6291460
  54.6 57.7 %copy-start.11 = (f32[1024,4,6]{2,1,0:T(4,128)}, f32[1024,4,6]{2,1,0:T(4,128)S(1)}, u32[]{:S(2)}) copy-start(f32[1024,4,6]{2,1,0:T(4,128)S(1)} %copy.268) | copy-start | bytes 294916
  66.1 3.9 copy-start.22
  112.3 8.3 %copy-start.6 = (f32[1024,6,32]{2,1,0:T(8,128)}, f32[1024,6,32]{2,1,0:T(8,128)S(1)}, u32[]{:S(2)}) copy-start(f32[1024,6,32]{2,1,0:T(8,128)S(1)} %get-tuple-element.158) | copy-start | bytes 2359300
  112.3 8.3 %copy-start.7 = (f32[1024,6,32]{2,1,0:T(8,128)}, f32[1024,6,32]{2,1,0:T(8,128)S(1)}, u32[]{:S(2)}) copy-start(f32[1024,6,32]{2,1,0:T(8,128)S(1)} %get-tuple-element.159) | copy-start | bytes 2359300
  121.7 4.2 copy-start.28
  134.5 33.4 %copy-start.8 = (bf16[256,1024]{1,0:T(8,128)(2,1)S(1)}, bf16[256,1024]{1,0:T(8,128)(2,1)}, u32[]{:S(2)}) copy-start(bf16[256,1024]{1,0:T(8,128)(2,1)} %param.11) | copy-start | bytes 1572868
  134.5 35.3 %copy-start.56 = (f32[1024]{0:T(1024)S(1)}, f32[1024]{0:T(1024)}, u32[]{:S(2)}) copy-start(f32[1024]{0:T(1024)} %param.17) | copy-start | bytes 12292
  136.5 58.0 %all-gather.7.cloned.1.call-start = ((), (), s32[]{:S(2)}) async-start(), calls=%async_computation.4 | async-start | bytes 2621440 | tf_op jit(solution)/shard_map/all_gather | solution.py:261
  169.8 30.2 %copy-start.63 = (f32[256]{0:T(256)}, f32[256]{0:T(256)S(1)}, u32[]{:S(2)}) copy-start(f32[256]{0:T(256)S(1)} %get-tuple-element.201) | copy-start | bytes 3076
  171.8 46.7 %all-gather.9.cloned.1.call-start = ((), (), s32[]{:S(2)}) async-start(), calls=%async_computation.5 | async-start | bytes 2621440 | tf_op jit(solution)/shard_map/all_gather | solution.py:222
  172.4 100.6 %reduce-scatter.5.cloned.1.call-start = ((), (), s32[]{:S(2)}) async-start(), calls=%async_computation.6 | async-start | bytes 2621440 | tf_op jit(solution)/shard_map/reduce_scatter | solution.py:284
  194.5 5.4 copy-start.69
  194.5 5.4 copy-start.72
  218.6 6.5 %copy-start.73 = (bf16[1024,704]{0,1:T(8,128)(2,1)S(1)}, bf16[1024,704]{0,1:T(8,128)(2,1)}, u32[]{:S(2)}) copy-start(bf16[1024,704]{0,1:T(8,128)(2,1)} %param.18) | copy-start | bytes 4325380
  230.7 213.4 %all-reduce.10.cloned.1.call-start = ((), (), s32[]{:S(2)}) async-start(), calls=%async_computation.9 | async-start | bytes 8650752 | tf_op jit(solution)/shard_map/psum | solution.py:292
  230.8 6.6 %copy-start.79 = (bf16[1024,704]{0,1:T(8,128)(2,1)S(1)}, bf16[1024,704]{0,1:T(8,128)(2,1)}, u32[]{:S(2)}) copy-start(bf16[1024,704]{0,1:T(8,128)(2,1)} %get-tuple-element.162) | copy-start | bytes 4325380
  234.1 6.1 %copy-start.34 = (bf16[1024,1024]{1,0:T(8,128)(2,1)}, bf16[1024,1024]{1,0:T(8,128)(2,1)S(1)}, u32[]{:S(2)}) copy-start(bf16[1024,1024]{1,0:T(8,128)(2,1)S(1)} %convolution_convert_fusion.1) | copy-start | bytes 6291460
  235.3 39.3 %collective-permute-start = (bf16[256,1024]{1,0:T(8,128)(2,1)}, bf16[256,1024]{1,0:T(8,128)(2,1)S(1)}, u32[]{:S(2)}, u32[]{:S(2)}) collective-permute-start(bf16[256,1024]{1,0:T(8,128)(2,1)} %get-tuple-element.174), channel_id=1, source_target_pairs={{0,1},{1,2},{2,3},{3,0},{4,5},{5,6},{6,7},{7,4},{8,9},{9,10},{10,1... | collective-permute-start | bytes 1572872 | tf_op jit(solution)/shard_map/ppermute | solution.py:174
  235.5 39.1 %collective-permute-start.2 = (bf16[256,1024]{1,0:T(8,128)(2,1)}, bf16[256,1024]{1,0:T(8,128)(2,1)S(1)}, u32[]{:S(2)}, u32[]{:S(2)}) collective-permute-start(bf16[256,1024]{1,0:T(8,128)(2,1)} %get-tuple-element.175), channel_id=1, source_target_pairs={{0,3},{1,0},{2,1},{3,2},{4,7},{5,4},{6,5},{7,6},{8,11},{9,8},{10,9... | collective-permute-start | bytes 1572872 | tf_op jit(solution)/shard_map/ppermute | solution.py:174
  237.0 37.6 %collective-permute-start.1 = (bf16[256,1024]{1,0:T(8,128)(2,1)}, bf16[256,1024]{1,0:T(8,128)(2,1)}, u32[]{:S(2)}, u32[]{:S(2)}) collective-permute-start(bf16[256,1024]{1,0:T(8,128)(2,1)} %get-tuple-element.176), channel_id=1, source_target_pairs={{0,2},{1,3},{2,0},{3,1},{4,6},{5,7},{6,4},{7,5},{8,10},{9,11},{10,... | collective-permute-start | bytes 1572872 | tf_op jit(solution)/shard_map/ppermute | solution.py:174
  243.0 31.2 %copy-start.17 = (bf16[256,1024]{1,0:T(8,128)(2,1)S(1)}, bf16[256,1024]{1,0:T(8,128)(2,1)}, u32[]{:S(2)}) copy-start(bf16[256,1024]{1,0:T(8,128)(2,1)} %reduce-scatter.3.cloned.1.call-done) | copy-start | bytes 1572868
  243.0 31.2 %copy-start.57 = (f32[1024]{0:T(1024)S(1)}, f32[1024]{0:T(1024)}, u32[]{:S(2)}) copy-start(f32[1024]{0:T(1024)} %param.17) | copy-start | bytes 12292
  243.0 31.2 %copy-start.64 = (f32[256]{0:T(256)S(1)}, f32[256]{0:T(256)}, u32[]{:S(2)}) copy-start(f32[256]{0:T(256)} %copy-done.63) | copy-start | bytes 3076
  245.8 29.8 %copy-start.35 = (bf16[256,1024]{1,0:T(8,128)(2,1)S(1)}, bf16[256,1024]{1,0:T(8,128)(2,1)}, u32[]{:S(2)}) copy-start(bf16[256,1024]{1,0:T(8,128)(2,1)} %param.21) | copy-start | bytes 1572868
  245.8 29.8 %copy-start.68 = (f32[256]{0:T(256)S(1)}, f32[256]{0:T(256)}, u32[]{:S(2)}) copy-start(f32[256]{0:T(256)} %get-tuple-element.200) | copy-start | bytes 3076
  278.6 4.8 copy-start.14
  278.6 4.7 copy-start.60
  278.6 4.7 copy-start.62
  281.2 13.9 %collective-permute-start.3 = (bf16[256,1024]{1,0:T(8,128)(2,1)S(1)}, bf16[256,1024]{1,0:T(8,128)(2,1)S(1)}, u32[]{:S(2)}, u32[]{:S(2)}) collective-permute-start(bf16[256,1024]{1,0:T(8,128)(2,1)S(1)} %get-tuple-element.157), channel_id=1, source_target_pairs={{0,1},{1,2},{2,3},{3,0},{4,5},{5,6},{6,7},{7,4},{8,9},{9,10},{10,1... | collective-permute-start | bytes 1572872 | tf_op jit(solution)/shard_map/ppermute | solution.py:190
  281.7 15.0 %collective-permute-start.4 = (bf16[256,1024]{1,0:T(8,128)(2,1)S(1)}, bf16[256,1024]{1,0:T(8,128)(2,1)}, u32[]{:S(2)}, u32[]{:S(2)}) collective-permute-start(bf16[256,1024]{1,0:T(8,128)(2,1)S(1)} %get-tuple-element.157), channel_id=1, source_target_pairs={{0,2},{1,3},{2,0},{3,1},{4,6},{5,7},{6,4},{7,5},{8,10},{9,11},{10,... | collective-permute-start | bytes 1572872 | tf_op jit(solution)/shard_map/ppermute | solution.py:190
  281.7 22.6 %collective-permute-start.5 = (bf16[256,1024]{1,0:T(8,128)(2,1)S(1)}, bf16[256,1024]{1,0:T(8,128)(2,1)}, u32[]{:S(2)}, u32[]{:S(2)}) collective-permute-start(bf16[256,1024]{1,0:T(8,128)(2,1)S(1)} %get-tuple-element.157), channel_id=1, source_target_pairs={{0,3},{1,0},{2,1},{3,2},{4,7},{5,4},{6,5},{7,6},{8,11},{9,8},{10,9... | collective-permute-start | bytes 1572872 | tf_op jit(solution)/shard_map/ppermute | solution.py:190
  283.4 241.1 %all-reduce.8.cloned.1.call-start = ((), (), s32[]{:S(2)}) async-start(), calls=%async_computation.8 | async-start | bytes 1949696 | tf_op jit(solution)/shard_map/psum | solution.py:359
  283.4 22.8 %copy-start.51 = (bf16[256,1024]{1,0:T(8,128)(2,1)S(1)}, bf16[256,1024]{1,0:T(8,128)(2,1)}, u32[]{:S(2)}) copy-start(bf16[256,1024]{1,0:T(8,128)(2,1)} %param.16) | copy-start | bytes 1572868
  309.8 8.2 %copy-start.24 = (f32[1024,4,2]{1,2,0:T(2,128)S(1)}, f32[1024,4,2]{1,2,0:T(2,128)}, u32[]{:S(2)}) copy-start(f32[1024,4,2]{1,2,0:T(2,128)} %copy.267) | copy-start | bytes 98308
  315.7 8.1 %copy-start.25 = (f32[1024,2,64]{2,1,0:T(2,128)S(1)}, f32[1024,2,64]{2,1,0:T(2,128)}, u32[]{:S(2)}) copy-start(f32[1024,2,64]{2,1,0:T(2,128)} %copy.228) | copy-start | bytes 1572868
  318.0 11.3 %copy-start.5 = (f32[4,512,512]{1,2,0:T(8,128)S(1)}, f32[4,512,512]{1,2,0:T(8,128)}, u32[]{:S(2)}) copy-start(f32[4,512,512]{1,2,0:T(8,128)} %copy-done.3) | copy-start | bytes 12582916
  323.7 5.6 %copy-start.27 = (bf16[1024,4,64]{0,2,1:T(8,128)(2,1)S(1)}, bf16[1024,4,64]{0,2,1:T(8,128)(2,1)}, u32[]{:S(2)}) copy-start(bf16[1024,4,64]{0,2,1:T(8,128)(2,1)} %multiply_convert_fusion.8) | copy-start | bytes 1572868
  323.7 5.6 %copy-start.31 = (bf16[512,256]{0,1:T(8,128)(2,1)S(1)}, bf16[512,256]{0,1:T(8,128)(2,1)}, u32[]{:S(2)}) copy-start(bf16[512,256]{0,1:T(8,128)(2,1)} %copy-done.30) | copy-start | bytes 786436
  330.4 3.6 slice-start.1
  342.8 6.4 %copy-start.23 = (f32[1024,4,2]{1,2,0:T(2,128)S(1)}, f32[1024,4,2]{1,2,0:T(2,128)}, u32[]{:S(2)}) copy-start(f32[1024,4,2]{1,2,0:T(2,128)} %copy.271) | copy-start | bytes 98308
  342.9 6.4 %copy-start.44 = (bf16[1024,4,64]{2,1,0:T(4,128)(2,1)S(1)}, bf16[1024,4,64]{2,1,0:T(4,128)(2,1)}, u32[]{:S(2)}) copy-start(bf16[1024,4,64]{2,1,0:T(4,128)(2,1)} %copy.246) | copy-start | bytes 1572868
  349.3 5.1 copy-start.49
  349.3 6.1 %copy-start.45 = (bf16[512,4,64]{0,2,1:T(8,128)(2,1)S(1)}, bf16[512,4,64]{0,2,1:T(8,128)(2,1)}, u32[]{:S(2)}) copy-start(bf16[512,4,64]{0,2,1:T(8,128)(2,1)} %fusion.36) | copy-start | bytes 786436
  349.3 8.5 %copy-start.12 = (f32[1024,32]{1,0:T(8,128)S(1)}, f32[1024,32]{1,0:T(8,128)}, u32[]{:S(2)}) copy-start(f32[1024,32]{1,0:T(8,128)} %get-tuple-element.194) | copy-start | bytes 393220
  349.3 8.5 %copy-start.13 = (f32[1024,32]{1,0:T(8,128)S(1)}, f32[1024,32]{1,0:T(8,128)}, u32[]{:S(2)}) copy-start(f32[1024,32]{1,0:T(8,128)} %get-tuple-element.195) | copy-start | bytes 393220
  387.3 6.3 %copy-start.38 = (bf16[1024,4,64]{0,2,1:T(8,128)(2,1)S(1)}, bf16[1024,4,64]{0,2,1:T(8,128)(2,1)}, u32[]{:S(2)}) copy-start(bf16[1024,4,64]{0,2,1:T(8,128)(2,1)} %copy-done.37) | copy-start | bytes 1572868
  387.4 9.6 %copy-start.52 = (bf16[1024,40]{0,1:T(8,128)(2,1)S(1)}, bf16[1024,40]{0,1:T(8,128)(2,1)}, u32[]{:S(2)}) copy-start(bf16[1024,40]{0,1:T(8,128)(2,1)} %param.14) | copy-start | bytes 245764
  387.5 10.2 %collective-permute-start.6 = (bf16[1024,160]{0,1:T(8,128)(2,1)S(1)}, bf16[1024,160]{0,1:T(8,128)(2,1)S(1)}, u32[]{:S(2)}, u32[]{:S(2)}) collective-permute-start(bf16[1024,160]{0,1:T(8,128)(2,1)S(1)} %get-tuple-element.179), channel_id=1, source_target_pairs={{0,1},{1,2},{2,3},{3,0},{4,5},{5,6},{6,7},{7,4},{8,9},{9,10},{10,1... | collective-permute-start | bytes 983048 | tf_op jit(solution)/shard_map/ppermute | solution.py:174
  391.6 8.3 %collective-permute-start.8 = (bf16[1024,160]{0,1:T(8,128)(2,1)S(1)}, bf16[1024,160]{0,1:T(8,128)(2,1)S(1)}, u32[]{:S(2)}, u32[]{:S(2)}) collective-permute-start(bf16[1024,160]{0,1:T(8,128)(2,1)S(1)} %get-tuple-element.180), channel_id=1, source_target_pairs={{0,3},{1,0},{2,1},{3,2},{4,7},{5,4},{6,5},{7,6},{8,11},{9,8},{10,9... | collective-permute-start | bytes 983048 | tf_op jit(solution)/shard_map/ppermute | solution.py:174
  391.8 14.6 %collective-permute-start.7 = (bf16[1024,160]{0,1:T(8,128)(2,1)S(1)}, bf16[1024,160]{0,1:T(8,128)(2,1)S(1)}, u32[]{:S(2)}, u32[]{:S(2)}) collective-permute-start(bf16[1024,160]{0,1:T(8,128)(2,1)S(1)} %get-tuple-element.181), channel_id=1, source_target_pairs={{0,2},{1,3},{2,0},{3,1},{4,6},{5,7},{6,4},{7,5},{8,10},{9,11},{10,... | collective-permute-start | bytes 983048 | tf_op jit(solution)/shard_map/ppermute | solution.py:174
  408.8 4.0 copy-start.10
  409.0 11.9 %collective-permute-start.9 = (bf16[256,1024]{1,0:T(8,128)(2,1)S(1)}, bf16[256,1024]{1,0:T(8,128)(2,1)S(1)}, u32[]{:S(2)}, u32[]{:S(2)}) collective-permute-start(bf16[256,1024]{1,0:T(8,128)(2,1)S(1)} %get-tuple-element.169), channel_id=1, source_target_pairs={{0,1},{1,2},{2,3},{3,0},{4,5},{5,6},{6,7},{7,4},{8,9},{9,10},{10,1... | collective-permute-start | bytes 1572872 | tf_op jit(solution)/shard_map/ppermute | solution.py:174
  409.0 14.0 %collective-permute-start.11 = (bf16[256,1024]{1,0:T(8,128)(2,1)S(1)}, bf16[256,1024]{1,0:T(8,128)(2,1)S(1)}, u32[]{:S(2)}, u32[]{:S(2)}) collective-permute-start(bf16[256,1024]{1,0:T(8,128)(2,1)S(1)} %get-tuple-element.170), channel_id=1, source_target_pairs={{0,3},{1,0},{2,1},{3,2},{4,7},{5,4},{6,5},{7,6},{8,11},{9,8},{10,9... | collective-permute-start | bytes 1572872 | tf_op jit(solution)/shard_map/ppermute | solution.py:174
  410.8 23.7 %copy-start.58 = (f32[1024]{0:T(1024)S(1)}, f32[1024]{0:T(1024)}, u32[]{:S(2)}) copy-start(f32[1024]{0:T(1024)} %param.13) | copy-start | bytes 12292
  410.8 23.7 %copy-start.66 = (f32[256]{0:T(256)S(1)}, f32[256]{0:T(256)}, u32[]{:S(2)}) copy-start(f32[256]{0:T(256)} %copy-done.65) | copy-start | bytes 3076
  410.8 23.7 %collective-permute-start.10 = (bf16[256,1024]{1,0:T(8,128)(2,1)S(1)}, bf16[256,1024]{1,0:T(8,128)(2,1)S(1)}, u32[]{:S(2)}, u32[]{:S(2)}) collective-permute-start(bf16[256,1024]{1,0:T(8,128)(2,1)S(1)} %get-tuple-element.171), channel_id=1, source_target_pairs={{0,2},{1,3},{2,0},{3,1},{4,6},{5,7},{6,4},{7,5},{8,10},{9,11},{10,... | collective-permute-start | bytes 1572872 | tf_op jit(solution)/shard_map/ppermute | solution.py:174
  414.5 110.0 %copy-start.15 = (f32[256,1024]{1,0:T(8,128)S(1)}, f32[256,1024]{1,0:T(8,128)}, u32[]{:S(2)}) copy-start(f32[256,1024]{1,0:T(8,128)} %copy-done.14) | copy-start | bytes 3145732
  414.5 110.0 %copy-start.67 = (f32[256]{0:T(256)S(1)}, f32[256]{0:T(256)}, u32[]{:S(2)}) copy-start(f32[256]{0:T(256)} %get-tuple-element.198) | copy-start | bytes 3076
  444.1 100.5 %all-gather.11.cloned.1.call-start = ((), (), s32[]{:S(2)}) async-start(), calls=%async_computation.7 | async-start | bytes 1843200 | tf_op jit(solution)/shard_map/all_gather | solution.py:367
  546.4 6.4 %copy-start.1 = (bf16[704,1024]{1,0:T(8,128)(2,1)S(1)}, bf16[704,1024]{1,0:T(8,128)(2,1)}, u32[]{:S(2)}) copy-start(bf16[704,1024]{1,0:T(8,128)(2,1)} %param.20) | copy-start | bytes 4325380
  (38 other events, 76.2 us)
Sparse Core Ops, SparseCore 0:
  11.8 25.2 all-gather.4
  136.7 31.1 reduce-scatter.2
  171.9 22.5 all-gather.6
  196.0 22.5 all-gather.8
  230.8 42.2 reduce-scatter.4
  283.5 160.5 all-reduce.9
  448.4 76.0 all-reduce.7
  526.0 18.5 all-gather.10

commit v6 on v5

--- a/solution.py
+++ b/solution.py
@@ -218,8 +218,8 @@
     inv_one = lax.rsqrt(jnp.mean(x_own * x_own, axis=-1, keepdims=True) + EPSILON)
     normed_one = (x_own * inv_one * gain_attn).astype(jnp.bfloat16)
     normed_all, grad_out_all = (
-        lax.all_gather(normed_one, "head", axis=0, tiled=True),
-        lax.all_gather(cotangent, "head", axis=0, tiled=True),
+        head_all_gather(normed_one, 0),
+        head_all_gather(cotangent, 0),
     )
     factor_a = jnp.dot(normed_all, a_weight, preferred_element_type=jnp.float32).reshape(
         total_rows, local_heads, rank_all
@@ -250,15 +250,12 @@
     mixed_rows, log_total = lax.map(attend_row, (query_rows, keys_rows, values_rows, doc_ids))
     mixed = mixed_rows.reshape(total_rows, local_heads * DH)
     piece = lax.slice_in_dim(mixed, 0, lax.axis_size("head") * own_rows, axis=0)
-    resid_own = x_own + lax.psum_scatter(
-        jnp.dot(piece, out_weight, preferred_element_type=jnp.float32).astype(jnp.bfloat16),
-        "head",
-        scatter_dimension=0,
-        tiled=True,
-    ).astype(jnp.float32)
+    resid_own = x_own + head_reduce_scatter(
+        jnp.dot(piece, out_weight, preferred_element_type=jnp.float32).astype(jnp.bfloat16), 0
+    )
     inv_two = lax.rsqrt(jnp.mean(resid_own * resid_own, axis=-1, keepdims=True) + EPSILON)
     normed_two = (resid_own * inv_two * gain_ffn).astype(jnp.bfloat16)
-    normed_two_all = lax.all_gather(normed_two, "head", axis=0, tiled=True)
+    normed_two_all = head_all_gather(normed_two, 0)
     gate_act = jnp.dot(normed_two_all, gate_weight, preferred_element_type=jnp.float32)
     up_act = jnp.dot(normed_two_all, up_weight, preferred_element_type=jnp.float32)
     sigmoid_gate = jax.nn.sigmoid(gate_act)
@@ -281,12 +278,9 @@
     grad_up = dot_first(normed_two_all, grad_up_act)
     gate_piece = lax.slice_in_dim(grad_gate_act, 0, lax.axis_size("head") * own_rows, axis=0)
     up_piece = lax.slice_in_dim(grad_up_act, 0, lax.axis_size("head") * own_rows, axis=0)
-    grad_normed_two = lax.psum_scatter(
-        (dot_last(gate_piece, gate_weight) + dot_last(up_piece, up_weight)).astype(jnp.bfloat16),
-        "head",
-        scatter_dimension=0,
-        tiled=True,
-    ).astype(jnp.float32)
+    grad_normed_two = head_reduce_scatter(
+        (dot_last(gate_piece, gate_weight) + dot_last(up_piece, up_weight)).astype(jnp.bfloat16), 0
+    )
     ffn_grads = (grad_gate.astype(jnp.bfloat16), grad_up.astype(jnp.bfloat16), grad_down.astype(jnp.bfloat16))
     ffn_grads, grad_normed_two = lax.optimization_barrier((ffn_grads, grad_normed_two))
     grad_gate, grad_up, grad_down = lax.psum(ffn_grads, "dp")

time: 570 us -> 578 us (1.014)
  local copies, waits for them, and re-layouts: 77.1 us -> 116 us
  waiting for transfers between devices: 261 us -> 227 us
  starting transfers between devices: 14.3 us -> 29.7 us
  matrix products: 138 us -> 125 us
    ppermute x9 -> x15, waiting for transfers between devices: 28.7 us -> 87.5 us  [head_reduce_scatter(): lax.ppermute(sent, 'head', [(device, (device + shift) % count) for device...]
    reduce_scatter x2 -> x0, waiting for transfers between devices: 58.5 us -> none  [the longest x1 31.3 us: local(): lax.psum_scatter(jnp.dot(piece, out_weight, preferred_element_type=jnp.fl...]
    all_gather x3 -> x0, waiting for transfers between devices: 56 us -> none  [the longest x1 22.1 us: local(): normed_two_all = lax.all_gather(normed_two, 'head', axis=0, tiled=True)]
    ppermute x3 -> x12, waiting for transfers between devices: 18.2 us -> 52.1 us  [head_all_gather(): lax.ppermute(values, 'head', [(device, (device + shift) % count) for devi...]
    dynamic_update_slice x3 -> x12, local copies, waits for them, and re-layouts: 4.56 us -> 17 us  [head_all_gather(): lax.dynamic_update_slice_in_dim(gathered, arrived, (own - shift) % count...]
    unnamed x172, local copies, waits for them, and re-layouts: 26.9 us -> 38.7 us
    ppermute x3 -> x12, starting transfers between devices: 2.03 us -> 13 us  [head_all_gather(): lax.ppermute(values, 'head', [(device, (device + shift) % count) for devi...]
    psum x1, waiting for transfers between devices: 7.99 us -> 0.01 us  [local(): grad_gate, grad_up, grad_down = lax.psum(ffn_grads, 'dp')]
  transfers between devices with their start and end apart: 20 -> 30, of which waited for: 16 -> 24; matrix products, arithmetic and copies ran while one was open for 24% -> 27% of each run, Pallas kernels for 0% -> 0%
where the time goes in v6:
time: 578 us; the launch traced here: 568 us
  waiting for transfers between devices  227 us (39%)
  matrix products  125 us (22%)
  local copies, waits for them, and re-layouts  116 us (20%)
  other arithmetic  54.8 us (9%)
  starting transfers between devices  29.7 us (5%)
  between operations  15.3 us (3%)
    ppermute x15, waiting for transfers between devices, head_reduce_scatter(): lax.ppermute(sent, 'head', [(device, (device + shift) % count) for device...  87.5 us
    psum x1, waiting for transfers between devices, local(): grad_a, grad_out, packed = lax.psum(tail, 'dp')  78.6 us
    ppermute x12, waiting for transfers between devices, head_all_gather(): lax.ppermute(values, 'head', [(device, (device + shift) % count) for devi...  52.1 us
    unnamed x172, local copies, waits for them, and re-layouts  38.7 us
    dynamic_update_slice x12, local copies, waits for them, and re-layouts, head_all_gather(): lax.dynamic_update_slice_in_dim(gathered, arrived, (own - shift) % count...  17 us
    ppermute x15, starting transfers between devices, head_reduce_scatter(): lax.ppermute(sent, 'head', [(device, (device + shift) % count) for device...  16.6 us
    ppermute x12, starting transfers between devices, head_all_gather(): lax.ppermute(values, 'head', [(device, (device + shift) % count) for devi...  13 us
    dot_general x6, matrix products, dot_first(): lax.dot_general(left, right, (((0,), (0,)), ((), ())), preferred_element_...  13 us
  transfers between devices with their start and end apart: 30, of which 24 were waited for; matrix products, arithmetic and copies ran while one was open for 27% of the time, Pallas kernels for 0%

profile of v6, /device:TPU:0, one launch (start us, length us, event | category | flops | bytes accessed | tf_op | source)
XLA Modules:
  0.0 567.7 jit_solution(14367598525135501489)
XLA Ops:
  11.4 3.0 collective-permute-start.1
  18.6 3.1 multiply_cosine_fusion
  21.7 15.3 %collective-permute-done = bf16[256,1024]{0,1:T(8,128)(2,1)} collective-permute-done((bf16[256,1024]{0,1:T(8,128)(2,1)}, bf16[256,1024]{0,1:T(8,128)(2,1)}, u32[]{:S(2)}, u32[]{:S(2)}) %collective-permute-start) | collective-permute-done | bytes 524320 | tf_op jit(solution)/shard_map/ppermute | solution.py:190
  46.4 2.9 fusion.78
  55.5 2.6 copy.351
  60.0 2.7 fusion.68
  62.7 2.2 copy.294
  64.8 2.1 copy.356
  69.0 2.6 multiply_subtract_fusion.1
  73.0 10.4 %fusion.65 = f32[1024,4,64]{2,1,0:T(4,128)} fusion(f32[1024,4,2]{1,2,0:T(2,128)S(1)} %copy-done.26, f32[1024,2,32]{2,1,0:T(2,128)S(1)} %get-tuple-element.172, f32[1024,2,32]{2,1,0:T(2,128)S(1)} %get-tuple-element.171), kind=kOutput, calls=%fused_computation.174 | convolution fusion | flops 6422528 | bytes 1605632 | tf_op jit(solution)/shard_map/thr,trd->thd/dot_general | solution.py:240
  83.4 2.7 copy.302
  88.1 10.9 %fusion.79 = f32[1024,4,64]{2,1,0:T(4,128)} fusion(f32[1024,4,2]{1,2,0:T(2,128)} %copy.350, f32[1024,2,64]{2,1,0:T(2,128)} %copy.294), kind=kOutput, calls=%fused_computation.187 | convolution fusion | flops 6291456 | bytes 1605632 | tf_op jit(solution)/shard_map/thr,trd->thd/dot_general | solution.py:244
  99.0 2.7 copy.295
  101.7 2.1 multiply_convert_fusion.8
  103.8 3.7 copy.353
  107.5 3.6 copy.352
  111.0 4.3 multiply_subtract_fusion
  115.4 8.3 %multiply_convert_fusion.5 = bf16[1024,4,64]{2,1,0:T(4,128)(2,1)S(1)} fusion(f32[1024,4,6]{2,1,0:T(4,128)S(1)} %copy-done.8, f32[1024,6,32]{2,1,0:T(8,128)S(1)} %get-tuple-element.165, f32[1024,6,32]{2,1,0:T(8,128)S(1)} %get-tuple-element.164), kind=kOutput, calls=%fused_computation.41 | convolution fusion | flops 19791872 | bytes 2195456 | tf_op jit(solution)/shard_map/thr,trd->thd/dot_general | solution.py:237
  139.4 2.1 fusion.37
  147.6 7.5 %collective-permute-done.3 = bf16[256,1024]{0,1:T(8,128)(2,1)S(1)} collective-permute-done((bf16[256,1024]{0,1:T(8,128)(2,1)S(1)}, bf16[256,1024]{0,1:T(8,128)(2,1)S(1)}, u32[]{:S(2)}, u32[]{:S(2)}) %collective-permute-start.3) | collective-permute-done | bytes 524320 | tf_op jit(solution)/shard_map/ppermute | solution.py:174
  155.1 2.3 collective-permute-start.13
  157.5 12.4 %collective-permute-done.4 = bf16[256,1024]{0,1:T(8,128)(2,1)S(1)} collective-permute-done((bf16[256,1024]{0,1:T(8,128)(2,1)S(1)}, bf16[256,1024]{0,1:T(8,128)(2,1)S(1)}, u32[]{:S(2)}, u32[]{:S(2)}) %collective-permute-start.4) | collective-permute-done | bytes 524320 | tf_op jit(solution)/shard_map/ppermute | solution.py:174
  185.7 6.7 %collective-permute-done.13 = bf16[256,1024]{1,0:T(8,128)(2,1)} collective-permute-done((bf16[256,1024]{1,0:T(8,128)(2,1)}, bf16[256,1024]{1,0:T(8,128)(2,1)}, u32[]{:S(2)}, u32[]{:S(2)}) %collective-permute-start.13) | collective-permute-done | bytes 524320 | tf_op jit(solution)/shard_map/ppermute | solution.py:190
  201.3 2.4 collective-permute-done.7
  204.8 7.4 %collective-permute-done.8 = bf16[256,1024]{0,1:T(8,128)(2,1)} collective-permute-done((bf16[256,1024]{0,1:T(8,128)(2,1)}, bf16[256,1024]{0,1:T(8,128)(2,1)}, u32[]{:S(2)}, u32[]{:S(2)}) %collective-permute-start.8) | collective-permute-done | bytes 524320 | tf_op jit(solution)/shard_map/ppermute | solution.py:190
  216.6 3.0 multiply_convert_fusion.2
  219.7 2.8 convolution_convert_fusion.2
  224.3 2.9 convolution_convert_fusion.3
  238.2 2.8 convolution_convert_fusion.4
  241.0 5.6 collective-permute-done.15
  247.1 12.1 %collective-permute-done.16 = bf16[256,1024]{0,1:T(8,128)(2,1)} collective-permute-done((bf16[256,1024]{0,1:T(8,128)(2,1)}, bf16[256,1024]{0,1:T(8,128)(2,1)}, u32[]{:S(2)}, u32[]{:S(2)}) %collective-permute-start.16) | collective-permute-done | bytes 524320 | tf_op jit(solution)/shard_map/ppermute | solution.py:174
  262.1 7.0 %collective-permute-done.9 = bf16[256,1024]{0,1:T(8,128)(2,1)} collective-permute-done((bf16[256,1024]{0,1:T(8,128)(2,1)}, bf16[256,1024]{0,1:T(8,128)(2,1)}, u32[]{:S(2)}, u32[]{:S(2)}) %collective-permute-start.9) | collective-permute-done | bytes 524320 | tf_op jit(solution)/shard_map/ppermute | solution.py:174
  269.6 11.3 %collective-permute-done.10 = bf16[256,1024]{0,1:T(8,128)(2,1)S(1)} collective-permute-done((bf16[256,1024]{0,1:T(8,128)(2,1)}, bf16[256,1024]{0,1:T(8,128)(2,1)S(1)}, u32[]{:S(2)}, u32[]{:S(2)}) %collective-permute-start.10) | collective-permute-done | bytes 524320 | tf_op jit(solution)/shard_map/ppermute | solution.py:174
  280.9 2.8 subtract_add_fusion
  287.9 11.7 %collective-permute-done.18 = bf16[256,1024]{0,1:T(8,128)(2,1)S(1)} collective-permute-done((bf16[256,1024]{0,1:T(8,128)(2,1)S(1)}, bf16[256,1024]{0,1:T(8,128)(2,1)S(1)}, u32[]{:S(2)}, u32[]{:S(2)}) %collective-permute-start.18) | collective-permute-done | bytes 524320 | tf_op jit(solution)/shard_map/ppermute | solution.py:190
  302.7 6.5 %collective-permute-done.20 = bf16[256,1024]{0,1:T(8,128)(2,1)} collective-permute-done((bf16[256,1024]{0,1:T(8,128)(2,1)S(1)}, bf16[256,1024]{0,1:T(8,128)(2,1)}, u32[]{:S(2)}, u32[]{:S(2)}) %collective-permute-start.20) | collective-permute-done | bytes 524320 | tf_op jit(solution)/shard_map/ppermute | solution.py:190
  311.1 2.5 convolution_convert_fusion.5
  314.8 5.8 %fusion.22 = bf16[1024,4,64]{0,2,1:T(8,128)(2,1)} fusion(bf16[512,4,64]{0,2,1:T(8,128)(2,1)S(1)} %bitcast.111, f32[4,512,1024]{2,1,0:T(8,128)} %copy-done.2, f32[4,512]{1,0:T(4,128)S(1)} %log_add_fusion, f32[512,4,64]{0,2,1:T(8,128)S(1)} %fusion.27), kind=kOutput, calls=%fused_computation.60 | convolution fusion | flops 273154048 | bytes 9707520 | tf_op jit(solution)/shard_map/while/body/eval_jaxpr/hqk,qhd->khd/dot_general | solution.py:152
  320.6 2.3 copy.323
  322.9 5.7 %fusion.26 = bf16[1024,2,64]{2,1,0:T(2,128)(2,1)} fusion(f32[1024,4,2]{1,2,0:T(2,128)S(1)} %copy-done.28, bf16[1024,4,64]{2,1,0:T(4,128)(2,1)} %copy.323), kind=kOutput, calls=%fused_computation.62 | convolution fusion | flops 6553600 | bytes 819200 | tf_op jit(solution)/shard_map/thr,thd->trd/dot_general | solution.py:310
  328.6 6.0 %convolution_multiply_fusion.4 = bf16[1024,4,2]{1,2,0:T(2,128)(2,1)} fusion(bf16[1024,4,64]{2,1,0:T(4,128)(2,1)} %copy.323, f32[1024,2,64]{2,1,0:T(2,128)} %copy.294), kind=kOutput, calls=%fused_computation.53 | convolution fusion | flops 6307840 | bytes 1064960 | tf_op jit(solution)/shard_map/thd,trd->thr/dot_general | solution.py:303
  339.6 2.6 multiply_reduce_fusion
  344.1 2.1 fusion.35
  347.9 2.3 copy.320
  350.2 6.8 %convolution_multiply_fusion.5 = bf16[1024,4,2]{1,2,0:T(2,128)(2,1)} fusion(bf16[1024,4,64]{2,1,0:T(4,128)(2,1)} %copy.320, f32[1024,2,32]{2,1,0:T(2,128)} %copy-done.25, f32[1024,2,32]{2,1,0:T(2,128)S(1)} %copy-done.24), kind=kOutput, calls=%fused_computation.54 | convolution fusion | flops 6438912 | bytes 1064960 | tf_op jit(solution)/shard_map/thd,trd->thr/dot_general | solution.py:302
  357.0 4.5 convolution_multiply_fusion.3
  368.1 3.1 add_convert_fusion.3
  371.2 2.2 pad_maximum_fusion.8
  375.3 2.5 copy.315
  377.8 9.1 %convolution_multiply_fusion.1 = bf16[1024,4,6]{2,1,0:T(4,128)(2,1)} fusion(bf16[1024,4,64]{2,1,0:T(4,128)(2,1)} %copy.315, f32[1024,6,32]{2,1,0:T(8,128)} %copy-done.7, f32[1024,6,32]{2,1,0:T(8,128)} %copy-done.6), kind=kOutput, calls=%fused_computation.49 | convolution fusion | flops 19316736 | bytes 2146304 | tf_op jit(solution)/shard_map/thd,trd->thr/dot_general | solution.py:301
  388.9 6.1 %convolution_multiply_fusion = f32[1024,6,64]{2,1,0:T(8,128)S(1)} fusion(f32[1024,4,6]{2,1,0:T(4,128)} %copy.351, bf16[1024,4,64]{2,1,0:T(4,128)(2,1)} %copy.315), kind=kOutput, calls=%fused_computation.37 | convolution fusion | flops 19267584 | bytes 2195456 | tf_op jit(solution)/shard_map/thr,thd->trd/dot_general | solution.py:305
  395.0 3.1 add_convert_fusion.1
  398.1 2.5 copy.328
  400.5 2.3 copy.329
  404.3 3.5 collective-permute-start.21
  412.0 2.2 collective-permute-done.21
  414.2 2.2 collective-permute-done.23
  416.4 6.9 %collective-permute-done.22 = bf16[1024,160]{0,1:T(8,128)(2,1)S(1)} collective-permute-done((bf16[1024,160]{0,1:T(8,128)(2,1)S(1)}, bf16[1024,160]{0,1:T(8,128)(2,1)S(1)}, u32[]{:S(2)}, u32[]{:S(2)}) %collective-permute-start.22) | collective-permute-done | bytes 327712 | tf_op jit(solution)/shard_map/ppermute | solution.py:174
  431.8 6.4 %collective-permute-done.24 = bf16[256,1024]{0,1:T(8,128)(2,1)S(1)} collective-permute-done((bf16[256,1024]{0,1:T(8,128)(2,1)S(1)}, bf16[256,1024]{0,1:T(8,128)(2,1)S(1)}, u32[]{:S(2)}, u32[]{:S(2)}) %collective-permute-start.24) | collective-permute-done | bytes 524320 | tf_op jit(solution)/shard_map/ppermute | solution.py:174
  439.7 11.4 %collective-permute-done.25 = bf16[256,1024]{0,1:T(8,128)(2,1)S(1)} collective-permute-done((bf16[256,1024]{0,1:T(8,128)(2,1)S(1)}, bf16[256,1024]{0,1:T(8,128)(2,1)S(1)}, u32[]{:S(2)}, u32[]{:S(2)}) %collective-permute-start.25) | collective-permute-done | bytes 524320 | tf_op jit(solution)/shard_map/ppermute | solution.py:174
  453.8 78.6 %all-reduce.8.cloned.1.call-done = (bf16[1037,160]{0,1:T(8,128)(2,1)}, bf16[1024,40]{0,1:T(8,128)(2,1)}, bf16[256,1024]{1,0:T(8,128)(2,1)}) async-done(((bf16[1037,160]{0,1:T(8,128)(2,1)}, bf16[1024,40]{0,1:T(8,128)(2,1)}, bf16[256,1024]{1,0:T(8,128)(2,1)}), (bf16[1037,160]{0,1:T(8,128)(2,1)}, bf16[1024,40]{0,1:T(8,128)(2,1)}, bf16[256,1024]{1,0:T(8,128)(2,1)})) %all-reduce.8.cloned.1.call-update) | async-done | bytes 938064 | tf_op jit(solution)/shard_map/psum | solution.py:353
  544.0 8.5 %all-gather.2.cloned.1.call-done = bf16[1037,640]{0,1:T(8,128)(2,1)} async-done(((bf16[1037,160]{0,1:T(8,128)(2,1)}), bf16[1037,640]{0,1:T(8,128)(2,1)}) %all-gather.2.cloned.1.call-update) | async-done | bytes 1327376 | tf_op jit(solution)/shard_map/all_gather | solution.py:361
  554.3 3.3 slice.177
  557.6 3.2 copy.340
  (318 shorter events, 160.9 us)
Async XLA Ops:
  7.2 209.4 %copy-start = (bf16[704,1024]{1,0:T(8,128)(2,1)S(1)}, bf16[704,1024]{1,0:T(8,128)(2,1)}, u32[]{:S(2)}) copy-start(bf16[704,1024]{1,0:T(8,128)(2,1)} %param.20) | copy-start | bytes 4325380
  7.2 446.5 %all-reduce.10.cloned.1.call-start = ((), (), s32[]{:S(2)}) async-start(), calls=%async_computation.2 | async-start | bytes 8650752 | tf_op jit(solution)/shard_map/psum | solution.py:286
  8.6 7.6 %copy-start.70 = (s32[1,1024]{1,0:T(1,128)S(1)}, s32[1,1024]{1,0:T(1,128)}, u32[]{:S(2)}) copy-start(s32[1,1024]{1,0:T(1,128)} %param.12) | copy-start | bytes 12292
  9.4 8.2 %copy-start.71 = (f32[256]{0:T(256)}, f32[256]{0:T(256)S(1)}, u32[]{:S(2)}) copy-start(f32[256]{0:T(256)S(1)} %get-tuple-element.211) | copy-start | bytes 3076
  11.4 26.7 %collective-permute-start.1 = (bf16[256,1024]{0,1:T(8,128)(2,1)}, bf16[256,1024]{0,1:T(8,128)(2,1)}, u32[]{:S(2)}, u32[]{:S(2)}) collective-permute-start(bf16[256,1024]{0,1:T(8,128)(2,1)} %get-tuple-element.163), channel_id=1, source_target_pairs={{0,2},{1,3},{2,0},{3,1},{4,6},{5,7},{6,4},{7,5},{8,10},{9,11},{10,... | collective-permute-start | bytes 1572872 | tf_op jit(solution)/shard_map/ppermute | solution.py:190
  14.4 22.6 %collective-permute-start = (bf16[256,1024]{0,1:T(8,128)(2,1)}, bf16[256,1024]{0,1:T(8,128)(2,1)}, u32[]{:S(2)}, u32[]{:S(2)}) collective-permute-start(bf16[256,1024]{0,1:T(8,128)(2,1)} %get-tuple-element.163), channel_id=1, source_target_pairs={{0,1},{1,2},{2,3},{3,0},{4,5},{5,6},{6,7},{7,4},{8,9},{9,10},{10,1... | collective-permute-start | bytes 1572872 | tf_op jit(solution)/shard_map/ppermute | solution.py:190
  14.4 24.8 %collective-permute-start.2 = (bf16[256,1024]{0,1:T(8,128)(2,1)}, bf16[256,1024]{0,1:T(8,128)(2,1)}, u32[]{:S(2)}, u32[]{:S(2)}) collective-permute-start(bf16[256,1024]{0,1:T(8,128)(2,1)} %get-tuple-element.163), channel_id=1, source_target_pairs={{0,3},{1,0},{2,1},{3,2},{4,7},{5,4},{6,5},{7,6},{8,11},{9,8},{10,9... | collective-permute-start | bytes 1572872 | tf_op jit(solution)/shard_map/ppermute | solution.py:190
  18.6 21.8 %copy-start.57 = (bf16[1024,40]{0,1:T(8,128)(2,1)S(1)}, bf16[1024,40]{0,1:T(8,128)(2,1)}, u32[]{:S(2)}) copy-start(bf16[1024,40]{0,1:T(8,128)(2,1)} %param.14) | copy-start | bytes 245764
  115.3 8.3 %copy-start.6 = (f32[1024,6,32]{2,1,0:T(8,128)}, f32[1024,6,32]{2,1,0:T(8,128)S(1)}, u32[]{:S(2)}) copy-start(f32[1024,6,32]{2,1,0:T(8,128)S(1)} %get-tuple-element.164) | copy-start | bytes 2359300
  115.3 8.3 %copy-start.7 = (f32[1024,6,32]{2,1,0:T(8,128)}, f32[1024,6,32]{2,1,0:T(8,128)S(1)}, u32[]{:S(2)}) copy-start(f32[1024,6,32]{2,1,0:T(8,128)S(1)} %get-tuple-element.165) | copy-start | bytes 2359300
  142.4 27.5 %copy-start.11 = (bf16[256,1024]{0,1:T(8,128)(2,1)S(1)}, bf16[256,1024]{0,1:T(8,128)(2,1)}, u32[]{:S(2)}) copy-start(bf16[256,1024]{0,1:T(8,128)(2,1)} %copy-done.9) | copy-start | bytes 1572868
  142.6 12.5 %collective-permute-start.3 = (bf16[256,1024]{0,1:T(8,128)(2,1)S(1)}, bf16[256,1024]{0,1:T(8,128)(2,1)S(1)}, u32[]{:S(2)}, u32[]{:S(2)}) collective-permute-start(bf16[256,1024]{0,1:T(8,128)(2,1)S(1)} %get-tuple-element.186), channel_id=1, source_target_pairs={{0,1},{1,2},{2,3},{3,0},{4,5},{5,6},{6,7},{7,4},{8,9},{9,10},{10,1... | collective-permute-start | bytes 1572872 | tf_op jit(solution)/shard_map/ppermute | solution.py:174
  142.7 14.8 %collective-permute-start.5 = (bf16[256,1024]{0,1:T(8,128)(2,1)S(1)}, bf16[256,1024]{0,1:T(8,128)(2,1)S(1)}, u32[]{:S(2)}, u32[]{:S(2)}) collective-permute-start(bf16[256,1024]{0,1:T(8,128)(2,1)S(1)} %get-tuple-element.187), channel_id=1, source_target_pairs={{0,3},{1,0},{2,1},{3,2},{4,7},{5,4},{6,5},{7,6},{8,11},{9,8},{10,9... | collective-permute-start | bytes 1572872 | tf_op jit(solution)/shard_map/ppermute | solution.py:174
  144.4 26.8 %copy-start.60 = (f32[1024]{0:T(1024)S(1)}, f32[1024]{0:T(1024)}, u32[]{:S(2)}) copy-start(f32[1024]{0:T(1024)} %param.17) | copy-start | bytes 12292
  144.4 25.5 %collective-permute-start.4 = (bf16[256,1024]{0,1:T(8,128)(2,1)S(1)}, bf16[256,1024]{0,1:T(8,128)(2,1)S(1)}, u32[]{:S(2)}, u32[]{:S(2)}) collective-permute-start(bf16[256,1024]{0,1:T(8,128)(2,1)S(1)} %get-tuple-element.188), channel_id=1, source_target_pairs={{0,2},{1,3},{2,0},{3,1},{4,6},{5,7},{6,4},{7,5},{8,10},{9,11},{10,... | collective-permute-start | bytes 1572872 | tf_op jit(solution)/shard_map/ppermute | solution.py:174
  145.9 32.2 %collective-permute-start.12 = (bf16[256,1024]{1,0:T(8,128)(2,1)}, bf16[256,1024]{1,0:T(8,128)(2,1)}, u32[]{:S(2)}, u32[]{:S(2)}) collective-permute-start(bf16[256,1024]{1,0:T(8,128)(2,1)} %param.21), channel_id=1, source_target_pairs={{0,1},{1,2},{2,3},{3,0},{4,5},{5,6},{6,7},{7,4},{8,9},{9,10},{10,1... | collective-permute-start | bytes 1572872 | tf_op jit(solution)/shard_map/ppermute | solution.py:190
  145.9 37.8 %collective-permute-start.14 = (bf16[256,1024]{1,0:T(8,128)(2,1)}, bf16[256,1024]{1,0:T(8,128)(2,1)}, u32[]{:S(2)}, u32[]{:S(2)}) collective-permute-start(bf16[256,1024]{1,0:T(8,128)(2,1)} %param.21), channel_id=1, source_target_pairs={{0,3},{1,0},{2,1},{3,2},{4,7},{5,4},{6,5},{7,6},{8,11},{9,8},{10,9... | collective-permute-start | bytes 1572872 | tf_op jit(solution)/shard_map/ppermute | solution.py:190
  155.1 37.3 %collective-permute-start.13 = (bf16[256,1024]{1,0:T(8,128)(2,1)}, bf16[256,1024]{1,0:T(8,128)(2,1)}, u32[]{:S(2)}, u32[]{:S(2)}) collective-permute-start(bf16[256,1024]{1,0:T(8,128)(2,1)} %param.21), channel_id=1, source_target_pairs={{0,2},{1,3},{2,0},{3,1},{4,6},{5,7},{6,4},{7,5},{8,10},{9,11},{10,... | collective-permute-start | bytes 1572872 | tf_op jit(solution)/shard_map/ppermute | solution.py:190
  173.5 26.7 %collective-permute-start.6 = (bf16[256,1024]{0,1:T(8,128)(2,1)}, bf16[256,1024]{0,1:T(8,128)(2,1)}, u32[]{:S(2)}, u32[]{:S(2)}) collective-permute-start(bf16[256,1024]{0,1:T(8,128)(2,1)} %get-tuple-element.159), channel_id=1, source_target_pairs={{0,1},{1,2},{2,3},{3,0},{4,5},{5,6},{6,7},{7,4},{8,9},{9,10},{10,1... | collective-permute-start | bytes 1572872 | tf_op jit(solution)/shard_map/ppermute | solution.py:190
  175.6 28.1 %collective-permute-start.7 = (bf16[256,1024]{0,1:T(8,128)(2,1)}, bf16[256,1024]{0,1:T(8,128)(2,1)}, u32[]{:S(2)}, u32[]{:S(2)}) collective-permute-start(bf16[256,1024]{0,1:T(8,128)(2,1)} %get-tuple-element.159), channel_id=1, source_target_pairs={{0,2},{1,3},{2,0},{3,1},{4,6},{5,7},{6,4},{7,5},{8,10},{9,11},{10,... | collective-permute-start | bytes 1572872 | tf_op jit(solution)/shard_map/ppermute | solution.py:190
  180.1 32.1 %collective-permute-start.8 = (bf16[256,1024]{0,1:T(8,128)(2,1)}, bf16[256,1024]{0,1:T(8,128)(2,1)}, u32[]{:S(2)}, u32[]{:S(2)}) collective-permute-start(bf16[256,1024]{0,1:T(8,128)(2,1)} %get-tuple-element.159), channel_id=1, source_target_pairs={{0,3},{1,0},{2,1},{3,2},{4,7},{5,4},{6,5},{7,6},{8,11},{9,8},{10,9... | collective-permute-start | bytes 1572872 | tf_op jit(solution)/shard_map/ppermute | solution.py:190
  196.5 16.7 %copy-start.76 = (bf16[1024,704]{0,1:T(8,128)(2,1)S(1)}, bf16[1024,704]{0,1:T(8,128)(2,1)}, u32[]{:S(2)}) copy-start(bf16[1024,704]{0,1:T(8,128)(2,1)} %param.18) | copy-start | bytes 4325380
  224.3 10.6 %copy-start.36 = (bf16[1024,1024]{0,1:T(8,128)(2,1)}, bf16[1024,1024]{0,1:T(8,128)(2,1)S(1)}, u32[]{:S(2)}) copy-start(bf16[1024,1024]{0,1:T(8,128)(2,1)S(1)} %convolution_convert_fusion.1) | copy-start | bytes 6291460
  232.3 14.3 %collective-permute-start.15 = (bf16[256,1024]{0,1:T(8,128)(2,1)}, bf16[256,1024]{0,1:T(8,128)(2,1)}, u32[]{:S(2)}, u32[]{:S(2)}) collective-permute-start(bf16[256,1024]{0,1:T(8,128)(2,1)} %get-tuple-element.180), channel_id=1, source_target_pairs={{0,1},{1,2},{2,3},{3,0},{4,5},{5,6},{6,7},{7,4},{8,9},{9,10},{10,1... | collective-permute-start | bytes 1572872 | tf_op jit(solution)/shard_map/ppermute | solution.py:174
  233.2 14.0 %collective-permute-start.17 = (bf16[256,1024]{0,1:T(8,128)(2,1)}, bf16[256,1024]{0,1:T(8,128)(2,1)}, u32[]{:S(2)}, u32[]{:S(2)}) collective-permute-start(bf16[256,1024]{0,1:T(8,128)(2,1)} %get-tuple-element.181), channel_id=1, source_target_pairs={{0,3},{1,0},{2,1},{3,2},{4,7},{5,4},{6,5},{7,6},{8,11},{9,8},{10,9... | collective-permute-start | bytes 1572872 | tf_op jit(solution)/shard_map/ppermute | solution.py:174
  234.5 24.7 %collective-permute-start.16 = (bf16[256,1024]{0,1:T(8,128)(2,1)}, bf16[256,1024]{0,1:T(8,128)(2,1)}, u32[]{:S(2)}, u32[]{:S(2)}) collective-permute-start(bf16[256,1024]{0,1:T(8,128)(2,1)} %get-tuple-element.182), channel_id=1, source_target_pairs={{0,2},{1,3},{2,0},{3,1},{4,6},{5,7},{6,4},{7,5},{8,10},{9,11},{10,... | collective-permute-start | bytes 1572872 | tf_op jit(solution)/shard_map/ppermute | solution.py:174
  236.1 33.0 %collective-permute-start.9 = (bf16[256,1024]{0,1:T(8,128)(2,1)}, bf16[256,1024]{0,1:T(8,128)(2,1)}, u32[]{:S(2)}, u32[]{:S(2)}) collective-permute-start(bf16[256,1024]{0,1:T(8,128)(2,1)} %get-tuple-element.183), channel_id=1, source_target_pairs={{0,1},{1,2},{2,3},{3,0},{4,5},{5,6},{6,7},{7,4},{8,9},{9,10},{10,1... | collective-permute-start | bytes 1572872 | tf_op jit(solution)/shard_map/ppermute | solution.py:174
  236.3 33.3 %collective-permute-start.11 = (bf16[256,1024]{0,1:T(8,128)(2,1)}, bf16[256,1024]{0,1:T(8,128)(2,1)}, u32[]{:S(2)}, u32[]{:S(2)}) collective-permute-start(bf16[256,1024]{0,1:T(8,128)(2,1)} %get-tuple-element.184), channel_id=1, source_target_pairs={{0,3},{1,0},{2,1},{3,2},{4,7},{5,4},{6,5},{7,6},{8,11},{9,8},{10,9... | collective-permute-start | bytes 1572872 | tf_op jit(solution)/shard_map/ppermute | solution.py:174
  241.0 19.9 %copy-start.14 = (f32[256,1024]{0,1:T(8,128)S(1)}, f32[256,1024]{0,1:T(8,128)}, u32[]{:S(2)}) copy-start(f32[256,1024]{0,1:T(8,128)} %copy-done.13) | copy-start | bytes 3145732
  241.0 19.9 %copy-start.61 = (f32[1024]{0:T(1024)S(1)}, f32[1024]{0:T(1024)}, u32[]{:S(2)}) copy-start(f32[1024]{0:T(1024)} %param.17) | copy-start | bytes 12292
  241.0 20.0 %copy-start.69 = (f32[256]{0:T(256)S(1)}, f32[256]{0:T(256)}, u32[]{:S(2)}) copy-start(f32[256]{0:T(256)} %copy-done.68) | copy-start | bytes 3076
  246.6 34.3 %copy-start.22 = (bf16[256,1024]{0,1:T(8,128)(2,1)S(1)}, bf16[256,1024]{0,1:T(8,128)(2,1)}, u32[]{:S(2)}) copy-start(bf16[256,1024]{0,1:T(8,128)(2,1)} %copy.307) | copy-start | bytes 1572868
  246.6 34.3 %copy-start.75 = (f32[256]{0:T(256)S(1)}, f32[256]{0:T(256)}, u32[]{:S(2)}) copy-start(f32[256]{0:T(256)} %get-tuple-element.212) | copy-start | bytes 3076
  246.6 34.3 %collective-permute-start.10 = (bf16[256,1024]{0,1:T(8,128)(2,1)}, bf16[256,1024]{0,1:T(8,128)(2,1)S(1)}, u32[]{:S(2)}, u32[]{:S(2)}) collective-permute-start(bf16[256,1024]{0,1:T(8,128)(2,1)} %get-tuple-element.185), channel_id=1, source_target_pairs={{0,2},{1,3},{2,0},{3,1},{4,6},{5,7},{6,4},{7,5},{8,10},{9,11},{10,... | collective-permute-start | bytes 1572872 | tf_op jit(solution)/shard_map/ppermute | solution.py:174
  286.0 13.6 %collective-permute-start.18 = (bf16[256,1024]{0,1:T(8,128)(2,1)S(1)}, bf16[256,1024]{0,1:T(8,128)(2,1)S(1)}, u32[]{:S(2)}, u32[]{:S(2)}) collective-permute-start(bf16[256,1024]{0,1:T(8,128)(2,1)S(1)} %get-tuple-element.157), channel_id=1, source_target_pairs={{0,1},{1,2},{2,3},{3,0},{4,5},{5,6},{6,7},{7,4},{8,9},{9,10},{10,1... | collective-permute-start | bytes 1572872 | tf_op jit(solution)/shard_map/ppermute | solution.py:190
  286.0 14.9 %collective-permute-start.19 = (bf16[256,1024]{0,1:T(8,128)(2,1)S(1)}, bf16[256,1024]{0,1:T(8,128)(2,1)}, u32[]{:S(2)}, u32[]{:S(2)}) collective-permute-start(bf16[256,1024]{0,1:T(8,128)(2,1)S(1)} %get-tuple-element.157), channel_id=1, source_target_pairs={{0,2},{1,3},{2,0},{3,1},{4,6},{5,7},{6,4},{7,5},{8,10},{9,11},{10,... | collective-permute-start | bytes 1572872 | tf_op jit(solution)/shard_map/ppermute | solution.py:190
  286.3 23.0 %collective-permute-start.20 = (bf16[256,1024]{0,1:T(8,128)(2,1)S(1)}, bf16[256,1024]{0,1:T(8,128)(2,1)}, u32[]{:S(2)}, u32[]{:S(2)}) collective-permute-start(bf16[256,1024]{0,1:T(8,128)(2,1)S(1)} %get-tuple-element.157), channel_id=1, source_target_pairs={{0,3},{1,0},{2,1},{3,2},{4,7},{5,4},{6,5},{7,6},{8,11},{9,8},{10,9... | collective-permute-start | bytes 1572872 | tf_op jit(solution)/shard_map/ppermute | solution.py:190
  287.8 244.6 %all-reduce.8.cloned.1.call-start = ((), (), s32[]{:S(2)}) async-start(), calls=%async_computation.1 | async-start | bytes 1949696 | tf_op jit(solution)/shard_map/psum | solution.py:353
  287.9 23.3 %copy-start.55 = (bf16[256,1024]{1,0:T(8,128)(2,1)S(1)}, bf16[256,1024]{1,0:T(8,128)(2,1)}, u32[]{:S(2)}) copy-start(bf16[256,1024]{1,0:T(8,128)(2,1)} %param.16) | copy-start | bytes 1572868
  314.8 8.1 %copy-start.28 = (f32[1024,4,2]{1,2,0:T(2,128)S(1)}, f32[1024,4,2]{1,2,0:T(2,128)}, u32[]{:S(2)}) copy-start(f32[1024,4,2]{1,2,0:T(2,128)} %copy.350) | copy-start | bytes 98308
  322.9 11.7 %copy-start.5 = (f32[4,512,512]{1,2,0:T(8,128)S(1)}, f32[4,512,512]{1,2,0:T(8,128)}, u32[]{:S(2)}) copy-start(f32[4,512,512]{1,2,0:T(8,128)} %copy-done.3) | copy-start | bytes 12582916
  350.2 6.8 %copy-start.27 = (f32[1024,4,2]{1,2,0:T(2,128)S(1)}, f32[1024,4,2]{1,2,0:T(2,128)}, u32[]{:S(2)}) copy-start(f32[1024,4,2]{1,2,0:T(2,128)} %copy.354) | copy-start | bytes 98308
  350.2 6.8 %copy-start.51 = (bf16[1024,4,64]{2,1,0:T(4,128)(2,1)S(1)}, bf16[1024,4,64]{2,1,0:T(4,128)(2,1)}, u32[]{:S(2)}) copy-start(bf16[1024,4,64]{2,1,0:T(4,128)(2,1)} %copy.320) | copy-start | bytes 1572868
  357.0 7.9 %copy-start.52 = (bf16[512,4,64]{0,2,1:T(8,128)(2,1)S(1)}, bf16[512,4,64]{0,2,1:T(8,128)(2,1)}, u32[]{:S(2)}) copy-start(bf16[512,4,64]{0,2,1:T(8,128)(2,1)} %fusion.36) | copy-start | bytes 786436
  361.5 6.6 %copy-start.15 = (f32[1024,32]{1,0:T(8,128)S(1)}, f32[1024,32]{1,0:T(8,128)}, u32[]{:S(2)}) copy-start(f32[1024,32]{1,0:T(8,128)} %get-tuple-element.206) | copy-start | bytes 393220
  361.5 6.6 %copy-start.16 = (f32[1024,32]{1,0:T(8,128)S(1)}, f32[1024,32]{1,0:T(8,128)}, u32[]{:S(2)}) copy-start(f32[1024,32]{1,0:T(8,128)} %get-tuple-element.207) | copy-start | bytes 393220
  402.9 6.8 %copy-start.40 = (bf16[1024,1024]{0,1:T(8,128)(2,1)S(1)}, bf16[1024,1024]{0,1:T(8,128)(2,1)}, u32[]{:S(2)}) copy-start(bf16[1024,1024]{0,1:T(8,128)(2,1)} %constant_dynamic-update-slice_fusion) | copy-start | bytes 6291460
  402.9 6.8 %copy-start.47 = (bf16[1024,4,64]{0,2,1:T(8,128)(2,1)S(1)}, bf16[1024,4,64]{0,2,1:T(8,128)(2,1)}, u32[]{:S(2)}) copy-start(bf16[1024,4,64]{0,2,1:T(8,128)(2,1)} %copy-done.46) | copy-start | bytes 1572868
  404.3 7.0 %copy-start.58 = (bf16[1024,40]{0,1:T(8,128)(2,1)S(1)}, bf16[1024,40]{0,1:T(8,128)(2,1)}, u32[]{:S(2)}) copy-start(bf16[1024,40]{0,1:T(8,128)(2,1)} %param.14) | copy-start | bytes 245764
  404.3 9.9 %collective-permute-start.21 = (bf16[1024,160]{0,1:T(8,128)(2,1)S(1)}, bf16[1024,160]{0,1:T(8,128)(2,1)S(1)}, u32[]{:S(2)}, u32[]{:S(2)}) collective-permute-start(bf16[1024,160]{0,1:T(8,128)(2,1)S(1)} %get-tuple-element.191), channel_id=1, source_target_pairs={{0,1},{1,2},{2,3},{3,0},{4,5},{5,6},{6,7},{7,4},{8,9},{9,10},{10,1... | collective-permute-start | bytes 983048 | tf_op jit(solution)/shard_map/ppermute | solution.py:174
  407.8 8.6 %collective-permute-start.23 = (bf16[1024,160]{0,1:T(8,128)(2,1)S(1)}, bf16[1024,160]{0,1:T(8,128)(2,1)S(1)}, u32[]{:S(2)}, u32[]{:S(2)}) collective-permute-start(bf16[1024,160]{0,1:T(8,128)(2,1)S(1)} %get-tuple-element.192), channel_id=1, source_target_pairs={{0,3},{1,0},{2,1},{3,2},{4,7},{5,4},{6,5},{7,6},{8,11},{9,8},{10,9... | collective-permute-start | bytes 983048 | tf_op jit(solution)/shard_map/ppermute | solution.py:174
  408.3 15.0 %collective-permute-start.22 = (bf16[1024,160]{0,1:T(8,128)(2,1)S(1)}, bf16[1024,160]{0,1:T(8,128)(2,1)S(1)}, u32[]{:S(2)}, u32[]{:S(2)}) collective-permute-start(bf16[1024,160]{0,1:T(8,128)(2,1)S(1)} %get-tuple-element.193), channel_id=1, source_target_pairs={{0,2},{1,3},{2,0},{3,1},{4,6},{5,7},{6,4},{7,5},{8,10},{9,11},{10,... | collective-permute-start | bytes 983048 | tf_op jit(solution)/shard_map/ppermute | solution.py:174
  425.6 12.6 %collective-permute-start.24 = (bf16[256,1024]{0,1:T(8,128)(2,1)S(1)}, bf16[256,1024]{0,1:T(8,128)(2,1)S(1)}, u32[]{:S(2)}, u32[]{:S(2)}) collective-permute-start(bf16[256,1024]{0,1:T(8,128)(2,1)S(1)} %get-tuple-element.175), channel_id=1, source_target_pairs={{0,1},{1,2},{2,3},{3,0},{4,5},{5,6},{6,7},{7,4},{8,9},{9,10},{10,1... | collective-permute-start | bytes 1572872 | tf_op jit(solution)/shard_map/ppermute | solution.py:174
  425.7 14.0 %collective-permute-start.26 = (bf16[256,1024]{0,1:T(8,128)(2,1)S(1)}, bf16[256,1024]{0,1:T(8,128)(2,1)S(1)}, u32[]{:S(2)}, u32[]{:S(2)}) collective-permute-start(bf16[256,1024]{0,1:T(8,128)(2,1)S(1)} %get-tuple-element.176), channel_id=1, source_target_pairs={{0,3},{1,0},{2,1},{3,2},{4,7},{5,4},{6,5},{7,6},{8,11},{9,8},{10,9... | collective-permute-start | bytes 1572872 | tf_op jit(solution)/shard_map/ppermute | solution.py:174
  427.4 23.7 %copy-start.12 = (bf16[256,1024]{0,1:T(8,128)(2,1)S(1)}, bf16[256,1024]{0,1:T(8,128)(2,1)}, u32[]{:S(2)}) copy-start(bf16[256,1024]{0,1:T(8,128)(2,1)} %copy-done.9) | copy-start | bytes 1572868
  427.4 23.7 %copy-start.63 = (f32[1024]{0:T(1024)S(1)}, f32[1024]{0:T(1024)}, u32[]{:S(2)}) copy-start(f32[1024]{0:T(1024)} %param.13) | copy-start | bytes 12292
  427.4 23.7 %copy-start.72 = (f32[256]{0:T(256)S(1)}, f32[256]{0:T(256)}, u32[]{:S(2)}) copy-start(f32[256]{0:T(256)} %copy-done.71) | copy-start | bytes 3076
  427.4 23.7 %collective-permute-start.25 = (bf16[256,1024]{0,1:T(8,128)(2,1)S(1)}, bf16[256,1024]{0,1:T(8,128)(2,1)S(1)}, u32[]{:S(2)}, u32[]{:S(2)}) collective-permute-start(bf16[256,1024]{0,1:T(8,128)(2,1)S(1)} %get-tuple-element.177), channel_id=1, source_target_pairs={{0,2},{1,3},{2,0},{3,1},{4,6},{5,7},{6,4},{7,5},{8,10},{9,11},{10,... | collective-permute-start | bytes 1572872 | tf_op jit(solution)/shard_map/ppermute | solution.py:174
  431.8 20.9 %copy-start.73 = (bf16[1024]{0:T(1024)(128)(2,1)S(1)}, bf16[1024]{0:T(1024)(128)(2,1)}, u32[]{:S(2)}) copy-start(bf16[1024]{0:T(1024)(128)(2,1)} %get-tuple-element.145) | copy-start | bytes 6148
  431.8 21.1 %copy-start.56 = (bf16[1024,160]{0,1:T(8,128)(2,1)S(1)}, bf16[1024,160]{0,1:T(8,128)(2,1)}, u32[]{:S(2)}) copy-start(bf16[1024,160]{0,1:T(8,128)(2,1)} %convolution_convert_fusion.7) | copy-start | bytes 983044
  431.8 100.6 %copy-start.37 = (bf16[256,1024]{0,1:T(8,128)(2,1)S(1)}, bf16[256,1024]{0,1:T(8,128)(2,1)}, u32[]{:S(2)}) copy-start(bf16[256,1024]{0,1:T(8,128)(2,1)} %get-tuple-element.135) | copy-start | bytes 1572868
  452.7 80.7 %copy-start.18 = (f32[256,1024]{0,1:T(8,128)S(1)}, f32[256,1024]{0,1:T(8,128)}, u32[]{:S(2)}) copy-start(f32[256,1024]{0,1:T(8,128)} %copy-done.17) | copy-start | bytes 3145732
  452.7 80.7 %copy-start.74 = (f32[256]{0:T(256)S(1)}, f32[256]{0:T(256)}, u32[]{:S(2)}) copy-start(f32[256]{0:T(256)} %get-tuple-element.210) | copy-start | bytes 3076
  453.7 98.8 %all-gather.2.cloned.1.call-start = ((), (), s32[]{:S(2)}) async-start(), calls=%async_computation | async-start | bytes 1843200 | tf_op jit(solution)/shard_map/all_gather | solution.py:361
  (46 other events, 112.9 us)
Sparse Core Ops, SparseCore 0:
  287.9 160.9 all-reduce.9
  453.9 78.4 all-reduce.7
  533.9 18.5 all-gather.1

commit v7 on v6

--- a/solution.py
+++ b/solution.py
@@ -194,6 +194,32 @@
             gathered, arrived, ((own - shift) % count) * width, axis=axis
         )
     return gathered
+
+
+def dp_all_reduce(flat):
+    count = lax.axis_size("dp")
+    own = lax.axis_index("dp")
+    steps = count.bit_length() - 1
+    assert count == 1 << steps
+    width = -(-flat.shape[0] // (count * 128)) * 128
+    blocks = jnp.pad(flat, (0, count * width - flat.shape[0])).reshape((2,) * steps + (width,))
+    kept = blocks.astype(jnp.float32)
+    for step in range(steps):
+        axis = steps - 1 - step
+        bit = (own >> step) & 1
+        sent = lax.dynamic_index_in_dim(kept, 1 - bit, axis, keepdims=False)
+        kept = lax.dynamic_index_in_dim(kept, bit, axis, keepdims=False)
+        pairs = [(device, device ^ (1 << step)) for device in range(count)]
+        kept = kept + lax.ppermute(sent.astype(jnp.bfloat16), "dp", pairs).astype(jnp.float32)
+    whole = kept.astype(jnp.bfloat16)[None]
+    for step in reversed(range(steps)):
+        bit = (own >> step) & 1
+        pairs = [(device, device ^ (1 << step)) for device in range(count)]
+        arrived = lax.ppermute(whole, "dp", pairs)
+        low_half = jnp.where(bit == 0, whole, arrived)
+        high_half = jnp.where(bit == 0, arrived, whole)
+        whole = jnp.stack([low_half, high_half], axis=1).reshape((-1,) + whole.shape[1:])
+    return whole.reshape(-1)[: flat.shape[0]]
 
 
 def local(
@@ -350,7 +376,12 @@
     tail, (grad_gate, grad_up, grad_down) = lax.optimization_barrier(
         (tail, (grad_gate, grad_up, grad_down))
     )
-    grad_a, grad_out, packed = lax.psum(tail, "dp")
+    sizes = [part.size for part in tail]
+    summed = dp_all_reduce(jnp.concatenate([part.reshape(-1) for part in tail]))
+    grad_a, grad_out, packed = (
+        summed[sum(sizes[:index]) : sum(sizes[: index + 1])].reshape(part.shape)
+        for index, part in enumerate(tail)
+    )
     grad_out, grad_gate, grad_up, grad_down = (
         grad_out.astype(jnp.float32),
         grad_gate.astype(jnp.float32),
@@ -358,7 +389,7 @@
         grad_down.astype(jnp.float32),
     )
     grad_a = grad_a.astype(jnp.float32)
-    packed = lax.all_gather(packed, "head", axis=1, tiled=True).astype(jnp.float32)
+    packed = head_all_gather(packed, 1).astype(jnp.float32)
     grad_b = packed[: grad_b_cols.shape[0]]
     gains = jnp.sum(
         packed[grad_b_cols.shape[0] :].reshape(gain_rows, head_count, basis_cols), axis=1

time: 578 us -> 587 us (1.016)
  waiting for transfers between devices: 227 us -> 169 us
  local copies, waits for them, and re-layouts: 116 us -> 159 us
  starting transfers between devices: 29.7 us -> 49.1 us
    psum x1 -> x0, waiting for transfers between devices: 78.6 us -> none  [local(): grad_a, grad_out, packed = lax.psum(tail, 'dp')]
    ppermute x0 -> x6, waiting for transfers between devices: none -> 22.6 us  [the longest x3 14.5 us: dp_all_reduce(): lax.ppermute(sent.astype(jnp.bfloat16), 'dp', pairs).astype(jnp.float32)]
    dynamic_update_slice x12 -> x15, local copies, waits for them, and re-layouts: 17 us -> 38.2 us  [head_all_gather(): lax.dynamic_update_slice_in_dim(gathered, arrived, (own - shift) % count...]
    ppermute x0 -> x6, starting transfers between devices: none -> 16.7 us  [the longest x3 9.96 us: dp_all_reduce(): arrived = lax.ppermute(whole, 'dp', pairs)]
    all_gather x1 -> x0, waiting for transfers between devices: 8.49 us -> none  [local(): lax.all_gather(packed, 'head', axis=1, tiled=True).astype(jnp.float32)]
    dynamic_update_slice x1 -> x2, local copies, waits for them, and re-layouts: 0.06 us -> 6.61 us  [head_all_gather(): lax.dynamic_update_slice_in_dim(jnp.zeros(shape, values.dtype), values, o...]
    ppermute x12 -> x15, waiting for transfers between devices: 52.1 us -> 58.5 us  [head_all_gather(): lax.ppermute(values, 'head', [(device, (device + shift) % count) for devi...]
    convert_element_type x0 -> x5, local copies, waits for them, and re-layouts: none -> 6.39 us  [the longest x3 3.61 us: dp_all_reduce(): sent.astype(jnp.bfloat16)]
  transfers between devices with their start and end apart: 30 -> 37, of which waited for: 24 -> 28; matrix products, arithmetic and copies ran while one was open for 27% -> 31% of each run, Pallas kernels for 0% -> 0%
where the time goes in v7:
time: 587 us; the launch traced here: 577 us
  waiting for transfers between devices  169 us (29%)
  local copies, waits for them, and re-layouts  159 us (27%)
  matrix products  125 us (21%)
  other arithmetic  59.2 us (10%)
  starting transfers between devices  49.1 us (8%)
  between operations  15.9 us (3%)
    ppermute x15, waiting for transfers between devices, head_reduce_scatter(): lax.ppermute(sent, 'head', [(device, (device + shift) % count) for device...  87.4 us
    ppermute x15, waiting for transfers between devices, head_all_gather(): lax.ppermute(values, 'head', [(device, (device + shift) % count) for devi...  58.5 us
    dynamic_update_slice x15, local copies, waits for them, and re-layouts, head_all_gather(): lax.dynamic_update_slice_in_dim(gathered, arrived, (own - shift) % count...  38.2 us
    unnamed x179, local copies, waits for them, and re-layouts  37.1 us
    ppermute x15, starting transfers between devices, head_reduce_scatter(): lax.ppermute(sent, 'head', [(device, (device + shift) % count) for device...  16.7 us
    ppermute x15, starting transfers between devices, head_all_gather(): lax.ppermute(values, 'head', [(device, (device + shift) % count) for devi...  15.8 us
    ppermute x3, waiting for transfers between devices, dp_all_reduce(): lax.ppermute(sent.astype(jnp.bfloat16), 'dp', pairs).astype(jnp.float32)  14.5 us
    dot_general x6, matrix products, dot_first(): lax.dot_general(left, right, (((0,), (0,)), ((), ())), preferred_element_...  13 us
  transfers between devices with their start and end apart: 37, of which 28 were waited for; matrix products, arithmetic and copies ran while one was open for 31% of the time, Pallas kernels for 0%

profile of v7, /device:TPU:0, one launch (start us, length us, event | category | flops | bytes accessed | tf_op | source)
XLA Modules:
  0.0 577.0 jit_solution(14984810735262856616)
XLA Ops:
  11.4 3.0 collective-permute-start.1
  18.6 3.1 multiply_cosine_fusion
  21.7 15.3 %collective-permute-done = bf16[256,1024]{0,1:T(8,128)(2,1)} collective-permute-done((bf16[256,1024]{0,1:T(8,128)(2,1)}, bf16[256,1024]{0,1:T(8,128)(2,1)}, u32[]{:S(2)}, u32[]{:S(2)}) %collective-permute-start) | collective-permute-done | bytes 524320 | tf_op jit(solution)/shard_map/ppermute | solution.py:190
  46.4 2.9 fusion.88
  55.5 2.6 copy.389
  60.0 2.7 fusion.78
  69.0 2.6 multiply_subtract_fusion.1
  73.0 10.4 %fusion.75 = f32[1024,4,64]{2,1,0:T(4,128)} fusion(f32[1024,4,2]{1,2,0:T(2,128)S(1)} %copy-done.27, f32[1024,2,32]{2,1,0:T(2,128)S(1)} %get-tuple-element.169, f32[1024,2,32]{2,1,0:T(2,128)S(1)} %get-tuple-element.168), kind=kOutput, calls=%fused_computation.207 | convolution fusion | flops 6422528 | bytes 1605632 | tf_op jit(solution)/shard_map/thr,trd->thd/dot_general | solution.py:266
  83.4 2.7 copy.324
  88.1 10.9 %fusion.89 = f32[1024,4,64]{2,1,0:T(4,128)} fusion(f32[1024,4,2]{1,2,0:T(2,128)} %copy.392, f32[1024,2,64]{2,1,0:T(2,128)} %copy.316), kind=kOutput, calls=%fused_computation.220 | convolution fusion | flops 6291456 | bytes 1605632 | tf_op jit(solution)/shard_map/thr,trd->thd/dot_general | solution.py:270
  99.0 2.7 copy.317
  103.8 3.7 copy.391
  107.5 3.6 copy.390
  111.1 4.3 multiply_subtract_fusion
  115.4 8.3 %multiply_convert_fusion.5 = bf16[1024,4,64]{2,1,0:T(4,128)(2,1)S(1)} fusion(f32[1024,4,6]{2,1,0:T(4,128)S(1)} %copy-done.8, f32[1024,6,32]{2,1,0:T(8,128)S(1)} %get-tuple-element.162, f32[1024,6,32]{2,1,0:T(8,128)S(1)} %get-tuple-element.161), kind=kOutput, calls=%fused_computation.41 | convolution fusion | flops 19791872 | bytes 2195456 | tf_op jit(solution)/shard_map/thr,trd->thd/dot_general | solution.py:263
  147.6 7.5 %collective-permute-done.3 = bf16[256,1024]{0,1:T(8,128)(2,1)S(1)} collective-permute-done((bf16[256,1024]{0,1:T(8,128)(2,1)S(1)}, bf16[256,1024]{0,1:T(8,128)(2,1)S(1)}, u32[]{:S(2)}, u32[]{:S(2)}) %collective-permute-start.3) | collective-permute-done | bytes 524320 | tf_op jit(solution)/shard_map/ppermute | solution.py:174
  155.1 2.4 collective-permute-start.13
  157.5 12.4 %collective-permute-done.4 = bf16[256,1024]{0,1:T(8,128)(2,1)S(1)} collective-permute-done((bf16[256,1024]{0,1:T(8,128)(2,1)S(1)}, bf16[256,1024]{0,1:T(8,128)(2,1)S(1)}, u32[]{:S(2)}, u32[]{:S(2)}) %collective-permute-start.4) | collective-permute-done | bytes 524320 | tf_op jit(solution)/shard_map/ppermute | solution.py:174
  185.7 6.7 %collective-permute-done.13 = bf16[256,1024]{1,0:T(8,128)(2,1)} collective-permute-done((bf16[256,1024]{1,0:T(8,128)(2,1)}, bf16[256,1024]{1,0:T(8,128)(2,1)}, u32[]{:S(2)}, u32[]{:S(2)}) %collective-permute-start.13) | collective-permute-done | bytes 524320 | tf_op jit(solution)/shard_map/ppermute | solution.py:190
  201.3 2.4 collective-permute-done.7
  204.8 7.4 %collective-permute-done.8 = bf16[256,1024]{0,1:T(8,128)(2,1)} collective-permute-done((bf16[256,1024]{0,1:T(8,128)(2,1)}, bf16[256,1024]{0,1:T(8,128)(2,1)}, u32[]{:S(2)}, u32[]{:S(2)}) %collective-permute-start.8) | collective-permute-done | bytes 524320 | tf_op jit(solution)/shard_map/ppermute | solution.py:190
  216.6 3.0 multiply_convert_fusion.2
  219.7 2.8 convolution_convert_fusion.2
  224.3 2.9 convolution_convert_fusion.3
  238.2 2.8 convolution_convert_fusion.4
  241.0 5.6 collective-permute-done.15
  247.1 12.1 %collective-permute-done.16 = bf16[256,1024]{0,1:T(8,128)(2,1)} collective-permute-done((bf16[256,1024]{0,1:T(8,128)(2,1)}, bf16[256,1024]{0,1:T(8,128)(2,1)}, u32[]{:S(2)}, u32[]{:S(2)}) %collective-permute-start.16) | collective-permute-done | bytes 524320 | tf_op jit(solution)/shard_map/ppermute | solution.py:174
  262.1 7.0 %collective-permute-done.9 = bf16[256,1024]{0,1:T(8,128)(2,1)} collective-permute-done((bf16[256,1024]{0,1:T(8,128)(2,1)}, bf16[256,1024]{0,1:T(8,128)(2,1)}, u32[]{:S(2)}, u32[]{:S(2)}) %collective-permute-start.9) | collective-permute-done | bytes 524320 | tf_op jit(solution)/shard_map/ppermute | solution.py:174
  269.6 11.3 %collective-permute-done.10 = bf16[256,1024]{0,1:T(8,128)(2,1)S(1)} collective-permute-done((bf16[256,1024]{0,1:T(8,128)(2,1)}, bf16[256,1024]{0,1:T(8,128)(2,1)S(1)}, u32[]{:S(2)}, u32[]{:S(2)}) %collective-permute-start.10) | collective-permute-done | bytes 524320 | tf_op jit(solution)/shard_map/ppermute | solution.py:174
  280.9 2.8 subtract_add_fusion
  287.8 11.8 %collective-permute-done.18 = bf16[256,1024]{0,1:T(8,128)(2,1)S(1)} collective-permute-done((bf16[256,1024]{0,1:T(8,128)(2,1)S(1)}, bf16[256,1024]{0,1:T(8,128)(2,1)S(1)}, u32[]{:S(2)}, u32[]{:S(2)}) %collective-permute-start.18) | collective-permute-done | bytes 524320 | tf_op jit(solution)/shard_map/ppermute | solution.py:190
  302.8 6.5 %collective-permute-done.20 = bf16[256,1024]{0,1:T(8,128)(2,1)} collective-permute-done((bf16[256,1024]{0,1:T(8,128)(2,1)S(1)}, bf16[256,1024]{0,1:T(8,128)(2,1)}, u32[]{:S(2)}, u32[]{:S(2)}) %collective-permute-start.20) | collective-permute-done | bytes 524320 | tf_op jit(solution)/shard_map/ppermute | solution.py:190
  311.1 2.5 convolution_convert_fusion.5
  314.8 5.8 %fusion.25 = bf16[1024,4,64]{0,2,1:T(8,128)(2,1)} fusion(bf16[512,4,64]{0,2,1:T(8,128)(2,1)S(1)} %bitcast.138, f32[4,512,1024]{2,1,0:T(8,128)} %copy-done.2, f32[4,512]{1,0:T(4,128)S(1)} %log_add_fusion, f32[512,4,64]{0,2,1:T(8,128)S(1)} %fusion.30), kind=kOutput, calls=%fused_computation.64 | convolution fusion | flops 273154048 | bytes 9707520 | tf_op jit(solution)/shard_map/while/body/eval_jaxpr/hqk,qhd->khd/dot_general | solution.py:152
  322.9 5.7 fusion.29
  328.6 6.0 %convolution_multiply_fusion.4 = bf16[1024,4,2]{1,2,0:T(2,128)(2,1)} fusion(bf16[1024,4,64]{2,1,0:T(4,128)(2,1)} %copy.345, f32[1024,2,64]{2,1,0:T(2,128)} %copy.316), kind=kOutput, calls=%fused_computation.57 | convolution fusion | flops 6307840 | bytes 1064960 | tf_op jit(solution)/shard_map/thd,trd->thr/dot_general | solution.py:329
  339.6 2.6 multiply_reduce_fusion
  350.2 6.8 %convolution_multiply_fusion.5 = bf16[1024,4,2]{1,2,0:T(2,128)(2,1)} fusion(bf16[1024,4,64]{2,1,0:T(4,128)(2,1)} %copy.342, f32[1024,2,32]{2,1,0:T(2,128)} %copy-done.26, f32[1024,2,32]{2,1,0:T(2,128)S(1)} %copy-done.25), kind=kOutput, calls=%fused_computation.58 | convolution fusion | flops 6438912 | bytes 1064960 | tf_op jit(solution)/shard_map/thd,trd->thr/dot_general | solution.py:328
  357.0 4.5 convolution_multiply_fusion.3
  368.1 3.1 add_convert_fusion.3
  375.3 2.7 copy.337
  378.0 9.1 %convolution_multiply_fusion.1 = bf16[1024,4,6]{2,1,0:T(4,128)(2,1)} fusion(bf16[1024,4,64]{2,1,0:T(4,128)(2,1)} %copy.337, f32[1024,6,32]{2,1,0:T(8,128)} %copy-done.7, f32[1024,6,32]{2,1,0:T(8,128)} %copy-done.6), kind=kOutput, calls=%fused_computation.53 | convolution fusion | flops 19316736 | bytes 2146304 | tf_op jit(solution)/shard_map/thd,trd->thr/dot_general | solution.py:327
  389.0 6.1 %convolution_multiply_fusion = f32[1024,6,64]{2,1,0:T(8,128)S(1)} fusion(f32[1024,4,6]{2,1,0:T(4,128)} %copy.389, bf16[1024,4,64]{2,1,0:T(4,128)(2,1)} %copy.337), kind=kOutput, calls=%fused_computation.37 | convolution fusion | flops 19267584 | bytes 2195456 | tf_op jit(solution)/shard_map/thr,thd->trd/dot_general | solution.py:331
  395.2 3.1 add_convert_fusion.1
  398.2 2.4 copy.350
  404.4 3.6 collective-permute-start.21
  412.0 2.6 collective-permute-done.21
  416.3 7.1 %collective-permute-done.22 = bf16[1024,160]{0,1:T(8,128)(2,1)S(1)} collective-permute-done((bf16[1024,160]{0,1:T(8,128)(2,1)S(1)}, bf16[1024,160]{0,1:T(8,128)(2,1)S(1)}, u32[]{:S(2)}, u32[]{:S(2)}) %collective-permute-start.22) | collective-permute-done | bytes 327712 | tf_op jit(solution)/shard_map/ppermute | solution.py:174
  432.2 5.9 %collective-permute-done.24 = bf16[256,1024]{0,1:T(8,128)(2,1)S(1)} collective-permute-done((bf16[256,1024]{0,1:T(8,128)(2,1)S(1)}, bf16[256,1024]{0,1:T(8,128)(2,1)S(1)}, u32[]{:S(2)}, u32[]{:S(2)}) %collective-permute-start.24) | collective-permute-done | bytes 524320 | tf_op jit(solution)/shard_map/ppermute | solution.py:174
  440.1 11.2 %collective-permute-done.25 = bf16[256,1024]{0,1:T(8,128)(2,1)S(1)} collective-permute-done((bf16[256,1024]{0,1:T(8,128)(2,1)S(1)}, bf16[256,1024]{0,1:T(8,128)(2,1)S(1)}, u32[]{:S(2)}, u32[]{:S(2)}) %collective-permute-start.25) | collective-permute-done | bytes 524320 | tf_op jit(solution)/shard_map/ppermute | solution.py:174
  455.1 2.4 reshape.341
  457.5 2.5 dynamic-slice_convert_fusion
  462.8 8.6 %collective-permute-done.27 = bf16[2,2,58752]{2,1,0:T(2,128)(2,1)S(1)} collective-permute-done((bf16[2,2,58752]{2,1,0:T(2,128)(2,1)S(1)}, bf16[2,2,58752]{2,1,0:T(2,128)(2,1)S(1)}, u32[]{:S(2)}, u32[]{:S(2)}) %collective-permute-start.27) | collective-permute-done | bytes 470048 | tf_op jit(solution)/shard_map/ppermute | solution.py:213
  475.2 3.7 collective-permute-done.28
  479.9 3.1 collective-permute-start.29
  486.1 3.5 collective-permute-start.30
  489.6 5.1 collective-permute-done.30
  495.8 4.9 collective-permute-start.31
  501.7 3.1 collective-permute-done.31
  527.1 6.6 %dynamic_update_slice.89 = bf16[1037,640]{1,0:T(8,128)(2,1)S(1)} dynamic-update-slice(bf16[1037,640]{1,0:T(8,128)(2,1)S(1)} %broadcast_in_dim.145, bf16[1037,160]{1,0:T(8,128)(2,1)S(1)} %reshape.338, s32[]{:T(128)} %constant.214.clone.1, s32[]{:T(128)S(6)} %select_n.271) | dynamic-update-slice | bytes 663684 | tf_op jit(solution)/shard_map/dynamic_update_slice | solution.py:186
  536.0 6.3 %collective-permute-done.33 = bf16[1037,160]{0,1:T(8,128)(2,1)} collective-permute-done((bf16[1037,160]{0,1:T(8,128)(2,1)}, bf16[1037,160]{0,1:T(8,128)(2,1)}, u32[]{:S(2)}, u32[]{:S(2)}) %collective-permute-start.33) | collective-permute-done | bytes 331872 | tf_op jit(solution)/shard_map/ppermute | solution.py:190
  543.5 6.3 %dynamic_update_slice.90 = bf16[1037,640]{1,0:T(8,128)(2,1)S(1)} dynamic-update-slice(bf16[1037,640]{1,0:T(8,128)(2,1)S(1)} %dynamic_update_slice.89, bf16[1037,160]{1,0:T(8,128)(2,1)S(1)} %copy.364, s32[]{:T(128)} %constant.214.clone.1, s32[]{:T(128)S(6)} %select_n.290) | dynamic-update-slice | bytes 663684 | tf_op jit(solution)/shard_map/dynamic_update_slice | solution.py:193
  551.0 6.6 %dynamic_update_slice.91 = bf16[1037,640]{1,0:T(8,128)(2,1)S(1)} dynamic-update-slice(bf16[1037,640]{1,0:T(8,128)(2,1)S(1)} %dynamic_update_slice.90, bf16[1037,160]{1,0:T(8,128)(2,1)S(1)} %copy.366, s32[]{:T(128)} %constant.214.clone.1, s32[]{:T(128)S(6)} %select_n.291) | dynamic-update-slice | bytes 663684 | tf_op jit(solution)/shard_map/dynamic_update_slice | solution.py:193
  558.9 8.3 %dynamic_update_slice.92 = bf16[1037,640]{1,0:T(8,128)(2,1)S(1)} dynamic-update-slice(bf16[1037,640]{1,0:T(8,128)(2,1)S(1)} %dynamic_update_slice.91, bf16[1037,160]{1,0:T(8,128)(2,1)S(1)} %copy.368, s32[]{:T(128)} %constant.214.clone.1, s32[]{:T(128)S(6)} %select_n.292) | dynamic-update-slice | bytes 663684 | tf_op jit(solution)/shard_map/dynamic_update_slice | solution.py:193
  (376 shorter events, 213.8 us)
Async XLA Ops:
  7.2 209.4 %copy-start = (bf16[704,1024]{1,0:T(8,128)(2,1)S(1)}, bf16[704,1024]{1,0:T(8,128)(2,1)}, u32[]{:S(2)}) copy-start(bf16[704,1024]{1,0:T(8,128)(2,1)} %param.20) | copy-start | bytes 4325380
  7.2 445.9 %all-reduce.7.cloned.1.call-start = ((), (), s32[]{:S(2)}) async-start(), calls=%async_computation | async-start | bytes 8650752 | tf_op jit(solution)/shard_map/psum | solution.py:312
  9.4 8.2 %copy-start.73 = (f32[256]{0:T(256)}, f32[256]{0:T(256)S(1)}, u32[]{:S(2)}) copy-start(f32[256]{0:T(256)S(1)} %get-tuple-element.214) | copy-start | bytes 3076
  11.4 26.7 %collective-permute-start.1 = (bf16[256,1024]{0,1:T(8,128)(2,1)}, bf16[256,1024]{0,1:T(8,128)(2,1)}, u32[]{:S(2)}, u32[]{:S(2)}) collective-permute-start(bf16[256,1024]{0,1:T(8,128)(2,1)} %get-tuple-element.160), channel_id=1, source_target_pairs={{0,2},{1,3},{2,0},{3,1},{4,6},{5,7},{6,4},{7,5},{8,10},{9,11},{10,... | collective-permute-start | bytes 1572872 | tf_op jit(solution)/shard_map/ppermute | solution.py:190
  14.4 22.6 %collective-permute-start = (bf16[256,1024]{0,1:T(8,128)(2,1)}, bf16[256,1024]{0,1:T(8,128)(2,1)}, u32[]{:S(2)}, u32[]{:S(2)}) collective-permute-start(bf16[256,1024]{0,1:T(8,128)(2,1)} %get-tuple-element.160), channel_id=1, source_target_pairs={{0,1},{1,2},{2,3},{3,0},{4,5},{5,6},{6,7},{7,4},{8,9},{9,10},{10,1... | collective-permute-start | bytes 1572872 | tf_op jit(solution)/shard_map/ppermute | solution.py:190
  14.4 24.8 %collective-permute-start.2 = (bf16[256,1024]{0,1:T(8,128)(2,1)}, bf16[256,1024]{0,1:T(8,128)(2,1)}, u32[]{:S(2)}, u32[]{:S(2)}) collective-permute-start(bf16[256,1024]{0,1:T(8,128)(2,1)} %get-tuple-element.160), channel_id=1, source_target_pairs={{0,3},{1,0},{2,1},{3,2},{4,7},{5,4},{6,5},{7,6},{8,11},{9,8},{10,9... | collective-permute-start | bytes 1572872 | tf_op jit(solution)/shard_map/ppermute | solution.py:190
  18.6 21.8 %copy-start.60 = (bf16[1024,40]{0,1:T(8,128)(2,1)S(1)}, bf16[1024,40]{0,1:T(8,128)(2,1)}, u32[]{:S(2)}) copy-start(bf16[1024,40]{0,1:T(8,128)(2,1)} %param.14) | copy-start | bytes 245764
  115.3 8.3 %copy-start.6 = (f32[1024,6,32]{2,1,0:T(8,128)}, f32[1024,6,32]{2,1,0:T(8,128)S(1)}, u32[]{:S(2)}) copy-start(f32[1024,6,32]{2,1,0:T(8,128)S(1)} %get-tuple-element.161) | copy-start | bytes 2359300
  115.4 8.3 %copy-start.7 = (f32[1024,6,32]{2,1,0:T(8,128)}, f32[1024,6,32]{2,1,0:T(8,128)S(1)}, u32[]{:S(2)}) copy-start(f32[1024,6,32]{2,1,0:T(8,128)S(1)} %get-tuple-element.162) | copy-start | bytes 2359300
  142.3 27.5 %copy-start.11 = (bf16[256,1024]{0,1:T(8,128)(2,1)S(1)}, bf16[256,1024]{0,1:T(8,128)(2,1)}, u32[]{:S(2)}) copy-start(bf16[256,1024]{0,1:T(8,128)(2,1)} %copy-done.9) | copy-start | bytes 1572868
  142.6 12.5 %collective-permute-start.3 = (bf16[256,1024]{0,1:T(8,128)(2,1)S(1)}, bf16[256,1024]{0,1:T(8,128)(2,1)S(1)}, u32[]{:S(2)}, u32[]{:S(2)}) collective-permute-start(bf16[256,1024]{0,1:T(8,128)(2,1)S(1)} %get-tuple-element.183), channel_id=1, source_target_pairs={{0,1},{1,2},{2,3},{3,0},{4,5},{5,6},{6,7},{7,4},{8,9},{9,10},{10,1... | collective-permute-start | bytes 1572872 | tf_op jit(solution)/shard_map/ppermute | solution.py:174
  142.7 14.8 %collective-permute-start.5 = (bf16[256,1024]{0,1:T(8,128)(2,1)S(1)}, bf16[256,1024]{0,1:T(8,128)(2,1)S(1)}, u32[]{:S(2)}, u32[]{:S(2)}) collective-permute-start(bf16[256,1024]{0,1:T(8,128)(2,1)S(1)} %get-tuple-element.184), channel_id=1, source_target_pairs={{0,3},{1,0},{2,1},{3,2},{4,7},{5,4},{6,5},{7,6},{8,11},{9,8},{10,9... | collective-permute-start | bytes 1572872 | tf_op jit(solution)/shard_map/ppermute | solution.py:174
  144.4 26.8 %copy-start.62 = (f32[1024]{0:T(1024)S(1)}, f32[1024]{0:T(1024)}, u32[]{:S(2)}) copy-start(f32[1024]{0:T(1024)} %param.17) | copy-start | bytes 12292
  144.4 25.5 %collective-permute-start.4 = (bf16[256,1024]{0,1:T(8,128)(2,1)S(1)}, bf16[256,1024]{0,1:T(8,128)(2,1)S(1)}, u32[]{:S(2)}, u32[]{:S(2)}) collective-permute-start(bf16[256,1024]{0,1:T(8,128)(2,1)S(1)} %get-tuple-element.185), channel_id=1, source_target_pairs={{0,2},{1,3},{2,0},{3,1},{4,6},{5,7},{6,4},{7,5},{8,10},{9,11},{10,... | collective-permute-start | bytes 1572872 | tf_op jit(solution)/shard_map/ppermute | solution.py:174
  145.9 32.1 %collective-permute-start.12 = (bf16[256,1024]{1,0:T(8,128)(2,1)}, bf16[256,1024]{1,0:T(8,128)(2,1)}, u32[]{:S(2)}, u32[]{:S(2)}) collective-permute-start(bf16[256,1024]{1,0:T(8,128)(2,1)} %param.21), channel_id=1, source_target_pairs={{0,1},{1,2},{2,3},{3,0},{4,5},{5,6},{6,7},{7,4},{8,9},{9,10},{10,1... | collective-permute-start | bytes 1572872 | tf_op jit(solution)/shard_map/ppermute | solution.py:190
  145.9 37.8 %collective-permute-start.14 = (bf16[256,1024]{1,0:T(8,128)(2,1)}, bf16[256,1024]{1,0:T(8,128)(2,1)}, u32[]{:S(2)}, u32[]{:S(2)}) collective-permute-start(bf16[256,1024]{1,0:T(8,128)(2,1)} %param.21), channel_id=1, source_target_pairs={{0,3},{1,0},{2,1},{3,2},{4,7},{5,4},{6,5},{7,6},{8,11},{9,8},{10,9... | collective-permute-start | bytes 1572872 | tf_op jit(solution)/shard_map/ppermute | solution.py:190
  155.1 37.3 %collective-permute-start.13 = (bf16[256,1024]{1,0:T(8,128)(2,1)}, bf16[256,1024]{1,0:T(8,128)(2,1)}, u32[]{:S(2)}, u32[]{:S(2)}) collective-permute-start(bf16[256,1024]{1,0:T(8,128)(2,1)} %param.21), channel_id=1, source_target_pairs={{0,2},{1,3},{2,0},{3,1},{4,6},{5,7},{6,4},{7,5},{8,10},{9,11},{10,... | collective-permute-start | bytes 1572872 | tf_op jit(solution)/shard_map/ppermute | solution.py:190
  173.5 26.7 %collective-permute-start.6 = (bf16[256,1024]{0,1:T(8,128)(2,1)}, bf16[256,1024]{0,1:T(8,128)(2,1)}, u32[]{:S(2)}, u32[]{:S(2)}) collective-permute-start(bf16[256,1024]{0,1:T(8,128)(2,1)} %get-tuple-element.156), channel_id=1, source_target_pairs={{0,1},{1,2},{2,3},{3,0},{4,5},{5,6},{6,7},{7,4},{8,9},{9,10},{10,1... | collective-permute-start | bytes 1572872 | tf_op jit(solution)/shard_map/ppermute | solution.py:190
  175.6 28.1 %collective-permute-start.7 = (bf16[256,1024]{0,1:T(8,128)(2,1)}, bf16[256,1024]{0,1:T(8,128)(2,1)}, u32[]{:S(2)}, u32[]{:S(2)}) collective-permute-start(bf16[256,1024]{0,1:T(8,128)(2,1)} %get-tuple-element.156), channel_id=1, source_target_pairs={{0,2},{1,3},{2,0},{3,1},{4,6},{5,7},{6,4},{7,5},{8,10},{9,11},{10,... | collective-permute-start | bytes 1572872 | tf_op jit(solution)/shard_map/ppermute | solution.py:190
  180.0 32.1 %collective-permute-start.8 = (bf16[256,1024]{0,1:T(8,128)(2,1)}, bf16[256,1024]{0,1:T(8,128)(2,1)}, u32[]{:S(2)}, u32[]{:S(2)}) collective-permute-start(bf16[256,1024]{0,1:T(8,128)(2,1)} %get-tuple-element.156), channel_id=1, source_target_pairs={{0,3},{1,0},{2,1},{3,2},{4,7},{5,4},{6,5},{7,6},{8,11},{9,8},{10,9... | collective-permute-start | bytes 1572872 | tf_op jit(solution)/shard_map/ppermute | solution.py:190
  196.5 16.7 %copy-start.78 = (bf16[1024,704]{0,1:T(8,128)(2,1)S(1)}, bf16[1024,704]{0,1:T(8,128)(2,1)}, u32[]{:S(2)}) copy-start(bf16[1024,704]{0,1:T(8,128)(2,1)} %param.18) | copy-start | bytes 4325380
  224.3 10.6 %copy-start.38 = (bf16[1024,1024]{0,1:T(8,128)(2,1)}, bf16[1024,1024]{0,1:T(8,128)(2,1)S(1)}, u32[]{:S(2)}) copy-start(bf16[1024,1024]{0,1:T(8,128)(2,1)S(1)} %convolution_convert_fusion.1) | copy-start | bytes 6291460
  232.3 14.3 %collective-permute-start.15 = (bf16[256,1024]{0,1:T(8,128)(2,1)}, bf16[256,1024]{0,1:T(8,128)(2,1)}, u32[]{:S(2)}, u32[]{:S(2)}) collective-permute-start(bf16[256,1024]{0,1:T(8,128)(2,1)} %get-tuple-element.177), channel_id=1, source_target_pairs={{0,1},{1,2},{2,3},{3,0},{4,5},{5,6},{6,7},{7,4},{8,9},{9,10},{10,1... | collective-permute-start | bytes 1572872 | tf_op jit(solution)/shard_map/ppermute | solution.py:174
  233.1 14.0 %collective-permute-start.17 = (bf16[256,1024]{0,1:T(8,128)(2,1)}, bf16[256,1024]{0,1:T(8,128)(2,1)}, u32[]{:S(2)}, u32[]{:S(2)}) collective-permute-start(bf16[256,1024]{0,1:T(8,128)(2,1)} %get-tuple-element.178), channel_id=1, source_target_pairs={{0,3},{1,0},{2,1},{3,2},{4,7},{5,4},{6,5},{7,6},{8,11},{9,8},{10,9... | collective-permute-start | bytes 1572872 | tf_op jit(solution)/shard_map/ppermute | solution.py:174
  234.5 24.7 %collective-permute-start.16 = (bf16[256,1024]{0,1:T(8,128)(2,1)}, bf16[256,1024]{0,1:T(8,128)(2,1)}, u32[]{:S(2)}, u32[]{:S(2)}) collective-permute-start(bf16[256,1024]{0,1:T(8,128)(2,1)} %get-tuple-element.179), channel_id=1, source_target_pairs={{0,2},{1,3},{2,0},{3,1},{4,6},{5,7},{6,4},{7,5},{8,10},{9,11},{10,... | collective-permute-start | bytes 1572872 | tf_op jit(solution)/shard_map/ppermute | solution.py:174
  236.1 33.0 %collective-permute-start.9 = (bf16[256,1024]{0,1:T(8,128)(2,1)}, bf16[256,1024]{0,1:T(8,128)(2,1)}, u32[]{:S(2)}, u32[]{:S(2)}) collective-permute-start(bf16[256,1024]{0,1:T(8,128)(2,1)} %get-tuple-element.180), channel_id=1, source_target_pairs={{0,1},{1,2},{2,3},{3,0},{4,5},{5,6},{6,7},{7,4},{8,9},{9,10},{10,1... | collective-permute-start | bytes 1572872 | tf_op jit(solution)/shard_map/ppermute | solution.py:174
  236.3 33.3 %collective-permute-start.11 = (bf16[256,1024]{0,1:T(8,128)(2,1)}, bf16[256,1024]{0,1:T(8,128)(2,1)}, u32[]{:S(2)}, u32[]{:S(2)}) collective-permute-start(bf16[256,1024]{0,1:T(8,128)(2,1)} %get-tuple-element.181), channel_id=1, source_target_pairs={{0,3},{1,0},{2,1},{3,2},{4,7},{5,4},{6,5},{7,6},{8,11},{9,8},{10,9... | collective-permute-start | bytes 1572872 | tf_op jit(solution)/shard_map/ppermute | solution.py:174
  241.0 19.9 %copy-start.14 = (f32[256,1024]{0,1:T(8,128)S(1)}, f32[256,1024]{0,1:T(8,128)}, u32[]{:S(2)}) copy-start(f32[256,1024]{0,1:T(8,128)} %copy-done.13) | copy-start | bytes 3145732
  241.0 20.0 %copy-start.63 = (f32[1024]{0:T(1024)S(1)}, f32[1024]{0:T(1024)}, u32[]{:S(2)}) copy-start(f32[1024]{0:T(1024)} %param.17) | copy-start | bytes 12292
  241.0 20.0 %copy-start.71 = (f32[256]{0:T(256)S(1)}, f32[256]{0:T(256)}, u32[]{:S(2)}) copy-start(f32[256]{0:T(256)} %copy-done.70) | copy-start | bytes 3076
  246.6 34.3 %copy-start.23 = (bf16[256,1024]{0,1:T(8,128)(2,1)S(1)}, bf16[256,1024]{0,1:T(8,128)(2,1)}, u32[]{:S(2)}) copy-start(bf16[256,1024]{0,1:T(8,128)(2,1)} %copy.329) | copy-start | bytes 1572868
  246.6 34.3 %copy-start.77 = (f32[256]{0:T(256)S(1)}, f32[256]{0:T(256)}, u32[]{:S(2)}) copy-start(f32[256]{0:T(256)} %get-tuple-element.215) | copy-start | bytes 3076
  246.6 34.3 %collective-permute-start.10 = (bf16[256,1024]{0,1:T(8,128)(2,1)}, bf16[256,1024]{0,1:T(8,128)(2,1)S(1)}, u32[]{:S(2)}, u32[]{:S(2)}) collective-permute-start(bf16[256,1024]{0,1:T(8,128)(2,1)} %get-tuple-element.182), channel_id=1, source_target_pairs={{0,2},{1,3},{2,0},{3,1},{4,6},{5,7},{6,4},{7,5},{8,10},{9,11},{10,... | collective-permute-start | bytes 1572872 | tf_op jit(solution)/shard_map/ppermute | solution.py:174
  286.0 13.6 %collective-permute-start.18 = (bf16[256,1024]{0,1:T(8,128)(2,1)S(1)}, bf16[256,1024]{0,1:T(8,128)(2,1)S(1)}, u32[]{:S(2)}, u32[]{:S(2)}) collective-permute-start(bf16[256,1024]{0,1:T(8,128)(2,1)S(1)} %get-tuple-element.154), channel_id=1, source_target_pairs={{0,1},{1,2},{2,3},{3,0},{4,5},{5,6},{6,7},{7,4},{8,9},{9,10},{10,1... | collective-permute-start | bytes 1572872 | tf_op jit(solution)/shard_map/ppermute | solution.py:190
  286.0 14.9 %collective-permute-start.19 = (bf16[256,1024]{0,1:T(8,128)(2,1)S(1)}, bf16[256,1024]{0,1:T(8,128)(2,1)}, u32[]{:S(2)}, u32[]{:S(2)}) collective-permute-start(bf16[256,1024]{0,1:T(8,128)(2,1)S(1)} %get-tuple-element.154), channel_id=1, source_target_pairs={{0,2},{1,3},{2,0},{3,1},{4,6},{5,7},{6,4},{7,5},{8,10},{9,11},{10,... | collective-permute-start | bytes 1572872 | tf_op jit(solution)/shard_map/ppermute | solution.py:190
  286.3 23.0 %collective-permute-start.20 = (bf16[256,1024]{0,1:T(8,128)(2,1)S(1)}, bf16[256,1024]{0,1:T(8,128)(2,1)}, u32[]{:S(2)}, u32[]{:S(2)}) collective-permute-start(bf16[256,1024]{0,1:T(8,128)(2,1)S(1)} %get-tuple-element.154), channel_id=1, source_target_pairs={{0,3},{1,0},{2,1},{3,2},{4,7},{5,4},{6,5},{7,6},{8,11},{9,8},{10,9... | collective-permute-start | bytes 1572872 | tf_op jit(solution)/shard_map/ppermute | solution.py:190
  287.8 23.3 %copy-start.57 = (bf16[256,1024]{1,0:T(8,128)(2,1)S(1)}, bf16[256,1024]{1,0:T(8,128)(2,1)}, u32[]{:S(2)}) copy-start(bf16[256,1024]{1,0:T(8,128)(2,1)} %param.16) | copy-start | bytes 1572868
  314.8 8.1 %copy-start.29 = (f32[1024,4,2]{1,2,0:T(2,128)S(1)}, f32[1024,4,2]{1,2,0:T(2,128)}, u32[]{:S(2)}) copy-start(f32[1024,4,2]{1,2,0:T(2,128)} %copy.392) | copy-start | bytes 98308
  322.9 11.7 %copy-start.5 = (f32[4,512,512]{1,2,0:T(8,128)S(1)}, f32[4,512,512]{1,2,0:T(8,128)}, u32[]{:S(2)}) copy-start(f32[4,512,512]{1,2,0:T(8,128)} %copy-done.3) | copy-start | bytes 12582916
  357.0 7.9 %copy-start.54 = (bf16[512,4,64]{0,2,1:T(8,128)(2,1)S(1)}, bf16[512,4,64]{0,2,1:T(8,128)(2,1)}, u32[]{:S(2)}) copy-start(bf16[512,4,64]{0,2,1:T(8,128)(2,1)} %fusion.39) | copy-start | bytes 786436
  404.4 10.1 %collective-permute-start.21 = (bf16[1024,160]{0,1:T(8,128)(2,1)S(1)}, bf16[1024,160]{0,1:T(8,128)(2,1)S(1)}, u32[]{:S(2)}, u32[]{:S(2)}) collective-permute-start(bf16[1024,160]{0,1:T(8,128)(2,1)S(1)} %get-tuple-element.188), channel_id=1, source_target_pairs={{0,1},{1,2},{2,3},{3,0},{4,5},{5,6},{6,7},{7,4},{8,9},{9,10},{10,1... | collective-permute-start | bytes 983048 | tf_op jit(solution)/shard_map/ppermute | solution.py:174
  408.0 8.3 %collective-permute-start.23 = (bf16[1024,160]{0,1:T(8,128)(2,1)S(1)}, bf16[1024,160]{0,1:T(8,128)(2,1)S(1)}, u32[]{:S(2)}, u32[]{:S(2)}) collective-permute-start(bf16[1024,160]{0,1:T(8,128)(2,1)S(1)} %get-tuple-element.189), channel_id=1, source_target_pairs={{0,3},{1,0},{2,1},{3,2},{4,7},{5,4},{6,5},{7,6},{8,11},{9,8},{10,9... | collective-permute-start | bytes 983048 | tf_op jit(solution)/shard_map/ppermute | solution.py:174
  408.2 15.2 %collective-permute-start.22 = (bf16[1024,160]{0,1:T(8,128)(2,1)S(1)}, bf16[1024,160]{0,1:T(8,128)(2,1)S(1)}, u32[]{:S(2)}, u32[]{:S(2)}) collective-permute-start(bf16[1024,160]{0,1:T(8,128)(2,1)S(1)} %get-tuple-element.190), channel_id=1, source_target_pairs={{0,2},{1,3},{2,0},{3,1},{4,6},{5,7},{6,4},{7,5},{8,10},{9,11},{10,... | collective-permute-start | bytes 983048 | tf_op jit(solution)/shard_map/ppermute | solution.py:174
  425.8 12.3 %collective-permute-start.24 = (bf16[256,1024]{0,1:T(8,128)(2,1)S(1)}, bf16[256,1024]{0,1:T(8,128)(2,1)S(1)}, u32[]{:S(2)}, u32[]{:S(2)}) collective-permute-start(bf16[256,1024]{0,1:T(8,128)(2,1)S(1)} %get-tuple-element.172), channel_id=1, source_target_pairs={{0,1},{1,2},{2,3},{3,0},{4,5},{5,6},{6,7},{7,4},{8,9},{9,10},{10,1... | collective-permute-start | bytes 1572872 | tf_op jit(solution)/shard_map/ppermute | solution.py:174
  425.9 14.2 %collective-permute-start.26 = (bf16[256,1024]{0,1:T(8,128)(2,1)S(1)}, bf16[256,1024]{0,1:T(8,128)(2,1)S(1)}, u32[]{:S(2)}, u32[]{:S(2)}) collective-permute-start(bf16[256,1024]{0,1:T(8,128)(2,1)S(1)} %get-tuple-element.173), channel_id=1, source_target_pairs={{0,3},{1,0},{2,1},{3,2},{4,7},{5,4},{6,5},{7,6},{8,11},{9,8},{10,9... | collective-permute-start | bytes 1572872 | tf_op jit(solution)/shard_map/ppermute | solution.py:174
  427.7 23.6 %copy-start.12 = (bf16[256,1024]{0,1:T(8,128)(2,1)S(1)}, bf16[256,1024]{0,1:T(8,128)(2,1)}, u32[]{:S(2)}) copy-start(bf16[256,1024]{0,1:T(8,128)(2,1)} %copy-done.9) | copy-start | bytes 1572868
  427.7 23.6 %copy-start.65 = (f32[1024]{0:T(1024)S(1)}, f32[1024]{0:T(1024)}, u32[]{:S(2)}) copy-start(f32[1024]{0:T(1024)} %param.13) | copy-start | bytes 12292
  427.7 23.6 %copy-start.74 = (f32[256]{0:T(256)S(1)}, f32[256]{0:T(256)}, u32[]{:S(2)}) copy-start(f32[256]{0:T(256)} %copy-done.73) | copy-start | bytes 3076
  427.7 23.6 %collective-permute-start.25 = (bf16[256,1024]{0,1:T(8,128)(2,1)S(1)}, bf16[256,1024]{0,1:T(8,128)(2,1)S(1)}, u32[]{:S(2)}, u32[]{:S(2)}) collective-permute-start(bf16[256,1024]{0,1:T(8,128)(2,1)S(1)} %get-tuple-element.174), channel_id=1, source_target_pairs={{0,2},{1,3},{2,0},{3,1},{4,6},{5,7},{6,4},{7,5},{8,10},{9,11},{10,... | collective-permute-start | bytes 1572872 | tf_op jit(solution)/shard_map/ppermute | solution.py:174
  432.2 20.7 %copy-start.75 = (bf16[1024]{0:T(1024)(128)(2,1)S(1)}, bf16[1024]{0:T(1024)(128)(2,1)}, u32[]{:S(2)}) copy-start(bf16[1024]{0:T(1024)(128)(2,1)} %get-tuple-element.145) | copy-start | bytes 6148
  432.2 20.9 %copy-start.59 = (bf16[1024,160]{0,1:T(8,128)(2,1)S(1)}, bf16[1024,160]{0,1:T(8,128)(2,1)}, u32[]{:S(2)}) copy-start(bf16[1024,160]{0,1:T(8,128)(2,1)} %convolution_convert_fusion.7) | copy-start | bytes 983044
  432.2 21.0 %copy-start.55 = (bf16[256,1024]{1,0:T(8,128)(2,1)S(1)}, bf16[256,1024]{1,0:T(8,128)(2,1)}, u32[]{:S(2)}) copy-start(bf16[256,1024]{1,0:T(8,128)(2,1)} %convolution_convert_fusion.6) | copy-start | bytes 1572868
  432.2 21.1 %copy-start.58 = (bf16[1024,40]{0,1:T(8,128)(2,1)S(1)}, bf16[1024,40]{0,1:T(8,128)(2,1)}, u32[]{:S(2)}) copy-start(bf16[1024,40]{0,1:T(8,128)(2,1)} %convolution_convert_fusion.8) | copy-start | bytes 245764
  460.5 10.9 %collective-permute-start.27 = (bf16[2,2,58752]{2,1,0:T(2,128)(2,1)S(1)}, bf16[2,2,58752]{2,1,0:T(2,128)(2,1)S(1)}, u32[]{:S(2)}, u32[]{:S(2)}) collective-permute-start(bf16[2,2,58752]{2,1,0:T(2,128)(2,1)S(1)} %bitcast.150), channel_id=1, source_target_pairs={{0,4},{4,0},{8,12},{12,8},{16,20},{20,16},{24,28},{28,24},{1,5},{5... | collective-permute-start | bytes 1410056 | tf_op jit(solution)/shard_map/ppermute | solution.py:213
  472.7 6.1 %collective-permute-start.28 = (bf16[2,58752]{1,0:T(2,128)(2,1)S(1)}, bf16[2,58752]{1,0:T(2,128)(2,1)S(1)}, u32[]{:S(2)}, u32[]{:S(2)}) collective-permute-start(bf16[2,58752]{1,0:T(2,128)(2,1)S(1)} %bitcast.151), channel_id=1, source_target_pairs={{0,8},{4,12},{8,0},{12,4},{16,24},{20,28},{24,16},{28,20},{1,9},{5... | collective-permute-start | bytes 705032 | tf_op jit(solution)/shard_map/ppermute | solution.py:213
  475.2 25.5 %copy-start.39 = (bf16[256,1024]{0,1:T(8,128)(2,1)S(1)}, bf16[256,1024]{0,1:T(8,128)(2,1)}, u32[]{:S(2)}) copy-start(bf16[256,1024]{0,1:T(8,128)(2,1)} %get-tuple-element.135) | copy-start | bytes 1572868
  479.9 6.0 %collective-permute-start.29 = (bf16[58752]{0:T(1024)(128)(2,1)S(1)}, bf16[58752]{0:T(1024)(128)(2,1)S(1)}, u32[]{:S(2)}, u32[]{:S(2)}) collective-permute-start(bf16[58752]{0:T(1024)(128)(2,1)S(1)} %convert_reduce_fusion), channel_id=1, source_target_pairs={{0,16},{4,20},{8,24},{12,28},{16,0},{20,4},{24,8},{28,12},{1,17},{... | collective-permute-start | bytes 352520 | tf_op jit(solution)/shard_map/ppermute | solution.py:213
  486.1 8.6 %collective-permute-start.30 = (bf16[1,58752]{1,0:T(2,128)(2,1)S(1)}, bf16[1,58752]{1,0:T(2,128)(2,1)S(1)}, u32[]{:S(2)}, u32[]{:S(2)}) collective-permute-start(bf16[1,58752]{1,0:T(2,128)(2,1)S(1)} %broadcast_in_dim.146), channel_id=1, source_target_pairs={{0,16},{4,20},{8,24},{12,28},{16,0},{20,4},{24,8},{28,12},{1,17},{... | collective-permute-start | bytes 352520 | tf_op jit(solution)/shard_map/ppermute | solution.py:218
  495.8 8.9 %collective-permute-start.31 = (bf16[2,58752]{1,0:T(2,128)(2,1)S(1)}, bf16[2,58752]{1,0:T(2,128)(2,1)S(1)}, u32[]{:S(2)}, u32[]{:S(2)}) collective-permute-start(bf16[2,58752]{1,0:T(2,128)(2,1)S(1)} %maximum_bitcast_fusion), channel_id=1, source_target_pairs={{0,8},{4,12},{8,0},{12,4},{16,24},{20,28},{24,16},{28,20},{1,9},{5... | collective-permute-start | bytes 705032 | tf_op jit(solution)/shard_map/ppermute | solution.py:218
  507.3 10.5 %collective-permute-start.32 = (bf16[4,58752]{1,0:T(4,128)(2,1)S(1)}, bf16[4,58752]{1,0:T(4,128)(2,1)}, u32[]{:S(2)}, u32[]{:S(2)}) collective-permute-start(bf16[4,58752]{1,0:T(4,128)(2,1)S(1)} %reshape.337), channel_id=1, source_target_pairs={{0,4},{4,0},{8,12},{12,8},{16,20},{20,16},{24,28},{28,24},{1,5},{5... | collective-permute-start | bytes 1410056 | tf_op jit(solution)/shard_map/ppermute | solution.py:218
  522.7 34.9 %collective-permute-start.35 = (bf16[1037,160]{0,1:T(8,128)(2,1)}, bf16[1037,160]{0,1:T(8,128)(2,1)}, u32[]{:S(2)}, u32[]{:S(2)}) collective-permute-start(bf16[1037,160]{0,1:T(8,128)(2,1)} %copy.363), channel_id=1, source_target_pairs={{0,3},{1,0},{2,1},{3,2},{4,7},{5,4},{6,5},{7,6},{8,11},{9,8},{10,9... | collective-permute-start | bytes 995528 | tf_op jit(solution)/shard_map/ppermute | solution.py:190
  522.7 27.1 %collective-permute-start.34 = (bf16[1037,160]{0,1:T(8,128)(2,1)}, bf16[1037,160]{0,1:T(8,128)(2,1)}, u32[]{:S(2)}, u32[]{:S(2)}) collective-permute-start(bf16[1037,160]{0,1:T(8,128)(2,1)} %copy.363), channel_id=1, source_target_pairs={{0,2},{1,3},{2,0},{3,1},{4,6},{5,7},{6,4},{7,5},{8,10},{9,11},{10,... | collective-permute-start | bytes 995528 | tf_op jit(solution)/shard_map/ppermute | solution.py:190
  525.0 17.3 %collective-permute-start.33 = (bf16[1037,160]{0,1:T(8,128)(2,1)}, bf16[1037,160]{0,1:T(8,128)(2,1)}, u32[]{:S(2)}, u32[]{:S(2)}) collective-permute-start(bf16[1037,160]{0,1:T(8,128)(2,1)} %copy.363), channel_id=1, source_target_pairs={{0,1},{1,2},{2,3},{3,0},{4,5},{5,6},{6,7},{7,4},{8,9},{9,10},{10,1... | collective-permute-start | bytes 995528 | tf_op jit(solution)/shard_map/ppermute | solution.py:190
  527.0 7.9 %copy-start.37 = (bf16[459,1024]{1,0:T(8,128)(2,1)S(1)}, bf16[459,1024]{1,0:T(8,128)(2,1)}, u32[]{:S(2)}) copy-start(bf16[459,1024]{1,0:T(8,128)(2,1)} %slice.172) | copy-start | bytes 2820100
  (55 other events, 177.7 us)
Sparse Core Ops, SparseCore 0:
  287.9 160.9 all-reduce.6

commit v8 on v7

--- a/solution.py
+++ b/solution.py
@@ -222,6 +222,28 @@
     return whole.reshape(-1)[: flat.shape[0]]
 
 
+def head_gather_relative(values):
+    count = lax.axis_size("head")
+    parts = [values]
+    for shift in range(1, count):
+        parts.append(
+            lax.ppermute(values, "head", [(device, (device + shift) % count) for device in range(count)])
+        )
+    return jnp.concatenate(parts, axis=0)
+
+
+def head_scatter_relative(values):
+    count = lax.axis_size("head")
+    width = values.shape[0] // count
+    total = values[:width].astype(jnp.float32)
+    for shift in range(1, count):
+        sent = values[(count - shift) * width : (count - shift + 1) * width]
+        total = total + lax.ppermute(
+            sent, "head", [(device, (device + shift) % count) for device in range(count)]
+        ).astype(jnp.float32)
+    return total
+
+
 def local(
     tokens,
     doc_ids,
@@ -245,7 +267,7 @@
     normed_one = (x_own * inv_one * gain_attn).astype(jnp.bfloat16)
     normed_all, grad_out_all = (
         head_all_gather(normed_one, 0),
-        head_all_gather(cotangent, 0),
+        head_gather_relative(cotangent),
     )
     factor_a = jnp.dot(normed_all, a_weight, preferred_element_type=jnp.float32).reshape(
         total_rows, local_heads, rank_all
@@ -281,7 +303,7 @@
     )
     inv_two = lax.rsqrt(jnp.mean(resid_own * resid_own, axis=-1, keepdims=True) + EPSILON)
     normed_two = (resid_own * inv_two * gain_ffn).astype(jnp.bfloat16)
-    normed_two_all = head_all_gather(normed_two, 0)
+    normed_two_all = head_gather_relative(normed_two)
     gate_act = jnp.dot(normed_two_all, gate_weight, preferred_element_type=jnp.float32)
     up_act = jnp.dot(normed_two_all, up_weight, preferred_element_type=jnp.float32)
     sigmoid_gate = jax.nn.sigmoid(gate_act)
@@ -290,8 +312,8 @@
     piece = lax.slice_in_dim(hidden, 0, lax.axis_size("head") * own_rows, axis=0)
     output = (
         resid_own
-        + head_reduce_scatter(
-            jnp.dot(piece, down_weight, preferred_element_type=jnp.float32).astype(jnp.bfloat16), 0
+        + head_scatter_relative(
+            jnp.dot(piece, down_weight, preferred_element_type=jnp.float32).astype(jnp.bfloat16)
         )
     ).astype(jnp.bfloat16)
     grad_down = dot_first(hidden, grad_out_all)
@@ -304,8 +326,8 @@
     grad_up = dot_first(normed_two_all, grad_up_act)
     gate_piece = lax.slice_in_dim(grad_gate_act, 0, lax.axis_size("head") * own_rows, axis=0)
     up_piece = lax.slice_in_dim(grad_up_act, 0, lax.axis_size("head") * own_rows, axis=0)
-    grad_normed_two = head_reduce_scatter(
-        (dot_last(gate_piece, gate_weight) + dot_last(up_piece, up_weight)).astype(jnp.bfloat16), 0
+    grad_normed_two = head_scatter_relative(
+        (dot_last(gate_piece, gate_weight) + dot_last(up_piece, up_weight)).astype(jnp.bfloat16)
     )
     ffn_grads = (grad_gate.astype(jnp.bfloat16), grad_up.astype(jnp.bfloat16), grad_down.astype(jnp.bfloat16))
     ffn_grads, grad_normed_two = lax.optimization_barrier((ffn_grads, grad_normed_two))
@@ -389,7 +411,7 @@
         grad_down.astype(jnp.float32),
     )
     grad_a = grad_a.astype(jnp.float32)
-    packed = head_all_gather(packed, 1).astype(jnp.float32)
+    packed = lax.all_gather(packed, "head", axis=1, tiled=True).astype(jnp.float32)
     grad_b = packed[: grad_b_cols.shape[0]]
     gains = jnp.sum(
         packed[grad_b_cols.shape[0] :].reshape(gain_rows, head_count, basis_cols), axis=1

time: 587 us -> 559 us (0.952)
  local copies, waits for them, and re-layouts: 159 us -> 107 us
  waiting for transfers between devices: 169 us -> 204 us
  starting transfers between devices: 49.1 us -> 42.4 us
  matrix products: 125 us -> 119 us
    ppermute x0 -> x12, waiting for transfers between devices: none -> 69 us  [the longest x6 41 us: head_gather_relative(): lax.ppermute(values, 'head', [(device, (device + shift) % count) for devi...]
    dynamic_update_slice x15 -> x6, local copies, waits for them, and re-layouts: 38.2 us -> 8.14 us  [head_all_gather(): lax.dynamic_update_slice_in_dim(gathered, arrived, (own - shift) % count...]
    ppermute x15 -> x9, waiting for transfers between devices: 87.4 us -> 58.5 us  [head_reduce_scatter(): lax.ppermute(sent, 'head', [(device, (device + shift) % count) for device...]
    ppermute x15 -> x6, waiting for transfers between devices: 58.5 us -> 33.9 us  [head_all_gather(): lax.ppermute(values, 'head', [(device, (device + shift) % count) for devi...]
    ppermute x6 -> x0, local copies, waits for them, and re-layouts: 9.74 us -> none  [head_all_gather(): lax.ppermute(values, 'head', [(device, (device + shift) % count) for devi...]
    ppermute x3, waiting for transfers between devices: 8.11 us -> 17.6 us  [dp_all_reduce(): arrived = lax.ppermute(whole, 'dp', pairs)]
    ppermute x0 -> x12, starting transfers between devices: none -> 8.58 us  [the longest x6 7.3 us: head_scatter_relative(): lax.ppermute(sent, 'head', [(device, (device + shift) % count) for device...]
    ppermute x15 -> x6, starting transfers between devices: 15.8 us -> 7.67 us  [head_all_gather(): lax.ppermute(values, 'head', [(device, (device + shift) % count) for devi...]
  transfers between devices with their start and end apart: 37 -> 35, of which waited for: 28 -> 27; matrix products, arithmetic and copies ran while one was open for 31% -> 24% of each run, Pallas kernels for 0% -> 0%
where the time goes in v8:
time: 559 us; the launch traced here: 549 us
  waiting for transfers between devices  204 us (36%)
  matrix products  119 us (21%)
  local copies, waits for them, and re-layouts  107 us (19%)
  other arithmetic  60.3 us (11%)
  starting transfers between devices  42.4 us (8%)
  between operations  15.7 us (3%)
    ppermute x9, waiting for transfers between devices, head_reduce_scatter(): lax.ppermute(sent, 'head', [(device, (device + shift) % count) for device...  58.5 us
    ppermute x6, waiting for transfers between devices, head_gather_relative(): lax.ppermute(values, 'head', [(device, (device + shift) % count) for devi...  41 us
    ppermute x6, waiting for transfers between devices, head_all_gather(): lax.ppermute(values, 'head', [(device, (device + shift) % count) for devi...  33.9 us
    unnamed x167, local copies, waits for them, and re-layouts  30 us
    ppermute x6, waiting for transfers between devices, head_scatter_relative(): lax.ppermute(sent, 'head', [(device, (device + shift) % count) for device...  28 us
    ppermute x3, waiting for transfers between devices, dp_all_reduce(): lax.ppermute(sent.astype(jnp.bfloat16), 'dp', pairs).astype(jnp.float32)  18.2 us
    ppermute x3, waiting for transfers between devices, dp_all_reduce(): arrived = lax.ppermute(whole, 'dp', pairs)  17.6 us
    dot_general x6, matrix products, dot_last(): lax.dot_general(left, right, (((1,), (1,)), ((), ())), preferred_element_...  12.1 us
  transfers between devices with their start and end apart: 35, of which 27 were waited for; matrix products, arithmetic and copies ran while one was open for 24% of the time, Pallas kernels for 0%

profile of v8, /device:TPU:0, one launch (start us, length us, event | category | flops | bytes accessed | tf_op | source)
XLA Modules:
  0.0 548.7 jit_solution(7246732786341813126)
XLA Ops:
  11.2 3.0 collective-permute-start.1
  18.4 3.0 multiply_cosine_fusion
  21.4 15.4 %collective-permute-done = bf16[256,1024]{1,0:T(8,128)(2,1)} collective-permute-done((bf16[256,1024]{1,0:T(8,128)(2,1)}, bf16[256,1024]{1,0:T(8,128)(2,1)}, u32[]{:S(2)}, u32[]{:S(2)}) %collective-permute-start) | collective-permute-done | bytes 524320 | tf_op jit(solution)/shard_map/ppermute | solution.py:190
  46.3 2.9 fusion.92
  57.7 2.7 fusion.82
  66.8 2.6 multiply_subtract_fusion.1
  70.6 10.4 %fusion.75 = f32[1024,4,64]{2,1,0:T(4,128)} fusion(f32[1024,4,2]{1,2,0:T(2,128)S(1)} %copy-done.25, f32[1024,2,32]{2,1,0:T(2,128)S(1)} %get-tuple-element.177, f32[1024,2,32]{2,1,0:T(2,128)S(1)} %get-tuple-element.176), kind=kOutput, calls=%fused_computation.198 | convolution fusion | flops 6422528 | bytes 1605632 | tf_op jit(solution)/shard_map/thr,trd->thd/dot_general | solution.py:288
  81.0 2.7 copy.356
  85.8 10.9 %fusion.93 = f32[1024,4,64]{2,1,0:T(4,128)} fusion(f32[1024,4,2]{1,2,0:T(2,128)} %copy.404, f32[1024,2,64]{2,1,0:T(2,128)} %copy.348), kind=kOutput, calls=%fused_computation.215 | convolution fusion | flops 6291456 | bytes 1605632 | tf_op jit(solution)/shard_map/thr,trd->thd/dot_general | solution.py:292
  96.7 2.7 copy.349
  101.5 3.6 copy.403
  105.1 3.6 copy.402
  108.7 4.1 multiply_subtract_fusion
  112.9 8.3 %multiply_convert_fusion.5 = bf16[1024,4,64]{2,1,0:T(4,128)(2,1)S(1)} fusion(f32[1024,4,6]{2,1,0:T(4,128)S(1)} %copy.401, f32[1024,6,32]{2,1,0:T(8,128)S(1)} %get-tuple-element.170, f32[1024,6,32]{2,1,0:T(8,128)S(1)} %get-tuple-element.169), kind=kOutput, calls=%fused_computation.42 | convolution fusion | flops 19791872 | bytes 2195456 | tf_op jit(solution)/shard_map/thr,trd->thd/dot_general | solution.py:285
  144.0 8.7 %collective-permute-done.3 = bf16[256,1024]{1,0:T(8,128)(2,1)S(1)} collective-permute-done((bf16[256,1024]{1,0:T(8,128)(2,1)S(1)}, bf16[256,1024]{1,0:T(8,128)(2,1)S(1)}, u32[]{:S(2)}, u32[]{:S(2)}) %collective-permute-start.3) | collective-permute-done | bytes 524320 | tf_op jit(solution)/shard_map/ppermute | solution.py:174
  154.3 13.1 %collective-permute-done.4 = bf16[256,1024]{1,0:T(8,128)(2,1)S(1)} collective-permute-done((bf16[256,1024]{1,0:T(8,128)(2,1)S(1)}, bf16[256,1024]{1,0:T(8,128)(2,1)S(1)}, u32[]{:S(2)}, u32[]{:S(2)}) %collective-permute-start.4) | collective-permute-done | bytes 524320 | tf_op jit(solution)/shard_map/ppermute | solution.py:174
  169.5 16.9 %collective-permute-done.12 = bf16[256,1024]{1,0:T(8,128)(2,1)S(1)} collective-permute-done((bf16[256,1024]{1,0:T(8,128)(2,1)S(1)}, bf16[256,1024]{1,0:T(8,128)(2,1)S(1)}, u32[]{:S(2)}, u32[]{:S(2)}) %collective-permute-start.12) | collective-permute-done | bytes 524320 | tf_op jit(solution)/shard_map/ppermute | solution.py:230
  188.0 11.2 %collective-permute-done.8 = bf16[256,1024]{1,0:T(8,128)(2,1)S(1)} collective-permute-done((bf16[256,1024]{1,0:T(8,128)(2,1)S(1)}, bf16[256,1024]{1,0:T(8,128)(2,1)S(1)}, u32[]{:S(2)}, u32[]{:S(2)}) %collective-permute-start.8) | collective-permute-done | bytes 524320 | tf_op jit(solution)/shard_map/ppermute | solution.py:230
  199.2 11.4 %collective-permute-done.7 = bf16[256,1024]{1,0:T(8,128)(2,1)S(1)} collective-permute-done((bf16[256,1024]{1,0:T(8,128)(2,1)S(1)}, bf16[256,1024]{1,0:T(8,128)(2,1)S(1)}, u32[]{:S(2)}, u32[]{:S(2)}) %collective-permute-start.7) | collective-permute-done | bytes 524320 | tf_op jit(solution)/shard_map/ppermute | solution.py:230
  214.0 3.1 multiply_convert_fusion.2
  217.1 2.8 convolution_convert_fusion.4
  233.0 2.9 convolution_convert_fusion.2
  235.8 2.8 convolution_convert_fusion.3
  238.6 8.5 %collective-permute-done.15 = bf16[256,1024]{1,0:T(8,128)(2,1)} collective-permute-done((bf16[256,1024]{1,0:T(8,128)(2,1)}, bf16[256,1024]{1,0:T(8,128)(2,1)}, u32[]{:S(2)}, u32[]{:S(2)}) %collective-permute-start.15) | collective-permute-done | bytes 524320 | tf_op jit(solution)/shard_map/ppermute | solution.py:241
  247.0 2.3 collective-permute-start.10
  249.4 12.4 %collective-permute-done.16 = bf16[256,1024]{1,0:T(8,128)(2,1)} collective-permute-done((bf16[256,1024]{1,0:T(8,128)(2,1)}, bf16[256,1024]{1,0:T(8,128)(2,1)}, u32[]{:S(2)}, u32[]{:S(2)}) %collective-permute-start.16) | collective-permute-done | bytes 524320 | tf_op jit(solution)/shard_map/ppermute | solution.py:241
  264.0 7.2 %collective-permute-done.10 = bf16[256,1024]{1,0:T(8,128)(2,1)S(1)} collective-permute-done((bf16[256,1024]{1,0:T(8,128)(2,1)}, bf16[256,1024]{1,0:T(8,128)(2,1)S(1)}, u32[]{:S(2)}, u32[]{:S(2)}) %collective-permute-start.10) | collective-permute-done | bytes 524320 | tf_op jit(solution)/shard_map/ppermute | solution.py:241
  271.2 2.7 subtract_add_fusion
  279.3 10.6 %collective-permute-done.18 = bf16[256,1024]{1,0:T(8,128)(2,1)S(1)} collective-permute-done((bf16[256,1024]{1,0:T(8,128)(2,1)S(1)}, bf16[256,1024]{1,0:T(8,128)(2,1)S(1)}, u32[]{:S(2)}, u32[]{:S(2)}) %collective-permute-start.18) | collective-permute-done | bytes 524320 | tf_op jit(solution)/shard_map/ppermute | solution.py:190
  293.2 7.5 %collective-permute-done.20 = bf16[256,1024]{1,0:T(8,128)(2,1)} collective-permute-done((bf16[256,1024]{1,0:T(8,128)(2,1)S(1)}, bf16[256,1024]{1,0:T(8,128)(2,1)}, u32[]{:S(2)}, u32[]{:S(2)}) %collective-permute-start.20) | collective-permute-done | bytes 524320 | tf_op jit(solution)/shard_map/ppermute | solution.py:190
  302.7 2.5 convolution_convert_fusion.6
  306.0 2.8 fusion.25
  308.9 2.3 copy.369
  311.2 5.7 %fusion.29 = bf16[1024,2,64]{2,1,0:T(2,128)(2,1)} fusion(f32[1024,4,2]{1,2,0:T(2,128)S(1)} %copy-done.27, bf16[1024,4,64]{2,1,0:T(4,128)(2,1)} %copy.369), kind=kOutput, calls=%fused_computation.67 | convolution fusion | flops 6553600 | bytes 819200 | tf_op jit(solution)/shard_map/thr,thd->trd/dot_general | solution.py:358
  316.9 6.0 %convolution_multiply_fusion.4 = bf16[1024,4,2]{1,2,0:T(2,128)(2,1)} fusion(bf16[1024,4,64]{2,1,0:T(4,128)(2,1)} %copy.369, f32[1024,2,64]{2,1,0:T(2,128)} %copy.348), kind=kOutput, calls=%fused_computation.58 | convolution fusion | flops 6307840 | bytes 1064960 | tf_op jit(solution)/shard_map/thd,trd->thr/dot_general | solution.py:351
  327.9 2.6 multiply_reduce_fusion
  336.3 2.3 copy.366
  338.6 6.7 %convolution_multiply_fusion.5 = bf16[1024,4,2]{1,2,0:T(2,128)(2,1)} fusion(bf16[1024,4,64]{2,1,0:T(4,128)(2,1)} %copy.366, f32[1024,2,32]{2,1,0:T(2,128)} %copy-done.24, f32[1024,2,32]{2,1,0:T(2,128)S(1)} %copy-done.23), kind=kOutput, calls=%fused_computation.59 | convolution fusion | flops 6438912 | bytes 1064960 | tf_op jit(solution)/shard_map/thd,trd->thr/dot_general | solution.py:350
  345.3 4.5 convolution_multiply_fusion.3
  356.4 3.1 add_convert_fusion.3
  361.7 2.3 copy.377
  364.0 2.3 copy.361
  366.3 9.2 %convolution_multiply_fusion.1 = bf16[1024,4,6]{2,1,0:T(4,128)(2,1)} fusion(bf16[1024,4,64]{2,1,0:T(4,128)(2,1)} %copy.361, f32[1024,6,32]{2,1,0:T(8,128)} %copy-done.9, f32[1024,6,32]{2,1,0:T(8,128)} %copy-done.8), kind=kOutput, calls=%fused_computation.54 | convolution fusion | flops 19316736 | bytes 2146304 | tf_op jit(solution)/shard_map/thd,trd->thr/dot_general | solution.py:349
  377.5 5.5 convolution_multiply_fusion
  383.0 2.7 add_convert_fusion.1
  390.8 2.6 collective-permute-start.21
  396.5 5.1 collective-permute-done.21
  402.5 7.1 %collective-permute-done.22 = bf16[1024,160]{0,1:T(8,128)(2,1)S(1)} collective-permute-done((bf16[1024,160]{0,1:T(8,128)(2,1)S(1)}, bf16[1024,160]{0,1:T(8,128)(2,1)S(1)}, u32[]{:S(2)}, u32[]{:S(2)}) %collective-permute-start.22) | collective-permute-done | bytes 327712 | tf_op jit(solution)/shard_map/ppermute | solution.py:174
  415.8 9.6 %collective-permute-done.24 = bf16[256,1024]{1,0:T(8,128)(2,1)S(1)} collective-permute-done((bf16[256,1024]{1,0:T(8,128)(2,1)S(1)}, bf16[256,1024]{1,0:T(8,128)(2,1)S(1)}, u32[]{:S(2)}, u32[]{:S(2)}) %collective-permute-start.24) | collective-permute-done | bytes 524320 | tf_op jit(solution)/shard_map/ppermute | solution.py:174
  426.4 11.2 %collective-permute-done.25 = bf16[256,1024]{1,0:T(8,128)(2,1)S(1)} collective-permute-done((bf16[256,1024]{1,0:T(8,128)(2,1)S(1)}, bf16[256,1024]{1,0:T(8,128)(2,1)S(1)}, u32[]{:S(2)}, u32[]{:S(2)}) %collective-permute-start.25) | collective-permute-done | bytes 524320 | tf_op jit(solution)/shard_map/ppermute | solution.py:174
  443.1 2.4 reshape.341
  445.6 2.5 dynamic-slice_convert_fusion
  450.9 9.8 %collective-permute-done.27 = bf16[2,2,58752]{2,1,0:T(2,128)(2,1)S(1)} collective-permute-done((bf16[2,2,58752]{2,1,0:T(2,128)(2,1)S(1)}, bf16[2,2,58752]{2,1,0:T(2,128)(2,1)S(1)}, u32[]{:S(2)}, u32[]{:S(2)}) %collective-permute-start.27) | collective-permute-done | bytes 470048 | tf_op jit(solution)/shard_map/ppermute | solution.py:213
  463.9 4.4 collective-permute-done.28
  469.3 2.4 collective-permute-start.29
  472.4 4.0 collective-permute-done.29
  477.8 6.4 %collective-permute-done.30 = bf16[1,58752]{1,0:T(2,128)(2,1)S(1)} collective-permute-done((bf16[1,58752]{1,0:T(2,128)(2,1)S(1)}, bf16[1,58752]{1,0:T(2,128)(2,1)S(1)}, u32[]{:S(2)}, u32[]{:S(2)}) %collective-permute-start.30) | collective-permute-done | bytes 117536 | tf_op jit(solution)/shard_map/ppermute | solution.py:218
  485.1 7.8 %collective-permute-start.31 = (bf16[2,58752]{1,0:T(2,128)(2,1)S(1)}, bf16[2,58752]{1,0:T(2,128)(2,1)S(1)}, u32[]{:S(2)}, u32[]{:S(2)}) collective-permute-start(bf16[2,58752]{1,0:T(2,128)(2,1)S(1)} %maximum_bitcast_fusion), channel_id=1, source_target_pairs={{0,8},{4,12},{8,0},{12,4},{16,24},{20,28},{24,16},{28,20},{1,9},{5... | collective-permute-start | bytes 705032 | tf_op jit(solution)/shard_map/ppermute | solution.py:218
  492.9 4.1 collective-permute-done.31
  501.3 7.1 %collective-permute-done.32 = bf16[4,58752]{1,0:T(4,128)(2,1)S(1)} collective-permute-done((bf16[4,58752]{1,0:T(4,128)(2,1)S(1)}, bf16[4,58752]{1,0:T(4,128)(2,1)S(1)}, u32[]{:S(2)}, u32[]{:S(2)}) %collective-permute-start.32) | collective-permute-done | bytes 470048 | tf_op jit(solution)/shard_map/ppermute | solution.py:218
  514.3 2.6 fusion.47
  526.5 6.8 %all-gather.2.cloned.1.call-done = bf16[1037,640]{0,1:T(8,128)(2,1)} async-done(((bf16[1037,160]{0,1:T(8,128)(2,1)}), bf16[1037,640]{0,1:T(8,128)(2,1)}) %all-gather.2.cloned.1.call-update) | async-done | bytes 1327376 | tf_op jit(solution)/shard_map/all_gather | solution.py:414
  535.1 3.2 slice.239
  538.4 3.2 copy.389
  (343 shorter events, 170.3 us)
Async XLA Ops:
  7.2 206.9 %copy-start = (bf16[704,1024]{1,0:T(8,128)(2,1)S(1)}, bf16[704,1024]{1,0:T(8,128)(2,1)}, u32[]{:S(2)}) copy-start(bf16[704,1024]{1,0:T(8,128)(2,1)} %param.20) | copy-start | bytes 4325380
  7.2 432.2 %all-reduce.7.cloned.1.call-start = ((), (), s32[]{:S(2)}) async-start(), calls=%async_computation.1 | async-start | bytes 8650752 | tf_op jit(solution)/shard_map/psum | solution.py:334
  7.3 8.7 %copy-start.63 = (s32[1,1024]{1,0:T(1,128)S(1)}, s32[1,1024]{1,0:T(1,128)}, u32[]{:S(2)}) copy-start(s32[1,1024]{1,0:T(1,128)} %param.12) | copy-start | bytes 12292
  9.2 8.2 %copy-start.64 = (f32[256]{0:T(256)}, f32[256]{0:T(256)S(1)}, u32[]{:S(2)}) copy-start(f32[256]{0:T(256)S(1)} %get-tuple-element.222) | copy-start | bytes 3076
  11.2 26.7 %collective-permute-start.1 = (bf16[256,1024]{1,0:T(8,128)(2,1)}, bf16[256,1024]{1,0:T(8,128)(2,1)}, u32[]{:S(2)}, u32[]{:S(2)}) collective-permute-start(bf16[256,1024]{1,0:T(8,128)(2,1)} %get-tuple-element.168), channel_id=1, source_target_pairs={{0,2},{1,3},{2,0},{3,1},{4,6},{5,7},{6,4},{7,5},{8,10},{9,11},{10,... | collective-permute-start | bytes 1572872 | tf_op jit(solution)/shard_map/ppermute | solution.py:190
  14.2 22.6 %collective-permute-start = (bf16[256,1024]{1,0:T(8,128)(2,1)}, bf16[256,1024]{1,0:T(8,128)(2,1)}, u32[]{:S(2)}, u32[]{:S(2)}) collective-permute-start(bf16[256,1024]{1,0:T(8,128)(2,1)} %get-tuple-element.168), channel_id=1, source_target_pairs={{0,1},{1,2},{2,3},{3,0},{4,5},{5,6},{6,7},{7,4},{8,9},{9,10},{10,1... | collective-permute-start | bytes 1572872 | tf_op jit(solution)/shard_map/ppermute | solution.py:190
  14.2 24.8 %collective-permute-start.2 = (bf16[256,1024]{1,0:T(8,128)(2,1)}, bf16[256,1024]{1,0:T(8,128)(2,1)}, u32[]{:S(2)}, u32[]{:S(2)}) collective-permute-start(bf16[256,1024]{1,0:T(8,128)(2,1)} %get-tuple-element.168), channel_id=1, source_target_pairs={{0,3},{1,0},{2,1},{3,2},{4,7},{5,4},{6,5},{7,6},{8,11},{9,8},{10,9... | collective-permute-start | bytes 1572872 | tf_op jit(solution)/shard_map/ppermute | solution.py:190
  18.4 21.7 %copy-start.51 = (bf16[1024,40]{0,1:T(8,128)(2,1)S(1)}, bf16[1024,40]{0,1:T(8,128)(2,1)}, u32[]{:S(2)}) copy-start(bf16[1024,40]{0,1:T(8,128)(2,1)} %param.14) | copy-start | bytes 245764
  40.1 9.2 %copy-start.6 = (bf16[1024,1024]{1,0:T(8,128)(2,1)}, bf16[1024,1024]{1,0:T(8,128)(2,1)S(1)}, u32[]{:S(2)}) copy-start(bf16[1024,1024]{1,0:T(8,128)(2,1)S(1)} %constant_dynamic-update-slice_fusion.8) | copy-start | bytes 6291460
  112.9 8.3 %copy-start.8 = (f32[1024,6,32]{2,1,0:T(8,128)}, f32[1024,6,32]{2,1,0:T(8,128)S(1)}, u32[]{:S(2)}) copy-start(f32[1024,6,32]{2,1,0:T(8,128)S(1)} %get-tuple-element.169) | copy-start | bytes 2359300
  112.9 8.3 %copy-start.9 = (f32[1024,6,32]{2,1,0:T(8,128)}, f32[1024,6,32]{2,1,0:T(8,128)S(1)}, u32[]{:S(2)}) copy-start(f32[1024,6,32]{2,1,0:T(8,128)S(1)} %get-tuple-element.170) | copy-start | bytes 2359300
  140.0 27.4 %copy-start.13 = (bf16[256,1024]{1,0:T(8,128)(2,1)S(1)}, bf16[256,1024]{1,0:T(8,128)(2,1)}, u32[]{:S(2)}) copy-start(bf16[256,1024]{1,0:T(8,128)(2,1)} %param.11) | copy-start | bytes 1572868
  140.2 28.4 %copy-start.55 = (f32[1024]{0:T(1024)S(1)}, f32[1024]{0:T(1024)}, u32[]{:S(2)}) copy-start(f32[1024]{0:T(1024)} %param.17) | copy-start | bytes 12292
  140.2 12.5 %collective-permute-start.3 = (bf16[256,1024]{1,0:T(8,128)(2,1)S(1)}, bf16[256,1024]{1,0:T(8,128)(2,1)S(1)}, u32[]{:S(2)}, u32[]{:S(2)}) collective-permute-start(bf16[256,1024]{1,0:T(8,128)(2,1)S(1)} %get-tuple-element.191), channel_id=1, source_target_pairs={{0,1},{1,2},{2,3},{3,0},{4,5},{5,6},{6,7},{7,4},{8,9},{9,10},{10,1... | collective-permute-start | bytes 1572872 | tf_op jit(solution)/shard_map/ppermute | solution.py:174
  140.2 14.1 %collective-permute-start.5 = (bf16[256,1024]{1,0:T(8,128)(2,1)S(1)}, bf16[256,1024]{1,0:T(8,128)(2,1)S(1)}, u32[]{:S(2)}, u32[]{:S(2)}) collective-permute-start(bf16[256,1024]{1,0:T(8,128)(2,1)S(1)} %get-tuple-element.192), channel_id=1, source_target_pairs={{0,3},{1,0},{2,1},{3,2},{4,7},{5,4},{6,5},{7,6},{8,11},{9,8},{10,9... | collective-permute-start | bytes 1572872 | tf_op jit(solution)/shard_map/ppermute | solution.py:174
  142.0 25.5 %collective-permute-start.4 = (bf16[256,1024]{1,0:T(8,128)(2,1)S(1)}, bf16[256,1024]{1,0:T(8,128)(2,1)S(1)}, u32[]{:S(2)}, u32[]{:S(2)}) collective-permute-start(bf16[256,1024]{1,0:T(8,128)(2,1)S(1)} %get-tuple-element.193), channel_id=1, source_target_pairs={{0,2},{1,3},{2,0},{3,1},{4,6},{5,7},{6,4},{7,5},{8,10},{9,11},{10,... | collective-permute-start | bytes 1572872 | tf_op jit(solution)/shard_map/ppermute | solution.py:174
  143.4 43.1 %collective-permute-start.13 = (bf16[256,1024]{1,0:T(8,128)(2,1)S(1)}, bf16[256,1024]{1,0:T(8,128)(2,1)S(1)}, u32[]{:S(2)}, u32[]{:S(2)}) collective-permute-start(bf16[256,1024]{1,0:T(8,128)(2,1)S(1)} %copy-done.42), channel_id=1, source_target_pairs={{0,2},{1,3},{2,0},{3,1},{4,6},{5,7},{6,4},{7,5},{8,10},{9,11},{10,... | collective-permute-start | bytes 1572872 | tf_op jit(solution)/shard_map/ppermute | solution.py:230
  144.0 42.4 %collective-permute-start.12 = (bf16[256,1024]{1,0:T(8,128)(2,1)S(1)}, bf16[256,1024]{1,0:T(8,128)(2,1)S(1)}, u32[]{:S(2)}, u32[]{:S(2)}) collective-permute-start(bf16[256,1024]{1,0:T(8,128)(2,1)S(1)} %copy-done.42), channel_id=1, source_target_pairs={{0,1},{1,2},{2,3},{3,0},{4,5},{5,6},{6,7},{7,4},{8,9},{9,10},{10,1... | collective-permute-start | bytes 1572872 | tf_op jit(solution)/shard_map/ppermute | solution.py:230
  152.7 35.3 %collective-permute-start.14 = (bf16[256,1024]{1,0:T(8,128)(2,1)S(1)}, bf16[256,1024]{1,0:T(8,128)(2,1)S(1)}, u32[]{:S(2)}, u32[]{:S(2)}) collective-permute-start(bf16[256,1024]{1,0:T(8,128)(2,1)S(1)} %copy-done.42), channel_id=1, source_target_pairs={{0,3},{1,0},{2,1},{3,2},{4,7},{5,4},{6,5},{7,6},{8,11},{9,8},{10,9... | collective-permute-start | bytes 1572872 | tf_op jit(solution)/shard_map/ppermute | solution.py:230
  168.0 18.6 %copy-start.10 = (f32[256,1024]{1,0:T(8,128)}, f32[256,1024]{1,0:T(8,128)S(1)}, u32[]{:S(2)}) copy-start(f32[256,1024]{1,0:T(8,128)S(1)} %get-tuple-element.166) | copy-start | bytes 3145732
  168.6 18.0 %copy-start.66 = (f32[256]{0:T(256)}, f32[256]{0:T(256)S(1)}, u32[]{:S(2)}) copy-start(f32[256]{0:T(256)S(1)} %get-tuple-element.224) | copy-start | bytes 3076
  168.7 41.9 %copy-start.71 = (bf16[1024,704]{0,1:T(8,128)(2,1)S(1)}, bf16[1024,704]{0,1:T(8,128)(2,1)}, u32[]{:S(2)}) copy-start(bf16[1024,704]{0,1:T(8,128)(2,1)} %param.19) | copy-start | bytes 4325380
  168.8 30.5 %collective-permute-start.8 = (bf16[256,1024]{1,0:T(8,128)(2,1)S(1)}, bf16[256,1024]{1,0:T(8,128)(2,1)S(1)}, u32[]{:S(2)}, u32[]{:S(2)}) collective-permute-start(bf16[256,1024]{1,0:T(8,128)(2,1)S(1)} %multiply_convert_fusion.6), channel_id=1, source_target_pairs={{0,3},{1,0},{2,1},{3,2},{4,7},{5,4},{6,5},{7,6},{8,11},{9,8},{10,9... | collective-permute-start | bytes 1572872 | tf_op jit(solution)/shard_map/ppermute | solution.py:230
  168.8 41.8 %collective-permute-start.7 = (bf16[256,1024]{1,0:T(8,128)(2,1)S(1)}, bf16[256,1024]{1,0:T(8,128)(2,1)S(1)}, u32[]{:S(2)}, u32[]{:S(2)}) collective-permute-start(bf16[256,1024]{1,0:T(8,128)(2,1)S(1)} %multiply_convert_fusion.6), channel_id=1, source_target_pairs={{0,2},{1,3},{2,0},{3,1},{4,6},{5,7},{6,4},{7,5},{8,10},{9,11},{10,... | collective-permute-start | bytes 1572872 | tf_op jit(solution)/shard_map/ppermute | solution.py:230
  186.4 24.2 %collective-permute-start.6 = (bf16[256,1024]{1,0:T(8,128)(2,1)S(1)}, bf16[256,1024]{1,0:T(8,128)(2,1)S(1)}, u32[]{:S(2)}, u32[]{:S(2)}) collective-permute-start(bf16[256,1024]{1,0:T(8,128)(2,1)S(1)} %multiply_convert_fusion.6), channel_id=1, source_target_pairs={{0,1},{1,2},{2,3},{3,0},{4,5},{5,6},{6,7},{7,4},{8,9},{9,10},{10,1... | collective-permute-start | bytes 1572872 | tf_op jit(solution)/shard_map/ppermute | solution.py:230
  188.0 24.3 %copy-start.70 = (bf16[1024,704]{0,1:T(8,128)(2,1)S(1)}, bf16[1024,704]{0,1:T(8,128)(2,1)}, u32[]{:S(2)}) copy-start(bf16[1024,704]{0,1:T(8,128)(2,1)} %param.18) | copy-start | bytes 4325380
  223.0 41.0 %collective-permute-start.9 = (bf16[256,1024]{1,0:T(8,128)(2,1)}, bf16[256,1024]{1,0:T(8,128)(2,1)}, u32[]{:S(2)}, u32[]{:S(2)}) collective-permute-start(bf16[256,1024]{1,0:T(8,128)(2,1)} %get-tuple-element.188), channel_id=1, source_target_pairs={{0,1},{1,2},{2,3},{3,0},{4,5},{5,6},{6,7},{7,4},{8,9},{9,10},{10,1... | collective-permute-start | bytes 1572872 | tf_op jit(solution)/shard_map/ppermute | solution.py:241
  223.0 41.0 %collective-permute-start.11 = (bf16[256,1024]{1,0:T(8,128)(2,1)}, bf16[256,1024]{1,0:T(8,128)(2,1)}, u32[]{:S(2)}, u32[]{:S(2)}) collective-permute-start(bf16[256,1024]{1,0:T(8,128)(2,1)} %get-tuple-element.189), channel_id=1, source_target_pairs={{0,3},{1,0},{2,1},{3,2},{4,7},{5,4},{6,5},{7,6},{8,11},{9,8},{10,9... | collective-permute-start | bytes 1572872 | tf_op jit(solution)/shard_map/ppermute | solution.py:241
  228.5 7.4 %copy-start.38 = (bf16[1024,1024]{1,0:T(8,128)(2,1)}, bf16[1024,1024]{1,0:T(8,128)(2,1)S(1)}, u32[]{:S(2)}) copy-start(bf16[1024,1024]{1,0:T(8,128)(2,1)S(1)} %add_convert_fusion.2) | copy-start | bytes 6291460
  229.8 17.3 %collective-permute-start.15 = (bf16[256,1024]{1,0:T(8,128)(2,1)}, bf16[256,1024]{1,0:T(8,128)(2,1)}, u32[]{:S(2)}, u32[]{:S(2)}) collective-permute-start(bf16[256,1024]{1,0:T(8,128)(2,1)} %get-tuple-element.185), channel_id=1, source_target_pairs={{0,1},{1,2},{2,3},{3,0},{4,5},{5,6},{6,7},{7,4},{8,9},{9,10},{10,1... | collective-permute-start | bytes 1572872 | tf_op jit(solution)/shard_map/ppermute | solution.py:241
  229.8 19.6 %collective-permute-start.17 = (bf16[256,1024]{1,0:T(8,128)(2,1)}, bf16[256,1024]{1,0:T(8,128)(2,1)}, u32[]{:S(2)}, u32[]{:S(2)}) collective-permute-start(bf16[256,1024]{1,0:T(8,128)(2,1)} %get-tuple-element.186), channel_id=1, source_target_pairs={{0,3},{1,0},{2,1},{3,2},{4,7},{5,4},{6,5},{7,6},{8,11},{9,8},{10,9... | collective-permute-start | bytes 1572872 | tf_op jit(solution)/shard_map/ppermute | solution.py:241
  231.5 30.3 %collective-permute-start.16 = (bf16[256,1024]{1,0:T(8,128)(2,1)}, bf16[256,1024]{1,0:T(8,128)(2,1)}, u32[]{:S(2)}, u32[]{:S(2)}) collective-permute-start(bf16[256,1024]{1,0:T(8,128)(2,1)} %get-tuple-element.187), channel_id=1, source_target_pairs={{0,2},{1,3},{2,0},{3,1},{4,6},{5,7},{6,4},{7,5},{8,10},{9,11},{10,... | collective-permute-start | bytes 1572872 | tf_op jit(solution)/shard_map/ppermute | solution.py:241
  238.6 25.1 %copy-start.11 = (f32[256,1024]{1,0:T(8,128)S(1)}, f32[256,1024]{1,0:T(8,128)}, u32[]{:S(2)}) copy-start(f32[256,1024]{1,0:T(8,128)} %copy-done.10) | copy-start | bytes 3145732
  238.6 25.1 %copy-start.56 = (f32[1024]{0:T(1024)S(1)}, f32[1024]{0:T(1024)}, u32[]{:S(2)}) copy-start(f32[1024]{0:T(1024)} %param.17) | copy-start | bytes 12292
  238.6 25.1 %copy-start.67 = (f32[256]{0:T(256)S(1)}, f32[256]{0:T(256)}, u32[]{:S(2)}) copy-start(f32[256]{0:T(256)} %copy-done.66) | copy-start | bytes 3076
  247.0 24.1 %copy-start.43 = (bf16[256,1024]{1,0:T(8,128)(2,1)S(1)}, bf16[256,1024]{1,0:T(8,128)(2,1)}, u32[]{:S(2)}) copy-start(bf16[256,1024]{1,0:T(8,128)(2,1)} %param.21) | copy-start | bytes 1572868
  247.0 24.1 %copy-start.69 = (f32[256]{0:T(256)S(1)}, f32[256]{0:T(256)}, u32[]{:S(2)}) copy-start(f32[256]{0:T(256)} %get-tuple-element.223) | copy-start | bytes 3076
  247.0 24.1 %collective-permute-start.10 = (bf16[256,1024]{1,0:T(8,128)(2,1)}, bf16[256,1024]{1,0:T(8,128)(2,1)S(1)}, u32[]{:S(2)}, u32[]{:S(2)}) collective-permute-start(bf16[256,1024]{1,0:T(8,128)(2,1)} %get-tuple-element.190), channel_id=1, source_target_pairs={{0,2},{1,3},{2,0},{3,1},{4,6},{5,7},{6,4},{7,5},{8,10},{9,11},{10,... | collective-permute-start | bytes 1572872 | tf_op jit(solution)/shard_map/ppermute | solution.py:241
  276.2 13.6 %collective-permute-start.18 = (bf16[256,1024]{1,0:T(8,128)(2,1)S(1)}, bf16[256,1024]{1,0:T(8,128)(2,1)S(1)}, u32[]{:S(2)}, u32[]{:S(2)}) collective-permute-start(bf16[256,1024]{1,0:T(8,128)(2,1)S(1)} %get-tuple-element.164), channel_id=1, source_target_pairs={{0,1},{1,2},{2,3},{3,0},{4,5},{5,6},{6,7},{7,4},{8,9},{9,10},{10,1... | collective-permute-start | bytes 1572872 | tf_op jit(solution)/shard_map/ppermute | solution.py:190
  276.2 14.9 %collective-permute-start.19 = (bf16[256,1024]{1,0:T(8,128)(2,1)S(1)}, bf16[256,1024]{1,0:T(8,128)(2,1)}, u32[]{:S(2)}, u32[]{:S(2)}) collective-permute-start(bf16[256,1024]{1,0:T(8,128)(2,1)S(1)} %get-tuple-element.164), channel_id=1, source_target_pairs={{0,2},{1,3},{2,0},{3,1},{4,6},{5,7},{6,4},{7,5},{8,10},{9,11},{10,... | collective-permute-start | bytes 1572872 | tf_op jit(solution)/shard_map/ppermute | solution.py:190
  277.7 23.0 %collective-permute-start.20 = (bf16[256,1024]{1,0:T(8,128)(2,1)S(1)}, bf16[256,1024]{1,0:T(8,128)(2,1)}, u32[]{:S(2)}, u32[]{:S(2)}) collective-permute-start(bf16[256,1024]{1,0:T(8,128)(2,1)S(1)} %get-tuple-element.164), channel_id=1, source_target_pairs={{0,3},{1,0},{2,1},{3,2},{4,7},{5,4},{6,5},{7,6},{8,11},{9,8},{10,9... | collective-permute-start | bytes 1572872 | tf_op jit(solution)/shard_map/ppermute | solution.py:190
  279.2 254.2 %all-gather.2.cloned.1.call-start = ((), (), s32[]{:S(2)}) async-start(), calls=%async_computation | async-start | bytes 1843200 | tf_op jit(solution)/shard_map/all_gather | solution.py:414
  279.2 23.4 %copy-start.50 = (bf16[256,1024]{1,0:T(8,128)(2,1)S(1)}, bf16[256,1024]{1,0:T(8,128)(2,1)}, u32[]{:S(2)}) copy-start(bf16[256,1024]{1,0:T(8,128)(2,1)} %param.16) | copy-start | bytes 1572868
  289.8 16.2 %slice-start = ((s8[8388608]{0:T(1024)(128)(4,1)}), s8[4194304]{0:T(1024)(128)(4,1)S(1)}, s32[]{:S(2)}) async-start(s8[8388608]{0:T(1024)(128)(4,1)} %bitcast.131), calls=%async_computation.2 | async-start | bytes 8388608
  311.2 11.7 %copy-start.5 = (f32[4,512,512]{1,2,0:T(8,128)S(1)}, f32[4,512,512]{1,2,0:T(8,128)}, u32[]{:S(2)}) copy-start(f32[4,512,512]{1,2,0:T(8,128)} %copy-done.3) | copy-start | bytes 12582916
  338.6 6.7 %copy-start.26 = (f32[1024,4,2]{1,2,0:T(2,128)S(1)}, f32[1024,4,2]{1,2,0:T(2,128)}, u32[]{:S(2)}) copy-start(f32[1024,4,2]{1,2,0:T(2,128)} %copy.398) | copy-start | bytes 98308
  338.6 6.7 %copy-start.47 = (bf16[1024,4,64]{2,1,0:T(4,128)(2,1)S(1)}, bf16[1024,4,64]{2,1,0:T(4,128)(2,1)}, u32[]{:S(2)}) copy-start(bf16[1024,4,64]{2,1,0:T(4,128)(2,1)} %copy.366) | copy-start | bytes 1572868
  345.3 7.9 %copy-start.48 = (bf16[512,4,64]{0,2,1:T(8,128)(2,1)S(1)}, bf16[512,4,64]{0,2,1:T(8,128)(2,1)}, u32[]{:S(2)}) copy-start(bf16[512,4,64]{0,2,1:T(8,128)(2,1)} %fusion.39) | copy-start | bytes 786436
  349.8 6.6 %copy-start.16 = (f32[1024,32]{1,0:T(8,128)S(1)}, f32[1024,32]{1,0:T(8,128)}, u32[]{:S(2)}) copy-start(f32[1024,32]{1,0:T(8,128)} %get-tuple-element.218) | copy-start | bytes 393220
  390.8 10.9 %collective-permute-start.21 = (bf16[1024,160]{0,1:T(8,128)(2,1)S(1)}, bf16[1024,160]{0,1:T(8,128)(2,1)S(1)}, u32[]{:S(2)}, u32[]{:S(2)}) collective-permute-start(bf16[1024,160]{0,1:T(8,128)(2,1)S(1)} %get-tuple-element.196), channel_id=1, source_target_pairs={{0,1},{1,2},{2,3},{3,0},{4,5},{5,6},{6,7},{7,4},{8,9},{9,10},{10,1... | collective-permute-start | bytes 983048 | tf_op jit(solution)/shard_map/ppermute | solution.py:174
  393.3 9.2 %collective-permute-start.23 = (bf16[1024,160]{0,1:T(8,128)(2,1)S(1)}, bf16[1024,160]{0,1:T(8,128)(2,1)S(1)}, u32[]{:S(2)}, u32[]{:S(2)}) collective-permute-start(bf16[1024,160]{0,1:T(8,128)(2,1)S(1)} %get-tuple-element.197), channel_id=1, source_target_pairs={{0,3},{1,0},{2,1},{3,2},{4,7},{5,4},{6,5},{7,6},{8,11},{9,8},{10,9... | collective-permute-start | bytes 983048 | tf_op jit(solution)/shard_map/ppermute | solution.py:174
  394.4 15.2 %collective-permute-start.22 = (bf16[1024,160]{0,1:T(8,128)(2,1)S(1)}, bf16[1024,160]{0,1:T(8,128)(2,1)S(1)}, u32[]{:S(2)}, u32[]{:S(2)}) collective-permute-start(bf16[1024,160]{0,1:T(8,128)(2,1)S(1)} %get-tuple-element.198), channel_id=1, source_target_pairs={{0,2},{1,3},{2,0},{3,1},{4,6},{5,7},{6,4},{7,5},{8,10},{9,11},{10,... | collective-permute-start | bytes 983048 | tf_op jit(solution)/shard_map/ppermute | solution.py:174
  412.2 13.2 %collective-permute-start.24 = (bf16[256,1024]{1,0:T(8,128)(2,1)S(1)}, bf16[256,1024]{1,0:T(8,128)(2,1)S(1)}, u32[]{:S(2)}, u32[]{:S(2)}) collective-permute-start(bf16[256,1024]{1,0:T(8,128)(2,1)S(1)} %get-tuple-element.180), channel_id=1, source_target_pairs={{0,1},{1,2},{2,3},{3,0},{4,5},{5,6},{6,7},{7,4},{8,9},{9,10},{10,1... | collective-permute-start | bytes 1572872 | tf_op jit(solution)/shard_map/ppermute | solution.py:174
  412.2 14.2 %collective-permute-start.26 = (bf16[256,1024]{1,0:T(8,128)(2,1)S(1)}, bf16[256,1024]{1,0:T(8,128)(2,1)S(1)}, u32[]{:S(2)}, u32[]{:S(2)}) collective-permute-start(bf16[256,1024]{1,0:T(8,128)(2,1)S(1)} %get-tuple-element.181), channel_id=1, source_target_pairs={{0,3},{1,0},{2,1},{3,2},{4,7},{5,4},{6,5},{7,6},{8,11},{9,8},{10,9... | collective-permute-start | bytes 1572872 | tf_op jit(solution)/shard_map/ppermute | solution.py:174
  414.1 23.6 %collective-permute-start.25 = (bf16[256,1024]{1,0:T(8,128)(2,1)S(1)}, bf16[256,1024]{1,0:T(8,128)(2,1)S(1)}, u32[]{:S(2)}, u32[]{:S(2)}) collective-permute-start(bf16[256,1024]{1,0:T(8,128)(2,1)S(1)} %get-tuple-element.182), channel_id=1, source_target_pairs={{0,2},{1,3},{2,0},{3,1},{4,6},{5,7},{6,4},{7,5},{8,10},{9,11},{10,... | collective-permute-start | bytes 1572872 | tf_op jit(solution)/shard_map/ppermute | solution.py:174
  415.2 22.5 %copy-start.14 = (bf16[256,1024]{1,0:T(8,128)(2,1)S(1)}, bf16[256,1024]{1,0:T(8,128)(2,1)}, u32[]{:S(2)}) copy-start(bf16[256,1024]{1,0:T(8,128)(2,1)} %param.11) | copy-start | bytes 1572868
  415.2 22.5 %copy-start.58 = (f32[1024]{0:T(1024)S(1)}, f32[1024]{0:T(1024)}, u32[]{:S(2)}) copy-start(f32[1024]{0:T(1024)} %param.13) | copy-start | bytes 12292
  415.2 22.5 %copy-start.65 = (f32[256]{0:T(256)S(1)}, f32[256]{0:T(256)}, u32[]{:S(2)}) copy-start(f32[256]{0:T(256)} %copy-done.64) | copy-start | bytes 3076
  448.6 12.1 %collective-permute-start.27 = (bf16[2,2,58752]{2,1,0:T(2,128)(2,1)S(1)}, bf16[2,2,58752]{2,1,0:T(2,128)(2,1)S(1)}, u32[]{:S(2)}, u32[]{:S(2)}) collective-permute-start(bf16[2,2,58752]{2,1,0:T(2,128)(2,1)S(1)} %bitcast.150), channel_id=1, source_target_pairs={{0,4},{4,0},{8,12},{12,8},{16,20},{20,16},{24,28},{28,24},{1,5},{5... | collective-permute-start | bytes 1410056 | tf_op jit(solution)/shard_map/ppermute | solution.py:213
  462.0 6.2 %collective-permute-start.28 = (bf16[2,58752]{1,0:T(2,128)(2,1)S(1)}, bf16[2,58752]{1,0:T(2,128)(2,1)S(1)}, u32[]{:S(2)}, u32[]{:S(2)}) collective-permute-start(bf16[2,58752]{1,0:T(2,128)(2,1)S(1)} %bitcast.151), channel_id=1, source_target_pairs={{0,8},{4,12},{8,0},{12,4},{16,24},{20,28},{24,16},{28,20},{1,9},{5... | collective-permute-start | bytes 705032 | tf_op jit(solution)/shard_map/ppermute | solution.py:213
  469.3 7.1 %collective-permute-start.29 = (bf16[58752]{0:T(1024)(128)(2,1)S(1)}, bf16[58752]{0:T(1024)(128)(2,1)S(1)}, u32[]{:S(2)}, u32[]{:S(2)}) collective-permute-start(bf16[58752]{0:T(1024)(128)(2,1)S(1)} %convert_reduce_fusion), channel_id=1, source_target_pairs={{0,16},{4,20},{8,24},{12,28},{16,0},{20,4},{24,8},{28,12},{1,17},{... | collective-permute-start | bytes 352520 | tf_op jit(solution)/shard_map/ppermute | solution.py:213
  476.5 7.7 %collective-permute-start.30 = (bf16[1,58752]{1,0:T(2,128)(2,1)S(1)}, bf16[1,58752]{1,0:T(2,128)(2,1)S(1)}, u32[]{:S(2)}, u32[]{:S(2)}) collective-permute-start(bf16[1,58752]{1,0:T(2,128)(2,1)S(1)} %broadcast_in_dim.142), channel_id=1, source_target_pairs={{0,16},{4,20},{8,24},{12,28},{16,0},{20,4},{24,8},{28,12},{1,17},{... | collective-permute-start | bytes 352520 | tf_op jit(solution)/shard_map/ppermute | solution.py:218
  485.1 11.9 %collective-permute-start.31 = (bf16[2,58752]{1,0:T(2,128)(2,1)S(1)}, bf16[2,58752]{1,0:T(2,128)(2,1)S(1)}, u32[]{:S(2)}, u32[]{:S(2)}) collective-permute-start(bf16[2,58752]{1,0:T(2,128)(2,1)S(1)} %maximum_bitcast_fusion), channel_id=1, source_target_pairs={{0,8},{4,12},{8,0},{12,4},{16,24},{20,28},{24,16},{28,20},{1,9},{5... | collective-permute-start | bytes 705032 | tf_op jit(solution)/shard_map/ppermute | solution.py:218
  499.8 8.7 %collective-permute-start.32 = (bf16[4,58752]{1,0:T(4,128)(2,1)S(1)}, bf16[4,58752]{1,0:T(4,128)(2,1)S(1)}, u32[]{:S(2)}, u32[]{:S(2)}) collective-permute-start(bf16[4,58752]{1,0:T(4,128)(2,1)S(1)} %reshape.337), channel_id=1, source_target_pairs={{0,4},{4,0},{8,12},{12,8},{16,20},{20,16},{24,28},{28,24},{1,5},{5... | collective-permute-start | bytes 1410056 | tf_op jit(solution)/shard_map/ppermute | solution.py:218
  (47 other events, 145.8 us)
Sparse Core Ops, SparseCore 0:
  279.3 159.7 all-reduce.6
  514.4 18.9 all-gather.1

commit v9 on v8

--- a/solution.py
+++ b/solution.py
@@ -244,6 +244,11 @@
     return total
 
 
+def map_rows(step, items):
+    outs = [step(tuple(item[row] for item in items)) for row in range(items[0].shape[0])]
+    return tuple(jnp.stack(parts) for parts in zip(*outs))
+
+
 def local(
     tokens,
     doc_ids,
@@ -295,7 +300,7 @@
     query_rows = queries.reshape(row_shape)
     keys_rows = key_rows.reshape(row_shape)
     values_rows = value_rows.reshape(row_shape)
-    mixed_rows, log_total = lax.map(attend_row, (query_rows, keys_rows, values_rows, doc_ids))
+    mixed_rows, log_total = map_rows(attend_row, (query_rows, keys_rows, values_rows, doc_ids))
     mixed = mixed_rows.reshape(total_rows, local_heads * DH)
     piece = lax.slice_in_dim(mixed, 0, lax.axis_size("head") * own_rows, axis=0)
     resid_own = x_own + head_reduce_scatter(
@@ -337,8 +342,8 @@
     output, grad_resid = lax.optimization_barrier((output, grad_resid))
     grad_branch = head_all_gather(grad_resid.astype(jnp.bfloat16), 0)
     grad_mixed = dot_last(grad_branch, out_weight).astype(jnp.bfloat16)
-    grad_out = dot_first(mixed, grad_branch)
-    grad_query_rows, grad_key_rows, grad_value_rows = lax.map(
+    grad_out = dp_all_reduce(dot_first(mixed, grad_branch).astype(jnp.bfloat16).reshape(-1))
+    grad_query_rows, grad_key_rows, grad_value_rows = map_rows(
         attend_back,
         (query_rows, keys_rows, values_rows, doc_ids, log_total, grad_mixed.reshape(row_shape)),
     )
@@ -390,9 +395,9 @@
         jnp.concatenate([grad_gain_attn_own, grad_gain_ffn_own]),
         (0, gain_rows * basis_cols - 2 * features),
     ).reshape(gain_rows, basis_cols)
+    grad_out = grad_out.reshape(out_weight.shape)
     tail = (
         grad_a.astype(jnp.bfloat16),
-        grad_out.astype(jnp.bfloat16),
         jnp.concatenate([grad_b_cols, gains], axis=0).astype(jnp.bfloat16),
     )
     tail, (grad_gate, grad_up, grad_down) = lax.optimization_barrier(
@@ -400,7 +405,7 @@
     )
     sizes = [part.size for part in tail]
     summed = dp_all_reduce(jnp.concatenate([part.reshape(-1) for part in tail]))
-    grad_a, grad_out, packed = (
+    grad_a, packed = (
         summed[sum(sizes[:index]) : sum(sizes[: index + 1])].reshape(part.shape)
         for index, part in enumerate(tail)
     )

time: 559 us -> 561 us (level)
    ppermute x9, waiting for transfers between devices: 58.5 us -> 51.5 us  [head_reduce_scatter(): lax.ppermute(sent, 'head', [(device, (device + shift) % count) for device...]
    ppermute x3 -> x6, waiting for transfers between devices: 18.2 us -> 23.1 us  [dp_all_reduce(): lax.ppermute(sent.astype(jnp.bfloat16), 'dp', pairs).astype(jnp.float32)]
    ppermute x3 -> x6, waiting for transfers between devices: 17.6 us -> 21.7 us  [dp_all_reduce(): arrived = lax.ppermute(whole, 'dp', pairs)]
    unnamed x167 -> x180, local copies, waits for them, and re-layouts: 30 us -> 31 us
  transfers between devices with their start and end apart: 35 -> 41, of which waited for: 27 -> 30; matrix products, arithmetic and copies ran while one was open for 24% -> 26% of each run, Pallas kernels for 0% -> 0%
where the time goes in v9:
time: 561 us; the launch traced here: 551 us
  waiting for transfers between devices  207 us (37%)
  matrix products  122 us (22%)
  local copies, waits for them, and re-layouts  104 us (19%)
  other arithmetic  59.4 us (11%)
  starting transfers between devices  43.3 us (8%)
  between operations  15.8 us (3%)
    ppermute x9, waiting for transfers between devices, head_reduce_scatter(): lax.ppermute(sent, 'head', [(device, (device + shift) % count) for device...  51.5 us
    ppermute x6, waiting for transfers between devices, head_gather_relative(): lax.ppermute(values, 'head', [(device, (device + shift) % count) for devi...  40.9 us
    ppermute x6, waiting for transfers between devices, head_all_gather(): lax.ppermute(values, 'head', [(device, (device + shift) % count) for devi...  33 us
    unnamed x180, local copies, waits for them, and re-layouts  31 us
    ppermute x6, waiting for transfers between devices, head_scatter_relative(): lax.ppermute(sent, 'head', [(device, (device + shift) % count) for device...  27.4 us
    ppermute x6, waiting for transfers between devices, dp_all_reduce(): lax.ppermute(sent.astype(jnp.bfloat16), 'dp', pairs).astype(jnp.float32)  23.1 us
    ppermute x6, waiting for transfers between devices, dp_all_reduce(): arrived = lax.ppermute(whole, 'dp', pairs)  21.7 us
    dot_general x6, matrix products, dot_first(): lax.dot_general(left, right, (((0,), (0,)), ((), ())), preferred_element_...  12.9 us
  transfers between devices with their start and end apart: 41, of which 30 were waited for; matrix products, arithmetic and copies ran while one was open for 26% of the time, Pallas kernels for 0%

profile of v9, /device:TPU:0, one launch (start us, length us, event | category | flops | bytes accessed | tf_op | source)
XLA Modules:
  0.0 551.1 jit_solution(14400600388024193929)
XLA Ops:
  11.2 3.0 collective-permute-start.1
  18.4 3.0 multiply_cosine_fusion
  21.4 15.4 %collective-permute-done = bf16[256,1024]{1,0:T(8,128)(2,1)} collective-permute-done((bf16[256,1024]{1,0:T(8,128)(2,1)}, bf16[256,1024]{1,0:T(8,128)(2,1)}, u32[]{:S(2)}, u32[]{:S(2)}) %collective-permute-start) | collective-permute-done | bytes 524320 | tf_op jit(solution)/shard_map/ppermute | solution.py:190
  46.3 2.9 fusion.96
  57.7 2.7 fusion.86
  60.4 2.2 copy.361
  66.8 2.6 multiply_subtract_fusion.1
  70.6 10.4 %fusion.79 = f32[1024,4,64]{2,1,0:T(4,128)} fusion(f32[1024,4,2]{1,2,0:T(2,128)S(1)} %copy-done.27, f32[1024,2,32]{2,1,0:T(2,128)S(1)} %get-tuple-element.124, f32[1024,2,32]{2,1,0:T(2,128)S(1)} %get-tuple-element.123), kind=kOutput, calls=%fused_computation.221 | convolution fusion | flops 6422528 | bytes 1605632 | tf_op jit(solution)/shard_map/thr,trd->thd/dot_general | solution.py:293
  81.0 2.7 copy.369
  85.8 10.9 %fusion.97 = f32[1024,4,64]{2,1,0:T(4,128)} fusion(f32[1024,4,2]{1,2,0:T(2,128)} %copy.422, f32[1024,2,64]{2,1,0:T(2,128)} %copy.361), kind=kOutput, calls=%fused_computation.238 | convolution fusion | flops 6291456 | bytes 1605632 | tf_op jit(solution)/shard_map/thr,trd->thd/dot_general | solution.py:297
  96.7 2.7 copy.362
  101.5 3.6 copy.421
  105.1 3.7 copy.420
  108.8 4.2 multiply_subtract_fusion
  113.0 8.4 %multiply_convert_fusion.5 = bf16[1024,4,64]{2,1,0:T(4,128)(2,1)S(1)} fusion(f32[1024,4,6]{2,1,0:T(4,128)S(1)} %copy.419, f32[1024,6,32]{2,1,0:T(8,128)S(1)} %get-tuple-element.117, f32[1024,6,32]{2,1,0:T(8,128)S(1)} %get-tuple-element.116), kind=kOutput, calls=%fused_computation.42 | convolution fusion | flops 19791872 | bytes 2195456 | tf_op jit(solution)/shard_map/thr,trd->thd/dot_general | solution.py:290
  144.2 8.7 %collective-permute-done.3 = bf16[256,1024]{1,0:T(8,128)(2,1)S(1)} collective-permute-done((bf16[256,1024]{1,0:T(8,128)(2,1)S(1)}, bf16[256,1024]{1,0:T(8,128)(2,1)S(1)}, u32[]{:S(2)}, u32[]{:S(2)}) %collective-permute-start.3) | collective-permute-done | bytes 524320 | tf_op jit(solution)/shard_map/ppermute | solution.py:174
  154.5 13.2 %collective-permute-done.4 = bf16[256,1024]{1,0:T(8,128)(2,1)S(1)} collective-permute-done((bf16[256,1024]{1,0:T(8,128)(2,1)S(1)}, bf16[256,1024]{1,0:T(8,128)(2,1)S(1)}, u32[]{:S(2)}, u32[]{:S(2)}) %collective-permute-start.4) | collective-permute-done | bytes 524320 | tf_op jit(solution)/shard_map/ppermute | solution.py:174
  169.6 16.9 %collective-permute-done.12 = bf16[256,1024]{1,0:T(8,128)(2,1)S(1)} collective-permute-done((bf16[256,1024]{1,0:T(8,128)(2,1)S(1)}, bf16[256,1024]{1,0:T(8,128)(2,1)S(1)}, u32[]{:S(2)}, u32[]{:S(2)}) %collective-permute-start.12) | collective-permute-done | bytes 524320 | tf_op jit(solution)/shard_map/ppermute | solution.py:230
  188.2 11.2 %collective-permute-done.8 = bf16[256,1024]{1,0:T(8,128)(2,1)S(1)} collective-permute-done((bf16[256,1024]{1,0:T(8,128)(2,1)S(1)}, bf16[256,1024]{1,0:T(8,128)(2,1)S(1)}, u32[]{:S(2)}, u32[]{:S(2)}) %collective-permute-start.8) | collective-permute-done | bytes 524320 | tf_op jit(solution)/shard_map/ppermute | solution.py:230
  199.4 11.4 %collective-permute-done.7 = bf16[256,1024]{1,0:T(8,128)(2,1)S(1)} collective-permute-done((bf16[256,1024]{1,0:T(8,128)(2,1)S(1)}, bf16[256,1024]{1,0:T(8,128)(2,1)S(1)}, u32[]{:S(2)}, u32[]{:S(2)}) %collective-permute-start.7) | collective-permute-done | bytes 524320 | tf_op jit(solution)/shard_map/ppermute | solution.py:230
  214.2 3.1 multiply_convert_fusion.2
  217.3 2.8 convolution_convert_fusion.4
  233.2 2.9 convolution_convert_fusion.2
  236.0 2.8 convolution_convert_fusion.3
  238.8 8.4 %collective-permute-done.15 = bf16[256,1024]{1,0:T(8,128)(2,1)} collective-permute-done((bf16[256,1024]{1,0:T(8,128)(2,1)}, bf16[256,1024]{1,0:T(8,128)(2,1)}, u32[]{:S(2)}, u32[]{:S(2)}) %collective-permute-start.15) | collective-permute-done | bytes 524320 | tf_op jit(solution)/shard_map/ppermute | solution.py:241
  247.2 2.4 collective-permute-start.10
  249.6 12.4 %collective-permute-done.16 = bf16[256,1024]{1,0:T(8,128)(2,1)} collective-permute-done((bf16[256,1024]{1,0:T(8,128)(2,1)}, bf16[256,1024]{1,0:T(8,128)(2,1)}, u32[]{:S(2)}, u32[]{:S(2)}) %collective-permute-start.16) | collective-permute-done | bytes 524320 | tf_op jit(solution)/shard_map/ppermute | solution.py:241
  264.7 6.6 %collective-permute-done.10 = bf16[256,1024]{1,0:T(8,128)(2,1)S(1)} collective-permute-done((bf16[256,1024]{1,0:T(8,128)(2,1)}, bf16[256,1024]{1,0:T(8,128)(2,1)S(1)}, u32[]{:S(2)}, u32[]{:S(2)}) %collective-permute-start.10) | collective-permute-done | bytes 524320 | tf_op jit(solution)/shard_map/ppermute | solution.py:241
  271.3 2.7 subtract_add_fusion
  279.4 10.7 %collective-permute-done.18 = bf16[256,1024]{1,0:T(8,128)(2,1)} collective-permute-done((bf16[256,1024]{1,0:T(8,128)(2,1)S(1)}, bf16[256,1024]{1,0:T(8,128)(2,1)}, u32[]{:S(2)}, u32[]{:S(2)}) %collective-permute-start.18) | collective-permute-done | bytes 524320 | tf_op jit(solution)/shard_map/ppermute | solution.py:190
  293.8 7.0 %collective-permute-done.20 = bf16[256,1024]{1,0:T(8,128)(2,1)} collective-permute-done((bf16[256,1024]{1,0:T(8,128)(2,1)S(1)}, bf16[256,1024]{1,0:T(8,128)(2,1)}, u32[]{:S(2)}, u32[]{:S(2)}) %collective-permute-start.20) | collective-permute-done | bytes 524320 | tf_op jit(solution)/shard_map/ppermute | solution.py:190
  302.7 3.5 fusion.27
  306.2 2.5 convolution_convert_fusion.6
  309.5 2.6 fusion.22
  312.2 2.3 copy.382
  314.5 5.7 %fusion.26 = bf16[1024,2,64]{2,1,0:T(2,128)(2,1)} fusion(f32[1024,4,2]{1,2,0:T(2,128)S(1)} %copy-done.31, bf16[1024,4,64]{2,1,0:T(4,128)(2,1)} %copy.382), kind=kOutput, calls=%fused_computation.63 | convolution fusion | flops 6553600 | bytes 819200 | tf_op jit(solution)/shard_map/thr,thd->trd/dot_general | solution.py:363
  320.2 6.0 %convolution_multiply_fusion.4 = bf16[1024,4,2]{1,2,0:T(2,128)(2,1)} fusion(bf16[1024,4,64]{2,1,0:T(4,128)(2,1)} %copy.382, f32[1024,2,64]{2,1,0:T(2,128)} %copy.361), kind=kOutput, calls=%fused_computation.54 | convolution fusion | flops 6307840 | bytes 1064960 | tf_op jit(solution)/shard_map/thd,trd->thr/dot_general | solution.py:356
  331.3 2.6 multiply_reduce_fusion
  333.9 2.2 multiply_convert_fusion
  339.8 2.3 copy.379
  342.2 6.7 %convolution_multiply_fusion.5 = bf16[1024,4,2]{1,2,0:T(2,128)(2,1)} fusion(bf16[1024,4,64]{2,1,0:T(4,128)(2,1)} %copy.379, f32[1024,2,32]{2,1,0:T(2,128)} %copy-done.26, f32[1024,2,32]{2,1,0:T(2,128)S(1)} %copy-done.25), kind=kOutput, calls=%fused_computation.55 | convolution fusion | flops 6438912 | bytes 1064960 | tf_op jit(solution)/shard_map/thd,trd->thr/dot_general | solution.py:355
  348.9 4.5 convolution_multiply_fusion.3
  356.0 8.8 %convolution_multiply_fusion.1 = bf16[1024,4,6]{2,1,0:T(4,128)(2,1)} fusion(bf16[1024,4,64]{2,1,0:T(4,128)(2,1)S(1)} %copy.374, f32[1024,6,32]{2,1,0:T(8,128)} %copy-done.9, f32[1024,6,32]{2,1,0:T(8,128)} %copy-done.8), kind=kOutput, calls=%fused_computation.50 | convolution fusion | flops 19316736 | bytes 2146304 | tf_op jit(solution)/shard_map/thd,trd->thr/dot_general | solution.py:354
  364.8 5.8 %convolution_multiply_fusion = f32[1024,6,64]{2,1,0:T(8,128)} fusion(f32[1024,4,6]{2,1,0:T(4,128)S(1)} %copy.419, bf16[1024,4,64]{2,1,0:T(4,128)(2,1)S(1)} %copy.374), kind=kOutput, calls=%fused_computation.37 | convolution fusion | flops 19267584 | bytes 2195456 | tf_op jit(solution)/shard_map/thr,thd->trd/dot_general | solution.py:358
  370.6 2.2 reshape.332
  386.2 6.2 %add_convert_fusion.1 = (bf16[1024,6,32]{2,1,0:T(8,128)(2,1)}, bf16[1024,6,32]{2,1,0:T(8,128)(2,1)S(1)}) fusion(f32[1024,6,64]{2,1,0:T(8,128)} %convolution_multiply_fusion, f32[1024,32]{1,0:T(8,128)S(1)} %copy-done.16, f32[1024,32]{1,0:T(8,128)S(1)} %copy-done.15), kind=kLoop, calls=%fused_computation.12 | loop fusion | flops 1572864 | bytes 2621440 | tf_op jit(solution)/shard_map/convert.19
  392.3 2.3 copy.387
  397.1 2.2 collective-permute-start.21
  408.6 7.1 %collective-permute-done.22 = bf16[1024,160]{0,1:T(8,128)(2,1)S(1)} collective-permute-done((bf16[1024,160]{0,1:T(8,128)(2,1)S(1)}, bf16[1024,160]{0,1:T(8,128)(2,1)S(1)}, u32[]{:S(2)}, u32[]{:S(2)}) %collective-permute-start.22) | collective-permute-done | bytes 327712 | tf_op jit(solution)/shard_map/ppermute | solution.py:174
  416.0 2.2 add_convert_fusion
  418.1 4.8 collective-permute-done.34
  423.9 10.6 %collective-permute-done.35 = bf16[32768]{0:T(1024)(128)(2,1)S(1)} collective-permute-done((bf16[32768]{0:T(1024)(128)(2,1)S(1)}, bf16[32768]{0:T(1024)(128)(2,1)S(1)}, u32[]{:S(2)}, u32[]{:S(2)}) %collective-permute-start.35) | collective-permute-done | bytes 65568 | tf_op jit(solution)/shard_map/ppermute | solution.py:213
  435.3 11.7 %collective-permute-done.36 = bf16[1,32768]{1,0:T(2,128)(2,1)S(1)} collective-permute-done((bf16[1,32768]{1,0:T(2,128)(2,1)S(1)}, bf16[1,32768]{1,0:T(2,128)(2,1)S(1)}, u32[]{:S(2)}, u32[]{:S(2)}) %collective-permute-start.36) | collective-permute-done | bytes 65568 | tf_op jit(solution)/shard_map/ppermute | solution.py:218
  453.9 5.9 %collective-permute-done.24 = bf16[256,1024]{1,0:T(8,128)(2,1)S(1)} collective-permute-done((bf16[256,1024]{1,0:T(8,128)(2,1)S(1)}, bf16[256,1024]{1,0:T(8,128)(2,1)S(1)}, u32[]{:S(2)}, u32[]{:S(2)}) %collective-permute-start.24) | collective-permute-done | bytes 524320 | tf_op jit(solution)/shard_map/ppermute | solution.py:174
  459.9 2.4 collective-permute-done.26
  462.3 11.0 %collective-permute-done.25 = bf16[256,1024]{1,0:T(8,128)(2,1)S(1)} collective-permute-done((bf16[256,1024]{1,0:T(8,128)(2,1)S(1)}, bf16[256,1024]{1,0:T(8,128)(2,1)S(1)}, u32[]{:S(2)}, u32[]{:S(2)}) %collective-permute-start.25) | collective-permute-done | bytes 524320 | tf_op jit(solution)/shard_map/ppermute | solution.py:174
  479.0 3.9 collective-permute-done.27
  485.8 2.5 collective-permute-done.28
  497.0 4.2 collective-permute-done.30
  501.6 2.2 collective-permute-start.31
  510.4 3.0 collective-permute-done.32
  526.4 9.5 %all-gather.2.cloned.1.call-done = bf16[1037,640]{0,1:T(8,128)(2,1)} async-done(((bf16[1037,160]{0,1:T(8,128)(2,1)}), bf16[1037,640]{0,1:T(8,128)(2,1)}) %all-gather.2.cloned.1.call-update) | async-done | bytes 1327376 | tf_op jit(solution)/shard_map/all_gather | solution.py:419
  537.6 3.2 slice.207
  540.8 3.2 copy.404
  (387 shorter events, 178.4 us)
Async XLA Ops:
  7.2 207.0 %copy-start = (bf16[704,1024]{1,0:T(8,128)(2,1)S(1)}, bf16[704,1024]{1,0:T(8,128)(2,1)}, u32[]{:S(2)}) copy-start(bf16[704,1024]{1,0:T(8,128)(2,1)} %param.20) | copy-start | bytes 4325380
  7.2 467.0 %all-reduce.7.cloned.1.call-start = ((), (), s32[]{:S(2)}) async-start(), calls=%async_computation.1 | async-start | bytes 8650752 | tf_op jit(solution)/shard_map/psum | solution.py:339
  11.2 26.7 %collective-permute-start.1 = (bf16[256,1024]{1,0:T(8,128)(2,1)}, bf16[256,1024]{1,0:T(8,128)(2,1)}, u32[]{:S(2)}, u32[]{:S(2)}) collective-permute-start(bf16[256,1024]{1,0:T(8,128)(2,1)} %get-tuple-element.115), channel_id=1, source_target_pairs={{0,2},{1,3},{2,0},{3,1},{4,6},{5,7},{6,4},{7,5},{8,10},{9,11},{10,... | collective-permute-start | bytes 1572872 | tf_op jit(solution)/shard_map/ppermute | solution.py:190
  14.2 22.6 %collective-permute-start = (bf16[256,1024]{1,0:T(8,128)(2,1)}, bf16[256,1024]{1,0:T(8,128)(2,1)}, u32[]{:S(2)}, u32[]{:S(2)}) collective-permute-start(bf16[256,1024]{1,0:T(8,128)(2,1)} %get-tuple-element.115), channel_id=1, source_target_pairs={{0,1},{1,2},{2,3},{3,0},{4,5},{5,6},{6,7},{7,4},{8,9},{9,10},{10,1... | collective-permute-start | bytes 1572872 | tf_op jit(solution)/shard_map/ppermute | solution.py:190
  14.2 24.8 %collective-permute-start.2 = (bf16[256,1024]{1,0:T(8,128)(2,1)}, bf16[256,1024]{1,0:T(8,128)(2,1)}, u32[]{:S(2)}, u32[]{:S(2)}) collective-permute-start(bf16[256,1024]{1,0:T(8,128)(2,1)} %get-tuple-element.115), channel_id=1, source_target_pairs={{0,3},{1,0},{2,1},{3,2},{4,7},{5,4},{6,5},{7,6},{8,11},{9,8},{10,9... | collective-permute-start | bytes 1572872 | tf_op jit(solution)/shard_map/ppermute | solution.py:190
  18.4 21.7 %copy-start.56 = (bf16[1024,40]{0,1:T(8,128)(2,1)S(1)}, bf16[1024,40]{0,1:T(8,128)(2,1)}, u32[]{:S(2)}) copy-start(bf16[1024,40]{0,1:T(8,128)(2,1)} %param.14) | copy-start | bytes 245764
  140.2 27.5 %copy-start.13 = (bf16[256,1024]{1,0:T(8,128)(2,1)S(1)}, bf16[256,1024]{1,0:T(8,128)(2,1)}, u32[]{:S(2)}) copy-start(bf16[256,1024]{1,0:T(8,128)(2,1)} %param.11) | copy-start | bytes 1572868
  140.4 28.4 %copy-start.60 = (f32[1024]{0:T(1024)S(1)}, f32[1024]{0:T(1024)}, u32[]{:S(2)}) copy-start(f32[1024]{0:T(1024)} %param.17) | copy-start | bytes 12292
  140.4 12.5 %collective-permute-start.3 = (bf16[256,1024]{1,0:T(8,128)(2,1)S(1)}, bf16[256,1024]{1,0:T(8,128)(2,1)S(1)}, u32[]{:S(2)}, u32[]{:S(2)}) collective-permute-start(bf16[256,1024]{1,0:T(8,128)(2,1)S(1)} %get-tuple-element.138), channel_id=1, source_target_pairs={{0,1},{1,2},{2,3},{3,0},{4,5},{5,6},{6,7},{7,4},{8,9},{9,10},{10,1... | collective-permute-start | bytes 1572872 | tf_op jit(solution)/shard_map/ppermute | solution.py:174
  140.4 14.0 %collective-permute-start.5 = (bf16[256,1024]{1,0:T(8,128)(2,1)S(1)}, bf16[256,1024]{1,0:T(8,128)(2,1)S(1)}, u32[]{:S(2)}, u32[]{:S(2)}) collective-permute-start(bf16[256,1024]{1,0:T(8,128)(2,1)S(1)} %get-tuple-element.139), channel_id=1, source_target_pairs={{0,3},{1,0},{2,1},{3,2},{4,7},{5,4},{6,5},{7,6},{8,11},{9,8},{10,9... | collective-permute-start | bytes 1572872 | tf_op jit(solution)/shard_map/ppermute | solution.py:174
  142.2 25.5 %collective-permute-start.4 = (bf16[256,1024]{1,0:T(8,128)(2,1)S(1)}, bf16[256,1024]{1,0:T(8,128)(2,1)S(1)}, u32[]{:S(2)}, u32[]{:S(2)}) collective-permute-start(bf16[256,1024]{1,0:T(8,128)(2,1)S(1)} %get-tuple-element.140), channel_id=1, source_target_pairs={{0,2},{1,3},{2,0},{3,1},{4,6},{5,7},{6,4},{7,5},{8,10},{9,11},{10,... | collective-permute-start | bytes 1572872 | tf_op jit(solution)/shard_map/ppermute | solution.py:174
  143.6 43.1 %collective-permute-start.13 = (bf16[256,1024]{1,0:T(8,128)(2,1)S(1)}, bf16[256,1024]{1,0:T(8,128)(2,1)S(1)}, u32[]{:S(2)}, u32[]{:S(2)}) collective-permute-start(bf16[256,1024]{1,0:T(8,128)(2,1)S(1)} %copy-done.43), channel_id=1, source_target_pairs={{0,2},{1,3},{2,0},{3,1},{4,6},{5,7},{6,4},{7,5},{8,10},{9,11},{10,... | collective-permute-start | bytes 1572872 | tf_op jit(solution)/shard_map/ppermute | solution.py:230
  144.2 42.4 %collective-permute-start.12 = (bf16[256,1024]{1,0:T(8,128)(2,1)S(1)}, bf16[256,1024]{1,0:T(8,128)(2,1)S(1)}, u32[]{:S(2)}, u32[]{:S(2)}) collective-permute-start(bf16[256,1024]{1,0:T(8,128)(2,1)S(1)} %copy-done.43), channel_id=1, source_target_pairs={{0,1},{1,2},{2,3},{3,0},{4,5},{5,6},{6,7},{7,4},{8,9},{9,10},{10,1... | collective-permute-start | bytes 1572872 | tf_op jit(solution)/shard_map/ppermute | solution.py:230
  152.9 35.3 %collective-permute-start.14 = (bf16[256,1024]{1,0:T(8,128)(2,1)S(1)}, bf16[256,1024]{1,0:T(8,128)(2,1)S(1)}, u32[]{:S(2)}, u32[]{:S(2)}) collective-permute-start(bf16[256,1024]{1,0:T(8,128)(2,1)S(1)} %copy-done.43), channel_id=1, source_target_pairs={{0,3},{1,0},{2,1},{3,2},{4,7},{5,4},{6,5},{7,6},{8,11},{9,8},{10,9... | collective-permute-start | bytes 1572872 | tf_op jit(solution)/shard_map/ppermute | solution.py:230
  168.2 18.6 %copy-start.10 = (f32[256,1024]{1,0:T(8,128)}, f32[256,1024]{1,0:T(8,128)S(1)}, u32[]{:S(2)}) copy-start(f32[256,1024]{1,0:T(8,128)S(1)} %get-tuple-element.113) | copy-start | bytes 3145732
  168.8 18.0 %copy-start.71 = (f32[256]{0:T(256)}, f32[256]{0:T(256)S(1)}, u32[]{:S(2)}) copy-start(f32[256]{0:T(256)S(1)} %get-tuple-element.177) | copy-start | bytes 3076
  169.0 41.9 %copy-start.77 = (bf16[1024,704]{0,1:T(8,128)(2,1)S(1)}, bf16[1024,704]{0,1:T(8,128)(2,1)}, u32[]{:S(2)}) copy-start(bf16[1024,704]{0,1:T(8,128)(2,1)} %param.19) | copy-start | bytes 4325380
  169.0 30.5 %collective-permute-start.8 = (bf16[256,1024]{1,0:T(8,128)(2,1)S(1)}, bf16[256,1024]{1,0:T(8,128)(2,1)S(1)}, u32[]{:S(2)}, u32[]{:S(2)}) collective-permute-start(bf16[256,1024]{1,0:T(8,128)(2,1)S(1)} %multiply_convert_fusion.6), channel_id=1, source_target_pairs={{0,3},{1,0},{2,1},{3,2},{4,7},{5,4},{6,5},{7,6},{8,11},{9,8},{10,9... | collective-permute-start | bytes 1572872 | tf_op jit(solution)/shard_map/ppermute | solution.py:230
  169.0 41.8 %collective-permute-start.7 = (bf16[256,1024]{1,0:T(8,128)(2,1)S(1)}, bf16[256,1024]{1,0:T(8,128)(2,1)S(1)}, u32[]{:S(2)}, u32[]{:S(2)}) collective-permute-start(bf16[256,1024]{1,0:T(8,128)(2,1)S(1)} %multiply_convert_fusion.6), channel_id=1, source_target_pairs={{0,2},{1,3},{2,0},{3,1},{4,6},{5,7},{6,4},{7,5},{8,10},{9,11},{10,... | collective-permute-start | bytes 1572872 | tf_op jit(solution)/shard_map/ppermute | solution.py:230
  186.6 24.2 %collective-permute-start.6 = (bf16[256,1024]{1,0:T(8,128)(2,1)S(1)}, bf16[256,1024]{1,0:T(8,128)(2,1)S(1)}, u32[]{:S(2)}, u32[]{:S(2)}) collective-permute-start(bf16[256,1024]{1,0:T(8,128)(2,1)S(1)} %multiply_convert_fusion.6), channel_id=1, source_target_pairs={{0,1},{1,2},{2,3},{3,0},{4,5},{5,6},{6,7},{7,4},{8,9},{9,10},{10,1... | collective-permute-start | bytes 1572872 | tf_op jit(solution)/shard_map/ppermute | solution.py:230
  188.2 24.3 %copy-start.76 = (bf16[1024,704]{0,1:T(8,128)(2,1)S(1)}, bf16[1024,704]{0,1:T(8,128)(2,1)}, u32[]{:S(2)}) copy-start(bf16[1024,704]{0,1:T(8,128)(2,1)} %param.18) | copy-start | bytes 4325380
  223.2 41.5 %collective-permute-start.9 = (bf16[256,1024]{1,0:T(8,128)(2,1)}, bf16[256,1024]{1,0:T(8,128)(2,1)}, u32[]{:S(2)}, u32[]{:S(2)}) collective-permute-start(bf16[256,1024]{1,0:T(8,128)(2,1)} %get-tuple-element.135), channel_id=1, source_target_pairs={{0,1},{1,2},{2,3},{3,0},{4,5},{5,6},{6,7},{7,4},{8,9},{9,10},{10,1... | collective-permute-start | bytes 1572872 | tf_op jit(solution)/shard_map/ppermute | solution.py:241
  223.2 41.5 %collective-permute-start.11 = (bf16[256,1024]{1,0:T(8,128)(2,1)}, bf16[256,1024]{1,0:T(8,128)(2,1)}, u32[]{:S(2)}, u32[]{:S(2)}) collective-permute-start(bf16[256,1024]{1,0:T(8,128)(2,1)} %get-tuple-element.136), channel_id=1, source_target_pairs={{0,3},{1,0},{2,1},{3,2},{4,7},{5,4},{6,5},{7,6},{8,11},{9,8},{10,9... | collective-permute-start | bytes 1572872 | tf_op jit(solution)/shard_map/ppermute | solution.py:241
  229.9 17.2 %collective-permute-start.15 = (bf16[256,1024]{1,0:T(8,128)(2,1)}, bf16[256,1024]{1,0:T(8,128)(2,1)}, u32[]{:S(2)}, u32[]{:S(2)}) collective-permute-start(bf16[256,1024]{1,0:T(8,128)(2,1)} %get-tuple-element.132), channel_id=1, source_target_pairs={{0,1},{1,2},{2,3},{3,0},{4,5},{5,6},{6,7},{7,4},{8,9},{9,10},{10,1... | collective-permute-start | bytes 1572872 | tf_op jit(solution)/shard_map/ppermute | solution.py:241
  230.0 19.6 %collective-permute-start.17 = (bf16[256,1024]{1,0:T(8,128)(2,1)}, bf16[256,1024]{1,0:T(8,128)(2,1)}, u32[]{:S(2)}, u32[]{:S(2)}) collective-permute-start(bf16[256,1024]{1,0:T(8,128)(2,1)} %get-tuple-element.133), channel_id=1, source_target_pairs={{0,3},{1,0},{2,1},{3,2},{4,7},{5,4},{6,5},{7,6},{8,11},{9,8},{10,9... | collective-permute-start | bytes 1572872 | tf_op jit(solution)/shard_map/ppermute | solution.py:241
  231.7 30.2 %collective-permute-start.16 = (bf16[256,1024]{1,0:T(8,128)(2,1)}, bf16[256,1024]{1,0:T(8,128)(2,1)}, u32[]{:S(2)}, u32[]{:S(2)}) collective-permute-start(bf16[256,1024]{1,0:T(8,128)(2,1)} %get-tuple-element.134), channel_id=1, source_target_pairs={{0,2},{1,3},{2,0},{3,1},{4,6},{5,7},{6,4},{7,5},{8,10},{9,11},{10,... | collective-permute-start | bytes 1572872 | tf_op jit(solution)/shard_map/ppermute | solution.py:241
  238.8 25.0 %copy-start.11 = (f32[256,1024]{1,0:T(8,128)S(1)}, f32[256,1024]{1,0:T(8,128)}, u32[]{:S(2)}) copy-start(f32[256,1024]{1,0:T(8,128)} %copy-done.10) | copy-start | bytes 3145732
  238.8 25.0 %copy-start.61 = (f32[1024]{0:T(1024)S(1)}, f32[1024]{0:T(1024)}, u32[]{:S(2)}) copy-start(f32[1024]{0:T(1024)} %param.17) | copy-start | bytes 12292
  238.8 25.0 %copy-start.72 = (f32[256]{0:T(256)S(1)}, f32[256]{0:T(256)}, u32[]{:S(2)}) copy-start(f32[256]{0:T(256)} %copy-done.71) | copy-start | bytes 3076
  247.2 24.1 %copy-start.44 = (bf16[256,1024]{1,0:T(8,128)(2,1)S(1)}, bf16[256,1024]{1,0:T(8,128)(2,1)}, u32[]{:S(2)}) copy-start(bf16[256,1024]{1,0:T(8,128)(2,1)} %param.21) | copy-start | bytes 1572868
  247.2 24.1 %copy-start.75 = (f32[256]{0:T(256)S(1)}, f32[256]{0:T(256)}, u32[]{:S(2)}) copy-start(f32[256]{0:T(256)} %get-tuple-element.176) | copy-start | bytes 3076
  247.2 24.1 %collective-permute-start.10 = (bf16[256,1024]{1,0:T(8,128)(2,1)}, bf16[256,1024]{1,0:T(8,128)(2,1)S(1)}, u32[]{:S(2)}, u32[]{:S(2)}) collective-permute-start(bf16[256,1024]{1,0:T(8,128)(2,1)} %get-tuple-element.137), channel_id=1, source_target_pairs={{0,2},{1,3},{2,0},{3,1},{4,6},{5,7},{6,4},{7,5},{8,10},{9,11},{10,... | collective-permute-start | bytes 1572872 | tf_op jit(solution)/shard_map/ppermute | solution.py:241
  276.3 13.7 %collective-permute-start.18 = (bf16[256,1024]{1,0:T(8,128)(2,1)S(1)}, bf16[256,1024]{1,0:T(8,128)(2,1)}, u32[]{:S(2)}, u32[]{:S(2)}) collective-permute-start(bf16[256,1024]{1,0:T(8,128)(2,1)S(1)} %get-tuple-element.111), channel_id=1, source_target_pairs={{0,1},{1,2},{2,3},{3,0},{4,5},{5,6},{6,7},{7,4},{8,9},{9,10},{10,1... | collective-permute-start | bytes 1572872 | tf_op jit(solution)/shard_map/ppermute | solution.py:190
  276.3 15.6 %collective-permute-start.19 = (bf16[256,1024]{1,0:T(8,128)(2,1)S(1)}, bf16[256,1024]{1,0:T(8,128)(2,1)}, u32[]{:S(2)}, u32[]{:S(2)}) collective-permute-start(bf16[256,1024]{1,0:T(8,128)(2,1)S(1)} %get-tuple-element.111), channel_id=1, source_target_pairs={{0,2},{1,3},{2,0},{3,1},{4,6},{5,7},{6,4},{7,5},{8,10},{9,11},{10,... | collective-permute-start | bytes 1572872 | tf_op jit(solution)/shard_map/ppermute | solution.py:190
  277.8 23.0 %collective-permute-start.20 = (bf16[256,1024]{1,0:T(8,128)(2,1)S(1)}, bf16[256,1024]{1,0:T(8,128)(2,1)}, u32[]{:S(2)}, u32[]{:S(2)}) collective-permute-start(bf16[256,1024]{1,0:T(8,128)(2,1)S(1)} %get-tuple-element.111), channel_id=1, source_target_pairs={{0,3},{1,0},{2,1},{3,2},{4,7},{5,4},{6,5},{7,6},{8,11},{9,8},{10,9... | collective-permute-start | bytes 1572872 | tf_op jit(solution)/shard_map/ppermute | solution.py:190
  279.3 23.4 %copy-start.23 = (bf16[1024,4,64]{0,2,1:T(8,128)(2,1)S(1)}, bf16[1024,4,64]{0,2,1:T(8,128)(2,1)}, u32[]{:S(2)}) copy-start(bf16[1024,4,64]{0,2,1:T(8,128)(2,1)} %copy-done.22) | copy-start | bytes 1572868
  279.3 256.5 %all-gather.2.cloned.1.call-start = ((), (), s32[]{:S(2)}) async-start(), calls=%async_computation | async-start | bytes 1843200 | tf_op jit(solution)/shard_map/all_gather | solution.py:419
  314.5 11.7 %copy-start.5 = (f32[4,512,512]{1,2,0:T(8,128)S(1)}, f32[4,512,512]{1,2,0:T(8,128)}, u32[]{:S(2)}) copy-start(f32[4,512,512]{1,2,0:T(8,128)} %copy-done.3) | copy-start | bytes 12582916
  378.2 24.4 %collective-permute-start.33 = (bf16[2,2,32768]{2,1,0:T(2,128)(2,1)}, bf16[2,2,32768]{2,1,0:T(2,128)(2,1)}, u32[]{:S(2)}, u32[]{:S(2)}) collective-permute-start(bf16[2,2,32768]{2,1,0:T(2,128)(2,1)} %bitcast.152), channel_id=1, source_target_pairs={{0,4},{4,0},{8,12},{12,8},{16,20},{20,16},{24,28},{28,24},{1,5},{5... | collective-permute-start | bytes 786440 | tf_op jit(solution)/shard_map/ppermute | solution.py:213
  397.1 10.7 %collective-permute-start.21 = (bf16[1024,160]{0,1:T(8,128)(2,1)S(1)}, bf16[1024,160]{0,1:T(8,128)(2,1)S(1)}, u32[]{:S(2)}, u32[]{:S(2)}) collective-permute-start(bf16[1024,160]{0,1:T(8,128)(2,1)S(1)} %get-tuple-element.143), channel_id=1, source_target_pairs={{0,1},{1,2},{2,3},{3,0},{4,5},{5,6},{6,7},{7,4},{8,9},{9,10},{10,1... | collective-permute-start | bytes 983048 | tf_op jit(solution)/shard_map/ppermute | solution.py:174
  399.4 9.3 %collective-permute-start.23 = (bf16[1024,160]{0,1:T(8,128)(2,1)S(1)}, bf16[1024,160]{0,1:T(8,128)(2,1)S(1)}, u32[]{:S(2)}, u32[]{:S(2)}) collective-permute-start(bf16[1024,160]{0,1:T(8,128)(2,1)S(1)} %get-tuple-element.144), channel_id=1, source_target_pairs={{0,3},{1,0},{2,1},{3,2},{4,7},{5,4},{6,5},{7,6},{8,11},{9,8},{10,9... | collective-permute-start | bytes 983048 | tf_op jit(solution)/shard_map/ppermute | solution.py:174
  400.5 15.2 %collective-permute-start.22 = (bf16[1024,160]{0,1:T(8,128)(2,1)S(1)}, bf16[1024,160]{0,1:T(8,128)(2,1)S(1)}, u32[]{:S(2)}, u32[]{:S(2)}) collective-permute-start(bf16[1024,160]{0,1:T(8,128)(2,1)S(1)} %get-tuple-element.145), channel_id=1, source_target_pairs={{0,2},{1,3},{2,0},{3,1},{4,6},{5,7},{6,4},{7,5},{8,10},{9,11},{10,... | collective-permute-start | bytes 983048 | tf_op jit(solution)/shard_map/ppermute | solution.py:174
  405.4 17.5 %collective-permute-start.34 = (bf16[2,32768]{1,0:T(2,128)(2,1)S(1)}, bf16[2,32768]{1,0:T(2,128)(2,1)S(1)}, u32[]{:S(2)}, u32[]{:S(2)}) collective-permute-start(bf16[2,32768]{1,0:T(2,128)(2,1)S(1)} %bitcast.175), channel_id=1, source_target_pairs={{0,8},{4,12},{8,0},{12,4},{16,24},{20,28},{24,16},{28,20},{1,9},{5... | collective-permute-start | bytes 393224 | tf_op jit(solution)/shard_map/ppermute | solution.py:213
  423.6 11.0 %collective-permute-start.35 = (bf16[32768]{0:T(1024)(128)(2,1)S(1)}, bf16[32768]{0:T(1024)(128)(2,1)S(1)}, u32[]{:S(2)}, u32[]{:S(2)}) collective-permute-start(bf16[32768]{0:T(1024)(128)(2,1)S(1)} %convert_reduce_fusion), channel_id=1, source_target_pairs={{0,16},{4,20},{8,24},{12,28},{16,0},{20,4},{24,8},{28,12},{1,17},{... | collective-permute-start | bytes 196616 | tf_op jit(solution)/shard_map/ppermute | solution.py:213
  434.7 12.3 %collective-permute-start.36 = (bf16[1,32768]{1,0:T(2,128)(2,1)S(1)}, bf16[1,32768]{1,0:T(2,128)(2,1)S(1)}, u32[]{:S(2)}, u32[]{:S(2)}) collective-permute-start(bf16[1,32768]{1,0:T(2,128)(2,1)S(1)} %broadcast_in_dim.41), channel_id=1, source_target_pairs={{0,16},{4,20},{8,24},{12,28},{16,0},{20,4},{24,8},{28,12},{1,17},{... | collective-permute-start | bytes 196616 | tf_op jit(solution)/shard_map/ppermute | solution.py:218
  447.2 26.1 %copy-start.14 = (bf16[256,1024]{1,0:T(8,128)(2,1)S(1)}, bf16[256,1024]{1,0:T(8,128)(2,1)}, u32[]{:S(2)}) copy-start(bf16[256,1024]{1,0:T(8,128)(2,1)} %param.11) | copy-start | bytes 1572868
  447.2 26.1 %copy-start.63 = (f32[1024]{0:T(1024)S(1)}, f32[1024]{0:T(1024)}, u32[]{:S(2)}) copy-start(f32[1024]{0:T(1024)} %param.13) | copy-start | bytes 12292
  447.2 26.1 %copy-start.70 = (f32[256]{0:T(256)S(1)}, f32[256]{0:T(256)}, u32[]{:S(2)}) copy-start(f32[256]{0:T(256)} %copy-done.69) | copy-start | bytes 3076
  447.6 5.3 collective-permute-start.37
  447.8 12.1 %collective-permute-start.24 = (bf16[256,1024]{1,0:T(8,128)(2,1)S(1)}, bf16[256,1024]{1,0:T(8,128)(2,1)S(1)}, u32[]{:S(2)}, u32[]{:S(2)}) collective-permute-start(bf16[256,1024]{1,0:T(8,128)(2,1)S(1)} %get-tuple-element.127), channel_id=1, source_target_pairs={{0,1},{1,2},{2,3},{3,0},{4,5},{5,6},{6,7},{7,4},{8,9},{9,10},{10,1... | collective-permute-start | bytes 1572872 | tf_op jit(solution)/shard_map/ppermute | solution.py:174
  447.8 14.4 %collective-permute-start.26 = (bf16[256,1024]{1,0:T(8,128)(2,1)S(1)}, bf16[256,1024]{1,0:T(8,128)(2,1)S(1)}, u32[]{:S(2)}, u32[]{:S(2)}) collective-permute-start(bf16[256,1024]{1,0:T(8,128)(2,1)S(1)} %get-tuple-element.128), channel_id=1, source_target_pairs={{0,3},{1,0},{2,1},{3,2},{4,7},{5,4},{6,5},{7,6},{8,11},{9,8},{10,9... | collective-permute-start | bytes 1572872 | tf_op jit(solution)/shard_map/ppermute | solution.py:174
  450.0 23.9 %copy-start.73 = (bf16[1024]{0:T(1024)(128)(2,1)S(1)}, bf16[1024]{0:T(1024)(128)(2,1)}, u32[]{:S(2)}) copy-start(bf16[1024]{0:T(1024)(128)(2,1)} %get-tuple-element.102) | copy-start | bytes 6148
  450.0 23.3 %collective-permute-start.25 = (bf16[256,1024]{1,0:T(8,128)(2,1)S(1)}, bf16[256,1024]{1,0:T(8,128)(2,1)S(1)}, u32[]{:S(2)}, u32[]{:S(2)}) collective-permute-start(bf16[256,1024]{1,0:T(8,128)(2,1)S(1)} %get-tuple-element.129), channel_id=1, source_target_pairs={{0,2},{1,3},{2,0},{3,1},{4,6},{5,7},{6,4},{7,5},{8,10},{9,11},{10,... | collective-permute-start | bytes 1572872 | tf_op jit(solution)/shard_map/ppermute | solution.py:174
  476.8 13.7 %copy-start.54 = (bf16[2,1,32768]{2,0,1:T(2,128)(2,1)S(1)}, bf16[2,1,32768]{2,0,1:T(2,128)(2,1)}, u32[]{:S(2)}) copy-start(bf16[2,1,32768]{2,0,1:T(2,128)(2,1)} %get-tuple-element.158) | copy-start | bytes 393220
  476.8 13.7 %copy-start.55 = (bf16[2,1,32768]{2,0,1:T(2,128)(2,1)S(1)}, bf16[2,1,32768]{2,0,1:T(2,128)(2,1)}, u32[]{:S(2)}) copy-start(bf16[2,1,32768]{2,0,1:T(2,128)(2,1)} %get-tuple-element.159) | copy-start | bytes 393220
  477.1 5.9 %collective-permute-start.27 = (bf16[2,2,25984]{2,1,0:T(2,128)(2,1)S(1)}, bf16[2,2,25984]{2,1,0:T(2,128)(2,1)S(1)}, u32[]{:S(2)}, u32[]{:S(2)}) collective-permute-start(bf16[2,2,25984]{2,1,0:T(2,128)(2,1)S(1)} %bitcast.174), channel_id=1, source_target_pairs={{0,4},{4,0},{8,12},{12,8},{16,20},{20,16},{24,28},{28,24},{1,5},{5... | collective-permute-start | bytes 623624 | tf_op jit(solution)/shard_map/ppermute | solution.py:213
  483.4 20.4 %copy-start.18 = (f32[256,1024]{1,0:T(8,128)S(1)}, f32[256,1024]{1,0:T(8,128)}, u32[]{:S(2)}) copy-start(f32[256,1024]{1,0:T(8,128)} %copy-done.17) | copy-start | bytes 3145732
  483.4 20.4 %copy-start.74 = (f32[256]{0:T(256)S(1)}, f32[256]{0:T(256)}, u32[]{:S(2)}) copy-start(f32[256]{0:T(256)} %get-tuple-element.174) | copy-start | bytes 3076
  483.5 4.8 collective-permute-start.28
  488.8 5.8 %collective-permute-start.29 = (bf16[25984]{0:T(1024)(128)(2,1)S(1)}, bf16[25984]{0:T(1024)(128)(2,1)}, u32[]{:S(2)}, u32[]{:S(2)}) collective-permute-start(bf16[25984]{0:T(1024)(128)(2,1)S(1)} %convert_reduce_fusion.1), channel_id=1, source_target_pairs={{0,16},{4,20},{8,24},{12,28},{16,0},{20,4},{24,8},{28,12},{1,17},{... | collective-permute-start | bytes 155912 | tf_op jit(solution)/shard_map/ppermute | solution.py:213
  491.2 18.0 %collective-permute-start.38 = (bf16[4,32768]{1,0:T(4,128)(2,1)S(1)}, bf16[4,32768]{1,0:T(4,128)(2,1)}, u32[]{:S(2)}, u32[]{:S(2)}) collective-permute-start(bf16[4,32768]{1,0:T(4,128)(2,1)S(1)} %reshape.329), channel_id=1, source_target_pairs={{0,4},{4,0},{8,12},{12,8},{16,20},{20,16},{24,28},{28,24},{1,5},{5... | collective-permute-start | bytes 786440 | tf_op jit(solution)/shard_map/ppermute | solution.py:218
  495.4 5.7 %collective-permute-start.30 = (bf16[1,25984]{1,0:T(2,128)(2,1)S(1)}, bf16[1,25984]{1,0:T(2,128)(2,1)S(1)}, u32[]{:S(2)}, u32[]{:S(2)}) collective-permute-start(bf16[1,25984]{1,0:T(2,128)(2,1)S(1)} %broadcast_in_dim.40), channel_id=1, source_target_pairs={{0,16},{4,20},{8,24},{12,28},{16,0},{20,4},{24,8},{28,12},{1,17},{... | collective-permute-start | bytes 155912 | tf_op jit(solution)/shard_map/ppermute | solution.py:218
  501.6 4.9 collective-permute-start.31
  507.6 5.9 %collective-permute-start.32 = (bf16[4,25984]{1,0:T(4,128)(2,1)S(1)}, bf16[4,25984]{1,0:T(4,128)(2,1)S(1)}, u32[]{:S(2)}, u32[]{:S(2)}) collective-permute-start(bf16[4,25984]{1,0:T(4,128)(2,1)S(1)} %reshape.324), channel_id=1, source_target_pairs={{0,4},{4,0},{8,12},{12,8},{16,20},{20,16},{24,28},{28,24},{1,5},{5... | collective-permute-start | bytes 623624 | tf_op jit(solution)/shard_map/ppermute | solution.py:218
  (59 other events, 228.8 us)
Sparse Core Ops, SparseCore 0:
  279.4 167.4 all-reduce.6
  516.2 19.6 all-gather.1

commit v10 on v9

--- a/solution.py
+++ b/solution.py
@@ -249,6 +249,22 @@
     return tuple(jnp.stack(parts) for parts in zip(*outs))
 
 
+def turn(block, cosine, sine):
+    half_depth = block.shape[-1] // 2
+    first_half, second_half = block[:, :half_depth], block[:, half_depth:]
+    return jnp.concatenate(
+        [first_half * cosine - second_half * sine, second_half * cosine + first_half * sine], axis=1
+    )
+
+
+def unturn(block, cosine, sine):
+    half_depth = block.shape[-1] // 2
+    first_half, second_half = block[:, :half_depth], block[:, half_depth:]
+    return jnp.concatenate(
+        [first_half * cosine + second_half * sine, second_half * cosine - first_half * sine], axis=1
+    )
+
+
 def local(
     tokens,
     doc_ids,
@@ -274,28 +290,37 @@
         head_all_gather(normed_one, 0),
         head_gather_relative(cotangent),
     )
-    factor_a = jnp.dot(normed_all, a_weight, preferred_element_type=jnp.float32).reshape(
-        total_rows, local_heads, rank_all
-    )
+    factor_a = jnp.dot(normed_all, a_weight, preferred_element_type=jnp.float32)
     factor_b = jnp.dot(normed_all, b_weight, preferred_element_type=jnp.float32)
     cosine, sine = rope_tables(total_rows, length)
-    basis_query = rotate(factor_b[:, : RQ * DH].reshape(total_rows, RQ, DH), cosine, sine)
-    basis_key = rotate(
-        factor_b[:, RQ * DH : (RQ + RK) * DH].reshape(total_rows, RK, DH), cosine, sine
-    )
-    basis_value = factor_b[:, (RQ + RK) * DH :].reshape(total_rows, RK, DH)
-    coef_query = factor_a[:, :, :RQ]
-    coef_key = factor_a[:, :, RQ : RQ + RK]
-    coef_value = factor_a[:, :, RQ + RK :]
-    queries = (jnp.einsum("thr,trd->thd", coef_query, basis_query, precision=PRECISE) / RQ).astype(
-        jnp.bfloat16
-    )
-    key_rows = (jnp.einsum("thr,trd->thd", coef_key, basis_key, precision=PRECISE) / RK).astype(
-        jnp.bfloat16
-    )
-    value_rows = (
-        jnp.einsum("thr,trd->thd", coef_value, basis_value, precision=PRECISE) / RK
-    ).astype(jnp.bfloat16)
+    basis_query = [
+        turn(factor_b[:, rank * DH : (rank + 1) * DH], cosine, sine) for rank in range(RQ)
+    ]
+    basis_key = [
+        turn(factor_b[:, (RQ + rank) * DH : (RQ + rank + 1) * DH], cosine, sine)
+        for rank in range(RK)
+    ]
+    basis_value = [
+        factor_b[:, (RQ + RK + rank) * DH : (RQ + RK + rank + 1) * DH] for rank in range(RK)
+    ]
+    coef = [
+        [factor_a[:, head * rank_all + column] [:, None] for column in range(rank_all)]
+        for head in range(local_heads)
+    ]
+
+    def combine(bases, offset):
+        return jnp.stack(
+            [
+                sum(coef[head][offset + rank] * bases[rank] for rank in range(len(bases)))
+                / len(bases)
+                for head in range(local_heads)
+            ],
+            axis=1,
+        ).astype(jnp.bfloat16)
+
+    queries = combine(basis_query, 0)
+    key_rows = combine(basis_key, RQ)
+    value_rows = combine(basis_value, RQ + RK)
     row_shape = (rows_dev, length, local_heads, DH)
     query_rows = queries.reshape(row_shape)
     keys_rows = key_rows.reshape(row_shape)
@@ -342,7 +367,7 @@
     output, grad_resid = lax.optimization_barrier((output, grad_resid))
     grad_branch = head_all_gather(grad_resid.astype(jnp.bfloat16), 0)
     grad_mixed = dot_last(grad_branch, out_weight).astype(jnp.bfloat16)
-    grad_out = dp_all_reduce(dot_first(mixed, grad_branch).astype(jnp.bfloat16).reshape(-1))
+    grad_out = dot_first(mixed, grad_branch)
     grad_query_rows, grad_key_rows, grad_value_rows = map_rows(
         attend_back,
         (query_rows, keys_rows, values_rows, doc_ids, log_total, grad_mixed.reshape(row_shape)),
@@ -351,29 +376,21 @@
     grad_query = rounded(grad_query_rows.reshape(head_shape))
     grad_key = rounded(grad_key_rows.reshape(head_shape))
     grad_value = rounded(grad_value_rows.reshape(head_shape))
-    grad_coef_query = jnp.einsum("thd,trd->thr", grad_query, basis_query, precision=PRECISE) / RQ
-    grad_coef_key = jnp.einsum("thd,trd->thr", grad_key, basis_key, precision=PRECISE) / RK
-    grad_coef_value = jnp.einsum("thd,trd->thr", grad_value, basis_value, precision=PRECISE) / RK
-    grad_basis_query = unrotate(
-        jnp.einsum("thr,thd->trd", coef_query, grad_query, precision=PRECISE) / RQ, cosine, sine
-    )
-    grad_basis_key = unrotate(
-        jnp.einsum("thr,thd->trd", coef_key, grad_key, precision=PRECISE) / RK, cosine, sine
-    )
-    grad_basis_value = jnp.einsum("thr,thd->trd", coef_value, grad_value, precision=PRECISE) / RK
-    grad_factor_a = (
-        jnp.concatenate([grad_coef_query, grad_coef_key, grad_coef_value], axis=-1)
-        .reshape(total_rows, local_heads * rank_all)
-        .astype(jnp.bfloat16)
-    )
-    grad_factor_b = jnp.concatenate(
-        [
-            grad_basis_query.reshape(total_rows, RQ * DH),
-            grad_basis_key.reshape(total_rows, RK * DH),
-            grad_basis_value.reshape(total_rows, RK * DH),
-        ],
-        axis=-1,
-    )
+    grads_by_part = ((grad_query, basis_query, 0), (grad_key, basis_key, RQ), (grad_value, basis_value, RQ + RK))
+    coef_columns = [None] * (local_heads * rank_all)
+    basis_grads = []
+    for grad_part, bases, offset in grads_by_part:
+        for rank, basis in enumerate(bases):
+            for head in range(local_heads):
+                coef_columns[head * rank_all + offset + rank] = jnp.sum(
+                    grad_part[:, head, :] * basis, axis=1
+                ) / len(bases)
+            basis_grad = sum(
+                coef[head][offset + rank] * grad_part[:, head, :] for head in range(local_heads)
+            ) / len(bases)
+            basis_grads.append(basis_grad if offset == RQ + RK else unturn(basis_grad, cosine, sine))
+    grad_factor_a = jnp.stack(coef_columns, axis=1).astype(jnp.bfloat16)
+    grad_factor_b = jnp.concatenate(basis_grads, axis=1)
     head_count = lax.axis_size("head")
     basis_cols = grad_factor_b.shape[1] // head_count
     factor_cols = head_reduce_scatter(grad_factor_b.astype(jnp.bfloat16), 1).astype(jnp.bfloat16)
@@ -395,9 +412,9 @@
         jnp.concatenate([grad_gain_attn_own, grad_gain_ffn_own]),
         (0, gain_rows * basis_cols - 2 * features),
     ).reshape(gain_rows, basis_cols)
-    grad_out = grad_out.reshape(out_weight.shape)
     tail = (
         grad_a.astype(jnp.bfloat16),
+        grad_out.astype(jnp.bfloat16),
         jnp.concatenate([grad_b_cols, gains], axis=0).astype(jnp.bfloat16),
     )
     tail, (grad_gate, grad_up, grad_down) = lax.optimization_barrier(
@@ -405,7 +422,7 @@
     )
     sizes = [part.size for part in tail]
     summed = dp_all_reduce(jnp.concatenate([part.reshape(-1) for part in tail]))
-    grad_a, packed = (
+    grad_a, grad_out, packed = (
         summed[sum(sizes[:index]) : sum(sizes[: index + 1])].reshape(part.shape)
         for index, part in enumerate(tail)
     )

time: 561 us -> 475 us (0.85)
  matrix products: 122 us -> 48.5 us
  local copies, waits for them, and re-layouts: 104 us -> 55.3 us
  waiting for transfers between devices: 207 us -> 254 us
  starting transfers between devices: 43.3 us -> 31.8 us
    dot_general x10 -> x1, matrix products: 68.5 us -> 0.74 us  [local(): factor_a = jnp.dot(normed_all, a_weight, preferred_element_type=jnp.float32)]
    psum x1, waiting for transfers between devices: 0.02 us -> 42.1 us  [local(): grad_gate, grad_up, grad_down = lax.psum(ffn_grads, 'dp')]
    unnamed x180 -> x320, local copies, waits for them, and re-layouts: 31 us -> 13.3 us
    slice x9 -> x3, local copies, waits for them, and re-layouts: 15.4 us -> 1.92 us  [local(): factor_a[:, head * rank_all + column][:, None]]
    unnamed x2 -> x18, other arithmetic: 0.01 us -> 9.5 us
    optimization_barrier x3 -> x0, local copies, waits for them, and re-layouts: 6.4 us -> none  [rounded(): lax.optimization_barrier(values_in.astype(jnp.bfloat16)).astype(jnp.float32)]
    ppermute x6 -> x3, starting transfers between devices: 8.76 us -> 3.11 us  [dp_all_reduce(): lax.ppermute(sent.astype(jnp.bfloat16), 'dp', pairs).astype(jnp.float32)]
    ppermute x6 -> x3, waiting for transfers between devices: 21.7 us -> 25.7 us  [dp_all_reduce(): arrived = lax.ppermute(whole, 'dp', pairs)]
  transfers between devices with their start and end apart: 41 -> 35, of which waited for: 30 -> 28; matrix products, arithmetic and copies ran while one was open for 26% -> 19% of each run, Pallas kernels for 0% -> 0%
where the time goes in v10:
time: 475 us; the launch traced here: 466 us
  waiting for transfers between devices  254 us (53%)
  other arithmetic  59.9 us (13%)
  local copies, waits for them, and re-layouts  55.3 us (12%)
  matrix products  48.5 us (10%)
  starting transfers between devices  31.8 us (7%)
  between operations  17.5 us (4%)
    ppermute x9, waiting for transfers between devices, head_reduce_scatter(): lax.ppermute(sent, 'head', [(device, (device + shift) % count) for device...  55.7 us
    psum x1, waiting for transfers between devices, local(): grad_gate, grad_up, grad_down = lax.psum(ffn_grads, 'dp')  42.1 us
    ppermute x6, waiting for transfers between devices, head_gather_relative(): lax.ppermute(values, 'head', [(device, (device + shift) % count) for devi...  40.9 us
    ppermute x6, waiting for transfers between devices, head_all_gather(): lax.ppermute(values, 'head', [(device, (device + shift) % count) for devi...  36.4 us
    ppermute x6, waiting for transfers between devices, head_scatter_relative(): lax.ppermute(sent, 'head', [(device, (device + shift) % count) for device...  27.6 us
    ppermute x3, waiting for transfers between devices, dp_all_reduce(): arrived = lax.ppermute(whole, 'dp', pairs)  25.7 us
    ppermute x3, waiting for transfers between devices, dp_all_reduce(): lax.ppermute(sent.astype(jnp.bfloat16), 'dp', pairs).astype(jnp.float32)  20.7 us
    unnamed x320, local copies, waits for them, and re-layouts  13.3 us
  transfers between devices with their start and end apart: 35, of which 28 were waited for; matrix products, arithmetic and copies ran while one was open for 19% of the time, Pallas kernels for 0%

profile of v10, /device:TPU:0, one launch (start us, length us, event | category | flops | bytes accessed | tf_op | source)
XLA Modules:
  0.0 466.5 jit_solution(17982052014270615556)
XLA Ops:
  11.2 3.0 collective-permute-start.1
  14.2 1.7 collective-permute-start.2
  18.9 17.9 %collective-permute-done = bf16[256,1024]{1,0:T(8,128)(2,1)} collective-permute-done((bf16[256,1024]{1,0:T(8,128)(2,1)}, bf16[256,1024]{1,0:T(8,128)(2,1)}, u32[]{:S(2)}, u32[]{:S(2)}) %collective-permute-start) | collective-permute-done | bytes 524320 | tf_op jit(solution)/shard_map/ppermute | solution.py:190
  43.1 1.6 fusion.225
  52.1 1.8 fusion.222
  54.5 2.1 fusion
  58.4 2.3 fusion.39
  61.9 1.7 collective-permute-start.5
  65.6 8.7 %collective-permute-done.3 = bf16[256,1024]{1,0:T(8,128)(2,1)S(1)} collective-permute-done((bf16[256,1024]{1,0:T(8,128)(2,1)S(1)}, bf16[256,1024]{1,0:T(8,128)(2,1)S(1)}, u32[]{:S(2)}, u32[]{:S(2)}) %collective-permute-start.3) | collective-permute-done | bytes 524320 | tf_op jit(solution)/shard_map/ppermute | solution.py:174
  74.3 1.6 collective-permute-done.5
  75.9 13.2 %collective-permute-done.4 = bf16[256,1024]{1,0:T(8,128)(2,1)S(1)} collective-permute-done((bf16[256,1024]{1,0:T(8,128)(2,1)S(1)}, bf16[256,1024]{1,0:T(8,128)(2,1)S(1)}, u32[]{:S(2)}, u32[]{:S(2)}) %collective-permute-start.4) | collective-permute-done | bytes 524320 | tf_op jit(solution)/shard_map/ppermute | solution.py:174
  91.1 16.9 %collective-permute-done.12 = bf16[256,1024]{1,0:T(8,128)(2,1)S(1)} collective-permute-done((bf16[256,1024]{1,0:T(8,128)(2,1)S(1)}, bf16[256,1024]{1,0:T(8,128)(2,1)S(1)}, u32[]{:S(2)}, u32[]{:S(2)}) %collective-permute-start.12) | collective-permute-done | bytes 524320 | tf_op jit(solution)/shard_map/ppermute | solution.py:230
  109.7 11.2 %collective-permute-done.8 = bf16[256,1024]{1,0:T(8,128)(2,1)S(1)} collective-permute-done((bf16[256,1024]{1,0:T(8,128)(2,1)S(1)}, bf16[256,1024]{1,0:T(8,128)(2,1)S(1)}, u32[]{:S(2)}, u32[]{:S(2)}) %collective-permute-start.8) | collective-permute-done | bytes 524320 | tf_op jit(solution)/shard_map/ppermute | solution.py:230
  120.8 11.4 %collective-permute-done.7 = bf16[256,1024]{1,0:T(8,128)(2,1)S(1)} collective-permute-done((bf16[256,1024]{1,0:T(8,128)(2,1)S(1)}, bf16[256,1024]{1,0:T(8,128)(2,1)S(1)}, u32[]{:S(2)}, u32[]{:S(2)}) %collective-permute-start.7) | collective-permute-done | bytes 524320 | tf_op jit(solution)/shard_map/ppermute | solution.py:230
  132.2 1.7 fusion.211
  133.9 1.7 fusion.212
  135.7 3.3 multiply_convert_fusion.2
  139.0 2.8 convolution_convert_fusion.4
  141.7 1.8 convolution_convert_fusion.1
  144.9 1.7 collective-permute-start.11
  146.6 1.8 fusion.226
  148.5 1.8 add_convert_fusion.1
  151.6 1.7 collective-permute-start.17
  154.8 2.8 convolution_convert_fusion.2
  157.6 2.8 convolution_convert_fusion.3
  160.4 8.5 %collective-permute-done.15 = bf16[256,1024]{1,0:T(8,128)(2,1)} collective-permute-done((bf16[256,1024]{1,0:T(8,128)(2,1)}, bf16[256,1024]{1,0:T(8,128)(2,1)}, u32[]{:S(2)}, u32[]{:S(2)}) %collective-permute-start.15) | collective-permute-done | bytes 524320 | tf_op jit(solution)/shard_map/ppermute | solution.py:241
  168.9 2.4 collective-permute-start.10
  171.3 12.4 %collective-permute-done.16 = bf16[256,1024]{1,0:T(8,128)(2,1)} collective-permute-done((bf16[256,1024]{1,0:T(8,128)(2,1)}, bf16[256,1024]{1,0:T(8,128)(2,1)}, u32[]{:S(2)}, u32[]{:S(2)}) %collective-permute-start.16) | collective-permute-done | bytes 524320 | tf_op jit(solution)/shard_map/ppermute | solution.py:241
  183.6 1.8 convert_add_fusion.2
  186.3 6.7 %collective-permute-done.10 = bf16[256,1024]{1,0:T(8,128)(2,1)S(1)} collective-permute-done((bf16[256,1024]{1,0:T(8,128)(2,1)}, bf16[256,1024]{1,0:T(8,128)(2,1)S(1)}, u32[]{:S(2)}, u32[]{:S(2)}) %collective-permute-start.10) | collective-permute-done | bytes 524320 | tf_op jit(solution)/shard_map/ppermute | solution.py:241
  193.0 2.7 subtract_add_fusion
  201.3 10.4 %collective-permute-done.18 = bf16[256,1024]{1,0:T(8,128)(2,1)S(1)} collective-permute-done((bf16[256,1024]{1,0:T(8,128)(2,1)S(1)}, bf16[256,1024]{1,0:T(8,128)(2,1)S(1)}, u32[]{:S(2)}, u32[]{:S(2)}) %collective-permute-start.18) | collective-permute-done | bytes 524320 | tf_op jit(solution)/shard_map/ppermute | solution.py:190
  212.9 1.9 constant_dynamic-update-slice_fusion.5
  214.8 7.7 %collective-permute-done.20 = bf16[256,1024]{1,0:T(8,128)(2,1)} collective-permute-done((bf16[256,1024]{1,0:T(8,128)(2,1)S(1)}, bf16[256,1024]{1,0:T(8,128)(2,1)}, u32[]{:S(2)}, u32[]{:S(2)}) %collective-permute-start.20) | collective-permute-done | bytes 524320 | tf_op jit(solution)/shard_map/ppermute | solution.py:190
  222.5 1.9 constant_dynamic-update-slice_fusion.4
  224.3 2.5 convolution_convert_fusion.6
  233.2 2.2 multiply_reduce_fusion
  235.4 1.7 multiply_convert_fusion
  246.9 1.9 fusion.25
  268.7 2.5 collective-permute-start.21
  273.2 3.4 convolution_convert_fusion.5
  277.3 2.8 collective-permute-done.21
  280.4 7.5 %collective-permute-done.22 = bf16[1024,160]{0,1:T(8,128)(2,1)} collective-permute-done((bf16[1024,160]{0,1:T(8,128)(2,1)S(1)}, bf16[1024,160]{0,1:T(8,128)(2,1)}, u32[]{:S(2)}, u32[]{:S(2)}) %collective-permute-start.22) | collective-permute-done | bytes 327712 | tf_op jit(solution)/shard_map/ppermute | solution.py:174
  289.3 2.2 add_convert_fusion
  291.7 2.1 collective-permute-start.26
  295.4 9.2 %collective-permute-done.24 = bf16[256,1024]{1,0:T(8,128)(2,1)S(1)} collective-permute-done((bf16[256,1024]{1,0:T(8,128)(2,1)S(1)}, bf16[256,1024]{1,0:T(8,128)(2,1)S(1)}, u32[]{:S(2)}, u32[]{:S(2)}) %collective-permute-start.24) | collective-permute-done | bytes 524320 | tf_op jit(solution)/shard_map/ppermute | solution.py:174
  306.1 11.0 %collective-permute-done.25 = bf16[256,1024]{1,0:T(8,128)(2,1)S(1)} collective-permute-done((bf16[256,1024]{1,0:T(8,128)(2,1)S(1)}, bf16[256,1024]{1,0:T(8,128)(2,1)S(1)}, u32[]{:S(2)}, u32[]{:S(2)}) %collective-permute-start.25) | collective-permute-done | bytes 524320 | tf_op jit(solution)/shard_map/ppermute | solution.py:174
  318.9 42.1 %all-reduce.7.cloned.1.call-done = (bf16[1024,704]{0,1:T(8,128)(2,1)}, bf16[1024,704]{0,1:T(8,128)(2,1)}, bf16[704,1024]{1,0:T(8,128)(2,1)}) async-done(((bf16[1024,704]{0,1:T(8,128)(2,1)}, bf16[1024,704]{0,1:T(8,128)(2,1)}, bf16[704,1024]{1,0:T(8,128)(2,1)}), (bf16[1024,704]{0,1:T(8,128)(2,1)}, bf16[1024,704]{0,1:T(8,128)(2,1)}, bf16[704,1024]{1,0:T(8,128)(2,1)})) %all-reduce.7.cloned.1.call-update) | async-done | bytes 4325392 | tf_op jit(solution)/shard_map/psum | solution.py:364
  362.8 2.4 reshape.2431
  365.3 2.5 dynamic-slice_convert_fusion
  370.6 10.1 %collective-permute-done.27 = bf16[2,2,58752]{2,1,0:T(2,128)(2,1)S(1)} collective-permute-done((bf16[2,2,58752]{2,1,0:T(2,128)(2,1)S(1)}, bf16[2,2,58752]{2,1,0:T(2,128)(2,1)S(1)}, u32[]{:S(2)}, u32[]{:S(2)}) %collective-permute-start.27) | collective-permute-done | bytes 470048 | tf_op jit(solution)/shard_map/ppermute | solution.py:213
  382.5 6.0 %collective-permute-done.28 = bf16[2,58752]{1,0:T(2,128)(2,1)S(1)} collective-permute-done((bf16[2,58752]{1,0:T(2,128)(2,1)S(1)}, bf16[2,58752]{1,0:T(2,128)(2,1)S(1)}, u32[]{:S(2)}, u32[]{:S(2)}) %collective-permute-start.28) | collective-permute-done | bytes 235040 | tf_op jit(solution)/shard_map/ppermute | solution.py:213
  391.7 4.6 collective-permute-done.29
  397.1 9.6 %collective-permute-done.30 = bf16[1,58752]{1,0:T(2,128)(2,1)S(1)} collective-permute-done((bf16[1,58752]{1,0:T(2,128)(2,1)S(1)}, bf16[1,58752]{1,0:T(2,128)(2,1)S(1)}, u32[]{:S(2)}, u32[]{:S(2)}) %collective-permute-start.30) | collective-permute-done | bytes 117536 | tf_op jit(solution)/shard_map/ppermute | solution.py:218
  407.7 6.6 %collective-permute-done.31 = bf16[2,58752]{1,0:T(2,128)(2,1)S(1)} collective-permute-done((bf16[2,58752]{1,0:T(2,128)(2,1)S(1)}, bf16[2,58752]{1,0:T(2,128)(2,1)S(1)}, u32[]{:S(2)}, u32[]{:S(2)}) %collective-permute-start.31) | collective-permute-done | bytes 235040 | tf_op jit(solution)/shard_map/ppermute | solution.py:218
  418.3 9.6 %collective-permute-done.32 = bf16[4,58752]{1,0:T(4,128)(2,1)S(1)} collective-permute-done((bf16[4,58752]{1,0:T(4,128)(2,1)S(1)}, bf16[4,58752]{1,0:T(4,128)(2,1)S(1)}, u32[]{:S(2)}, u32[]{:S(2)}) %collective-permute-start.32) | collective-permute-done | bytes 470048 | tf_op jit(solution)/shard_map/ppermute | solution.py:218
  432.0 1.5 reshape.2428
  434.5 2.6 fusion.46
  437.2 1.9 convert_element_type.441
  439.1 1.9 convert_element_type.442
  441.1 1.9 convert_element_type.443
  446.9 4.4 all-gather.2.cloned.1.call-done
  453.0 3.2 slice.762
  456.2 3.2 copy.85
  (554 shorter events, 110.4 us)
Async XLA Ops:
  7.2 128.5 %copy-start = (bf16[704,1024]{1,0:T(8,128)(2,1)S(1)}, bf16[704,1024]{1,0:T(8,128)(2,1)}, u32[]{:S(2)}) copy-start(bf16[704,1024]{1,0:T(8,128)(2,1)} %param.20) | copy-start | bytes 4325380
  7.2 353.7 %all-reduce.7.cloned.1.call-start = ((), (), s32[]{:S(2)}) async-start(), calls=%async_computation.1 | async-start | bytes 8650752 | tf_op jit(solution)/shard_map/psum | solution.py:364
  7.3 8.7 %copy-start.137 = (s32[1,1024]{1,0:T(1,128)S(1)}, s32[1,1024]{1,0:T(1,128)}, u32[]{:S(2)}) copy-start(s32[1,1024]{1,0:T(1,128)} %param.12) | copy-start | bytes 12292
  9.2 8.3 %copy-start.147 = (f32[256]{0:T(256)}, f32[256]{0:T(256)S(1)}, u32[]{:S(2)}) copy-start(f32[256]{0:T(256)S(1)} %get-tuple-element.250) | copy-start | bytes 3076
  11.2 26.7 %collective-permute-start.1 = (bf16[256,1024]{1,0:T(8,128)(2,1)}, bf16[256,1024]{1,0:T(8,128)(2,1)}, u32[]{:S(2)}, u32[]{:S(2)}) collective-permute-start(bf16[256,1024]{1,0:T(8,128)(2,1)} %get-tuple-element.137), channel_id=1, source_target_pairs={{0,2},{1,3},{2,0},{3,1},{4,6},{5,7},{6,4},{7,5},{8,10},{9,11},{10,... | collective-permute-start | bytes 1572872 | tf_op jit(solution)/shard_map/ppermute | solution.py:190
  14.2 22.6 %collective-permute-start = (bf16[256,1024]{1,0:T(8,128)(2,1)}, bf16[256,1024]{1,0:T(8,128)(2,1)}, u32[]{:S(2)}, u32[]{:S(2)}) collective-permute-start(bf16[256,1024]{1,0:T(8,128)(2,1)} %get-tuple-element.137), channel_id=1, source_target_pairs={{0,1},{1,2},{2,3},{3,0},{4,5},{5,6},{6,7},{7,4},{8,9},{9,10},{10,1... | collective-permute-start | bytes 1572872 | tf_op jit(solution)/shard_map/ppermute | solution.py:190
  14.2 24.8 %collective-permute-start.2 = (bf16[256,1024]{1,0:T(8,128)(2,1)}, bf16[256,1024]{1,0:T(8,128)(2,1)}, u32[]{:S(2)}, u32[]{:S(2)}) collective-permute-start(bf16[256,1024]{1,0:T(8,128)(2,1)} %get-tuple-element.137), channel_id=1, source_target_pairs={{0,3},{1,0},{2,1},{3,2},{4,7},{5,4},{6,5},{7,6},{8,11},{9,8},{10,9... | collective-permute-start | bytes 1572872 | tf_op jit(solution)/shard_map/ppermute | solution.py:190
  17.6 22.6 %copy-start.78 = (bf16[1024,40]{0,1:T(8,128)(2,1)S(1)}, bf16[1024,40]{0,1:T(8,128)(2,1)}, u32[]{:S(2)}) copy-start(bf16[1024,40]{0,1:T(8,128)(2,1)} %param.14) | copy-start | bytes 245764
  42.3 14.2 %copy-start.82 = (f32[1024,1]{0,1:T(1,128)}, f32[1024,1]{0,1:T(1,128)S(1)}, u32[]{:S(2)}) copy-start(f32[1024,1]{0,1:T(1,128)S(1)} %get-tuple-element.224) | copy-start | bytes 12292
  42.3 14.2 %copy-start.84 = (f32[1024,1]{0,1:T(1,128)}, f32[1024,1]{0,1:T(1,128)S(1)}, u32[]{:S(2)}) copy-start(f32[1024,1]{0,1:T(1,128)S(1)} %get-tuple-element.239) | copy-start | bytes 12292
  42.3 14.2 %copy-start.86 = (f32[1024,1]{0,1:T(1,128)}, f32[1024,1]{0,1:T(1,128)S(1)}, u32[]{:S(2)}) copy-start(f32[1024,1]{0,1:T(1,128)S(1)} %get-tuple-element.241) | copy-start | bytes 12292
  42.3 14.2 %copy-start.88 = (f32[1024,1]{0,1:T(1,128)}, f32[1024,1]{0,1:T(1,128)S(1)}, u32[]{:S(2)}) copy-start(f32[1024,1]{0,1:T(1,128)S(1)} %get-tuple-element.240) | copy-start | bytes 12292
  42.4 14.2 %copy-start.90 = (f32[1024,1]{0,1:T(1,128)}, f32[1024,1]{0,1:T(1,128)S(1)}, u32[]{:S(2)}) copy-start(f32[1024,1]{0,1:T(1,128)S(1)} %get-tuple-element.242) | copy-start | bytes 12292
  43.0 7.8 %copy-start.96 = (f32[1024,1]{0,1:T(1,128)}, f32[1024,1]{0,1:T(1,128)S(1)}, u32[]{:S(2)}) copy-start(f32[1024,1]{0,1:T(1,128)S(1)} %get-tuple-element.210) | copy-start | bytes 12292
  43.0 7.8 %copy-start.98 = (f32[1024,1]{0,1:T(1,128)}, f32[1024,1]{0,1:T(1,128)S(1)}, u32[]{:S(2)}) copy-start(f32[1024,1]{0,1:T(1,128)S(1)} %get-tuple-element.212) | copy-start | bytes 12292
  43.1 7.8 %copy-start.110 = (f32[1024,1]{0,1:T(1,128)}, f32[1024,1]{0,1:T(1,128)S(1)}, u32[]{:S(2)}) copy-start(f32[1024,1]{0,1:T(1,128)S(1)} %get-tuple-element.209) | copy-start | bytes 12292
  43.1 13.5 %copy-start.92 = (f32[1024,1]{0,1:T(1,128)}, f32[1024,1]{0,1:T(1,128)S(1)}, u32[]{:S(2)}) copy-start(f32[1024,1]{0,1:T(1,128)S(1)} %get-tuple-element.205) | copy-start | bytes 12292
  44.7 11.9 %copy-start.37 = (f32[1024,640]{0,1:T(8,128)}, f32[1024,640]{0,1:T(8,128)S(1)}, u32[]{:S(2)}) copy-start(f32[1024,640]{0,1:T(8,128)S(1)} %fusion.225) | copy-start | bytes 7864324
  61.6 27.5 %copy-start.8 = (bf16[256,1024]{1,0:T(8,128)(2,1)S(1)}, bf16[256,1024]{1,0:T(8,128)(2,1)}, u32[]{:S(2)}) copy-start(bf16[256,1024]{1,0:T(8,128)(2,1)} %param.11) | copy-start | bytes 1572868
  61.8 28.5 %copy-start.126 = (f32[1024]{0:T(1024)S(1)}, f32[1024]{0:T(1024)}, u32[]{:S(2)}) copy-start(f32[1024]{0:T(1024)} %param.17) | copy-start | bytes 12292
  61.8 12.5 %collective-permute-start.3 = (bf16[256,1024]{1,0:T(8,128)(2,1)S(1)}, bf16[256,1024]{1,0:T(8,128)(2,1)S(1)}, u32[]{:S(2)}, u32[]{:S(2)}) collective-permute-start(bf16[256,1024]{1,0:T(8,128)(2,1)S(1)} %get-tuple-element.170), channel_id=1, source_target_pairs={{0,1},{1,2},{2,3},{3,0},{4,5},{5,6},{6,7},{7,4},{8,9},{9,10},{10,1... | collective-permute-start | bytes 1572872 | tf_op jit(solution)/shard_map/ppermute | solution.py:174
  61.9 14.1 %collective-permute-start.5 = (bf16[256,1024]{1,0:T(8,128)(2,1)S(1)}, bf16[256,1024]{1,0:T(8,128)(2,1)S(1)}, u32[]{:S(2)}, u32[]{:S(2)}) collective-permute-start(bf16[256,1024]{1,0:T(8,128)(2,1)S(1)} %get-tuple-element.171), channel_id=1, source_target_pairs={{0,3},{1,0},{2,1},{3,2},{4,7},{5,4},{6,5},{7,6},{8,11},{9,8},{10,9... | collective-permute-start | bytes 1572872 | tf_op jit(solution)/shard_map/ppermute | solution.py:174
  63.6 25.5 %collective-permute-start.4 = (bf16[256,1024]{1,0:T(8,128)(2,1)S(1)}, bf16[256,1024]{1,0:T(8,128)(2,1)S(1)}, u32[]{:S(2)}, u32[]{:S(2)}) collective-permute-start(bf16[256,1024]{1,0:T(8,128)(2,1)S(1)} %get-tuple-element.172), channel_id=1, source_target_pairs={{0,2},{1,3},{2,0},{3,1},{4,6},{5,7},{6,4},{7,5},{8,10},{9,11},{10,... | collective-permute-start | bytes 1572872 | tf_op jit(solution)/shard_map/ppermute | solution.py:174
  65.1 43.0 %collective-permute-start.13 = (bf16[256,1024]{1,0:T(8,128)(2,1)S(1)}, bf16[256,1024]{1,0:T(8,128)(2,1)S(1)}, u32[]{:S(2)}, u32[]{:S(2)}) collective-permute-start(bf16[256,1024]{1,0:T(8,128)(2,1)S(1)} %copy-done.52), channel_id=1, source_target_pairs={{0,2},{1,3},{2,0},{3,1},{4,6},{5,7},{6,4},{7,5},{8,10},{9,11},{10,... | collective-permute-start | bytes 1572872 | tf_op jit(solution)/shard_map/ppermute | solution.py:230
  65.6 42.4 %collective-permute-start.12 = (bf16[256,1024]{1,0:T(8,128)(2,1)S(1)}, bf16[256,1024]{1,0:T(8,128)(2,1)S(1)}, u32[]{:S(2)}, u32[]{:S(2)}) collective-permute-start(bf16[256,1024]{1,0:T(8,128)(2,1)S(1)} %copy-done.52), channel_id=1, source_target_pairs={{0,1},{1,2},{2,3},{3,0},{4,5},{5,6},{6,7},{7,4},{8,9},{9,10},{10,1... | collective-permute-start | bytes 1572872 | tf_op jit(solution)/shard_map/ppermute | solution.py:230
  74.3 35.3 %collective-permute-start.14 = (bf16[256,1024]{1,0:T(8,128)(2,1)S(1)}, bf16[256,1024]{1,0:T(8,128)(2,1)S(1)}, u32[]{:S(2)}, u32[]{:S(2)}) collective-permute-start(bf16[256,1024]{1,0:T(8,128)(2,1)S(1)} %copy-done.52), channel_id=1, source_target_pairs={{0,3},{1,0},{2,1},{3,2},{4,7},{5,4},{6,5},{7,6},{8,11},{9,8},{10,9... | collective-permute-start | bytes 1572872 | tf_op jit(solution)/shard_map/ppermute | solution.py:230
  89.6 18.6 %copy-start.5 = (f32[256,1024]{1,0:T(8,128)}, f32[256,1024]{1,0:T(8,128)S(1)}, u32[]{:S(2)}) copy-start(f32[256,1024]{1,0:T(8,128)S(1)} %get-tuple-element.135) | copy-start | bytes 3145732
  90.4 41.9 %copy-start.153 = (bf16[1024,704]{0,1:T(8,128)(2,1)S(1)}, bf16[1024,704]{0,1:T(8,128)(2,1)}, u32[]{:S(2)}) copy-start(bf16[1024,704]{0,1:T(8,128)(2,1)} %param.19) | copy-start | bytes 4325380
  90.4 30.4 %collective-permute-start.8 = (bf16[256,1024]{1,0:T(8,128)(2,1)S(1)}, bf16[256,1024]{1,0:T(8,128)(2,1)S(1)}, u32[]{:S(2)}, u32[]{:S(2)}) collective-permute-start(bf16[256,1024]{1,0:T(8,128)(2,1)S(1)} %multiply_convert_fusion.5), channel_id=1, source_target_pairs={{0,3},{1,0},{2,1},{3,2},{4,7},{5,4},{6,5},{7,6},{8,11},{9,8},{10,9... | collective-permute-start | bytes 1572872 | tf_op jit(solution)/shard_map/ppermute | solution.py:230
  90.5 41.8 %collective-permute-start.7 = (bf16[256,1024]{1,0:T(8,128)(2,1)S(1)}, bf16[256,1024]{1,0:T(8,128)(2,1)S(1)}, u32[]{:S(2)}, u32[]{:S(2)}) collective-permute-start(bf16[256,1024]{1,0:T(8,128)(2,1)S(1)} %multiply_convert_fusion.5), channel_id=1, source_target_pairs={{0,2},{1,3},{2,0},{3,1},{4,6},{5,7},{6,4},{7,5},{8,10},{9,11},{10,... | collective-permute-start | bytes 1572872 | tf_op jit(solution)/shard_map/ppermute | solution.py:230
  108.0 24.2 %collective-permute-start.6 = (bf16[256,1024]{1,0:T(8,128)(2,1)S(1)}, bf16[256,1024]{1,0:T(8,128)(2,1)S(1)}, u32[]{:S(2)}, u32[]{:S(2)}) collective-permute-start(bf16[256,1024]{1,0:T(8,128)(2,1)S(1)} %multiply_convert_fusion.5), channel_id=1, source_target_pairs={{0,1},{1,2},{2,3},{3,0},{4,5},{5,6},{6,7},{7,4},{8,9},{9,10},{10,1... | collective-permute-start | bytes 1572872 | tf_op jit(solution)/shard_map/ppermute | solution.py:230
  109.6 24.3 %copy-start.152 = (bf16[1024,704]{0,1:T(8,128)(2,1)S(1)}, bf16[1024,704]{0,1:T(8,128)(2,1)}, u32[]{:S(2)}) copy-start(bf16[1024,704]{0,1:T(8,128)(2,1)} %param.18) | copy-start | bytes 4325380
  144.9 41.4 %collective-permute-start.9 = (bf16[256,1024]{1,0:T(8,128)(2,1)}, bf16[256,1024]{1,0:T(8,128)(2,1)}, u32[]{:S(2)}, u32[]{:S(2)}) collective-permute-start(bf16[256,1024]{1,0:T(8,128)(2,1)} %get-tuple-element.167), channel_id=1, source_target_pairs={{0,1},{1,2},{2,3},{3,0},{4,5},{5,6},{6,7},{7,4},{8,9},{9,10},{10,1... | collective-permute-start | bytes 1572872 | tf_op jit(solution)/shard_map/ppermute | solution.py:241
  144.9 41.4 %collective-permute-start.11 = (bf16[256,1024]{1,0:T(8,128)(2,1)}, bf16[256,1024]{1,0:T(8,128)(2,1)}, u32[]{:S(2)}, u32[]{:S(2)}) collective-permute-start(bf16[256,1024]{1,0:T(8,128)(2,1)} %get-tuple-element.168), channel_id=1, source_target_pairs={{0,3},{1,0},{2,1},{3,2},{4,7},{5,4},{6,5},{7,6},{8,11},{9,8},{10,9... | collective-permute-start | bytes 1572872 | tf_op jit(solution)/shard_map/ppermute | solution.py:241
  151.6 17.3 %collective-permute-start.15 = (bf16[256,1024]{1,0:T(8,128)(2,1)}, bf16[256,1024]{1,0:T(8,128)(2,1)}, u32[]{:S(2)}, u32[]{:S(2)}) collective-permute-start(bf16[256,1024]{1,0:T(8,128)(2,1)} %get-tuple-element.164), channel_id=1, source_target_pairs={{0,1},{1,2},{2,3},{3,0},{4,5},{5,6},{6,7},{7,4},{8,9},{9,10},{10,1... | collective-permute-start | bytes 1572872 | tf_op jit(solution)/shard_map/ppermute | solution.py:241
  151.6 19.6 %collective-permute-start.17 = (bf16[256,1024]{1,0:T(8,128)(2,1)}, bf16[256,1024]{1,0:T(8,128)(2,1)}, u32[]{:S(2)}, u32[]{:S(2)}) collective-permute-start(bf16[256,1024]{1,0:T(8,128)(2,1)} %get-tuple-element.165), channel_id=1, source_target_pairs={{0,3},{1,0},{2,1},{3,2},{4,7},{5,4},{6,5},{7,6},{8,11},{9,8},{10,9... | collective-permute-start | bytes 1572872 | tf_op jit(solution)/shard_map/ppermute | solution.py:241
  153.4 30.3 %collective-permute-start.16 = (bf16[256,1024]{1,0:T(8,128)(2,1)}, bf16[256,1024]{1,0:T(8,128)(2,1)}, u32[]{:S(2)}, u32[]{:S(2)}) collective-permute-start(bf16[256,1024]{1,0:T(8,128)(2,1)} %get-tuple-element.166), channel_id=1, source_target_pairs={{0,2},{1,3},{2,0},{3,1},{4,6},{5,7},{6,4},{7,5},{8,10},{9,11},{10,... | collective-permute-start | bytes 1572872 | tf_op jit(solution)/shard_map/ppermute | solution.py:241
  160.4 25.1 %copy-start.6 = (f32[256,1024]{1,0:T(8,128)S(1)}, f32[256,1024]{1,0:T(8,128)}, u32[]{:S(2)}) copy-start(f32[256,1024]{1,0:T(8,128)} %copy-done.5) | copy-start | bytes 3145732
  168.9 24.1 %copy-start.53 = (bf16[256,1024]{1,0:T(8,128)(2,1)S(1)}, bf16[256,1024]{1,0:T(8,128)(2,1)}, u32[]{:S(2)}) copy-start(bf16[256,1024]{1,0:T(8,128)(2,1)} %param.21) | copy-start | bytes 1572868
  168.9 24.1 %copy-start.151 = (f32[256]{0:T(256)S(1)}, f32[256]{0:T(256)}, u32[]{:S(2)}) copy-start(f32[256]{0:T(256)} %get-tuple-element.251) | copy-start | bytes 3076
  168.9 24.1 %collective-permute-start.10 = (bf16[256,1024]{1,0:T(8,128)(2,1)}, bf16[256,1024]{1,0:T(8,128)(2,1)S(1)}, u32[]{:S(2)}, u32[]{:S(2)}) collective-permute-start(bf16[256,1024]{1,0:T(8,128)(2,1)} %get-tuple-element.169), channel_id=1, source_target_pairs={{0,2},{1,3},{2,0},{3,1},{4,6},{5,7},{6,4},{7,5},{8,10},{9,11},{10,... | collective-permute-start | bytes 1572872 | tf_op jit(solution)/shard_map/ppermute | solution.py:241
  198.0 13.6 %collective-permute-start.18 = (bf16[256,1024]{1,0:T(8,128)(2,1)S(1)}, bf16[256,1024]{1,0:T(8,128)(2,1)S(1)}, u32[]{:S(2)}, u32[]{:S(2)}) collective-permute-start(bf16[256,1024]{1,0:T(8,128)(2,1)S(1)} %get-tuple-element.133), channel_id=1, source_target_pairs={{0,1},{1,2},{2,3},{3,0},{4,5},{5,6},{6,7},{7,4},{8,9},{9,10},{10,1... | collective-permute-start | bytes 1572872 | tf_op jit(solution)/shard_map/ppermute | solution.py:190
  198.0 14.9 %collective-permute-start.19 = (bf16[256,1024]{1,0:T(8,128)(2,1)S(1)}, bf16[256,1024]{1,0:T(8,128)(2,1)}, u32[]{:S(2)}, u32[]{:S(2)}) collective-permute-start(bf16[256,1024]{1,0:T(8,128)(2,1)S(1)} %get-tuple-element.133), channel_id=1, source_target_pairs={{0,2},{1,3},{2,0},{3,1},{4,6},{5,7},{6,4},{7,5},{8,10},{9,11},{10,... | collective-permute-start | bytes 1572872 | tf_op jit(solution)/shard_map/ppermute | solution.py:190
  199.5 23.0 %collective-permute-start.20 = (bf16[256,1024]{1,0:T(8,128)(2,1)S(1)}, bf16[256,1024]{1,0:T(8,128)(2,1)}, u32[]{:S(2)}, u32[]{:S(2)}) collective-permute-start(bf16[256,1024]{1,0:T(8,128)(2,1)S(1)} %get-tuple-element.133), channel_id=1, source_target_pairs={{0,3},{1,0},{2,1},{3,2},{4,7},{5,4},{6,5},{7,6},{8,11},{9,8},{10,9... | collective-permute-start | bytes 1572872 | tf_op jit(solution)/shard_map/ppermute | solution.py:190
  201.0 250.2 %all-gather.2.cloned.1.call-start = ((), (), s32[]{:S(2)}) async-start(), calls=%async_computation | async-start | bytes 1843200 | tf_op jit(solution)/shard_map/all_gather | solution.py:436
  201.3 23.1 %copy-start.77 = (bf16[256,1024]{1,0:T(8,128)(2,1)S(1)}, bf16[256,1024]{1,0:T(8,128)(2,1)}, u32[]{:S(2)}) copy-start(bf16[256,1024]{1,0:T(8,128)(2,1)} %param.16) | copy-start | bytes 1572868
  268.7 7.9 %copy-start.79 = (bf16[1024,40]{0,1:T(8,128)(2,1)S(1)}, bf16[1024,40]{0,1:T(8,128)(2,1)}, u32[]{:S(2)}) copy-start(bf16[1024,40]{0,1:T(8,128)(2,1)} %param.14) | copy-start | bytes 245764
  268.7 11.4 %collective-permute-start.21 = (bf16[1024,160]{0,1:T(8,128)(2,1)}, bf16[1024,160]{0,1:T(8,128)(2,1)S(1)}, u32[]{:S(2)}, u32[]{:S(2)}) collective-permute-start(bf16[1024,160]{0,1:T(8,128)(2,1)} %get-tuple-element.173), channel_id=1, source_target_pairs={{0,1},{1,2},{2,3},{3,0},{4,5},{5,6},{6,7},{7,4},{8,9},{9,10},{10,1... | collective-permute-start | bytes 983048 | tf_op jit(solution)/shard_map/ppermute | solution.py:174
  271.2 9.2 %collective-permute-start.23 = (bf16[1024,160]{0,1:T(8,128)(2,1)S(1)}, bf16[1024,160]{0,1:T(8,128)(2,1)}, u32[]{:S(2)}, u32[]{:S(2)}) collective-permute-start(bf16[1024,160]{0,1:T(8,128)(2,1)S(1)} %get-tuple-element.174), channel_id=1, source_target_pairs={{0,3},{1,0},{2,1},{3,2},{4,7},{5,4},{6,5},{7,6},{8,11},{9,8},{10,9... | collective-permute-start | bytes 983048 | tf_op jit(solution)/shard_map/ppermute | solution.py:174
  272.3 15.6 %collective-permute-start.22 = (bf16[1024,160]{0,1:T(8,128)(2,1)S(1)}, bf16[1024,160]{0,1:T(8,128)(2,1)}, u32[]{:S(2)}, u32[]{:S(2)}) collective-permute-start(bf16[1024,160]{0,1:T(8,128)(2,1)S(1)} %get-tuple-element.175), channel_id=1, source_target_pairs={{0,2},{1,3},{2,0},{3,1},{4,6},{5,7},{6,4},{7,5},{8,10},{9,11},{10,... | collective-permute-start | bytes 983048 | tf_op jit(solution)/shard_map/ppermute | solution.py:174
  291.6 13.0 %collective-permute-start.24 = (bf16[256,1024]{1,0:T(8,128)(2,1)S(1)}, bf16[256,1024]{1,0:T(8,128)(2,1)S(1)}, u32[]{:S(2)}, u32[]{:S(2)}) collective-permute-start(bf16[256,1024]{1,0:T(8,128)(2,1)S(1)} %get-tuple-element.161), channel_id=1, source_target_pairs={{0,1},{1,2},{2,3},{3,0},{4,5},{5,6},{6,7},{7,4},{8,9},{9,10},{10,1... | collective-permute-start | bytes 1572872 | tf_op jit(solution)/shard_map/ppermute | solution.py:174
  291.7 14.4 %collective-permute-start.26 = (bf16[256,1024]{1,0:T(8,128)(2,1)S(1)}, bf16[256,1024]{1,0:T(8,128)(2,1)S(1)}, u32[]{:S(2)}, u32[]{:S(2)}) collective-permute-start(bf16[256,1024]{1,0:T(8,128)(2,1)S(1)} %get-tuple-element.162), channel_id=1, source_target_pairs={{0,3},{1,0},{2,1},{3,2},{4,7},{5,4},{6,5},{7,6},{8,11},{9,8},{10,9... | collective-permute-start | bytes 1572872 | tf_op jit(solution)/shard_map/ppermute | solution.py:174
  293.8 23.3 %collective-permute-start.25 = (bf16[256,1024]{1,0:T(8,128)(2,1)S(1)}, bf16[256,1024]{1,0:T(8,128)(2,1)S(1)}, u32[]{:S(2)}, u32[]{:S(2)}) collective-permute-start(bf16[256,1024]{1,0:T(8,128)(2,1)S(1)} %get-tuple-element.163), channel_id=1, source_target_pairs={{0,2},{1,3},{2,0},{3,1},{4,6},{5,7},{6,4},{7,5},{8,10},{9,11},{10,... | collective-permute-start | bytes 1572872 | tf_op jit(solution)/shard_map/ppermute | solution.py:174
  294.9 22.3 %copy-start.9 = (bf16[256,1024]{1,0:T(8,128)(2,1)S(1)}, bf16[256,1024]{1,0:T(8,128)(2,1)}, u32[]{:S(2)}) copy-start(bf16[256,1024]{1,0:T(8,128)(2,1)} %param.11) | copy-start | bytes 1572868
  294.9 22.3 %copy-start.128 = (f32[1024]{0:T(1024)S(1)}, f32[1024]{0:T(1024)}, u32[]{:S(2)}) copy-start(f32[1024]{0:T(1024)} %param.13) | copy-start | bytes 12292
  294.9 22.3 %copy-start.148 = (f32[256]{0:T(256)S(1)}, f32[256]{0:T(256)}, u32[]{:S(2)}) copy-start(f32[256]{0:T(256)} %copy-done.147) | copy-start | bytes 3076
  295.4 23.2 %copy-start.149 = (bf16[1024]{0:T(1024)(128)(2,1)S(1)}, bf16[1024]{0:T(1024)(128)(2,1)}, u32[]{:S(2)}) copy-start(bf16[1024]{0:T(1024)(128)(2,1)} %get-tuple-element.92) | copy-start | bytes 6148
  295.4 65.5 %copy-start.73 = (bf16[256,1024]{1,0:T(8,128)(2,1)S(1)}, bf16[256,1024]{1,0:T(8,128)(2,1)}, u32[]{:S(2)}) copy-start(bf16[256,1024]{1,0:T(8,128)(2,1)} %convolution_convert_fusion.5) | copy-start | bytes 1572868
  368.3 12.4 %collective-permute-start.27 = (bf16[2,2,58752]{2,1,0:T(2,128)(2,1)S(1)}, bf16[2,2,58752]{2,1,0:T(2,128)(2,1)S(1)}, u32[]{:S(2)}, u32[]{:S(2)}) collective-permute-start(bf16[2,2,58752]{2,1,0:T(2,128)(2,1)S(1)} %bitcast.429), channel_id=1, source_target_pairs={{0,4},{4,0},{8,12},{12,8},{16,20},{20,16},{24,28},{28,24},{1,5},{5... | collective-permute-start | bytes 1410056 | tf_op jit(solution)/shard_map/ppermute | solution.py:213
  382.0 6.5 %collective-permute-start.28 = (bf16[2,58752]{1,0:T(2,128)(2,1)S(1)}, bf16[2,58752]{1,0:T(2,128)(2,1)S(1)}, u32[]{:S(2)}, u32[]{:S(2)}) collective-permute-start(bf16[2,58752]{1,0:T(2,128)(2,1)S(1)} %bitcast.430), channel_id=1, source_target_pairs={{0,8},{4,12},{8,0},{12,4},{16,24},{20,28},{24,16},{28,20},{1,9},{5... | collective-permute-start | bytes 705032 | tf_op jit(solution)/shard_map/ppermute | solution.py:213
  389.5 6.8 %collective-permute-start.29 = (bf16[58752]{0:T(1024)(128)(2,1)S(1)}, bf16[58752]{0:T(1024)(128)(2,1)S(1)}, u32[]{:S(2)}, u32[]{:S(2)}) collective-permute-start(bf16[58752]{0:T(1024)(128)(2,1)S(1)} %convert_reduce_fusion), channel_id=1, source_target_pairs={{0,16},{4,20},{8,24},{12,28},{16,0},{20,4},{24,8},{28,12},{1,17},{... | collective-permute-start | bytes 352520 | tf_op jit(solution)/shard_map/ppermute | solution.py:213
  396.5 10.2 %collective-permute-start.30 = (bf16[1,58752]{1,0:T(2,128)(2,1)S(1)}, bf16[1,58752]{1,0:T(2,128)(2,1)S(1)}, u32[]{:S(2)}, u32[]{:S(2)}) collective-permute-start(bf16[1,58752]{1,0:T(2,128)(2,1)S(1)} %broadcast_in_dim.38), channel_id=1, source_target_pairs={{0,16},{4,20},{8,24},{12,28},{16,0},{20,4},{24,8},{28,12},{1,17},{... | collective-permute-start | bytes 352520 | tf_op jit(solution)/shard_map/ppermute | solution.py:218
  407.6 6.7 %collective-permute-start.31 = (bf16[2,58752]{1,0:T(2,128)(2,1)S(1)}, bf16[2,58752]{1,0:T(2,128)(2,1)S(1)}, u32[]{:S(2)}, u32[]{:S(2)}) collective-permute-start(bf16[2,58752]{1,0:T(2,128)(2,1)S(1)} %maximum_bitcast_fusion), channel_id=1, source_target_pairs={{0,8},{4,12},{8,0},{12,4},{16,24},{20,28},{24,16},{28,20},{1,9},{5... | collective-permute-start | bytes 705032 | tf_op jit(solution)/shard_map/ppermute | solution.py:218
  417.0 10.8 %collective-permute-start.32 = (bf16[4,58752]{1,0:T(4,128)(2,1)S(1)}, bf16[4,58752]{1,0:T(4,128)(2,1)S(1)}, u32[]{:S(2)}, u32[]{:S(2)}) collective-permute-start(bf16[4,58752]{1,0:T(4,128)(2,1)S(1)} %reshape.2427), channel_id=1, source_target_pairs={{0,4},{4,0},{8,12},{12,8},{16,20},{20,16},{24,28},{28,24},{1,5},{5... | collective-permute-start | bytes 1410056 | tf_op jit(solution)/shard_map/ppermute | solution.py:218
  (127 other events, 429.2 us)
Sparse Core Ops, SparseCore 0:
  201.2 159.7 all-reduce.6
  434.6 16.6 all-gather.1

commit v11 on v10

--- a/solution.py
+++ b/solution.py
@@ -384,12 +384,15 @@
             for head in range(local_heads):
                 coef_columns[head * rank_all + offset + rank] = jnp.sum(
                     grad_part[:, head, :] * basis, axis=1
-                ) / len(bases)
+                )
             basis_grad = sum(
                 coef[head][offset + rank] * grad_part[:, head, :] for head in range(local_heads)
             ) / len(bases)
             basis_grads.append(basis_grad if offset == RQ + RK else unturn(basis_grad, cosine, sine))
-    grad_factor_a = jnp.stack(coef_columns, axis=1).astype(jnp.bfloat16)
+    rank_of = jnp.array([RQ] * RQ + [RK] * (2 * RK) * 1, jnp.float32)
+    grad_factor_a = (
+        jnp.stack(coef_columns, axis=1) / jnp.tile(rank_of, local_heads)[None, :]
+    ).astype(jnp.bfloat16)
     grad_factor_b = jnp.concatenate(basis_grads, axis=1)
     head_count = lax.axis_size("head")
     basis_cols = grad_factor_b.shape[1] // head_count
@@ -416,9 +419,6 @@
         grad_a.astype(jnp.bfloat16),
         grad_out.astype(jnp.bfloat16),
         jnp.concatenate([grad_b_cols, gains], axis=0).astype(jnp.bfloat16),
-    )
-    tail, (grad_gate, grad_up, grad_down) = lax.optimization_barrier(
-        (tail, (grad_gate, grad_up, grad_down))
     )
     sizes = [part.size for part in tail]
     summed = dp_all_reduce(jnp.concatenate([part.reshape(-1) for part in tail]))

time: 475 us -> 566 us (1.19)
  waiting for transfers between devices: 254 us -> 336 us
  starting transfers between devices: 31.8 us -> 38.8 us
  other arithmetic: 59.9 us -> 66.1 us
    psum x1, waiting for transfers between devices: 42.1 us -> 140 us  [local(): grad_gate, grad_up, grad_down = lax.psum(ffn_grads, 'dp')]
    ppermute x3, waiting for transfers between devices: 25.7 us -> 16.6 us  [dp_all_reduce(): arrived = lax.ppermute(whole, 'dp', pairs)]
    ppermute x3, starting transfers between devices: 1.96 us -> 8 us  [dp_all_reduce(): arrived = lax.ppermute(whole, 'dp', pairs)]
    unnamed x320 -> x382, local copies, waits for them, and re-layouts: 13.3 us -> 14 us
  transfers between devices with their start and end apart: 35 -> 35, of which waited for: 28 -> 27; matrix products, arithmetic and copies ran while one was open for 19% -> 8% of each run, Pallas kernels for 0% -> 0%
where the time goes in v11:
time: 566 us; the launch traced here: 557 us
  waiting for transfers between devices  336 us (59%)
  other arithmetic  66.1 us (12%)
  local copies, waits for them, and re-layouts  51.8 us (9%)
  matrix products  45.9 us (8%)
  starting transfers between devices  38.8 us (7%)
  between operations  18.8 us (3%)
    psum x1, waiting for transfers between devices, local(): grad_gate, grad_up, grad_down = lax.psum(ffn_grads, 'dp')  140 us
    ppermute x9, waiting for transfers between devices, head_reduce_scatter(): lax.ppermute(sent, 'head', [(device, (device + shift) % count) for device...  57.8 us
    ppermute x6, waiting for transfers between devices, head_gather_relative(): lax.ppermute(values, 'head', [(device, (device + shift) % count) for devi...  41 us
    ppermute x6, waiting for transfers between devices, head_all_gather(): lax.ppermute(values, 'head', [(device, (device + shift) % count) for devi...  35.9 us
    ppermute x6, waiting for transfers between devices, head_scatter_relative(): lax.ppermute(sent, 'head', [(device, (device + shift) % count) for device...  27.6 us
    ppermute x3, waiting for transfers between devices, dp_all_reduce(): lax.ppermute(sent.astype(jnp.bfloat16), 'dp', pairs).astype(jnp.float32)  17 us
    ppermute x3, waiting for transfers between devices, dp_all_reduce(): arrived = lax.ppermute(whole, 'dp', pairs)  16.6 us
    unnamed x382, local copies, waits for them, and re-layouts  14 us
  transfers between devices with their start and end apart: 35, of which 27 were waited for; matrix products, arithmetic and copies ran while one was open for 8% of the time, Pallas kernels for 0%

profile of v11, /device:TPU:0, one launch (start us, length us, event | category | flops | bytes accessed | tf_op | source)
XLA Modules:
  0.0 557.1 jit_solution(10864399352630552851)
XLA Ops:
  12.0 3.0 collective-permute-start.1
  15.0 1.7 collective-permute-start.2
  19.7 17.9 %collective-permute-done = bf16[256,1024]{1,0:T(8,128)(2,1)} collective-permute-done((bf16[256,1024]{1,0:T(8,128)(2,1)}, bf16[256,1024]{1,0:T(8,128)(2,1)}, u32[]{:S(2)}, u32[]{:S(2)}) %collective-permute-start) | collective-permute-done | bytes 524320 | tf_op jit(solution)/shard_map/ppermute | solution.py:190
  43.9 1.6 fusion.227
  52.9 1.8 fusion.224
  55.2 2.1 fusion
  59.2 2.3 fusion.40
  62.6 1.7 collective-permute-start.5
  66.4 8.7 %collective-permute-done.3 = bf16[256,1024]{1,0:T(8,128)(2,1)S(1)} collective-permute-done((bf16[256,1024]{1,0:T(8,128)(2,1)S(1)}, bf16[256,1024]{1,0:T(8,128)(2,1)S(1)}, u32[]{:S(2)}, u32[]{:S(2)}) %collective-permute-start.3) | collective-permute-done | bytes 524320 | tf_op jit(solution)/shard_map/ppermute | solution.py:174
  76.6 13.2 %collective-permute-done.4 = bf16[256,1024]{1,0:T(8,128)(2,1)S(1)} collective-permute-done((bf16[256,1024]{1,0:T(8,128)(2,1)S(1)}, bf16[256,1024]{1,0:T(8,128)(2,1)S(1)}, u32[]{:S(2)}, u32[]{:S(2)}) %collective-permute-start.4) | collective-permute-done | bytes 524320 | tf_op jit(solution)/shard_map/ppermute | solution.py:174
  91.8 17.0 %collective-permute-done.12 = bf16[256,1024]{1,0:T(8,128)(2,1)S(1)} collective-permute-done((bf16[256,1024]{1,0:T(8,128)(2,1)S(1)}, bf16[256,1024]{1,0:T(8,128)(2,1)S(1)}, u32[]{:S(2)}, u32[]{:S(2)}) %collective-permute-start.12) | collective-permute-done | bytes 524320 | tf_op jit(solution)/shard_map/ppermute | solution.py:230
  110.4 11.2 %collective-permute-done.8 = bf16[256,1024]{1,0:T(8,128)(2,1)S(1)} collective-permute-done((bf16[256,1024]{1,0:T(8,128)(2,1)S(1)}, bf16[256,1024]{1,0:T(8,128)(2,1)S(1)}, u32[]{:S(2)}, u32[]{:S(2)}) %collective-permute-start.8) | collective-permute-done | bytes 524320 | tf_op jit(solution)/shard_map/ppermute | solution.py:230
  121.6 11.4 %collective-permute-done.7 = bf16[256,1024]{1,0:T(8,128)(2,1)S(1)} collective-permute-done((bf16[256,1024]{1,0:T(8,128)(2,1)S(1)}, bf16[256,1024]{1,0:T(8,128)(2,1)S(1)}, u32[]{:S(2)}, u32[]{:S(2)}) %collective-permute-start.7) | collective-permute-done | bytes 524320 | tf_op jit(solution)/shard_map/ppermute | solution.py:230
  133.0 1.7 fusion.213
  134.7 1.7 fusion.214
  136.4 3.3 multiply_convert_fusion.2
  139.7 2.8 convolution_convert_fusion.4
  142.5 1.8 convolution_convert_fusion.1
  145.6 1.7 collective-permute-start.11
  147.3 1.8 fusion.228
  149.2 1.8 add_convert_fusion.1
  152.2 1.7 collective-permute-start.17
  155.4 2.8 convolution_convert_fusion.2
  158.2 2.8 convolution_convert_fusion.3
  161.0 8.6 %collective-permute-done.15 = bf16[256,1024]{1,0:T(8,128)(2,1)} collective-permute-done((bf16[256,1024]{1,0:T(8,128)(2,1)}, bf16[256,1024]{1,0:T(8,128)(2,1)}, u32[]{:S(2)}, u32[]{:S(2)}) %collective-permute-start.15) | collective-permute-done | bytes 524320 | tf_op jit(solution)/shard_map/ppermute | solution.py:241
  169.6 2.3 collective-permute-start.10
  171.9 12.4 %collective-permute-done.16 = bf16[256,1024]{1,0:T(8,128)(2,1)} collective-permute-done((bf16[256,1024]{1,0:T(8,128)(2,1)}, bf16[256,1024]{1,0:T(8,128)(2,1)}, u32[]{:S(2)}, u32[]{:S(2)}) %collective-permute-start.16) | collective-permute-done | bytes 524320 | tf_op jit(solution)/shard_map/ppermute | solution.py:241
  184.3 1.8 convert_add_fusion.2
  187.1 6.6 %collective-permute-done.10 = bf16[256,1024]{1,0:T(8,128)(2,1)S(1)} collective-permute-done((bf16[256,1024]{1,0:T(8,128)(2,1)}, bf16[256,1024]{1,0:T(8,128)(2,1)S(1)}, u32[]{:S(2)}, u32[]{:S(2)}) %collective-permute-start.10) | collective-permute-done | bytes 524320 | tf_op jit(solution)/shard_map/ppermute | solution.py:241
  193.7 2.7 subtract_add_fusion
  200.8 1.6 collective-permute-start.20
  202.4 9.4 %collective-permute-done.18 = bf16[256,1024]{1,0:T(8,128)(2,1)} collective-permute-done((bf16[256,1024]{1,0:T(8,128)(2,1)S(1)}, bf16[256,1024]{1,0:T(8,128)(2,1)}, u32[]{:S(2)}, u32[]{:S(2)}) %collective-permute-start.18) | collective-permute-done | bytes 524320 | tf_op jit(solution)/shard_map/ppermute | solution.py:190
  211.8 1.9 constant_dynamic-update-slice_fusion.6
  214.9 8.2 %collective-permute-done.20 = bf16[256,1024]{1,0:T(8,128)(2,1)S(1)} collective-permute-done((bf16[256,1024]{1,0:T(8,128)(2,1)S(1)}, bf16[256,1024]{1,0:T(8,128)(2,1)S(1)}, u32[]{:S(2)}, u32[]{:S(2)}) %collective-permute-start.20) | collective-permute-done | bytes 524320 | tf_op jit(solution)/shard_map/ppermute | solution.py:190
  224.0 2.4 fusion.29
  234.5 2.2 multiply_reduce_fusion
  236.8 1.7 multiply_convert_fusion
  252.6 1.9 fusion.25
  271.5 5.8 %collective-permute-done.21 = bf16[1024,160]{0,1:T(8,128)(2,1)S(1)} collective-permute-done((bf16[1024,160]{0,1:T(8,128)(2,1)}, bf16[1024,160]{0,1:T(8,128)(2,1)S(1)}, u32[]{:S(2)}, u32[]{:S(2)}) %collective-permute-start.21) | collective-permute-done | bytes 327712 | tf_op jit(solution)/shard_map/ppermute | solution.py:174
  277.6 7.5 %collective-permute-done.22 = bf16[1024,160]{0,1:T(8,128)(2,1)} collective-permute-done((bf16[1024,160]{0,1:T(8,128)(2,1)S(1)}, bf16[1024,160]{0,1:T(8,128)(2,1)}, u32[]{:S(2)}, u32[]{:S(2)}) %collective-permute-start.22) | collective-permute-done | bytes 327712 | tf_op jit(solution)/shard_map/ppermute | solution.py:174
  286.5 2.1 add_convert_fusion
  289.9 2.1 collective-permute-start.26
  294.8 8.3 %collective-permute-done.24 = bf16[256,1024]{1,0:T(8,128)(2,1)} collective-permute-done((bf16[256,1024]{1,0:T(8,128)(2,1)}, bf16[256,1024]{1,0:T(8,128)(2,1)}, u32[]{:S(2)}, u32[]{:S(2)}) %collective-permute-start.24) | collective-permute-done | bytes 524320 | tf_op jit(solution)/shard_map/ppermute | solution.py:174
  304.6 11.0 %collective-permute-done.25 = bf16[256,1024]{1,0:T(8,128)(2,1)} collective-permute-done((bf16[256,1024]{1,0:T(8,128)(2,1)}, bf16[256,1024]{1,0:T(8,128)(2,1)}, u32[]{:S(2)}, u32[]{:S(2)}) %collective-permute-start.25) | collective-permute-done | bytes 524320 | tf_op jit(solution)/shard_map/ppermute | solution.py:174
  315.7 3.0 fusion.50
  320.2 2.4 reshape.2032
  322.6 2.5 dynamic-slice_convert_fusion
  327.9 9.2 %collective-permute-done.27 = bf16[2,2,58752]{2,1,0:T(2,128)(2,1)S(1)} collective-permute-done((bf16[2,2,58752]{2,1,0:T(2,128)(2,1)S(1)}, bf16[2,2,58752]{2,1,0:T(2,128)(2,1)S(1)}, u32[]{:S(2)}, u32[]{:S(2)}) %collective-permute-start.27) | collective-permute-done | bytes 470048 | tf_op jit(solution)/shard_map/ppermute | solution.py:213
  338.5 1.7 collective-permute-start.28
  340.6 4.0 collective-permute-done.28
  345.7 2.7 collective-permute-start.29
  349.1 3.8 collective-permute-done.29
  353.0 1.8 collective-permute-start.30
  354.9 5.4 collective-permute-done.30
  361.2 4.6 collective-permute-start.31
  365.8 4.1 collective-permute-done.31
  374.3 7.1 %collective-permute-done.32 = bf16[4,58752]{1,0:T(4,128)(2,1)S(1)} collective-permute-done((bf16[4,58752]{1,0:T(4,128)(2,1)S(1)}, bf16[4,58752]{1,0:T(4,128)(2,1)S(1)}, u32[]{:S(2)}, u32[]{:S(2)}) %collective-permute-start.32) | collective-permute-done | bytes 470048 | tf_op jit(solution)/shard_map/ppermute | solution.py:218
  388.0 2.5 fusion.47
  394.4 139.6 %all-reduce.7.cloned.1.call-done = (bf16[1024,704]{0,1:T(8,128)(2,1)}, bf16[1024,704]{0,1:T(8,128)(2,1)}, bf16[704,1024]{1,0:T(8,128)(2,1)}) async-done(((bf16[1024,704]{0,1:T(8,128)(2,1)}, bf16[1024,704]{0,1:T(8,128)(2,1)}, bf16[704,1024]{1,0:T(8,128)(2,1)}), (bf16[1024,704]{0,1:T(8,128)(2,1)}, bf16[1024,704]{0,1:T(8,128)(2,1)}, bf16[704,1024]{1,0:T(8,128)(2,1)})) %all-reduce.7.cloned.1.call-update) | async-done | bytes 4325392 | tf_op jit(solution)/shard_map/psum | solution.py:364
  534.0 3.4 convert_element_type.449
  537.4 1.9 convert_element_type.450
  539.3 1.9 convert_element_type.451
  543.0 3.2 slice.762
  546.2 3.2 copy.86
  (558 shorter events, 111.7 us)
Async XLA Ops:
  8.0 128.4 %copy-start = (bf16[704,1024]{1,0:T(8,128)(2,1)S(1)}, bf16[704,1024]{1,0:T(8,128)(2,1)}, u32[]{:S(2)}) copy-start(bf16[704,1024]{1,0:T(8,128)(2,1)} %param.21) | copy-start | bytes 4325380
  8.0 525.9 %all-reduce.7.cloned.1.call-start = ((), (), s32[]{:S(2)}) async-start(), calls=%async_computation.1 | async-start | bytes 8650752 | tf_op jit(solution)/shard_map/psum | solution.py:364
  8.1 8.7 %copy-start.169 = (s32[1,1024]{1,0:T(1,128)S(1)}, s32[1,1024]{1,0:T(1,128)}, u32[]{:S(2)}) copy-start(s32[1,1024]{1,0:T(1,128)} %param.13) | copy-start | bytes 12292
  10.0 8.3 %copy-start.174 = (f32[256]{0:T(256)}, f32[256]{0:T(256)S(1)}, u32[]{:S(2)}) copy-start(f32[256]{0:T(256)S(1)} %get-tuple-element.238) | copy-start | bytes 3076
  12.0 26.7 %collective-permute-start.1 = (bf16[256,1024]{1,0:T(8,128)(2,1)}, bf16[256,1024]{1,0:T(8,128)(2,1)}, u32[]{:S(2)}, u32[]{:S(2)}) collective-permute-start(bf16[256,1024]{1,0:T(8,128)(2,1)} %get-tuple-element.125), channel_id=1, source_target_pairs={{0,2},{1,3},{2,0},{3,1},{4,6},{5,7},{6,4},{7,5},{8,10},{9,11},{10,... | collective-permute-start | bytes 1572872 | tf_op jit(solution)/shard_map/ppermute | solution.py:190
  15.0 22.6 %collective-permute-start = (bf16[256,1024]{1,0:T(8,128)(2,1)}, bf16[256,1024]{1,0:T(8,128)(2,1)}, u32[]{:S(2)}, u32[]{:S(2)}) collective-permute-start(bf16[256,1024]{1,0:T(8,128)(2,1)} %get-tuple-element.125), channel_id=1, source_target_pairs={{0,1},{1,2},{2,3},{3,0},{4,5},{5,6},{6,7},{7,4},{8,9},{9,10},{10,1... | collective-permute-start | bytes 1572872 | tf_op jit(solution)/shard_map/ppermute | solution.py:190
  15.0 24.8 %collective-permute-start.2 = (bf16[256,1024]{1,0:T(8,128)(2,1)}, bf16[256,1024]{1,0:T(8,128)(2,1)}, u32[]{:S(2)}, u32[]{:S(2)}) collective-permute-start(bf16[256,1024]{1,0:T(8,128)(2,1)} %get-tuple-element.125), channel_id=1, source_target_pairs={{0,3},{1,0},{2,1},{3,2},{4,7},{5,4},{6,5},{7,6},{8,11},{9,8},{10,9... | collective-permute-start | bytes 1572872 | tf_op jit(solution)/shard_map/ppermute | solution.py:190
  18.4 22.6 %copy-start.81 = (bf16[1024,40]{0,1:T(8,128)(2,1)S(1)}, bf16[1024,40]{0,1:T(8,128)(2,1)}, u32[]{:S(2)}) copy-start(bf16[1024,40]{0,1:T(8,128)(2,1)} %param.15) | copy-start | bytes 245764
  43.1 14.2 %copy-start.85 = (f32[1024,1]{0,1:T(1,128)}, f32[1024,1]{0,1:T(1,128)S(1)}, u32[]{:S(2)}) copy-start(f32[1024,1]{0,1:T(1,128)S(1)} %get-tuple-element.229) | copy-start | bytes 12292
  43.1 14.2 %copy-start.87 = (f32[1024,1]{0,1:T(1,128)}, f32[1024,1]{0,1:T(1,128)S(1)}, u32[]{:S(2)}) copy-start(f32[1024,1]{0,1:T(1,128)S(1)} %get-tuple-element.228) | copy-start | bytes 12292
  43.1 14.2 %copy-start.89 = (f32[1024,1]{0,1:T(1,128)}, f32[1024,1]{0,1:T(1,128)S(1)}, u32[]{:S(2)}) copy-start(f32[1024,1]{0,1:T(1,128)S(1)} %get-tuple-element.230) | copy-start | bytes 12292
  43.8 7.8 %copy-start.95 = (f32[1024,1]{0,1:T(1,128)}, f32[1024,1]{0,1:T(1,128)S(1)}, u32[]{:S(2)}) copy-start(f32[1024,1]{0,1:T(1,128)S(1)} %get-tuple-element.198) | copy-start | bytes 12292
  43.8 7.8 %copy-start.97 = (f32[1024,1]{0,1:T(1,128)}, f32[1024,1]{0,1:T(1,128)S(1)}, u32[]{:S(2)}) copy-start(f32[1024,1]{0,1:T(1,128)S(1)} %get-tuple-element.200) | copy-start | bytes 12292
  43.8 7.8 %copy-start.109 = (f32[1024,1]{0,1:T(1,128)}, f32[1024,1]{0,1:T(1,128)S(1)}, u32[]{:S(2)}) copy-start(f32[1024,1]{0,1:T(1,128)S(1)} %get-tuple-element.197) | copy-start | bytes 12292
  43.9 13.5 %copy-start.91 = (f32[1024,1]{0,1:T(1,128)}, f32[1024,1]{0,1:T(1,128)S(1)}, u32[]{:S(2)}) copy-start(f32[1024,1]{0,1:T(1,128)S(1)} %get-tuple-element.193) | copy-start | bytes 12292
  45.5 11.9 %copy-start.38 = (f32[1024,640]{0,1:T(8,128)}, f32[1024,640]{0,1:T(8,128)S(1)}, u32[]{:S(2)}) copy-start(f32[1024,640]{0,1:T(8,128)S(1)} %fusion.227) | copy-start | bytes 7864324
  62.3 27.5 %copy-start.8 = (bf16[256,1024]{1,0:T(8,128)(2,1)S(1)}, bf16[256,1024]{1,0:T(8,128)(2,1)}, u32[]{:S(2)}) copy-start(bf16[256,1024]{1,0:T(8,128)(2,1)} %param.12) | copy-start | bytes 1572868
  62.5 28.4 %copy-start.129 = (f32[1024]{0:T(1024)S(1)}, f32[1024]{0:T(1024)}, u32[]{:S(2)}) copy-start(f32[1024]{0:T(1024)} %param.18) | copy-start | bytes 12292
  62.5 12.5 %collective-permute-start.3 = (bf16[256,1024]{1,0:T(8,128)(2,1)S(1)}, bf16[256,1024]{1,0:T(8,128)(2,1)S(1)}, u32[]{:S(2)}, u32[]{:S(2)}) collective-permute-start(bf16[256,1024]{1,0:T(8,128)(2,1)S(1)} %get-tuple-element.158), channel_id=1, source_target_pairs={{0,1},{1,2},{2,3},{3,0},{4,5},{5,6},{6,7},{7,4},{8,9},{9,10},{10,1... | collective-permute-start | bytes 1572872 | tf_op jit(solution)/shard_map/ppermute | solution.py:174
  62.6 14.0 %collective-permute-start.5 = (bf16[256,1024]{1,0:T(8,128)(2,1)S(1)}, bf16[256,1024]{1,0:T(8,128)(2,1)S(1)}, u32[]{:S(2)}, u32[]{:S(2)}) collective-permute-start(bf16[256,1024]{1,0:T(8,128)(2,1)S(1)} %get-tuple-element.159), channel_id=1, source_target_pairs={{0,3},{1,0},{2,1},{3,2},{4,7},{5,4},{6,5},{7,6},{8,11},{9,8},{10,9... | collective-permute-start | bytes 1572872 | tf_op jit(solution)/shard_map/ppermute | solution.py:174
  64.3 25.5 %collective-permute-start.4 = (bf16[256,1024]{1,0:T(8,128)(2,1)S(1)}, bf16[256,1024]{1,0:T(8,128)(2,1)S(1)}, u32[]{:S(2)}, u32[]{:S(2)}) collective-permute-start(bf16[256,1024]{1,0:T(8,128)(2,1)S(1)} %get-tuple-element.160), channel_id=1, source_target_pairs={{0,2},{1,3},{2,0},{3,1},{4,6},{5,7},{6,4},{7,5},{8,10},{9,11},{10,... | collective-permute-start | bytes 1572872 | tf_op jit(solution)/shard_map/ppermute | solution.py:174
  65.8 43.1 %collective-permute-start.13 = (bf16[256,1024]{1,0:T(8,128)(2,1)S(1)}, bf16[256,1024]{1,0:T(8,128)(2,1)S(1)}, u32[]{:S(2)}, u32[]{:S(2)}) collective-permute-start(bf16[256,1024]{1,0:T(8,128)(2,1)S(1)} %copy-done.56), channel_id=1, source_target_pairs={{0,2},{1,3},{2,0},{3,1},{4,6},{5,7},{6,4},{7,5},{8,10},{9,11},{10,... | collective-permute-start | bytes 1572872 | tf_op jit(solution)/shard_map/ppermute | solution.py:230
  66.4 42.4 %collective-permute-start.12 = (bf16[256,1024]{1,0:T(8,128)(2,1)S(1)}, bf16[256,1024]{1,0:T(8,128)(2,1)S(1)}, u32[]{:S(2)}, u32[]{:S(2)}) collective-permute-start(bf16[256,1024]{1,0:T(8,128)(2,1)S(1)} %copy-done.56), channel_id=1, source_target_pairs={{0,1},{1,2},{2,3},{3,0},{4,5},{5,6},{6,7},{7,4},{8,9},{9,10},{10,1... | collective-permute-start | bytes 1572872 | tf_op jit(solution)/shard_map/ppermute | solution.py:230
  75.1 35.3 %collective-permute-start.14 = (bf16[256,1024]{1,0:T(8,128)(2,1)S(1)}, bf16[256,1024]{1,0:T(8,128)(2,1)S(1)}, u32[]{:S(2)}, u32[]{:S(2)}) collective-permute-start(bf16[256,1024]{1,0:T(8,128)(2,1)S(1)} %copy-done.56), channel_id=1, source_target_pairs={{0,3},{1,0},{2,1},{3,2},{4,7},{5,4},{6,5},{7,6},{8,11},{9,8},{10,9... | collective-permute-start | bytes 1572872 | tf_op jit(solution)/shard_map/ppermute | solution.py:230
  90.3 18.6 %copy-start.5 = (f32[256,1024]{1,0:T(8,128)}, f32[256,1024]{1,0:T(8,128)S(1)}, u32[]{:S(2)}) copy-start(f32[256,1024]{1,0:T(8,128)S(1)} %get-tuple-element.123) | copy-start | bytes 3145732
  90.9 18.0 %copy-start.176 = (f32[256]{0:T(256)}, f32[256]{0:T(256)S(1)}, u32[]{:S(2)}) copy-start(f32[256]{0:T(256)S(1)} %get-tuple-element.240) | copy-start | bytes 3076
  91.1 41.9 %copy-start.184 = (bf16[1024,704]{0,1:T(8,128)(2,1)S(1)}, bf16[1024,704]{0,1:T(8,128)(2,1)}, u32[]{:S(2)}) copy-start(bf16[1024,704]{0,1:T(8,128)(2,1)} %param.20) | copy-start | bytes 4325380
  91.1 30.5 %collective-permute-start.8 = (bf16[256,1024]{1,0:T(8,128)(2,1)S(1)}, bf16[256,1024]{1,0:T(8,128)(2,1)S(1)}, u32[]{:S(2)}, u32[]{:S(2)}) collective-permute-start(bf16[256,1024]{1,0:T(8,128)(2,1)S(1)} %multiply_convert_fusion.5), channel_id=1, source_target_pairs={{0,3},{1,0},{2,1},{3,2},{4,7},{5,4},{6,5},{7,6},{8,11},{9,8},{10,9... | collective-permute-start | bytes 1572872 | tf_op jit(solution)/shard_map/ppermute | solution.py:230
  91.2 41.8 %collective-permute-start.7 = (bf16[256,1024]{1,0:T(8,128)(2,1)S(1)}, bf16[256,1024]{1,0:T(8,128)(2,1)S(1)}, u32[]{:S(2)}, u32[]{:S(2)}) collective-permute-start(bf16[256,1024]{1,0:T(8,128)(2,1)S(1)} %multiply_convert_fusion.5), channel_id=1, source_target_pairs={{0,2},{1,3},{2,0},{3,1},{4,6},{5,7},{6,4},{7,5},{8,10},{9,11},{10,... | collective-permute-start | bytes 1572872 | tf_op jit(solution)/shard_map/ppermute | solution.py:230
  108.8 24.2 %collective-permute-start.6 = (bf16[256,1024]{1,0:T(8,128)(2,1)S(1)}, bf16[256,1024]{1,0:T(8,128)(2,1)S(1)}, u32[]{:S(2)}, u32[]{:S(2)}) collective-permute-start(bf16[256,1024]{1,0:T(8,128)(2,1)S(1)} %multiply_convert_fusion.5), channel_id=1, source_target_pairs={{0,1},{1,2},{2,3},{3,0},{4,5},{5,6},{6,7},{7,4},{8,9},{9,10},{10,1... | collective-permute-start | bytes 1572872 | tf_op jit(solution)/shard_map/ppermute | solution.py:230
  110.4 24.3 %copy-start.183 = (bf16[1024,704]{0,1:T(8,128)(2,1)S(1)}, bf16[1024,704]{0,1:T(8,128)(2,1)}, u32[]{:S(2)}) copy-start(bf16[1024,704]{0,1:T(8,128)(2,1)} %param.19) | copy-start | bytes 4325380
  145.6 41.5 %collective-permute-start.9 = (bf16[256,1024]{1,0:T(8,128)(2,1)}, bf16[256,1024]{1,0:T(8,128)(2,1)}, u32[]{:S(2)}, u32[]{:S(2)}) collective-permute-start(bf16[256,1024]{1,0:T(8,128)(2,1)} %get-tuple-element.155), channel_id=1, source_target_pairs={{0,1},{1,2},{2,3},{3,0},{4,5},{5,6},{6,7},{7,4},{8,9},{9,10},{10,1... | collective-permute-start | bytes 1572872 | tf_op jit(solution)/shard_map/ppermute | solution.py:241
  145.6 41.5 %collective-permute-start.11 = (bf16[256,1024]{1,0:T(8,128)(2,1)}, bf16[256,1024]{1,0:T(8,128)(2,1)}, u32[]{:S(2)}, u32[]{:S(2)}) collective-permute-start(bf16[256,1024]{1,0:T(8,128)(2,1)} %get-tuple-element.156), channel_id=1, source_target_pairs={{0,3},{1,0},{2,1},{3,2},{4,7},{5,4},{6,5},{7,6},{8,11},{9,8},{10,9... | collective-permute-start | bytes 1572872 | tf_op jit(solution)/shard_map/ppermute | solution.py:241
  152.2 17.3 %collective-permute-start.15 = (bf16[256,1024]{1,0:T(8,128)(2,1)}, bf16[256,1024]{1,0:T(8,128)(2,1)}, u32[]{:S(2)}, u32[]{:S(2)}) collective-permute-start(bf16[256,1024]{1,0:T(8,128)(2,1)} %get-tuple-element.152), channel_id=1, source_target_pairs={{0,1},{1,2},{2,3},{3,0},{4,5},{5,6},{6,7},{7,4},{8,9},{9,10},{10,1... | collective-permute-start | bytes 1572872 | tf_op jit(solution)/shard_map/ppermute | solution.py:241
  152.2 19.7 %collective-permute-start.17 = (bf16[256,1024]{1,0:T(8,128)(2,1)}, bf16[256,1024]{1,0:T(8,128)(2,1)}, u32[]{:S(2)}, u32[]{:S(2)}) collective-permute-start(bf16[256,1024]{1,0:T(8,128)(2,1)} %get-tuple-element.153), channel_id=1, source_target_pairs={{0,3},{1,0},{2,1},{3,2},{4,7},{5,4},{6,5},{7,6},{8,11},{9,8},{10,9... | collective-permute-start | bytes 1572872 | tf_op jit(solution)/shard_map/ppermute | solution.py:241
  154.0 30.3 %collective-permute-start.16 = (bf16[256,1024]{1,0:T(8,128)(2,1)}, bf16[256,1024]{1,0:T(8,128)(2,1)}, u32[]{:S(2)}, u32[]{:S(2)}) collective-permute-start(bf16[256,1024]{1,0:T(8,128)(2,1)} %get-tuple-element.154), channel_id=1, source_target_pairs={{0,2},{1,3},{2,0},{3,1},{4,6},{5,7},{6,4},{7,5},{8,10},{9,11},{10,... | collective-permute-start | bytes 1572872 | tf_op jit(solution)/shard_map/ppermute | solution.py:241
  161.0 25.2 %copy-start.6 = (f32[256,1024]{1,0:T(8,128)S(1)}, f32[256,1024]{1,0:T(8,128)}, u32[]{:S(2)}) copy-start(f32[256,1024]{1,0:T(8,128)} %copy-done.5) | copy-start | bytes 3145732
  161.0 25.2 %copy-start.130 = (f32[1024]{0:T(1024)S(1)}, f32[1024]{0:T(1024)}, u32[]{:S(2)}) copy-start(f32[1024]{0:T(1024)} %param.18) | copy-start | bytes 12292
  161.0 25.2 %copy-start.177 = (f32[256]{0:T(256)S(1)}, f32[256]{0:T(256)}, u32[]{:S(2)}) copy-start(f32[256]{0:T(256)} %copy-done.176) | copy-start | bytes 3076
  169.6 24.1 %copy-start.57 = (bf16[256,1024]{1,0:T(8,128)(2,1)S(1)}, bf16[256,1024]{1,0:T(8,128)(2,1)}, u32[]{:S(2)}) copy-start(bf16[256,1024]{1,0:T(8,128)(2,1)} %param.22) | copy-start | bytes 1572868
  169.6 24.1 %copy-start.181 = (f32[256]{0:T(256)S(1)}, f32[256]{0:T(256)}, u32[]{:S(2)}) copy-start(f32[256]{0:T(256)} %get-tuple-element.239) | copy-start | bytes 3076
  169.6 24.1 %collective-permute-start.10 = (bf16[256,1024]{1,0:T(8,128)(2,1)}, bf16[256,1024]{1,0:T(8,128)(2,1)S(1)}, u32[]{:S(2)}, u32[]{:S(2)}) collective-permute-start(bf16[256,1024]{1,0:T(8,128)(2,1)} %get-tuple-element.157), channel_id=1, source_target_pairs={{0,2},{1,3},{2,0},{3,1},{4,6},{5,7},{6,4},{7,5},{8,10},{9,11},{10,... | collective-permute-start | bytes 1572872 | tf_op jit(solution)/shard_map/ppermute | solution.py:241
  197.4 26.6 %copy-start.55 = (bf16[1024,4,64]{0,2,1:T(8,128)(2,1)S(1)}, bf16[1024,4,64]{0,2,1:T(8,128)(2,1)}, u32[]{:S(2)}) copy-start(bf16[1024,4,64]{0,2,1:T(8,128)(2,1)} %copy-done.54) | copy-start | bytes 1572868
  198.7 13.1 %collective-permute-start.18 = (bf16[256,1024]{1,0:T(8,128)(2,1)S(1)}, bf16[256,1024]{1,0:T(8,128)(2,1)}, u32[]{:S(2)}, u32[]{:S(2)}) collective-permute-start(bf16[256,1024]{1,0:T(8,128)(2,1)S(1)} %get-tuple-element.121), channel_id=1, source_target_pairs={{0,1},{1,2},{2,3},{3,0},{4,5},{5,6},{6,7},{7,4},{8,9},{9,10},{10,1... | collective-permute-start | bytes 1572872 | tf_op jit(solution)/shard_map/ppermute | solution.py:190
  199.3 14.8 %collective-permute-start.19 = (bf16[256,1024]{1,0:T(8,128)(2,1)S(1)}, bf16[256,1024]{1,0:T(8,128)(2,1)S(1)}, u32[]{:S(2)}, u32[]{:S(2)}) collective-permute-start(bf16[256,1024]{1,0:T(8,128)(2,1)S(1)} %get-tuple-element.121), channel_id=1, source_target_pairs={{0,2},{1,3},{2,0},{3,1},{4,6},{5,7},{6,4},{7,5},{8,10},{9,11},{10,... | collective-permute-start | bytes 1572872 | tf_op jit(solution)/shard_map/ppermute | solution.py:190
  200.8 22.4 %collective-permute-start.20 = (bf16[256,1024]{1,0:T(8,128)(2,1)S(1)}, bf16[256,1024]{1,0:T(8,128)(2,1)S(1)}, u32[]{:S(2)}, u32[]{:S(2)}) collective-permute-start(bf16[256,1024]{1,0:T(8,128)(2,1)S(1)} %get-tuple-element.121), channel_id=1, source_target_pairs={{0,3},{1,0},{2,1},{3,2},{4,7},{5,4},{6,5},{7,6},{8,11},{9,8},{10,9... | collective-permute-start | bytes 1572872 | tf_op jit(solution)/shard_map/ppermute | solution.py:190
  214.9 11.5 %copy-start.79 = (bf16[256,1024]{1,0:T(8,128)(2,1)S(1)}, bf16[256,1024]{1,0:T(8,128)(2,1)}, u32[]{:S(2)}) copy-start(bf16[256,1024]{1,0:T(8,128)(2,1)} %param.17) | copy-start | bytes 1572868
  267.6 9.7 %collective-permute-start.21 = (bf16[1024,160]{0,1:T(8,128)(2,1)}, bf16[1024,160]{0,1:T(8,128)(2,1)S(1)}, u32[]{:S(2)}, u32[]{:S(2)}) collective-permute-start(bf16[1024,160]{0,1:T(8,128)(2,1)} %get-tuple-element.161), channel_id=1, source_target_pairs={{0,1},{1,2},{2,3},{3,0},{4,5},{5,6},{6,7},{7,4},{8,9},{9,10},{10,1... | collective-permute-start | bytes 983048 | tf_op jit(solution)/shard_map/ppermute | solution.py:174
  268.4 9.2 %collective-permute-start.23 = (bf16[1024,160]{0,1:T(8,128)(2,1)S(1)}, bf16[1024,160]{0,1:T(8,128)(2,1)}, u32[]{:S(2)}, u32[]{:S(2)}) collective-permute-start(bf16[1024,160]{0,1:T(8,128)(2,1)S(1)} %get-tuple-element.162), channel_id=1, source_target_pairs={{0,3},{1,0},{2,1},{3,2},{4,7},{5,4},{6,5},{7,6},{8,11},{9,8},{10,9... | collective-permute-start | bytes 983048 | tf_op jit(solution)/shard_map/ppermute | solution.py:174
  269.5 15.6 %collective-permute-start.22 = (bf16[1024,160]{0,1:T(8,128)(2,1)S(1)}, bf16[1024,160]{0,1:T(8,128)(2,1)}, u32[]{:S(2)}, u32[]{:S(2)}) collective-permute-start(bf16[1024,160]{0,1:T(8,128)(2,1)S(1)} %get-tuple-element.163), channel_id=1, source_target_pairs={{0,2},{1,3},{2,0},{3,1},{4,6},{5,7},{6,4},{7,5},{8,10},{9,11},{10,... | collective-permute-start | bytes 983048 | tf_op jit(solution)/shard_map/ppermute | solution.py:174
  289.9 13.3 %collective-permute-start.24 = (bf16[256,1024]{1,0:T(8,128)(2,1)}, bf16[256,1024]{1,0:T(8,128)(2,1)}, u32[]{:S(2)}, u32[]{:S(2)}) collective-permute-start(bf16[256,1024]{1,0:T(8,128)(2,1)} %get-tuple-element.149), channel_id=1, source_target_pairs={{0,1},{1,2},{2,3},{3,0},{4,5},{5,6},{6,7},{7,4},{8,9},{9,10},{10,1... | collective-permute-start | bytes 1572872 | tf_op jit(solution)/shard_map/ppermute | solution.py:174
  289.9 14.8 %collective-permute-start.26 = (bf16[256,1024]{1,0:T(8,128)(2,1)}, bf16[256,1024]{1,0:T(8,128)(2,1)}, u32[]{:S(2)}, u32[]{:S(2)}) collective-permute-start(bf16[256,1024]{1,0:T(8,128)(2,1)} %get-tuple-element.150), channel_id=1, source_target_pairs={{0,3},{1,0},{2,1},{3,2},{4,7},{5,4},{6,5},{7,6},{8,11},{9,8},{10,9... | collective-permute-start | bytes 1572872 | tf_op jit(solution)/shard_map/ppermute | solution.py:174
  292.0 23.6 %collective-permute-start.25 = (bf16[256,1024]{1,0:T(8,128)(2,1)}, bf16[256,1024]{1,0:T(8,128)(2,1)}, u32[]{:S(2)}, u32[]{:S(2)}) collective-permute-start(bf16[256,1024]{1,0:T(8,128)(2,1)} %get-tuple-element.151), channel_id=1, source_target_pairs={{0,2},{1,3},{2,0},{3,1},{4,6},{5,7},{6,4},{7,5},{8,10},{9,11},{10,... | collective-permute-start | bytes 1572872 | tf_op jit(solution)/shard_map/ppermute | solution.py:174
  293.1 22.6 %copy-start.9 = (bf16[256,1024]{1,0:T(8,128)(2,1)S(1)}, bf16[256,1024]{1,0:T(8,128)(2,1)}, u32[]{:S(2)}) copy-start(bf16[256,1024]{1,0:T(8,128)(2,1)} %param.12) | copy-start | bytes 1572868
  293.1 22.6 %copy-start.132 = (f32[1024]{0:T(1024)S(1)}, f32[1024]{0:T(1024)}, u32[]{:S(2)}) copy-start(f32[1024]{0:T(1024)} %param.14) | copy-start | bytes 12292
  293.1 22.6 %copy-start.175 = (f32[256]{0:T(256)S(1)}, f32[256]{0:T(256)}, u32[]{:S(2)}) copy-start(f32[256]{0:T(256)} %copy-done.174) | copy-start | bytes 3076
  294.8 23.8 %copy-start.178 = (bf16[1024]{0:T(1024)(128)(2,1)S(1)}, bf16[1024]{0:T(1024)(128)(2,1)}, u32[]{:S(2)}) copy-start(bf16[1024]{0:T(1024)(128)(2,1)} %get-tuple-element.80) | copy-start | bytes 6148
  325.6 11.6 %collective-permute-start.27 = (bf16[2,2,58752]{2,1,0:T(2,128)(2,1)S(1)}, bf16[2,2,58752]{2,1,0:T(2,128)(2,1)S(1)}, u32[]{:S(2)}, u32[]{:S(2)}) collective-permute-start(bf16[2,2,58752]{2,1,0:T(2,128)(2,1)S(1)} %bitcast.467), channel_id=1, source_target_pairs={{0,4},{4,0},{8,12},{12,8},{16,20},{20,16},{24,28},{28,24},{1,5},{5... | collective-permute-start | bytes 1410056 | tf_op jit(solution)/shard_map/ppermute | solution.py:213
  338.5 6.1 %collective-permute-start.28 = (bf16[2,58752]{1,0:T(2,128)(2,1)S(1)}, bf16[2,58752]{1,0:T(2,128)(2,1)S(1)}, u32[]{:S(2)}, u32[]{:S(2)}) collective-permute-start(bf16[2,58752]{1,0:T(2,128)(2,1)S(1)} %bitcast.468), channel_id=1, source_target_pairs={{0,8},{4,12},{8,0},{12,4},{16,24},{20,28},{24,16},{28,20},{1,9},{5... | collective-permute-start | bytes 705032 | tf_op jit(solution)/shard_map/ppermute | solution.py:213
  345.7 7.2 %collective-permute-start.29 = (bf16[58752]{0:T(1024)(128)(2,1)S(1)}, bf16[58752]{0:T(1024)(128)(2,1)S(1)}, u32[]{:S(2)}, u32[]{:S(2)}) collective-permute-start(bf16[58752]{0:T(1024)(128)(2,1)S(1)} %convert_reduce_fusion), channel_id=1, source_target_pairs={{0,16},{4,20},{8,24},{12,28},{16,0},{20,4},{24,8},{28,12},{1,17},{... | collective-permute-start | bytes 352520 | tf_op jit(solution)/shard_map/ppermute | solution.py:213
  353.0 7.3 %collective-permute-start.30 = (bf16[1,58752]{1,0:T(2,128)(2,1)S(1)}, bf16[1,58752]{1,0:T(2,128)(2,1)S(1)}, u32[]{:S(2)}, u32[]{:S(2)}) collective-permute-start(bf16[1,58752]{1,0:T(2,128)(2,1)S(1)} %broadcast_in_dim.38), channel_id=1, source_target_pairs={{0,16},{4,20},{8,24},{12,28},{16,0},{20,4},{24,8},{28,12},{1,17},{... | collective-permute-start | bytes 352520 | tf_op jit(solution)/shard_map/ppermute | solution.py:218
  361.2 8.7 %collective-permute-start.31 = (bf16[2,58752]{1,0:T(2,128)(2,1)S(1)}, bf16[2,58752]{1,0:T(2,128)(2,1)S(1)}, u32[]{:S(2)}, u32[]{:S(2)}) collective-permute-start(bf16[2,58752]{1,0:T(2,128)(2,1)S(1)} %maximum_bitcast_fusion), channel_id=1, source_target_pairs={{0,8},{4,12},{8,0},{12,4},{16,24},{20,28},{24,16},{28,20},{1,9},{5... | collective-permute-start | bytes 705032 | tf_op jit(solution)/shard_map/ppermute | solution.py:218
  372.6 8.7 %collective-permute-start.32 = (bf16[4,58752]{1,0:T(4,128)(2,1)S(1)}, bf16[4,58752]{1,0:T(4,128)(2,1)S(1)}, u32[]{:S(2)}, u32[]{:S(2)}) collective-permute-start(bf16[4,58752]{1,0:T(4,128)(2,1)S(1)} %reshape.2028), channel_id=1, source_target_pairs={{0,4},{4,0},{8,12},{12,8},{16,20},{20,16},{24,28},{28,24},{1,5},{5... | collective-permute-start | bytes 1410056 | tf_op jit(solution)/shard_map/ppermute | solution.py:218
  374.2 167.0 %all-gather.2.cloned.1.call-start = ((), (), s32[]{:S(2)}) async-start(), calls=%async_computation | async-start | bytes 1843200 | tf_op jit(solution)/shard_map/all_gather | solution.py:436
  (158 other events, 583.3 us)
Sparse Core Ops, SparseCore 0:
  374.3 159.5 all-reduce.6
Sparse Core Ops, SparseCore 1:
  388.1 22.7 all-gather.1

commit v12 on v11

--- a/solution.py
+++ b/solution.py
@@ -356,11 +356,12 @@
     grad_up = dot_first(normed_two_all, grad_up_act)
     gate_piece = lax.slice_in_dim(grad_gate_act, 0, lax.axis_size("head") * own_rows, axis=0)
     up_piece = lax.slice_in_dim(grad_up_act, 0, lax.axis_size("head") * own_rows, axis=0)
-    grad_normed_two = head_scatter_relative(
-        (dot_last(gate_piece, gate_weight) + dot_last(up_piece, up_weight)).astype(jnp.bfloat16)
+    normed_two_part = (dot_last(gate_piece, gate_weight) + dot_last(up_piece, up_weight)).astype(
+        jnp.bfloat16
     )
     ffn_grads = (grad_gate.astype(jnp.bfloat16), grad_up.astype(jnp.bfloat16), grad_down.astype(jnp.bfloat16))
-    ffn_grads, grad_normed_two = lax.optimization_barrier((ffn_grads, grad_normed_two))
+    ffn_grads, normed_two_part = lax.optimization_barrier((ffn_grads, normed_two_part))
+    grad_normed_two = head_scatter_relative(normed_two_part)
     grad_gate, grad_up, grad_down = lax.psum(ffn_grads, "dp")
     resid_part, grad_gain_ffn_own = norm_backward(resid_own, inv_two, gain_ffn, grad_normed_two)
     grad_resid = cotangent.astype(jnp.float32) + resid_part
@@ -421,6 +422,9 @@
         jnp.concatenate([grad_b_cols, gains], axis=0).astype(jnp.bfloat16),
     )
     sizes = [part.size for part in tail]
+    tail, (grad_gate, grad_up, grad_down) = lax.optimization_barrier(
+        (tail, (grad_gate, grad_up, grad_down))
+    )
     summed = dp_all_reduce(jnp.concatenate([part.reshape(-1) for part in tail]))
     grad_a, grad_out, packed = (
         summed[sum(sizes[:index]) : sum(sizes[: index + 1])].reshape(part.shape)

time: 566 us -> 485 us (0.86)
  waiting for transfers between devices: 336 us -> 262 us
  starting transfers between devices: 38.8 us -> 31.2 us
    psum x1, waiting for transfers between devices: 140 us -> 49.9 us  [local(): grad_gate, grad_up, grad_down = lax.psum(ffn_grads, 'dp')]
    ppermute x9, waiting for transfers between devices: 57.8 us -> 47.4 us  [head_reduce_scatter(): lax.ppermute(sent, 'head', [(device, (device + shift) % count) for device...]
    ppermute x6, waiting for transfers between devices: 27.6 us -> 37.2 us  [head_scatter_relative(): lax.ppermute(sent, 'head', [(device, (device + shift) % count) for device...]
    ppermute x3, waiting for transfers between devices: 16.6 us -> 25.4 us  [dp_all_reduce(): arrived = lax.ppermute(whole, 'dp', pairs)]
    ppermute x3, starting transfers between devices: 8 us -> 2.3 us  [dp_all_reduce(): arrived = lax.ppermute(whole, 'dp', pairs)]
    unnamed x382 -> x318, local copies, waits for them, and re-layouts: 14 us -> 11.8 us
  transfers between devices with their start and end apart: 35 -> 35, of which waited for: 27 -> 28; matrix products, arithmetic and copies ran while one was open for 8% -> 17% of each run, Pallas kernels for 0% -> 0%
where the time goes in v12:
time: 485 us; the launch traced here: 477 us
  waiting for transfers between devices  262 us (54%)
  other arithmetic  62.4 us (13%)
  local copies, waits for them, and re-layouts  52 us (11%)
  matrix products  51.5 us (11%)
  starting transfers between devices  31.2 us (6%)
  between operations  16.9 us (3%)
    psum x1, waiting for transfers between devices, local(): grad_gate, grad_up, grad_down = lax.psum(ffn_grads, 'dp')  49.9 us
    ppermute x9, waiting for transfers between devices, head_reduce_scatter(): lax.ppermute(sent, 'head', [(device, (device + shift) % count) for device...  47.4 us
    ppermute x6, waiting for transfers between devices, head_gather_relative(): lax.ppermute(values, 'head', [(device, (device + shift) % count) for devi...  41 us
    ppermute x6, waiting for transfers between devices, head_scatter_relative(): lax.ppermute(sent, 'head', [(device, (device + shift) % count) for device...  37.2 us
    ppermute x6, waiting for transfers between devices, head_all_gather(): lax.ppermute(values, 'head', [(device, (device + shift) % count) for devi...  35.9 us
    ppermute x3, waiting for transfers between devices, dp_all_reduce(): arrived = lax.ppermute(whole, 'dp', pairs)  25.4 us
    ppermute x3, waiting for transfers between devices, dp_all_reduce(): lax.ppermute(sent.astype(jnp.bfloat16), 'dp', pairs).astype(jnp.float32)  20.8 us
    dot_general x6, matrix products, dot_first(): lax.dot_general(left, right, (((0,), (0,)), ((), ())), preferred_element_...  14 us
  transfers between devices with their start and end apart: 35, of which 28 were waited for; matrix products, arithmetic and copies ran while one was open for 17% of the time, Pallas kernels for 0%

profile of v12, /device:TPU:0, one launch (start us, length us, event | category | flops | bytes accessed | tf_op | source)
XLA Modules:
  0.0 476.6 jit_solution(14537634654294523577)
XLA Ops:
  11.2 3.0 collective-permute-start.1
  14.2 1.7 collective-permute-start.2
  18.9 17.9 %collective-permute-done = bf16[256,1024]{1,0:T(8,128)(2,1)} collective-permute-done((bf16[256,1024]{1,0:T(8,128)(2,1)}, bf16[256,1024]{1,0:T(8,128)(2,1)}, u32[]{:S(2)}, u32[]{:S(2)}) %collective-permute-start) | collective-permute-done | bytes 524320 | tf_op jit(solution)/shard_map/ppermute | solution.py:190
  43.1 1.6 fusion.226
  52.0 1.8 fusion.223
  54.4 2.1 fusion
  58.4 2.3 fusion.39
  61.8 1.7 collective-permute-start.5
  65.6 8.7 %collective-permute-done.3 = bf16[256,1024]{1,0:T(8,128)(2,1)S(1)} collective-permute-done((bf16[256,1024]{1,0:T(8,128)(2,1)S(1)}, bf16[256,1024]{1,0:T(8,128)(2,1)S(1)}, u32[]{:S(2)}, u32[]{:S(2)}) %collective-permute-start.3) | collective-permute-done | bytes 524320 | tf_op jit(solution)/shard_map/ppermute | solution.py:174
  75.9 13.2 %collective-permute-done.4 = bf16[256,1024]{1,0:T(8,128)(2,1)S(1)} collective-permute-done((bf16[256,1024]{1,0:T(8,128)(2,1)S(1)}, bf16[256,1024]{1,0:T(8,128)(2,1)S(1)}, u32[]{:S(2)}, u32[]{:S(2)}) %collective-permute-start.4) | collective-permute-done | bytes 524320 | tf_op jit(solution)/shard_map/ppermute | solution.py:174
  91.0 16.9 %collective-permute-done.12 = bf16[256,1024]{1,0:T(8,128)(2,1)S(1)} collective-permute-done((bf16[256,1024]{1,0:T(8,128)(2,1)S(1)}, bf16[256,1024]{1,0:T(8,128)(2,1)S(1)}, u32[]{:S(2)}, u32[]{:S(2)}) %collective-permute-start.12) | collective-permute-done | bytes 524320 | tf_op jit(solution)/shard_map/ppermute | solution.py:230
  109.6 11.2 %collective-permute-done.8 = bf16[256,1024]{1,0:T(8,128)(2,1)S(1)} collective-permute-done((bf16[256,1024]{1,0:T(8,128)(2,1)S(1)}, bf16[256,1024]{1,0:T(8,128)(2,1)S(1)}, u32[]{:S(2)}, u32[]{:S(2)}) %collective-permute-start.8) | collective-permute-done | bytes 524320 | tf_op jit(solution)/shard_map/ppermute | solution.py:230
  120.8 11.4 %collective-permute-done.7 = bf16[256,1024]{1,0:T(8,128)(2,1)S(1)} collective-permute-done((bf16[256,1024]{1,0:T(8,128)(2,1)S(1)}, bf16[256,1024]{1,0:T(8,128)(2,1)S(1)}, u32[]{:S(2)}, u32[]{:S(2)}) %collective-permute-start.7) | collective-permute-done | bytes 524320 | tf_op jit(solution)/shard_map/ppermute | solution.py:230
  132.2 1.7 fusion.212
  133.9 1.7 fusion.213
  135.6 3.3 multiply_convert_fusion.2
  138.9 2.8 convolution_convert_fusion.4
  141.7 1.8 fusion.227
  143.6 3.3 add_convert_fusion.1
  146.8 2.8 convolution_convert_fusion.2
  149.6 2.8 convolution_convert_fusion.3
  154.0 1.7 collective-permute-start.17
  157.2 1.9 convolution_convert_fusion.1
  159.3 1.9 collective-permute-start.11
  161.2 5.2 %collective-permute-done.15 = bf16[256,1024]{1,0:T(8,128)(2,1)S(1)} collective-permute-done((bf16[256,1024]{1,0:T(8,128)(2,1)S(1)}, bf16[256,1024]{1,0:T(8,128)(2,1)S(1)}, u32[]{:S(2)}, u32[]{:S(2)}) %collective-permute-start.15) | collective-permute-done | bytes 524320 | tf_op jit(solution)/shard_map/ppermute | solution.py:241
  166.5 2.4 collective-permute-start.10
  168.9 12.4 %collective-permute-done.16 = bf16[256,1024]{1,0:T(8,128)(2,1)S(1)} collective-permute-done((bf16[256,1024]{1,0:T(8,128)(2,1)S(1)}, bf16[256,1024]{1,0:T(8,128)(2,1)S(1)}, u32[]{:S(2)}, u32[]{:S(2)}) %collective-permute-start.16) | collective-permute-done | bytes 524320 | tf_op jit(solution)/shard_map/ppermute | solution.py:241
  182.3 6.6 %collective-permute-done.9 = bf16[256,1024]{1,0:T(8,128)(2,1)S(1)} collective-permute-done((bf16[256,1024]{1,0:T(8,128)(2,1)S(1)}, bf16[256,1024]{1,0:T(8,128)(2,1)S(1)}, u32[]{:S(2)}, u32[]{:S(2)}) %collective-permute-start.9) | collective-permute-done | bytes 524320 | tf_op jit(solution)/shard_map/ppermute | solution.py:241
  190.6 11.4 %collective-permute-done.10 = bf16[256,1024]{1,0:T(8,128)(2,1)S(1)} collective-permute-done((bf16[256,1024]{1,0:T(8,128)(2,1)S(1)}, bf16[256,1024]{1,0:T(8,128)(2,1)S(1)}, u32[]{:S(2)}, u32[]{:S(2)}) %collective-permute-start.10) | collective-permute-done | bytes 524320 | tf_op jit(solution)/shard_map/ppermute | solution.py:241
  209.6 9.2 %collective-permute-done.18 = bf16[256,1024]{1,0:T(8,128)(2,1)S(1)} collective-permute-done((bf16[256,1024]{1,0:T(8,128)(2,1)S(1)}, bf16[256,1024]{1,0:T(8,128)(2,1)S(1)}, u32[]{:S(2)}, u32[]{:S(2)}) %collective-permute-start.18) | collective-permute-done | bytes 524320 | tf_op jit(solution)/shard_map/ppermute | solution.py:190
  219.6 1.8 collective-permute-done.19
  221.4 1.9 constant_dynamic-update-slice_fusion.5
  223.3 7.0 %collective-permute-done.20 = bf16[256,1024]{1,0:T(8,128)(2,1)} collective-permute-done((bf16[256,1024]{1,0:T(8,128)(2,1)S(1)}, bf16[256,1024]{1,0:T(8,128)(2,1)}, u32[]{:S(2)}, u32[]{:S(2)}) %collective-permute-start.20) | collective-permute-done | bytes 524320 | tf_op jit(solution)/shard_map/ppermute | solution.py:190
  230.3 1.9 constant_dynamic-update-slice_fusion.4
  232.1 2.5 convolution_convert_fusion.6
  241.0 2.2 multiply_reduce_fusion
  243.2 1.7 multiply_convert_fusion
  256.2 2.1 fusion.25
  270.0 1.8 collective-permute-start.21
  274.2 1.9 multiply_reduce_fusion.5
  277.1 3.9 stack.233
  281.0 3.3 convolution_convert_fusion.5
  285.2 3.4 collective-permute-done.22
  290.0 2.1 add_convert_fusion
  292.4 1.9 collective-permute-start.26
  297.2 8.4 %collective-permute-done.24 = bf16[256,1024]{1,0:T(8,128)(2,1)S(1)} collective-permute-done((bf16[256,1024]{1,0:T(8,128)(2,1)S(1)}, bf16[256,1024]{1,0:T(8,128)(2,1)S(1)}, u32[]{:S(2)}, u32[]{:S(2)}) %collective-permute-start.24) | collective-permute-done | bytes 524320 | tf_op jit(solution)/shard_map/ppermute | solution.py:174
  306.6 11.2 %collective-permute-done.25 = bf16[256,1024]{1,0:T(8,128)(2,1)S(1)} collective-permute-done((bf16[256,1024]{1,0:T(8,128)(2,1)S(1)}, bf16[256,1024]{1,0:T(8,128)(2,1)S(1)}, u32[]{:S(2)}, u32[]{:S(2)}) %collective-permute-start.25) | collective-permute-done | bytes 524320 | tf_op jit(solution)/shard_map/ppermute | solution.py:174
  319.6 49.9 %all-reduce.7.cloned.1.call-done = (bf16[1024,704]{0,1:T(8,128)(2,1)}, bf16[1024,704]{0,1:T(8,128)(2,1)}, bf16[704,1024]{1,0:T(8,128)(2,1)}) async-done(((bf16[1024,704]{0,1:T(8,128)(2,1)}, bf16[1024,704]{0,1:T(8,128)(2,1)}, bf16[704,1024]{1,0:T(8,128)(2,1)}), (bf16[1024,704]{0,1:T(8,128)(2,1)}, bf16[1024,704]{0,1:T(8,128)(2,1)}, bf16[704,1024]{1,0:T(8,128)(2,1)})) %all-reduce.7.cloned.1.call-update) | async-done | bytes 4325392 | tf_op jit(solution)/shard_map/psum | solution.py:365
  373.2 2.4 reshape.2033
  375.6 2.5 dynamic-slice_convert_fusion
  381.0 10.0 %collective-permute-done.27 = bf16[2,2,58752]{2,1,0:T(2,128)(2,1)S(1)} collective-permute-done((bf16[2,2,58752]{2,1,0:T(2,128)(2,1)S(1)}, bf16[2,2,58752]{2,1,0:T(2,128)(2,1)S(1)}, u32[]{:S(2)}, u32[]{:S(2)}) %collective-permute-start.27) | collective-permute-done | bytes 470048 | tf_op jit(solution)/shard_map/ppermute | solution.py:213
  392.8 6.0 %collective-permute-done.28 = bf16[2,58752]{1,0:T(2,128)(2,1)S(1)} collective-permute-done((bf16[2,58752]{1,0:T(2,128)(2,1)S(1)}, bf16[2,58752]{1,0:T(2,128)(2,1)S(1)}, u32[]{:S(2)}, u32[]{:S(2)}) %collective-permute-start.28) | collective-permute-done | bytes 235040 | tf_op jit(solution)/shard_map/ppermute | solution.py:213
  402.0 4.7 collective-permute-done.29
  407.4 9.6 %collective-permute-done.30 = bf16[1,58752]{1,0:T(2,128)(2,1)S(1)} collective-permute-done((bf16[1,58752]{1,0:T(2,128)(2,1)S(1)}, bf16[1,58752]{1,0:T(2,128)(2,1)S(1)}, u32[]{:S(2)}, u32[]{:S(2)}) %collective-permute-start.30) | collective-permute-done | bytes 117536 | tf_op jit(solution)/shard_map/ppermute | solution.py:218
  418.0 6.6 %collective-permute-done.31 = bf16[2,58752]{1,0:T(2,128)(2,1)S(1)} collective-permute-done((bf16[2,58752]{1,0:T(2,128)(2,1)S(1)}, bf16[2,58752]{1,0:T(2,128)(2,1)S(1)}, u32[]{:S(2)}, u32[]{:S(2)}) %collective-permute-start.31) | collective-permute-done | bytes 235040 | tf_op jit(solution)/shard_map/ppermute | solution.py:218
  427.4 1.7 collective-permute-start.32
  429.1 9.2 %collective-permute-done.32 = bf16[4,58752]{1,0:T(4,128)(2,1)S(1)} collective-permute-done((bf16[4,58752]{1,0:T(4,128)(2,1)S(1)}, bf16[4,58752]{1,0:T(4,128)(2,1)S(1)}, u32[]{:S(2)}, u32[]{:S(2)}) %collective-permute-start.32) | collective-permute-done | bytes 470048 | tf_op jit(solution)/shard_map/ppermute | solution.py:218
  444.2 2.6 fusion.46
  446.8 1.9 convert_element_type.444
  448.7 1.9 convert_element_type.445
  450.7 1.9 convert_element_type.446
  456.4 4.9 %all-gather.2.cloned.1.call-done = bf16[1037,640]{0,1:T(8,128)(2,1)} async-done(((bf16[1037,160]{0,1:T(8,128)(2,1)}), bf16[1037,640]{0,1:T(8,128)(2,1)}) %all-gather.2.cloned.1.call-update) | async-done | bytes 1327376 | tf_op jit(solution)/shard_map/all_gather | solution.py:440
  463.1 3.2 slice.758
  466.3 3.2 copy.86
  (493 shorter events, 111.9 us)
Async XLA Ops:
  7.2 128.4 %copy-start = (bf16[704,1024]{1,0:T(8,128)(2,1)S(1)}, bf16[704,1024]{1,0:T(8,128)(2,1)}, u32[]{:S(2)}) copy-start(bf16[704,1024]{1,0:T(8,128)(2,1)} %param.21) | copy-start | bytes 4325380
  7.2 362.2 %all-reduce.7.cloned.1.call-start = ((), (), s32[]{:S(2)}) async-start(), calls=%async_computation.1 | async-start | bytes 8650752 | tf_op jit(solution)/shard_map/psum | solution.py:365
  7.3 8.7 %copy-start.141 = (s32[1,1024]{1,0:T(1,128)S(1)}, s32[1,1024]{1,0:T(1,128)}, u32[]{:S(2)}) copy-start(s32[1,1024]{1,0:T(1,128)} %param.13) | copy-start | bytes 12292
  9.2 8.3 %copy-start.142 = (f32[256]{0:T(256)}, f32[256]{0:T(256)S(1)}, u32[]{:S(2)}) copy-start(f32[256]{0:T(256)S(1)} %get-tuple-element.250) | copy-start | bytes 3076
  11.2 26.7 %collective-permute-start.1 = (bf16[256,1024]{1,0:T(8,128)(2,1)}, bf16[256,1024]{1,0:T(8,128)(2,1)}, u32[]{:S(2)}, u32[]{:S(2)}) collective-permute-start(bf16[256,1024]{1,0:T(8,128)(2,1)} %get-tuple-element.137), channel_id=1, source_target_pairs={{0,2},{1,3},{2,0},{3,1},{4,6},{5,7},{6,4},{7,5},{8,10},{9,11},{10,... | collective-permute-start | bytes 1572872 | tf_op jit(solution)/shard_map/ppermute | solution.py:190
  14.2 22.6 %collective-permute-start = (bf16[256,1024]{1,0:T(8,128)(2,1)}, bf16[256,1024]{1,0:T(8,128)(2,1)}, u32[]{:S(2)}, u32[]{:S(2)}) collective-permute-start(bf16[256,1024]{1,0:T(8,128)(2,1)} %get-tuple-element.137), channel_id=1, source_target_pairs={{0,1},{1,2},{2,3},{3,0},{4,5},{5,6},{6,7},{7,4},{8,9},{9,10},{10,1... | collective-permute-start | bytes 1572872 | tf_op jit(solution)/shard_map/ppermute | solution.py:190
  14.2 24.8 %collective-permute-start.2 = (bf16[256,1024]{1,0:T(8,128)(2,1)}, bf16[256,1024]{1,0:T(8,128)(2,1)}, u32[]{:S(2)}, u32[]{:S(2)}) collective-permute-start(bf16[256,1024]{1,0:T(8,128)(2,1)} %get-tuple-element.137), channel_id=1, source_target_pairs={{0,3},{1,0},{2,1},{3,2},{4,7},{5,4},{6,5},{7,6},{8,11},{9,8},{10,9... | collective-permute-start | bytes 1572872 | tf_op jit(solution)/shard_map/ppermute | solution.py:190
  17.6 22.6 %copy-start.78 = (bf16[1024,40]{0,1:T(8,128)(2,1)S(1)}, bf16[1024,40]{0,1:T(8,128)(2,1)}, u32[]{:S(2)}) copy-start(bf16[1024,40]{0,1:T(8,128)(2,1)} %param.15) | copy-start | bytes 245764
  42.3 14.2 %copy-start.83 = (f32[1024,1]{0,1:T(1,128)}, f32[1024,1]{0,1:T(1,128)S(1)}, u32[]{:S(2)}) copy-start(f32[1024,1]{0,1:T(1,128)S(1)} %get-tuple-element.224) | copy-start | bytes 12292
  42.3 14.2 %copy-start.85 = (f32[1024,1]{0,1:T(1,128)}, f32[1024,1]{0,1:T(1,128)S(1)}, u32[]{:S(2)}) copy-start(f32[1024,1]{0,1:T(1,128)S(1)} %get-tuple-element.239) | copy-start | bytes 12292
  42.3 14.2 %copy-start.87 = (f32[1024,1]{0,1:T(1,128)}, f32[1024,1]{0,1:T(1,128)S(1)}, u32[]{:S(2)}) copy-start(f32[1024,1]{0,1:T(1,128)S(1)} %get-tuple-element.241) | copy-start | bytes 12292
  42.3 14.2 %copy-start.89 = (f32[1024,1]{0,1:T(1,128)}, f32[1024,1]{0,1:T(1,128)S(1)}, u32[]{:S(2)}) copy-start(f32[1024,1]{0,1:T(1,128)S(1)} %get-tuple-element.240) | copy-start | bytes 12292
  42.3 14.2 %copy-start.91 = (f32[1024,1]{0,1:T(1,128)}, f32[1024,1]{0,1:T(1,128)S(1)}, u32[]{:S(2)}) copy-start(f32[1024,1]{0,1:T(1,128)S(1)} %get-tuple-element.242) | copy-start | bytes 12292
  43.0 7.8 %copy-start.95 = (f32[1024,1]{0,1:T(1,128)}, f32[1024,1]{0,1:T(1,128)S(1)}, u32[]{:S(2)}) copy-start(f32[1024,1]{0,1:T(1,128)S(1)} %get-tuple-element.208) | copy-start | bytes 12292
  43.1 13.5 %copy-start.93 = (f32[1024,1]{0,1:T(1,128)}, f32[1024,1]{0,1:T(1,128)S(1)}, u32[]{:S(2)}) copy-start(f32[1024,1]{0,1:T(1,128)S(1)} %get-tuple-element.205) | copy-start | bytes 12292
  44.7 11.9 %copy-start.37 = (f32[1024,640]{0,1:T(8,128)}, f32[1024,640]{0,1:T(8,128)S(1)}, u32[]{:S(2)}) copy-start(f32[1024,640]{0,1:T(8,128)S(1)} %fusion.226) | copy-start | bytes 7864324
  61.6 27.5 %copy-start.8 = (bf16[256,1024]{1,0:T(8,128)(2,1)S(1)}, bf16[256,1024]{1,0:T(8,128)(2,1)}, u32[]{:S(2)}) copy-start(bf16[256,1024]{1,0:T(8,128)(2,1)} %param.12) | copy-start | bytes 1572868
  61.7 28.4 %copy-start.82 = (f32[1024]{0:T(1024)S(1)}, f32[1024]{0:T(1024)}, u32[]{:S(2)}) copy-start(f32[1024]{0:T(1024)} %param.18) | copy-start | bytes 12292
  61.8 12.5 %collective-permute-start.3 = (bf16[256,1024]{1,0:T(8,128)(2,1)S(1)}, bf16[256,1024]{1,0:T(8,128)(2,1)S(1)}, u32[]{:S(2)}, u32[]{:S(2)}) collective-permute-start(bf16[256,1024]{1,0:T(8,128)(2,1)S(1)} %get-tuple-element.170), channel_id=1, source_target_pairs={{0,1},{1,2},{2,3},{3,0},{4,5},{5,6},{6,7},{7,4},{8,9},{9,10},{10,1... | collective-permute-start | bytes 1572872 | tf_op jit(solution)/shard_map/ppermute | solution.py:174
  61.8 14.1 %collective-permute-start.5 = (bf16[256,1024]{1,0:T(8,128)(2,1)S(1)}, bf16[256,1024]{1,0:T(8,128)(2,1)S(1)}, u32[]{:S(2)}, u32[]{:S(2)}) collective-permute-start(bf16[256,1024]{1,0:T(8,128)(2,1)S(1)} %get-tuple-element.171), channel_id=1, source_target_pairs={{0,3},{1,0},{2,1},{3,2},{4,7},{5,4},{6,5},{7,6},{8,11},{9,8},{10,9... | collective-permute-start | bytes 1572872 | tf_op jit(solution)/shard_map/ppermute | solution.py:174
  63.6 25.5 %collective-permute-start.4 = (bf16[256,1024]{1,0:T(8,128)(2,1)S(1)}, bf16[256,1024]{1,0:T(8,128)(2,1)S(1)}, u32[]{:S(2)}, u32[]{:S(2)}) collective-permute-start(bf16[256,1024]{1,0:T(8,128)(2,1)S(1)} %get-tuple-element.172), channel_id=1, source_target_pairs={{0,2},{1,3},{2,0},{3,1},{4,6},{5,7},{6,4},{7,5},{8,10},{9,11},{10,... | collective-permute-start | bytes 1572872 | tf_op jit(solution)/shard_map/ppermute | solution.py:174
  65.0 43.0 %collective-permute-start.13 = (bf16[256,1024]{1,0:T(8,128)(2,1)S(1)}, bf16[256,1024]{1,0:T(8,128)(2,1)S(1)}, u32[]{:S(2)}, u32[]{:S(2)}) collective-permute-start(bf16[256,1024]{1,0:T(8,128)(2,1)S(1)} %copy-done.51), channel_id=1, source_target_pairs={{0,2},{1,3},{2,0},{3,1},{4,6},{5,7},{6,4},{7,5},{8,10},{9,11},{10,... | collective-permute-start | bytes 1572872 | tf_op jit(solution)/shard_map/ppermute | solution.py:230
  65.6 42.4 %collective-permute-start.12 = (bf16[256,1024]{1,0:T(8,128)(2,1)S(1)}, bf16[256,1024]{1,0:T(8,128)(2,1)S(1)}, u32[]{:S(2)}, u32[]{:S(2)}) collective-permute-start(bf16[256,1024]{1,0:T(8,128)(2,1)S(1)} %copy-done.51), channel_id=1, source_target_pairs={{0,1},{1,2},{2,3},{3,0},{4,5},{5,6},{6,7},{7,4},{8,9},{9,10},{10,1... | collective-permute-start | bytes 1572872 | tf_op jit(solution)/shard_map/ppermute | solution.py:230
  74.3 35.3 %collective-permute-start.14 = (bf16[256,1024]{1,0:T(8,128)(2,1)S(1)}, bf16[256,1024]{1,0:T(8,128)(2,1)S(1)}, u32[]{:S(2)}, u32[]{:S(2)}) collective-permute-start(bf16[256,1024]{1,0:T(8,128)(2,1)S(1)} %copy-done.51), channel_id=1, source_target_pairs={{0,3},{1,0},{2,1},{3,2},{4,7},{5,4},{6,5},{7,6},{8,11},{9,8},{10,9... | collective-permute-start | bytes 1572872 | tf_op jit(solution)/shard_map/ppermute | solution.py:230
  89.5 18.6 %copy-start.5 = (f32[256,1024]{1,0:T(8,128)}, f32[256,1024]{1,0:T(8,128)S(1)}, u32[]{:S(2)}) copy-start(f32[256,1024]{1,0:T(8,128)S(1)} %get-tuple-element.135) | copy-start | bytes 3145732
  90.3 41.9 %copy-start.150 = (bf16[1024,704]{0,1:T(8,128)(2,1)S(1)}, bf16[1024,704]{0,1:T(8,128)(2,1)}, u32[]{:S(2)}) copy-start(bf16[1024,704]{0,1:T(8,128)(2,1)} %param.20) | copy-start | bytes 4325380
  90.3 30.5 %collective-permute-start.8 = (bf16[256,1024]{1,0:T(8,128)(2,1)S(1)}, bf16[256,1024]{1,0:T(8,128)(2,1)S(1)}, u32[]{:S(2)}, u32[]{:S(2)}) collective-permute-start(bf16[256,1024]{1,0:T(8,128)(2,1)S(1)} %multiply_convert_fusion.5), channel_id=1, source_target_pairs={{0,3},{1,0},{2,1},{3,2},{4,7},{5,4},{6,5},{7,6},{8,11},{9,8},{10,9... | collective-permute-start | bytes 1572872 | tf_op jit(solution)/shard_map/ppermute | solution.py:230
  90.4 41.8 %collective-permute-start.7 = (bf16[256,1024]{1,0:T(8,128)(2,1)S(1)}, bf16[256,1024]{1,0:T(8,128)(2,1)S(1)}, u32[]{:S(2)}, u32[]{:S(2)}) collective-permute-start(bf16[256,1024]{1,0:T(8,128)(2,1)S(1)} %multiply_convert_fusion.5), channel_id=1, source_target_pairs={{0,2},{1,3},{2,0},{3,1},{4,6},{5,7},{6,4},{7,5},{8,10},{9,11},{10,... | collective-permute-start | bytes 1572872 | tf_op jit(solution)/shard_map/ppermute | solution.py:230
  108.0 24.2 %collective-permute-start.6 = (bf16[256,1024]{1,0:T(8,128)(2,1)S(1)}, bf16[256,1024]{1,0:T(8,128)(2,1)S(1)}, u32[]{:S(2)}, u32[]{:S(2)}) collective-permute-start(bf16[256,1024]{1,0:T(8,128)(2,1)S(1)} %multiply_convert_fusion.5), channel_id=1, source_target_pairs={{0,1},{1,2},{2,3},{3,0},{4,5},{5,6},{6,7},{7,4},{8,9},{9,10},{10,1... | collective-permute-start | bytes 1572872 | tf_op jit(solution)/shard_map/ppermute | solution.py:230
  109.6 24.3 %copy-start.149 = (bf16[1024,704]{0,1:T(8,128)(2,1)S(1)}, bf16[1024,704]{0,1:T(8,128)(2,1)}, u32[]{:S(2)}) copy-start(bf16[1024,704]{0,1:T(8,128)(2,1)} %param.19) | copy-start | bytes 4325380
  154.0 12.5 %collective-permute-start.15 = (bf16[256,1024]{1,0:T(8,128)(2,1)S(1)}, bf16[256,1024]{1,0:T(8,128)(2,1)S(1)}, u32[]{:S(2)}, u32[]{:S(2)}) collective-permute-start(bf16[256,1024]{1,0:T(8,128)(2,1)S(1)} %get-tuple-element.164), channel_id=1, source_target_pairs={{0,1},{1,2},{2,3},{3,0},{4,5},{5,6},{6,7},{7,4},{8,9},{9,10},{10,1... | collective-permute-start | bytes 1572872 | tf_op jit(solution)/shard_map/ppermute | solution.py:241
  154.0 14.8 %collective-permute-start.17 = (bf16[256,1024]{1,0:T(8,128)(2,1)S(1)}, bf16[256,1024]{1,0:T(8,128)(2,1)S(1)}, u32[]{:S(2)}, u32[]{:S(2)}) collective-permute-start(bf16[256,1024]{1,0:T(8,128)(2,1)S(1)} %get-tuple-element.165), channel_id=1, source_target_pairs={{0,3},{1,0},{2,1},{3,2},{4,7},{5,4},{6,5},{7,6},{8,11},{9,8},{10,9... | collective-permute-start | bytes 1572872 | tf_op jit(solution)/shard_map/ppermute | solution.py:241
  155.8 25.5 %collective-permute-start.16 = (bf16[256,1024]{1,0:T(8,128)(2,1)S(1)}, bf16[256,1024]{1,0:T(8,128)(2,1)S(1)}, u32[]{:S(2)}, u32[]{:S(2)}) collective-permute-start(bf16[256,1024]{1,0:T(8,128)(2,1)S(1)} %get-tuple-element.166), channel_id=1, source_target_pairs={{0,2},{1,3},{2,0},{3,1},{4,6},{5,7},{6,4},{7,5},{8,10},{9,11},{10,... | collective-permute-start | bytes 1572872 | tf_op jit(solution)/shard_map/ppermute | solution.py:241
  159.1 22.1 %copy-start.6 = (f32[256,1024]{1,0:T(8,128)S(1)}, f32[256,1024]{1,0:T(8,128)}, u32[]{:S(2)}) copy-start(f32[256,1024]{1,0:T(8,128)} %copy-done.5) | copy-start | bytes 3145732
  159.1 22.1 %copy-start.38 = (bf16[1024,1024]{1,0:T(8,128)(2,1)S(1)}, bf16[1024,1024]{1,0:T(8,128)(2,1)}, u32[]{:S(2)}) copy-start(bf16[1024,1024]{1,0:T(8,128)(2,1)} %add_convert_fusion.1) | copy-start | bytes 6291460
  159.3 42.7 %copy-start.52 = (bf16[256,1024]{1,0:T(8,128)(2,1)S(1)}, bf16[256,1024]{1,0:T(8,128)(2,1)}, u32[]{:S(2)}) copy-start(bf16[256,1024]{1,0:T(8,128)(2,1)} %param.22) | copy-start | bytes 1572868
  159.3 42.7 %copy-start.147 = (f32[256]{0:T(256)S(1)}, f32[256]{0:T(256)}, u32[]{:S(2)}) copy-start(f32[256]{0:T(256)} %get-tuple-element.251) | copy-start | bytes 3076
  159.3 29.7 %collective-permute-start.9 = (bf16[256,1024]{1,0:T(8,128)(2,1)S(1)}, bf16[256,1024]{1,0:T(8,128)(2,1)S(1)}, u32[]{:S(2)}, u32[]{:S(2)}) collective-permute-start(bf16[256,1024]{1,0:T(8,128)(2,1)S(1)} %get-tuple-element.167), channel_id=1, source_target_pairs={{0,1},{1,2},{2,3},{3,0},{4,5},{5,6},{6,7},{7,4},{8,9},{9,10},{10,1... | collective-permute-start | bytes 1572872 | tf_op jit(solution)/shard_map/ppermute | solution.py:241
  159.3 31.2 %collective-permute-start.11 = (bf16[256,1024]{1,0:T(8,128)(2,1)S(1)}, bf16[256,1024]{1,0:T(8,128)(2,1)S(1)}, u32[]{:S(2)}, u32[]{:S(2)}) collective-permute-start(bf16[256,1024]{1,0:T(8,128)(2,1)S(1)} %get-tuple-element.168), channel_id=1, source_target_pairs={{0,3},{1,0},{2,1},{3,2},{4,7},{5,4},{6,5},{7,6},{8,11},{9,8},{10,9... | collective-permute-start | bytes 1572872 | tf_op jit(solution)/shard_map/ppermute | solution.py:241
  166.5 35.5 %collective-permute-start.10 = (bf16[256,1024]{1,0:T(8,128)(2,1)S(1)}, bf16[256,1024]{1,0:T(8,128)(2,1)S(1)}, u32[]{:S(2)}, u32[]{:S(2)}) collective-permute-start(bf16[256,1024]{1,0:T(8,128)(2,1)S(1)} %get-tuple-element.169), channel_id=1, source_target_pairs={{0,2},{1,3},{2,0},{3,1},{4,6},{5,7},{6,4},{7,5},{8,10},{9,11},{10,... | collective-permute-start | bytes 1572872 | tf_op jit(solution)/shard_map/ppermute | solution.py:241
  205.8 13.0 %collective-permute-start.18 = (bf16[256,1024]{1,0:T(8,128)(2,1)S(1)}, bf16[256,1024]{1,0:T(8,128)(2,1)S(1)}, u32[]{:S(2)}, u32[]{:S(2)}) collective-permute-start(bf16[256,1024]{1,0:T(8,128)(2,1)S(1)} %get-tuple-element.133), channel_id=1, source_target_pairs={{0,1},{1,2},{2,3},{3,0},{4,5},{5,6},{6,7},{7,4},{8,9},{9,10},{10,1... | collective-permute-start | bytes 1572872 | tf_op jit(solution)/shard_map/ppermute | solution.py:190
  206.5 14.9 %collective-permute-start.19 = (bf16[256,1024]{1,0:T(8,128)(2,1)S(1)}, bf16[256,1024]{1,0:T(8,128)(2,1)}, u32[]{:S(2)}, u32[]{:S(2)}) collective-permute-start(bf16[256,1024]{1,0:T(8,128)(2,1)S(1)} %get-tuple-element.133), channel_id=1, source_target_pairs={{0,2},{1,3},{2,0},{3,1},{4,6},{5,7},{6,4},{7,5},{8,10},{9,11},{10,... | collective-permute-start | bytes 1572872 | tf_op jit(solution)/shard_map/ppermute | solution.py:190
  208.0 22.3 %collective-permute-start.20 = (bf16[256,1024]{1,0:T(8,128)(2,1)S(1)}, bf16[256,1024]{1,0:T(8,128)(2,1)}, u32[]{:S(2)}, u32[]{:S(2)}) collective-permute-start(bf16[256,1024]{1,0:T(8,128)(2,1)S(1)} %get-tuple-element.133), channel_id=1, source_target_pairs={{0,3},{1,0},{2,1},{3,2},{4,7},{5,4},{6,5},{7,6},{8,11},{9,8},{10,9... | collective-permute-start | bytes 1572872 | tf_op jit(solution)/shard_map/ppermute | solution.py:190
  209.5 251.8 %all-gather.2.cloned.1.call-start = ((), (), s32[]{:S(2)}) async-start(), calls=%async_computation | async-start | bytes 1843200 | tf_op jit(solution)/shard_map/all_gather | solution.py:440
  209.6 22.6 %copy-start.76 = (bf16[256,1024]{1,0:T(8,128)(2,1)S(1)}, bf16[256,1024]{1,0:T(8,128)(2,1)}, u32[]{:S(2)}) copy-start(bf16[256,1024]{1,0:T(8,128)(2,1)} %param.17) | copy-start | bytes 1572868
  270.0 15.1 %collective-permute-start.21 = (bf16[1024,160]{0,1:T(8,128)(2,1)}, bf16[1024,160]{0,1:T(8,128)(2,1)}, u32[]{:S(2)}, u32[]{:S(2)}) collective-permute-start(bf16[1024,160]{0,1:T(8,128)(2,1)} %get-tuple-element.173), channel_id=1, source_target_pairs={{0,1},{1,2},{2,3},{3,0},{4,5},{5,6},{6,7},{7,4},{8,9},{9,10},{10,1... | collective-permute-start | bytes 983048 | tf_op jit(solution)/shard_map/ppermute | solution.py:174
  271.9 13.3 %collective-permute-start.23 = (bf16[1024,160]{0,1:T(8,128)(2,1)}, bf16[1024,160]{0,1:T(8,128)(2,1)}, u32[]{:S(2)}, u32[]{:S(2)}) collective-permute-start(bf16[1024,160]{0,1:T(8,128)(2,1)} %get-tuple-element.174), channel_id=1, source_target_pairs={{0,3},{1,0},{2,1},{3,2},{4,7},{5,4},{6,5},{7,6},{8,11},{9,8},{10,9... | collective-permute-start | bytes 983048 | tf_op jit(solution)/shard_map/ppermute | solution.py:174
  272.9 15.6 %collective-permute-start.22 = (bf16[1024,160]{0,1:T(8,128)(2,1)}, bf16[1024,160]{0,1:T(8,128)(2,1)}, u32[]{:S(2)}, u32[]{:S(2)}) collective-permute-start(bf16[1024,160]{0,1:T(8,128)(2,1)} %get-tuple-element.175), channel_id=1, source_target_pairs={{0,2},{1,3},{2,0},{3,1},{4,6},{5,7},{6,4},{7,5},{8,10},{9,11},{10,... | collective-permute-start | bytes 983048 | tf_op jit(solution)/shard_map/ppermute | solution.py:174
  292.3 13.3 %collective-permute-start.24 = (bf16[256,1024]{1,0:T(8,128)(2,1)S(1)}, bf16[256,1024]{1,0:T(8,128)(2,1)S(1)}, u32[]{:S(2)}, u32[]{:S(2)}) collective-permute-start(bf16[256,1024]{1,0:T(8,128)(2,1)S(1)} %get-tuple-element.161), channel_id=1, source_target_pairs={{0,1},{1,2},{2,3},{3,0},{4,5},{5,6},{6,7},{7,4},{8,9},{9,10},{10,1... | collective-permute-start | bytes 1572872 | tf_op jit(solution)/shard_map/ppermute | solution.py:174
  292.4 14.2 %collective-permute-start.26 = (bf16[256,1024]{1,0:T(8,128)(2,1)S(1)}, bf16[256,1024]{1,0:T(8,128)(2,1)S(1)}, u32[]{:S(2)}, u32[]{:S(2)}) collective-permute-start(bf16[256,1024]{1,0:T(8,128)(2,1)S(1)} %get-tuple-element.162), channel_id=1, source_target_pairs={{0,3},{1,0},{2,1},{3,2},{4,7},{5,4},{6,5},{7,6},{8,11},{9,8},{10,9... | collective-permute-start | bytes 1572872 | tf_op jit(solution)/shard_map/ppermute | solution.py:174
  294.3 23.6 %copy-start.9 = (bf16[256,1024]{1,0:T(8,128)(2,1)S(1)}, bf16[256,1024]{1,0:T(8,128)(2,1)}, u32[]{:S(2)}) copy-start(bf16[256,1024]{1,0:T(8,128)(2,1)} %param.12) | copy-start | bytes 1572868
  294.3 23.6 %copy-start.128 = (f32[1024]{0:T(1024)S(1)}, f32[1024]{0:T(1024)}, u32[]{:S(2)}) copy-start(f32[1024]{0:T(1024)} %param.14) | copy-start | bytes 12292
  294.3 23.6 %copy-start.143 = (f32[256]{0:T(256)S(1)}, f32[256]{0:T(256)}, u32[]{:S(2)}) copy-start(f32[256]{0:T(256)} %copy-done.142) | copy-start | bytes 3076
  294.3 23.6 %collective-permute-start.25 = (bf16[256,1024]{1,0:T(8,128)(2,1)S(1)}, bf16[256,1024]{1,0:T(8,128)(2,1)S(1)}, u32[]{:S(2)}, u32[]{:S(2)}) collective-permute-start(bf16[256,1024]{1,0:T(8,128)(2,1)S(1)} %get-tuple-element.163), channel_id=1, source_target_pairs={{0,2},{1,3},{2,0},{3,1},{4,6},{5,7},{6,4},{7,5},{8,10},{9,11},{10,... | collective-permute-start | bytes 1572872 | tf_op jit(solution)/shard_map/ppermute | solution.py:174
  297.2 22.1 %copy-start.144 = (bf16[1024]{0:T(1024)(128)(2,1)S(1)}, bf16[1024]{0:T(1024)(128)(2,1)}, u32[]{:S(2)}) copy-start(bf16[1024]{0:T(1024)(128)(2,1)} %get-tuple-element.84) | copy-start | bytes 6148
  297.2 22.3 %copy-start.57 = (bf16[1024,160]{0,1:T(8,128)(2,1)S(1)}, bf16[1024,160]{0,1:T(8,128)(2,1)}, u32[]{:S(2)}) copy-start(bf16[1024,160]{0,1:T(8,128)(2,1)} %convolution_convert_fusion.7) | copy-start | bytes 983044
  297.2 72.2 %copy-start.72 = (bf16[256,1024]{1,0:T(8,128)(2,1)S(1)}, bf16[256,1024]{1,0:T(8,128)(2,1)}, u32[]{:S(2)}) copy-start(bf16[256,1024]{1,0:T(8,128)(2,1)} %convolution_convert_fusion.5) | copy-start | bytes 1572868
  297.2 73.1 %copy-start.77 = (bf16[1024,40]{0,1:T(8,128)(2,1)S(1)}, bf16[1024,40]{0,1:T(8,128)(2,1)}, u32[]{:S(2)}) copy-start(bf16[1024,40]{0,1:T(8,128)(2,1)} %convolution_convert_fusion.8) | copy-start | bytes 245764
  378.6 12.4 %collective-permute-start.27 = (bf16[2,2,58752]{2,1,0:T(2,128)(2,1)S(1)}, bf16[2,2,58752]{2,1,0:T(2,128)(2,1)S(1)}, u32[]{:S(2)}, u32[]{:S(2)}) collective-permute-start(bf16[2,2,58752]{2,1,0:T(2,128)(2,1)S(1)} %bitcast.467), channel_id=1, source_target_pairs={{0,4},{4,0},{8,12},{12,8},{16,20},{20,16},{24,28},{28,24},{1,5},{5... | collective-permute-start | bytes 1410056 | tf_op jit(solution)/shard_map/ppermute | solution.py:213
  392.3 6.5 %collective-permute-start.28 = (bf16[2,58752]{1,0:T(2,128)(2,1)S(1)}, bf16[2,58752]{1,0:T(2,128)(2,1)S(1)}, u32[]{:S(2)}, u32[]{:S(2)}) collective-permute-start(bf16[2,58752]{1,0:T(2,128)(2,1)S(1)} %bitcast.468), channel_id=1, source_target_pairs={{0,8},{4,12},{8,0},{12,4},{16,24},{20,28},{24,16},{28,20},{1,9},{5... | collective-permute-start | bytes 705032 | tf_op jit(solution)/shard_map/ppermute | solution.py:213
  399.9 6.8 %collective-permute-start.29 = (bf16[58752]{0:T(1024)(128)(2,1)S(1)}, bf16[58752]{0:T(1024)(128)(2,1)S(1)}, u32[]{:S(2)}, u32[]{:S(2)}) collective-permute-start(bf16[58752]{0:T(1024)(128)(2,1)S(1)} %convert_reduce_fusion), channel_id=1, source_target_pairs={{0,16},{4,20},{8,24},{12,28},{16,0},{20,4},{24,8},{28,12},{1,17},{... | collective-permute-start | bytes 352520 | tf_op jit(solution)/shard_map/ppermute | solution.py:213
  406.9 10.2 %collective-permute-start.30 = (bf16[1,58752]{1,0:T(2,128)(2,1)S(1)}, bf16[1,58752]{1,0:T(2,128)(2,1)S(1)}, u32[]{:S(2)}, u32[]{:S(2)}) collective-permute-start(bf16[1,58752]{1,0:T(2,128)(2,1)S(1)} %broadcast_in_dim.38), channel_id=1, source_target_pairs={{0,16},{4,20},{8,24},{12,28},{16,0},{20,4},{24,8},{28,12},{1,17},{... | collective-permute-start | bytes 352520 | tf_op jit(solution)/shard_map/ppermute | solution.py:218
  417.9 6.7 %collective-permute-start.31 = (bf16[2,58752]{1,0:T(2,128)(2,1)S(1)}, bf16[2,58752]{1,0:T(2,128)(2,1)S(1)}, u32[]{:S(2)}, u32[]{:S(2)}) collective-permute-start(bf16[2,58752]{1,0:T(2,128)(2,1)S(1)} %maximum_bitcast_fusion), channel_id=1, source_target_pairs={{0,8},{4,12},{8,0},{12,4},{16,24},{20,28},{24,16},{28,20},{1,9},{5... | collective-permute-start | bytes 705032 | tf_op jit(solution)/shard_map/ppermute | solution.py:218
  427.4 10.9 %collective-permute-start.32 = (bf16[4,58752]{1,0:T(4,128)(2,1)S(1)}, bf16[4,58752]{1,0:T(4,128)(2,1)S(1)}, u32[]{:S(2)}, u32[]{:S(2)}) collective-permute-start(bf16[4,58752]{1,0:T(4,128)(2,1)S(1)} %reshape.2029), channel_id=1, source_target_pairs={{0,4},{4,0},{8,12},{12,8},{16,20},{20,16},{24,28},{28,24},{1,5},{5... | collective-permute-start | bytes 1410056 | tf_op jit(solution)/shard_map/ppermute | solution.py:218
  (126 other events, 453.6 us)
Sparse Core Ops, SparseCore 0:
  209.6 159.7 all-reduce.6
  444.2 17.0 all-gather.1
